TPU v7x, 128 devices: a whole 4x4x4 slice. The times are simulated.
128 devices in a mesh: member: 4 (over x_lo, core), band: 32 (over y, z, x_hi).
Axes of the slice: x: 4 (x_hi: 2, x_lo: 2; x = x_hi * 2 + x_lo), y: 4, z: 4, core: 2. Of those that a mesh axis runs over, the one named last changes fastest.
Arguments:
- parent_state: float32 [32, 3, 512, 4096], P('member', None, 'band'), parts along dimension 0, may hold values from -6 to 6
- nest_state: float32 [32, 3, 768, 768], P('member', None, 'band'), parts along dimension 0, may hold values from -6 to 6
- offsets: int32 [32, 2], P('member'), parts along dimension 0, may hold values from 2 to 3838, as said below
Outputs:
- parent_out: float32 [32, 3, 512, 4096], P('member', None, 'band'), parts along dimension 0
- nest_out: float32 [32, 3, 768, 768], P('member', None, 'band'), parts along dimension 0
There are 4 independent parts, one for each index of `member`. A program takes and returns all parts, laid end to end along the dimension named above; each array names one. Nothing has to cross between parts.
Inputs may be any that keep to these rules, and one draw needn't show every extreme that they name: Column 0 holds row offsets from 2 to 254, column 1 column offsets from 2 to 3838; in each column some member takes the lowest and some member the highest of its range.
All inputs are finite; a program needn't handle non-finite values.
Results may differ from a plain program's by a relative error of at most 0.00012.
Values sent between devices are 32-bit elements; how exact they have to be, the bound alone decides.
No kernel may reach another device: no remote copies, remote signals or barrier semaphores. Data moves between devices by JAX's collectives and lax.ppermute only.
A program may use at most 256 MiB of HBM per device.

v0:
```python
import jax
import jax.numpy as jnp
from jax import lax
from jax.sharding import PartitionSpec as P

NSTEPS = 3


courant = 0.9
friction = 0.02
rotation = 0.05
highest = lax.Precision.HIGHEST


def with_halo(cells, sides, width):
    for axis, dim in sides:
        count = lax.axis_size(axis)
        ends = count - 1
        head = lax.slice_in_dim(cells, 0, width, axis=dim)
        tail = lax.slice_in_dim(cells, cells.shape[dim] - width, cells.shape[dim], axis=dim)
        cells = jnp.concatenate(
            [
                lax.ppermute(tail, axis, [(i, (i + 1) % count) for i in range(ends)]),
                cells,
                lax.ppermute(head, axis, [((i + 1) % count, i) for i in range(ends)]),
            ],
            axis=dim,
        )
    return cells


def interp_matrix(fine, coarse_count):
    rows = jnp.arange(fine, dtype=jnp.int32)[:, None] + 1
    cols = jnp.arange(coarse_count, dtype=jnp.int32)[None, :]
    base = rows // 3
    frac = rows % 3
    upper = frac.astype(jnp.float32) / 3.0
    lower = (3 - frac).astype(jnp.float32) / 3.0
    return jnp.where(cols == base, lower, 0.0) + jnp.where(cols == base + 1, upper, 0.0)


def shift_cols(field):
    return 0.5 * (jnp.roll(field, -1, axis=-1) - jnp.roll(field, 1, axis=-1))


def parent_rows_ext(fields):
    return with_halo(fields, (("band", 2),), 1)


def pad_tile(fields, side_part, ends_part, first_band, last_band):
    extended = with_halo(fields, (("band", 2),), 1)
    top_row = jnp.where(first_band, ends_part[:, :, 0], extended[:, :, 0])
    bottom_row = jnp.where(last_band, ends_part[:, :, 1], extended[:, :, -1])
    rows_full = jnp.concatenate(
        [top_row[:, :, None], extended[:, :, 1:-1], bottom_row[:, :, None]], axis=2
    )
    return jnp.concatenate(
        [side_part[:, :, 0][..., None], rows_full, side_part[:, :, 1][..., None]], axis=3
    )


def nest_step(state, side, ends, first_band, last_band):
    height, zonal, meridional = (state[:, 0], state[:, 1], state[:, 2])
    flows = pad_tile(state[:, 1:3], side[:, 1:3], ends[:, 1:3], first_band, last_band)
    height_new = height - courant * (
        0.5 * (flows[:, 0, 1:-1, 2:] - flows[:, 0, 1:-1, :-2])
        + 0.5 * (flows[:, 1, 2:, 1:-1] - flows[:, 1, :-2, 1:-1])
    )
    padded = pad_tile(height_new[:, None], side[:, 0:1], ends[:, 0:1], first_band, last_band)[:, 0]
    zonal_new = (
        (1.0 - friction) * zonal
        - courant * (0.5 * (padded[:, 1:-1, 2:] - padded[:, 1:-1, :-2]))
        + rotation * meridional
    )
    merid_new = (
        (1.0 - friction) * meridional
        - courant * (0.5 * (padded[:, 2:, 1:-1] - padded[:, :-2, 1:-1]))
        - rotation * zonal
    )
    return jnp.stack([height_new, zonal_new, merid_new], axis=1)


def per_device(parent_state, nest_state, offsets):
    members = parent_state.shape[0]
    band_rows = parent_state.shape[2]
    nest_rows = nest_state.shape[2]
    nest_width = nest_state.shape[3]
    tile_coarse = nest_rows // 3
    span = nest_width // 3
    bands = lax.axis_size("band")
    band_index = lax.axis_index("band")
    first_band = band_index == 0
    last_band = band_index == bands - 1
    rows_off = offsets[:, 0]
    cols_off = offsets[:, 1]
    height, zonal, meridional = (parent_state[:, 0], parent_state[:, 1], parent_state[:, 2])
    flows = parent_rows_ext(parent_state[:, 1:3])
    height_new = height - courant * (shift_cols(zonal) + 0.5 * (flows[:, 1, 2:] - flows[:, 1, :-2]))
    height_ext = parent_rows_ext(height_new[:, None])[:, 0]
    zonal_new = (1.0 - friction) * zonal - courant * shift_cols(height_new) + rotation * meridional
    merid_new = (
        (1.0 - friction) * meridional
        - courant * (0.5 * (height_ext[:, 2:] - height_ext[:, :-2]))
        - rotation * zonal
    )
    stepped = jnp.stack([height_new, zonal_new, merid_new], axis=1)

    def take_pair(field, col0):
        return lax.dynamic_slice_in_dim(field, col0, 2, axis=2)

    near = jax.vmap(take_pair)(stepped, cols_off - 1)
    far = jax.vmap(take_pair)(stepped, cols_off + span - 1)
    west = 2.0 / 3.0 * near[..., 0] + 1.0 / 3.0 * near[..., 1]
    east = 1.0 / 3.0 * far[..., 0] + 2.0 / 3.0 * far[..., 1]
    strip = jnp.stack([west, east], axis=2)
    column_all = lax.all_gather(strip, "band", axis=3, tiled=True)

    def side_window(columns, row0):
        return lax.dynamic_slice_in_dim(
            columns, row0 - 1 + band_index * tile_coarse, tile_coarse + 2, axis=2
        )

    side_rows = jax.vmap(side_window)(column_all, rows_off)
    side = jnp.einsum(
        "ip,mfsp->mfsi", interp_matrix(nest_rows + 2, tile_coarse + 2), side_rows, precision=highest
    )
    global_rows = band_index * band_rows + jnp.arange(band_rows, dtype=jnp.int32)
    row_start = rows_off[:, None]
    top_weight = jnp.where(global_rows[None, :] == row_start - 1, 2.0 / 3.0, 0.0) + jnp.where(
        global_rows[None, :] == row_start, 1.0 / 3.0, 0.0
    )
    bottom_weight = jnp.where(
        global_rows[None, :] == row_start + span - 1, 1.0 / 3.0, 0.0
    ) + jnp.where(global_rows[None, :] == row_start + span, 2.0 / 3.0, 0.0)
    row_weights = jnp.stack([top_weight, bottom_weight], axis=1)
    partial_rows = jnp.einsum("msl,mfln->mfsn", row_weights, stepped, precision=highest)
    ends_full = lax.psum(partial_rows, "band")

    def ends_window(rows_pair, col0):
        return lax.dynamic_slice_in_dim(rows_pair, col0 - 1, span + 2, axis=2)

    ends_cols = jax.vmap(ends_window)(ends_full, cols_off)
    inner_weights = interp_matrix(nest_width + 2, span + 2)[1:-1]
    ends = jnp.einsum("jq,mfsq->mfsj", inner_weights, ends_cols, precision=highest)
    nest = nest_state
    for _ in range(NSTEPS):
        nest = nest_step(nest, side, ends, first_band, last_band)
    coarse = nest.reshape(members, 3, tile_coarse, 3, span, 3).mean(axis=(3, 5))
    whole = lax.all_gather(coarse, "band", axis=2, tiled=True)
    padded_whole = jnp.pad(whole, ((0, 0), (0, 0), (band_rows, band_rows), (0, 0)))

    def band_block(block_rows, row0):
        begin = jnp.clip(band_index * band_rows - row0 + band_rows, 0, span + band_rows)
        return lax.dynamic_slice_in_dim(block_rows, begin, band_rows, axis=1)

    patch = jax.vmap(band_block)(padded_whole, rows_off)
    relative_rows = global_rows[None, :] - rows_off[:, None]
    covered = (relative_rows >= 0) & (relative_rows < span)

    def place(field, block_patch, covered_rows, col0):
        current = lax.dynamic_slice_in_dim(field, col0, span, axis=2)
        merged = jnp.where(covered_rows[None, :, None], block_patch, current)
        return lax.dynamic_update_slice_in_dim(field, merged, col0, axis=2)

    parent_out = jax.vmap(place)(stepped, patch, covered, cols_off)
    return (parent_out, nest)


def solution(mesh):
    in_specs = (P("member", None, "band", None), P("member", None, "band", None), P("member", None))
    out_specs = (P("member", None, "band", None), P("member", None, "band", None))
    return jax.shard_map(
        per_device, mesh=mesh, in_specs=in_specs, out_specs=out_specs, check_vma=False
    )
```

profile of v0, /device:TPU:1, one launch (start us, length us, event | category | flops | bytes accessed | tf_op | source)
XLA Modules:
  0.0 843.9 jit_solution(13168513329500485766)
XLA Ops:
  9.0 6.1 collective-permute-start.4
  17.0 2.8 fusion.100
  20.0 5.6 collective-permute-start.1
  31.3 2.3 slice.289
  33.6 3.6 fusion.102
  37.3 4.8 copy.344
  47.6 3.0 fusion.9
  52.9 6.7 fusion.13
  61.9 6.3 collective-permute-start.2
  77.6 3.1 fusion.3
  80.8 3.1 pad_maximum_fusion
  83.9 4.4 convolution_bitcast_fusion
  88.4 48.5 %copy.296 = f32[8,3,16,4096]{2,1,0,3:T(4,128)} copy(f32[8,3,16,4096]{3,2,1,0:T(8,128)} %pad_maximum_fusion) | data formatting | bytes 12582912 | tf_op jit(solution)/shard_map/stack | solution.py:106
  139.7 99.4 %all_gather.6 = f32[8,3,2,512]{0,2,1,3:T(2,128)S(1)} all-gather(f32[8,3,2,16]{0,2,1,3:T(2,128)S(1)} %copy.304), channel_id=1, replica_groups=mesh['member'=4,'band'=32] {'band'}, dimensions={3}, use_global_device_ids=true | all-gather | bytes 101376 | tf_op jit(solution)/shard_map/all_gather | solution.py:116
  239.1 7.4 copy.305
  246.5 2.9 gather_fusion.3
  250.2 175.3 %all-reduce.7.cloned.1.call-done = f32[8,3,2,4096]{3,2,1,0:T(2,128)} async-done(((f32[8,3,2,4096]{3,2,1,0:T(2,128)}), f32[8,3,2,4096]{3,2,1,0:T(2,128)}) %all-reduce.7.cloned.1.call-update) | async-done | bytes 786448 | tf_op jit(solution)/shard_map/psum | solution.py:137
  425.5 36.1 %copy.291 = f32[8,3,2,4096]{1,2,0,3:T(2,128)} copy(f32[8,3,2,4096]{3,2,1,0:T(2,128)} %all-reduce.7.cloned.1.call-done) | data formatting | bytes 1572864 | tf_op jit(solution)/shard_map/psum | solution.py:137
  461.7 5.5 gather_fusion
  467.1 2.6 copy.292
  473.2 4.5 collective-permute-start.6
  479.5 4.2 collective-permute-done.7
  486.7 5.5 collective-permute-start.8
  493.8 5.2 collective-permute-start.10
  500.3 4.8 collective-permute-done.11
  507.2 6.1 collective-permute-start.12
  515.0 5.8 collective-permute-start.14
  522.2 14.0 %copy.319 = f32[8,1,24,768]{0,1,3,2:T(1,128)} copy(f32[8,1,24,768]{3,0,2,1:T(8,128)S(1)} %fusion.34) | data formatting | bytes 1179648 | tf_op jit(solution)/shard_map/sub | solution.py:65
  537.8 5.0 copy.340
  542.8 5.1 copy.341
  548.0 50.1 %maximum_reduce_fusion = f32[8,3,8,256]{0,1,3,2:T(4,128)} fusion(f32[8,1,8,3,256,3]{0,1,5,4,3,2:T(1,128)} %bitcast.154, f32[8,1,8,3,256,3]{0,1,5,4,3,2:T(1,128)} %bitcast.153, f32[8,1,8,3,256,3]{0,1,5,4,3,2:T(1,128)} %bitcast.152), kind=kLoop, calls=%fused_computation.9 | loop fusion | flops 1277952 | bytes 1966080 | tf_op jit(solution)/shard_map/reduce_sum | solution.py:148
  598.1 2.7 copy.326
  601.7 6.8 gather_fusion.5
  608.5 3.7 copy.330
  612.3 1.7 copy.332
  614.1 118.3 %all-gather.2.cloned.1.call-done = f32[8,3,256,256]{3,0,1,2:T(8,128)} async-done(((f32[8,3,8,256]{3,0,1,2:T(8,128)}), f32[8,3,256,256]{3,0,1,2:T(8,128)}) %all-gather.2.cloned.1.call-update) | async-done | bytes 6291472 | tf_op jit(solution)/shard_map/all_gather | solution.py:149
  732.4 9.7 %copy.328 = f32[8,3,256,256]{3,1,0,2:T(4,128)} copy(f32[8,3,256,256]{3,0,1,2:T(8,128)} %all-gather.2.cloned.1.call-done) | data formatting | bytes 12582912 | tf_op jit(solution)/shard_map/all_gather | solution.py:149
  742.1 11.3 %pad.8 = f32[8,3,288,256]{3,1,0,2:T(4,128)} pad(f32[8,3,256,256]{3,1,0,2:T(4,128)} %copy.328, f32[]{:T(128)} %constant.108.clone.1), padding=0_0x0_0x16_16x0_0 | pad | bytes 13369348 | tf_op jit(solution)/shard_map/jit(_pad)/pad | solution.py:150
  753.4 4.6 gather_fusion.4
  758.3 78.4 %while.1 = (s32[]{:T(128)}, f32[8,3,16,4096]{3,2,1,0:T(8,128)}, s32[8,4]{0,1:T(4,128)S(1)}, f32[8,3,16,256]{3,2,1,0:T(8,128)S(1)}, s32[]{:T(128)}, /*index=5*/s32[4]{0:T(128)S(1)}, s32[]{:T(128)}) while((s32[]{:T(128)}, f32[8,3,16,4096]{3,2,1,0:T(8,128)}, s32[8,4]{0,1:T(4,128)S(1)}, f32[8,3,16,256]{3,2,1,0:T(8,128)S(1)}, s32[]{:T(128)}, ...), condition=%wide.while_cond, body=%wide.while_body.sunk | while | flops 12317 | bytes 245963 | solution.py:163
  758.9 3.3 and_reduce_fusion.2
  762.2 2.8 dynamic-slice_select_fusion.2
  765.0 3.1 dynamic-update-slice.3
  768.7 3.3 and_reduce_fusion.2
  772.0 2.8 dynamic-slice_select_fusion.2
  774.8 3.1 dynamic-update-slice.3
  778.5 3.3 and_reduce_fusion.2
  781.8 2.8 dynamic-slice_select_fusion.2
  784.6 3.1 dynamic-update-slice.3
  788.3 3.3 and_reduce_fusion.2
  791.6 2.8 dynamic-slice_select_fusion.2
  794.4 3.1 dynamic-update-slice.3
  798.1 3.3 and_reduce_fusion.2
  801.4 2.8 dynamic-slice_select_fusion.2
  804.2 3.1 dynamic-update-slice.3
  807.9 3.3 and_reduce_fusion.2
  811.2 2.8 dynamic-slice_select_fusion.2
  814.0 3.1 dynamic-update-slice.3
  817.7 3.3 and_reduce_fusion.2
  821.0 2.8 dynamic-slice_select_fusion.2
  823.8 3.1 dynamic-update-slice.3
  827.5 3.3 and_reduce_fusion.2
  830.8 2.8 dynamic-slice_select_fusion.2
  833.6 3.1 dynamic-update-slice.3
  (188 shorter events, 57.0 us)
Async XLA Ops:
  7.2 418.4 %all-reduce.7.cloned.1.call-start = ((), (), s32[]{:S(2)}) async-start(), calls=%async_computation | async-start | bytes 1572864 | tf_op jit(solution)/shard_map/psum | solution.py:137
  9.0 461.6 %collective-permute-start.4 = (f32[8,2,1,768]{3,0,2,1:T(8,128)}, f32[8,2,1,768]{3,0,2,1:T(8,128)}, u32[]{:S(2)}, u32[]{:S(2)}) collective-permute-start(f32[8,2,1,768]{3,0,2,1:T(8,128)} %copy.351), channel_id=1, source_target_pairs={{0,1},{1,2},{2,3},{3,4},{4,5},{5,6},{6,7},{7,8},{8,9},{9,10},{10,1... | collective-permute-start | bytes 147464 | tf_op jit(solution)/shard_map/ppermute | solution.py:23
  15.7 454.9 %collective-permute-start.5 = (f32[8,2,1,768]{3,0,2,1:T(8,128)}, f32[8,2,1,768]{3,0,2,1:T(8,128)}, u32[]{:S(2)}, u32[]{:S(2)}) collective-permute-start(f32[8,2,1,768]{3,0,2,1:T(8,128)} %copy.353), channel_id=1, source_target_pairs={{1,0},{2,1},{3,2},{4,3},{5,4},{6,5},{7,6},{8,7},{9,8},{10,9},{11,1... | collective-permute-start | bytes 147464 | tf_op jit(solution)/shard_map/ppermute | solution.py:25
  17.0 14.2 %copy-start = (f32[8,3,16,4096]{3,2,1,0:T(8,128)S(1)}, f32[8,3,16,4096]{3,2,1,0:T(8,128)}, u32[]{:S(2)}) copy-start(f32[8,3,16,4096]{3,2,1,0:T(8,128)} %param.3) | copy-start | bytes 18874372
  20.0 24.6 %collective-permute-start.1 = (f32[8,2,1,4096]{3,0,2,1:T(8,128)S(1)}, f32[8,2,1,4096]{3,0,2,1:T(8,128)S(1)}, u32[]{:S(2)}, u32[]{:S(2)}) collective-permute-start(f32[8,2,1,4096]{3,0,2,1:T(8,128)S(1)} %copy.347), channel_id=1, source_target_pairs={{0,1},{1,2},{2,3},{3,4},{4,5},{5,6},{6,7},{7,8},{8,9},{9,10},{10,1... | collective-permute-start | bytes 786440 | tf_op jit(solution)/shard_map/ppermute | solution.py:23
  25.8 18.8 %collective-permute-start = (f32[8,2,1,4096]{3,0,2,1:T(8,128)S(1)}, f32[8,2,1,4096]{3,0,2,1:T(8,128)S(1)}, u32[]{:S(2)}, u32[]{:S(2)}) collective-permute-start(f32[8,2,1,4096]{3,0,2,1:T(8,128)S(1)} %copy.345), channel_id=1, source_target_pairs={{1,0},{2,1},{3,2},{4,3},{5,4},{6,5},{7,6},{8,7},{9,8},{10,9},{11,1... | collective-permute-start | bytes 786440 | tf_op jit(solution)/shard_map/ppermute | solution.py:25
  37.3 5.4 copy-start.24
  37.3 4.8 copy-start.27
  37.3 6.1 copy-start.5
  42.6 2.5 copy-start.16
  43.3 2.8 slice-start
  44.6 2.4 slice-start.1
  44.6 3.0 copy-start.4
  50.7 1.6 copy-start.1
  50.7 2.2 copy-start.2
  59.6 14.6 %slice-start.2 = ((f32[8,3,24,768]{3,2,1,0:T(8,128)}), f32[8,2,24,768]{3,2,1,0:T(8,128)S(1)}, s32[]{:S(2)}) async-start(f32[8,3,24,768]{3,2,1,0:T(8,128)} %param.4), calls=%async_computation.4 | async-start | bytes 2359296 | tf_op jit(solution)/shard_map/slice | solution.py:64
  60.7 15.2 %collective-permute-start.3 = (f32[8,1,1,4096]{3,0,2,1:T(8,128)}, f32[8,1,1,4096]{3,0,2,1:T(8,128)}, u32[]{:S(2)}, u32[]{:S(2)}) collective-permute-start(f32[8,1,1,4096]{3,0,2,1:T(8,128)} %copy.285), channel_id=1, source_target_pairs={{1,0},{2,1},{3,2},{4,3},{5,4},{6,5},{7,6},{8,7},{9,8},{10,9},{11,1... | collective-permute-start | bytes 393224 | tf_op jit(solution)/shard_map/ppermute | solution.py:25
  61.9 15.0 %collective-permute-start.2 = (f32[8,1,1,4096]{3,0,2,1:T(8,128)S(1)}, f32[8,1,1,4096]{3,0,2,1:T(8,128)S(1)}, u32[]{:S(2)}, u32[]{:S(2)}) collective-permute-start(f32[8,1,1,4096]{3,0,2,1:T(8,128)S(1)} %copy.284), channel_id=1, source_target_pairs={{0,1},{1,2},{2,3},{3,4},{4,5},{5,6},{6,7},{7,8},{8,9},{9,10},{10,1... | collective-permute-start | bytes 393224 | tf_op jit(solution)/shard_map/ppermute | solution.py:23
  77.6 3.1 copy-start.3
  80.8 3.1 copy-start.19
  80.8 3.1 copy-start.20
  88.3 644.1 %all-gather.2.cloned.1.call-start = ((), (), s32[]{:S(2)}) async-start(), calls=%async_computation.1 | async-start | bytes 6488064 | tf_op jit(solution)/shard_map/all_gather | solution.py:149
  239.1 7.4 copy-start.14
  239.1 10.5 %copy-start.28 = (f32[26]{0:T(128)S(1)}, f32[26]{0:T(128)}, u32[]{:S(2)}) copy-start(f32[26]{0:T(128)} %get-tuple-element.136) | copy-start | bytes 316
  239.1 10.5 %copy-start.29 = (f32[26]{0:T(128)S(1)}, f32[26]{0:T(128)}, u32[]{:S(2)}) copy-start(f32[26]{0:T(128)} %get-tuple-element.137) | copy-start | bytes 316
  250.2 211.4 %copy-start.13 = (s32[8]{0:T(128)S(1)}, s32[8]{0:T(128)}, u32[]{:S(2)}) copy-start(s32[8]{0:T(128)} %get-tuple-element.122) | copy-start | bytes 100
  461.6 8.1 copy-start.18
  461.6 8.1 copy-start.21
  461.6 8.1 copy-start.22
  461.6 8.1 copy-start.23
  461.6 9.9 %copy-start.6 = (f32[8,2,24,768]{3,0,2,1:T(8,128)S(1)}, f32[8,2,24,768]{3,0,2,1:T(8,128)}, u32[]{:S(2)}) copy-start(f32[8,2,24,768]{3,0,2,1:T(8,128)} %copy.352) | copy-start | bytes 3538948
  470.6 0.9 copy-start.11
  471.6 13.2 %copy-start.7 = (f32[8,1,24,768]{3,2,1,0:T(8,128)S(1)}, f32[8,1,24,768]{3,2,1,0:T(8,128)}, u32[]{:S(2)}) copy-start(f32[8,1,24,768]{3,2,1,0:T(8,128)} %get-tuple-element.86) | copy-start | bytes 1769476
  471.6 13.2 %copy-start.8 = (f32[8,1,24,768]{3,2,1,0:T(8,128)S(1)}, f32[8,1,24,768]{3,2,1,0:T(8,128)}, u32[]{:S(2)}) copy-start(f32[8,1,24,768]{3,2,1,0:T(8,128)} %get-tuple-element.88) | copy-start | bytes 1769476
  473.2 6.3 collective-permute-start.6
  477.6 6.1 collective-permute-start.7
  479.4 25.6 %copy-start.9 = (f32[8,1,26,1]{3,0,2,1:T(8,128)}, f32[8,1,26,1]{3,0,2,1:T(8,128)S(1)}, u32[]{:S(2)}) copy-start(f32[8,1,26,1]{3,0,2,1:T(8,128)S(1)} %copy.311) | copy-start | bytes 2500
  484.8 8.6 %copy-start.12 = (f32[8,3,2,768]{3,0,2,1:T(8,128)S(1)}, f32[8,3,2,768]{3,0,2,1:T(8,128)}, u32[]{:S(2)}) copy-start(f32[8,3,2,768]{3,0,2,1:T(8,128)} %copy-done.11) | copy-start | bytes 442372
  485.4 6.8 collective-permute-start.9
  486.7 6.7 collective-permute-start.8
  493.8 6.5 collective-permute-start.10
  499.0 6.1 collective-permute-start.11
  505.9 7.5 collective-permute-start.13
  507.2 7.3 collective-permute-start.12
  515.0 21.2 %collective-permute-start.14 = (f32[8,1,1,768]{3,0,2,1:T(8,128)S(1)}, f32[8,1,1,768]{3,0,2,1:T(8,128)S(1)}, u32[]{:S(2)}, u32[]{:S(2)}) collective-permute-start(f32[8,1,1,768]{3,0,2,1:T(8,128)S(1)} %get-tuple-element.95), channel_id=1, source_target_pairs={{0,1},{1,2},{2,3},{3,4},{4,5},{5,6},{6,7},{7,8},{8,9},{9,10},{10,1... | collective-permute-start | bytes 73736 | tf_op jit(solution)/shard_map/ppermute | solution.py:23
  520.8 16.2 %copy-start.10 = (f32[8,1,26,1]{3,0,2,1:T(8,128)S(1)}, f32[8,1,26,1]{3,0,2,1:T(8,128)}, u32[]{:S(2)}) copy-start(f32[8,1,26,1]{3,0,2,1:T(8,128)} %copy-done.9) | copy-start | bytes 2500
  520.8 15.4 %collective-permute-start.15 = (f32[8,1,1,768]{3,0,2,1:T(8,128)S(1)}, f32[8,1,1,768]{3,0,2,1:T(8,128)S(1)}, u32[]{:S(2)}, u32[]{:S(2)}) collective-permute-start(f32[8,1,1,768]{3,0,2,1:T(8,128)S(1)} %get-tuple-element.96), channel_id=1, source_target_pairs={{1,0},{2,1},{3,2},{4,3},{5,4},{6,5},{7,6},{8,7},{9,8},{10,9},{11,1... | collective-permute-start | bytes 73736 | tf_op jit(solution)/shard_map/ppermute | solution.py:25
  598.1 3.5 copy-start.26
  598.1 3.5 copy-start.30
  598.1 3.6 copy-start.17
  598.1 3.6 copy-start.25
  753.4 4.9 copy-start.15
Sparse Core Ops, SparseCore 0:
  88.4 337.0 all-reduce.6
  601.6 130.6 all-gather.1
where the time goes:
time: 861 us; the launch traced here: 844 us
  waiting for transfers between devices  305 us (35%)
  local copies, waits for them, and re-layouts  236 us (27%)
  other arithmetic  127 us (15%)
  blocking collectives  99.4 us (12%)
  starting transfers between devices  55.8 us (6%)
  between operations  15.3 us (2%)
    psum x1, waiting for transfers between devices, per_device(): ends_full = lax.psum(partial_rows, 'band')  175 us
    all_gather x1, waiting for transfers between devices, per_device(): whole = lax.all_gather(coarse, 'band', axis=2, tiled=True)  118 us
    all_gather x1, blocking collectives, per_device(): column_all = lax.all_gather(strip, 'band', axis=3, tiled=True)  99.4 us
    reduce_sum x1, other arithmetic, per_device(): coarse = nest.reshape(members, 3, tile_coarse, 3, span, 3).mean(axis=(3, 5))  50.1 us
    another operation x1, local copies, waits for them, and re-layouts, per_device(): stepped = jnp.stack([height_new, zonal_new, merid_new], axis=1)  48.5 us
    scatter x16, other arithmetic  48.3 us
    ppermute x8, starting transfers between devices, with_halo(): lax.ppermute(tail, axis, [(i, (i + 1) % count) for i in range(ends)])  45.1 us
    psum x1, local copies, waits for them, and re-layouts, per_device(): ends_full = lax.psum(partial_rows, 'band')  36.1 us
  transfers between devices with their start and end apart: 18, of which 6 were waited for; matrix products, arithmetic and copies ran while one was open for 22% of the time, Pallas kernels for 0%

commit v1 on v0

v1 whole, which is shorter than its diff:
```python
import jax
import jax.numpy as jnp
from jax import lax
from jax.sharding import PartitionSpec as P

NSTEPS = 3


courant = 0.9
friction = 0.02
rotation = 0.05
highest = lax.Precision.HIGHEST


def shift_pairs(count, shift):
    if shift > 0:
        return [(i, i + shift) for i in range(count - shift)]
    return [(i, i + shift) for i in range(-shift, count)]


def with_halo(cells, width):
    count = lax.axis_size("band")
    head = cells[:, :, :width]
    tail = cells[:, :, cells.shape[2] - width :]
    return jnp.concatenate(
        [
            lax.ppermute(tail, "band", shift_pairs(count, 1)),
            cells,
            lax.ppermute(head, "band", shift_pairs(count, -1)),
        ],
        axis=2,
    )


def interp_matrix(fine, coarse_count):
    rows = jnp.arange(fine, dtype=jnp.int32)[:, None] + 1
    cols = jnp.arange(coarse_count, dtype=jnp.int32)[None, :]
    base = rows // 3
    frac = rows % 3
    upper = frac.astype(jnp.float32) / 3.0
    lower = (3 - frac).astype(jnp.float32) / 3.0
    return jnp.where(cols == base, lower, 0.0) + jnp.where(cols == base + 1, upper, 0.0)


def shift_cols(field):
    return 0.5 * (jnp.roll(field, -1, axis=-1) - jnp.roll(field, 1, axis=-1))


def parent_step(parent_state):
    height, zonal, meridional = (parent_state[:, 0], parent_state[:, 1], parent_state[:, 2])
    merid_ext = with_halo(meridional[:, None], 1)[:, 0]
    height_new = height - courant * (
        shift_cols(zonal) + 0.5 * (merid_ext[:, 2:] - merid_ext[:, :-2])
    )
    height_ext = with_halo(height_new[:, None], 1)[:, 0]
    zonal_new = (1.0 - friction) * zonal - courant * shift_cols(height_new) + rotation * meridional
    merid_new = (
        (1.0 - friction) * meridional
        - courant * (0.5 * (height_ext[:, 2:] - height_ext[:, :-2]))
        - rotation * zonal
    )
    return jnp.stack([height_new, zonal_new, merid_new], axis=1)


def per_device(parent_state, nest_state, offsets):
    members = parent_state.shape[0]
    band_rows = parent_state.shape[2]
    nest_rows = nest_state.shape[2]
    nest_width = nest_state.shape[3]
    span = nest_width // 3
    tile_coarse = nest_rows // 3
    bands = lax.axis_size("band")
    band_index = lax.axis_index("band")
    parent_total = bands * band_rows
    nest_total = bands * nest_rows
    halo = 2 * NSTEPS
    ext_rows = nest_rows + 2 * halo
    rows_off = offsets[:, 0]
    cols_off = offsets[:, 1]
    two = jnp.float32(2.0) / jnp.float32(3.0)
    one = jnp.float32(1.0) / jnp.float32(3.0)

    stepped = parent_step(parent_state)

    colslice = jax.vmap(lambda f, c0: lax.dynamic_slice_in_dim(f, c0 - 1, span + 2, axis=2))(
        stepped, cols_off
    )

    west = two * colslice[..., 0] + one * colslice[..., 1]
    east = one * colslice[..., span] + two * colslice[..., span + 1]
    strip = jnp.stack([west, east], axis=2)
    gathered = lax.all_gather(strip.reshape(1, -1), "band", axis=0, tiled=True)
    strip_all = (
        gathered.reshape(bands, members, 3, 2, band_rows)
        .transpose(1, 2, 3, 0, 4)
        .reshape(members, 3, 2, parent_total)
    )

    global_rows = band_index * band_rows + jnp.arange(band_rows, dtype=jnp.int32)
    row_start = rows_off[:, None]
    south_weight = jnp.where(global_rows[None, :] == row_start - 1, two, 0.0) + jnp.where(
        global_rows[None, :] == row_start, one, 0.0
    )
    north_weight = jnp.where(global_rows[None, :] == row_start + span - 1, one, 0.0) + jnp.where(
        global_rows[None, :] == row_start + span, two, 0.0
    )
    row_weights = jnp.stack([south_weight, north_weight], axis=1)
    ends_part = jnp.einsum("msl,mflq->mfsq", row_weights, colslice, precision=highest)
    ends_full = lax.psum(ends_part, "band")
    inner_weights = interp_matrix(nest_width + 2, span + 2)[1:-1]
    ends = jnp.einsum("jq,mfsq->mfsj", inner_weights, ends_full, precision=highest)

    nest_global = band_index * nest_rows - halo + jnp.arange(ext_rows, dtype=jnp.int32)
    base = (nest_global + 2) // 3
    frac = (nest_global + 2) % 3
    lower = (3 - frac).astype(jnp.float32) / 3.0
    upper = frac.astype(jnp.float32) / 3.0
    first_row = rows_off[:, None] - 1 + base[None, :]
    all_rows = jnp.arange(parent_total, dtype=jnp.int32)[None, None, :]
    side_weights = jnp.where(all_rows == first_row[:, :, None], lower[None, :, None], 0.0) + jnp.where(
        all_rows == first_row[:, :, None] + 1, upper[None, :, None], 0.0
    )
    side_ext = jnp.einsum("mkr,mfsr->mfsk", side_weights, strip_all, precision=highest)

    nest_ext = with_halo(nest_state, halo)
    is_south = (nest_global == -1)[None, :, None]
    is_north = (nest_global == nest_total)[None, :, None]

    def fix(field, f):
        return jnp.where(
            is_south,
            ends[:, f, 0][:, None, :],
            jnp.where(is_north, ends[:, f, 1][:, None, :], field),
        )

    def dx(field, f):
        west_col = side_ext[:, f, 0][:, :, None]
        east_col = side_ext[:, f, 1][:, :, None]
        right = jnp.concatenate([field[:, :, 1:], east_col], axis=2)
        left = jnp.concatenate([west_col, field[:, :, :-1]], axis=2)
        return 0.5 * (right - left)

    def dy(field):
        zero = jnp.zeros_like(field[:, :1])
        up = jnp.concatenate([field[:, 1:], zero], axis=1)
        down = jnp.concatenate([zero, field[:, :-1]], axis=1)
        return 0.5 * (up - down)

    height, zonal, meridional = (nest_ext[:, 0], nest_ext[:, 1], nest_ext[:, 2])
    for _ in range(NSTEPS):
        zonal_fixed = fix(zonal, 1)
        merid_fixed = fix(meridional, 2)
        height_new = height - courant * (dx(zonal_fixed, 1) + dy(merid_fixed))
        height_fixed = fix(height_new, 0)
        zonal_new = (1.0 - friction) * zonal - courant * dx(height_fixed, 0) + rotation * meridional
        merid_new = (1.0 - friction) * meridional - courant * dy(height_fixed) - rotation * zonal
        height, zonal, meridional = height_new, zonal_new, merid_new
    nest = jnp.stack([height, zonal, meridional], axis=1)[:, :, halo : halo + nest_rows]

    block_cols = (
        jnp.arange(nest_width, dtype=jnp.int32)[:, None] // 3
        == jnp.arange(span, dtype=jnp.int32)[None, :]
    ).astype(jnp.float32)
    col_sums = jnp.einsum("mfrj,jp->mfrp", nest, block_cols, precision=highest)
    coarse = col_sums.reshape(members, 3, tile_coarse, 3, span).sum(axis=3) / 9.0

    shift = (rows_off + tile_coarse - 1) // tile_coarse - 1
    moved = coarse
    step = 1
    while step < bands:
        recv = lax.ppermute(moved, "band", [(i, (i + step) % bands) for i in range(bands)])
        take = ((shift // step) % 2 == 1)[:, None, None, None]
        moved = jnp.where(take, recv, moved)
        step *= 2
    half = bands // 2
    low_half = band_index < half
    pieces = []
    for i in range(3):
        got = []
        for h in range(2):
            pairs = [((2 * p - 1 + i) % bands, p) for p in range(h * half, (h + 1) * half)]
            got.append(lax.ppermute(moved, "band", pairs))
        pieces.append(jnp.where(low_half, got[0], got[1]))
    near = jnp.concatenate(pieces, axis=2)
    lead = tile_coarse * (shift + 1) - rows_off
    patch = jax.vmap(lambda blk, e: lax.dynamic_slice_in_dim(blk, e, band_rows, axis=1))(near, lead)

    relative_rows = global_rows[None, :] - rows_off[:, None]
    covered = (relative_rows >= 0) & (relative_rows < span)
    parent_out = stepped
    for m in range(members):
        start = (m, 0, 0, cols_off[m])
        current = lax.dynamic_slice(parent_out, start, (1, 3, band_rows, span))
        merged = jnp.where(covered[m][None, None, :, None], patch[m : m + 1], current)
        parent_out = lax.dynamic_update_slice(parent_out, merged, start)
    return (parent_out, nest)


def solution(mesh):
    in_specs = (P("member", None, "band", None), P("member", None, "band", None), P("member", None))
    out_specs = (P("member", None, "band", None), P("member", None, "band", None))
    return jax.shard_map(
        per_device, mesh=mesh, in_specs=in_specs, out_specs=out_specs, check_vma=False
    )
```

time: 861 us -> 519 us (0.60)
  the two profiles are of different devices: /device:TPU:1 before, /device:TPU:112 now
where the time goes in v1:
time: 519 us; the launch traced here: 512 us
  blocking collectives  249 us (48%)
  local copies, waits for them, and re-layouts  98.6 us (19%)
  starting transfers between devices  70.8 us (14%)
  waiting for transfers between devices  42.7 us (8%)
  other arithmetic  26.3 us (5%)
  between operations  16.4 us (3%)
  matrix products  8.63 us (2%)
    psum x1, blocking collectives, per_device(): ends_full = lax.psum(ends_part, 'band')  161 us
    all_gather x1, blocking collectives, per_device(): gathered = lax.all_gather(strip.reshape(1, -1), 'band', axis=0, tiled=True)  87.8 us
    another operation x1, local copies, waits for them, and re-layouts, parent_step(): return jnp.stack([height_new, zonal_new, merid_new], axis=1)  48.6 us
    ppermute x5, starting transfers between devices, per_device(): lax.ppermute(moved, 'band', [(i, (i + step) % bands) for i in range(bands)])  30.6 us
    ppermute x5, waiting for transfers between devices, per_device(): lax.ppermute(moved, 'band', [(i, (i + step) % bands) for i in range(bands)])  23.3 us
    dynamic_update_slice x8, local copies, waits for them, and re-layouts, per_device(): parent_out = lax.dynamic_update_slice(parent_out, merged, start)  15.4 us
    ppermute x6, starting transfers between devices, per_device(): got.append(lax.ppermute(moved, 'band', pairs))  15.2 us
    ppermute x6, waiting for transfers between devices, per_device(): got.append(lax.ppermute(moved, 'band', pairs))  14 us
  transfers between devices with their start and end apart: 17, of which 9 were waited for; matrix products, arithmetic and copies ran while one was open for 18% of the time, Pallas kernels for 0%

profile of v1, /device:TPU:112, one launch (start us, length us, event | category | flops | bytes accessed | tf_op | source)
XLA Modules:
  0.0 512.3 jit_solution(7739907059420473272)
XLA Ops:
  0.6 1.7 fusion.114
  2.5 4.9 collective-permute-start
  8.1 3.3 collective-permute-start.1
  11.5 1.3 fusion.118
  12.9 4.0 collective-permute-start.4
  17.0 0.9 copy.328
  17.9 4.2 collective-permute-start.5
  22.1 3.9 slice_bitcast_fusion.3
  26.0 2.1 fusion.117
  29.0 1.0 copy.265
  30.1 2.3 maximum_bitcast_fusion
  32.4 2.5 fusion.8
  36.0 3.1 collective-permute-start.2
  39.2 5.3 %collective-permute-start.3 = (f32[8,1,1,4096]{3,0,2,1:T(8,128)S(1)}, f32[8,1,1,4096]{3,0,2,1:T(8,128)S(1)}, u32[]{:S(2)}, u32[]{:S(2)}) collective-permute-start(f32[8,1,1,4096]{3,0,2,1:T(8,128)S(1)} %copy.271), channel_id=1, source_target_pairs={{1,0},{2,1},{3,2},{4,3},{5,4},{6,5},{7,6},{8,7},{9,8},{10,9},{11,1... | collective-permute-start | bytes 393224 | tf_op jit(solution)/shard_map/ppermute | solution.py:29
  44.6 0.8 fusion.11
  45.4 1.0 collective-permute-done.2
  46.6 4.3 collective-permute-done.3
  51.6 0.8 fusion.5
  52.4 3.2 pad_maximum_fusion
  55.6 48.6 %copy.279 = f32[8,3,16,4096]{2,1,0,3:T(4,128)} copy(f32[8,3,16,4096]{3,2,0,1:T(8,128)} %pad_maximum_fusion) | data formatting | bytes 12582912 | tf_op jit(solution)/shard_map/stack | solution.py:62
  104.2 6.8 %gather_fusion = f32[8,3,16,258]{2,1,3,0:T(4,128)} fusion(f32[8,3,16,4096]{2,1,0,3:T(4,128)} %copy.279, s32[8]{0:T(128)S(1)} %get-tuple-element.116), kind=kCustom, calls=%fused_computation | custom fusion | bytes 792704 | tf_op jit(solution)/shard_map/vmap()/gather | solution.py:85
  111.7 0.7 fusion.71
  112.5 5.8 %fusion.12 = f32[8,3,2,258]{3,2,1,0:T(2,128)S(1)} fusion(f32[8,3,16,258]{2,1,3,0:T(4,128)} %gather_fusion, f32[8,1,16]{2,1,0:T(1,128)S(1)} %get-tuple-element.125, f32[8,1,16]{2,1,0:T(1,128)S(1)} %get-tuple-element.124), kind=kOutput, calls=%fused_computation.43 | convolution fusion | flops 2377984 | bytes 446848 | tf_op jit(solution)/shard_map/msl,mflq->mfsq/dot_general | solution.py:108
  118.3 161.2 %psum.7 = f32[8,3,2,258]{3,2,1,0:T(2,128)S(1)} all-reduce(f32[8,3,2,258]{3,2,1,0:T(2,128)S(1)} %fusion.12), channel_id=1, replica_groups=mesh['member'=4,'band'=32] {'band'}, use_global_device_ids=true, to_apply=%region_0.1 | all-reduce | flops 12384 | bytes 99072 | tf_op jit(solution)/shard_map/psum | solution.py:109
  279.6 87.8 %all-gather = f32[32,1,768]{2,1,0:T(1,128)S(1)} all-gather(f32[1,1,768]{2,1,0:T(1,128)S(1)} %reshape.699), channel_id=1, replica_groups=mesh['member'=4,'band'=32] {'band'}, dimensions={0}, use_global_device_ids=true | all-gather | bytes 101376 | tf_op jit(solution)/shard_map/all_gather | solution.py:92
  368.3 0.9 fusion.48
  369.8 0.9 fusion.40
  370.9 1.2 copy.278
  374.2 0.9 select_select_fusion.5
  376.7 0.9 select_select_fusion.1
  380.0 1.1 fusion.46
  381.5 4.1 collective-permute-start.6
  385.7 5.0 collective-permute-done.6
  390.9 6.9 %collective-permute-start.7 = (f32[8,3,8,256]{3,1,0,2:T(4,128)S(1)}, f32[8,3,8,256]{3,1,0,2:T(4,128)S(1)}, u32[]{:S(2)}, u32[]{:S(2)}) collective-permute-start(f32[8,3,8,256]{3,1,0,2:T(4,128)S(1)} %broadcast_select_fusion), channel_id=1, source_target_pairs={{0,2},{1,3},{2,4},{3,5},{4,6},{5,7},{6,8},{7,9},{8,10},{9,11},{10,... | collective-permute-start | bytes 589832 | tf_op jit(solution)/shard_map/ppermute | solution.py:171
  397.8 3.9 collective-permute-done.7
  401.8 6.9 %collective-permute-start.8 = (f32[8,3,8,256]{3,1,0,2:T(4,128)S(1)}, f32[8,3,8,256]{3,1,0,2:T(4,128)S(1)}, u32[]{:S(2)}, u32[]{:S(2)}) collective-permute-start(f32[8,3,8,256]{3,1,0,2:T(4,128)S(1)} %broadcast_select_fusion.1), channel_id=1, source_target_pairs={{0,4},{1,5},{2,6},{3,7},{4,8},{5,9},{6,10},{7,11},{8,12},{9,13},{1... | collective-permute-start | bytes 589832 | tf_op jit(solution)/shard_map/ppermute | solution.py:171
  408.7 6.7 %collective-permute-done.8 = f32[8,3,8,256]{3,1,0,2:T(4,128)S(1)} collective-permute-done((f32[8,3,8,256]{3,1,0,2:T(4,128)S(1)}, f32[8,3,8,256]{3,1,0,2:T(4,128)S(1)}, u32[]{:S(2)}, u32[]{:S(2)}) %collective-permute-start.8) | collective-permute-done | bytes 196640 | tf_op jit(solution)/shard_map/ppermute | solution.py:171
  415.5 12.6 %collective-permute-start.9 = (f32[8,3,8,256]{3,1,0,2:T(4,128)S(1)}, f32[8,3,8,256]{3,1,0,2:T(4,128)S(1)}, u32[]{:S(2)}, u32[]{:S(2)}) collective-permute-start(f32[8,3,8,256]{3,1,0,2:T(4,128)S(1)} %broadcast_select_fusion.2), channel_id=1, source_target_pairs={{0,8},{1,9},{2,10},{3,11},{4,12},{5,13},{6,14},{7,15},{8,16},{9,17... | collective-permute-start | bytes 589832 | tf_op jit(solution)/shard_map/ppermute | solution.py:171
  444.1 7.8 %collective-permute-done.10 = f32[8,3,8,256]{3,1,0,2:T(4,128)S(1)} collective-permute-done((f32[8,3,8,256]{3,1,0,2:T(4,128)S(1)}, f32[8,3,8,256]{3,1,0,2:T(4,128)S(1)}, u32[]{:S(2)}, u32[]{:S(2)}) %collective-permute-start.10) | collective-permute-done | bytes 196640 | tf_op jit(solution)/shard_map/ppermute | solution.py:171
  452.8 1.3 collective-permute-start.12
  454.1 9.4 %collective-permute-start.13 = (f32[8,3,8,256]{3,1,0,2:T(4,128)S(1)}, f32[8,3,8,256]{3,1,0,2:T(4,128)S(1)}, u32[]{:S(2)}, u32[]{:S(2)}) collective-permute-start(f32[8,3,8,256]{3,1,0,2:T(4,128)S(1)} %broadcast_select_fusion.4), channel_id=1, source_target_pairs={{0,0},{2,1},{4,2},{6,3},{8,4},{10,5},{12,6},{14,7},{16,8},{18,9},{... | collective-permute-start | bytes 589832 | tf_op jit(solution)/shard_map/ppermute | solution.py:182
  463.5 1.9 collective-permute-start.14
  466.1 1.3 collective-permute-start.16
  467.4 1.0 collective-permute-done.12
  468.4 5.0 collective-permute-done.14
  473.5 8.0 %collective-permute-done.16 = f32[8,3,8,256]{3,1,0,2:T(4,128)S(1)} collective-permute-done((f32[8,3,8,256]{3,1,0,2:T(4,128)S(1)}, f32[8,3,8,256]{3,1,0,2:T(4,128)S(1)}, u32[]{:S(2)}, u32[]{:S(2)}) %collective-permute-start.16) | collective-permute-done | bytes 196640 | tf_op jit(solution)/shard_map/ppermute | solution.py:182
  481.9 0.9 gather_fusion.1
  482.9 1.0 copy_select_fusion.7
  483.9 1.9 dynamic_update_slice.24
  485.8 1.0 copy_select_fusion.6
  486.8 1.9 dynamic_update_slice.25
  488.7 1.0 copy_select_fusion.5
  489.6 1.9 dynamic_update_slice.26
  491.6 1.0 copy_select_fusion.4
  492.6 1.9 dynamic_update_slice.27
  494.5 1.0 copy_select_fusion.3
  495.5 1.9 dynamic_update_slice.28
  497.4 1.0 copy_select_fusion.2
  498.4 1.9 dynamic_update_slice.29
  500.3 1.0 copy_select_fusion.1
  501.3 1.9 dynamic_update_slice.30
  503.2 1.0 copy_select_fusion
  504.1 1.9 dynamic_update_slice.31
  506.1 6.2 %copy.315 = f32[8,3,16,4096]{3,2,1,0:T(8,128)} copy(f32[8,3,16,4096]{3,2,0,1:T(8,128)} %dynamic_update_slice.31) | data formatting | bytes 12582912
  (104 shorter events, 16.3 us)
Async XLA Ops:
  2.5 26.4 %collective-permute-start = (f32[8,1,1,4096]{3,0,2,1:T(8,128)S(1)}, f32[8,1,1,4096]{3,0,2,1:T(8,128)S(1)}, u32[]{:S(2)}, u32[]{:S(2)}) collective-permute-start(f32[8,1,1,4096]{3,0,2,1:T(8,128)S(1)} %copy.324), channel_id=1, source_target_pairs={{0,1},{1,2},{2,3},{3,4},{4,5},{5,6},{6,7},{7,8},{8,9},{9,10},{10,1... | collective-permute-start | bytes 393224 | tf_op jit(solution)/shard_map/ppermute | solution.py:27
  8.1 20.8 %collective-permute-start.1 = (f32[8,1,1,4096]{3,0,2,1:T(8,128)}, f32[8,1,1,4096]{3,0,2,1:T(8,128)}, u32[]{:S(2)}, u32[]{:S(2)}) collective-permute-start(f32[8,1,1,4096]{3,0,2,1:T(8,128)} %copy.326), channel_id=1, source_target_pairs={{1,0},{2,1},{3,2},{4,3},{5,4},{6,5},{7,6},{8,7},{9,8},{10,9},{11,1... | collective-permute-start | bytes 393224 | tf_op jit(solution)/shard_map/ppermute | solution.py:29
  12.9 357.8 %collective-permute-start.4 = (f32[8,3,6,768]{3,0,2,1:T(8,128)S(1)}, f32[8,3,6,768]{3,0,2,1:T(8,128)S(1)}, u32[]{:S(2)}, u32[]{:S(2)}) collective-permute-start(f32[8,3,6,768]{3,0,2,1:T(8,128)S(1)} %copy.327), channel_id=1, source_target_pairs={{0,1},{1,2},{2,3},{3,4},{4,5},{5,6},{6,7},{7,8},{8,9},{9,10},{10,1... | collective-permute-start | bytes 1327112 | tf_op jit(solution)/shard_map/ppermute | solution.py:27
  17.9 353.0 %collective-permute-start.5 = (f32[8,3,6,768]{3,0,2,1:T(8,128)}, f32[8,3,6,768]{3,0,2,1:T(8,128)}, u32[]{:S(2)}, u32[]{:S(2)}) collective-permute-start(f32[8,3,6,768]{3,0,2,1:T(8,128)} %copy.328), channel_id=1, source_target_pairs={{1,0},{2,1},{3,2},{4,3},{5,4},{6,5},{7,6},{8,7},{9,8},{10,9},{11,1... | collective-permute-start | bytes 1327112 | tf_op jit(solution)/shard_map/ppermute | solution.py:29
  26.0 2.2 copy-start.3
  30.0 2.3 copy-start
  32.3 12.2 %slice-start = ((s8[6291456]{0:T(1024)(128)(4,1)}), s8[4194304]{0:T(1024)(128)(4,1)S(1)}, s32[]{:S(2)}) async-start(s8[6291456]{0:T(1024)(128)(4,1)} %bitcast.197), calls=%async_computation | async-start | bytes 8388608
  32.4 12.2 %slice-start.1 = ((s8[6291456]{0:T(1024)(128)(4,1)}), s8[2097152]{0:T(1024)(128)(4,1)S(1)}, s32[]{:S(2)}) async-start(s8[6291456]{0:T(1024)(128)(4,1)} %bitcast.197), calls=%async_computation.1 | async-start | bytes 4194304
  36.0 10.4 %collective-permute-start.2 = (f32[8,1,1,4096]{3,0,2,1:T(8,128)S(1)}, f32[8,1,1,4096]{3,0,2,1:T(8,128)S(1)}, u32[]{:S(2)}, u32[]{:S(2)}) collective-permute-start(f32[8,1,1,4096]{3,0,2,1:T(8,128)S(1)} %copy.270), channel_id=1, source_target_pairs={{0,1},{1,2},{2,3},{3,4},{4,5},{5,6},{6,7},{7,8},{8,9},{9,10},{10,1... | collective-permute-start | bytes 393224 | tf_op jit(solution)/shard_map/ppermute | solution.py:27
  39.2 11.7 %collective-permute-start.3 = (f32[8,1,1,4096]{3,0,2,1:T(8,128)S(1)}, f32[8,1,1,4096]{3,0,2,1:T(8,128)S(1)}, u32[]{:S(2)}, u32[]{:S(2)}) collective-permute-start(f32[8,1,1,4096]{3,0,2,1:T(8,128)S(1)} %copy.271), channel_id=1, source_target_pairs={{1,0},{2,1},{3,2},{4,3},{5,4},{6,5},{7,6},{8,7},{9,8},{10,9},{11,1... | collective-permute-start | bytes 393224 | tf_op jit(solution)/shard_map/ppermute | solution.py:29
  369.5 2.6 copy-start.2
  380.0 1.4 copy-start.1
  381.5 9.1 %collective-permute-start.6 = (f32[8,3,8,256]{3,1,0,2:T(4,128)S(1)}, f32[8,3,8,256]{3,1,0,2:T(4,128)S(1)}, u32[]{:S(2)}, u32[]{:S(2)}) collective-permute-start(f32[8,3,8,256]{3,1,0,2:T(4,128)S(1)} %copy_multiply_fusion), channel_id=1, source_target_pairs={{0,1},{1,2},{2,3},{3,4},{4,5},{5,6},{6,7},{7,8},{8,9},{9,10},{10,1... | collective-permute-start | bytes 589832 | tf_op jit(solution)/shard_map/ppermute | solution.py:171
  390.9 10.8 %collective-permute-start.7 = (f32[8,3,8,256]{3,1,0,2:T(4,128)S(1)}, f32[8,3,8,256]{3,1,0,2:T(4,128)S(1)}, u32[]{:S(2)}, u32[]{:S(2)}) collective-permute-start(f32[8,3,8,256]{3,1,0,2:T(4,128)S(1)} %broadcast_select_fusion), channel_id=1, source_target_pairs={{0,2},{1,3},{2,4},{3,5},{4,6},{5,7},{6,8},{7,9},{8,10},{9,11},{10,... | collective-permute-start | bytes 589832 | tf_op jit(solution)/shard_map/ppermute | solution.py:171
  401.8 13.6 %collective-permute-start.8 = (f32[8,3,8,256]{3,1,0,2:T(4,128)S(1)}, f32[8,3,8,256]{3,1,0,2:T(4,128)S(1)}, u32[]{:S(2)}, u32[]{:S(2)}) collective-permute-start(f32[8,3,8,256]{3,1,0,2:T(4,128)S(1)} %broadcast_select_fusion.1), channel_id=1, source_target_pairs={{0,4},{1,5},{2,6},{3,7},{4,8},{5,9},{6,10},{7,11},{8,12},{9,13},{1... | collective-permute-start | bytes 589832 | tf_op jit(solution)/shard_map/ppermute | solution.py:171
  415.5 28.3 %collective-permute-start.9 = (f32[8,3,8,256]{3,1,0,2:T(4,128)S(1)}, f32[8,3,8,256]{3,1,0,2:T(4,128)S(1)}, u32[]{:S(2)}, u32[]{:S(2)}) collective-permute-start(f32[8,3,8,256]{3,1,0,2:T(4,128)S(1)} %broadcast_select_fusion.2), channel_id=1, source_target_pairs={{0,8},{1,9},{2,10},{3,11},{4,12},{5,13},{6,14},{7,15},{8,16},{9,17... | collective-permute-start | bytes 589832 | tf_op jit(solution)/shard_map/ppermute | solution.py:171
  444.0 8.0 %collective-permute-start.10 = (f32[8,3,8,256]{3,1,0,2:T(4,128)S(1)}, f32[8,3,8,256]{3,1,0,2:T(4,128)S(1)}, u32[]{:S(2)}, u32[]{:S(2)}) collective-permute-start(f32[8,3,8,256]{3,1,0,2:T(4,128)S(1)} %broadcast_select_fusion.3), channel_id=1, source_target_pairs={{0,16},{1,17},{2,18},{3,19},{4,20},{5,21},{6,22},{7,23},{8,24},{9,... | collective-permute-start | bytes 589832 | tf_op jit(solution)/shard_map/ppermute | solution.py:171
  452.1 14.0 %collective-permute-start.11 = (f32[8,3,8,256]{3,1,0,2:T(4,128)S(1)}, f32[8,3,8,256]{3,1,0,2:T(4,128)S(1)}, u32[]{:S(2)}, u32[]{:S(2)}) collective-permute-start(f32[8,3,8,256]{3,1,0,2:T(4,128)S(1)} %broadcast_select_fusion.4), channel_id=1, source_target_pairs={{31,0},{1,1},{3,2},{5,3},{7,4},{9,5},{11,6},{13,7},{15,8},{17,9},{... | collective-permute-start | bytes 589832 | tf_op jit(solution)/shard_map/ppermute | solution.py:182
  452.8 15.6 %collective-permute-start.12 = (f32[8,3,8,256]{3,1,0,2:T(4,128)S(1)}, f32[8,3,8,256]{3,1,0,2:T(4,128)S(1)}, u32[]{:S(2)}, u32[]{:S(2)}) collective-permute-start(f32[8,3,8,256]{3,1,0,2:T(4,128)S(1)} %broadcast_select_fusion.4), channel_id=1, source_target_pairs={{31,16},{1,17},{3,18},{5,19},{7,20},{9,21},{11,22},{13,23},{15,24}... | collective-permute-start | bytes 589832 | tf_op jit(solution)/shard_map/ppermute | solution.py:182
  454.1 14.4 %collective-permute-start.13 = (f32[8,3,8,256]{3,1,0,2:T(4,128)S(1)}, f32[8,3,8,256]{3,1,0,2:T(4,128)S(1)}, u32[]{:S(2)}, u32[]{:S(2)}) collective-permute-start(f32[8,3,8,256]{3,1,0,2:T(4,128)S(1)} %broadcast_select_fusion.4), channel_id=1, source_target_pairs={{0,0},{2,1},{4,2},{6,3},{8,4},{10,5},{12,6},{14,7},{16,8},{18,9},{... | collective-permute-start | bytes 589832 | tf_op jit(solution)/shard_map/ppermute | solution.py:182
  463.5 10.0 %collective-permute-start.14 = (f32[8,3,8,256]{3,1,0,2:T(4,128)S(1)}, f32[8,3,8,256]{3,1,0,2:T(4,128)S(1)}, u32[]{:S(2)}, u32[]{:S(2)}) collective-permute-start(f32[8,3,8,256]{3,1,0,2:T(4,128)S(1)} %broadcast_select_fusion.4), channel_id=1, source_target_pairs={{0,16},{2,17},{4,18},{6,19},{8,20},{10,21},{12,22},{14,23},{16,24}... | collective-permute-start | bytes 589832 | tf_op jit(solution)/shard_map/ppermute | solution.py:182
  465.4 8.1 %collective-permute-start.15 = (f32[8,3,8,256]{3,1,0,2:T(4,128)S(1)}, f32[8,3,8,256]{3,1,0,2:T(4,128)S(1)}, u32[]{:S(2)}, u32[]{:S(2)}) collective-permute-start(f32[8,3,8,256]{3,1,0,2:T(4,128)S(1)} %broadcast_select_fusion.4), channel_id=1, source_target_pairs={{1,0},{3,1},{5,2},{7,3},{9,4},{11,5},{13,6},{15,7},{17,8},{19,9},{... | collective-permute-start | bytes 589832 | tf_op jit(solution)/shard_map/ppermute | solution.py:182
  466.1 15.4 %collective-permute-start.16 = (f32[8,3,8,256]{3,1,0,2:T(4,128)S(1)}, f32[8,3,8,256]{3,1,0,2:T(4,128)S(1)}, u32[]{:S(2)}, u32[]{:S(2)}) collective-permute-start(f32[8,3,8,256]{3,1,0,2:T(4,128)S(1)} %broadcast_select_fusion.4), channel_id=1, source_target_pairs={{1,16},{3,17},{5,18},{7,19},{9,20},{11,21},{13,22},{15,23},{17,24}... | collective-permute-start | bytes 589832 | tf_op jit(solution)/shard_map/ppermute | solution.py:182

commit v2 on v1

--- a/solution.py
+++ b/solution.py
@@ -82,19 +82,17 @@
 
     stepped = parent_step(parent_state)
 
-    colslice = jax.vmap(lambda f, c0: lax.dynamic_slice_in_dim(f, c0 - 1, span + 2, axis=2))(
-        stepped, cols_off
+    colslice = jnp.concatenate(
+        [
+            lax.dynamic_slice(stepped, (m, 0, 0, cols_off[m] - 1), (1, 3, band_rows, span + 2))
+            for m in range(members)
+        ],
+        axis=0,
     )
 
     west = two * colslice[..., 0] + one * colslice[..., 1]
     east = one * colslice[..., span] + two * colslice[..., span + 1]
-    strip = jnp.stack([west, east], axis=2)
-    gathered = lax.all_gather(strip.reshape(1, -1), "band", axis=0, tiled=True)
-    strip_all = (
-        gathered.reshape(bands, members, 3, 2, band_rows)
-        .transpose(1, 2, 3, 0, 4)
-        .reshape(members, 3, 2, parent_total)
-    )
+    strip = jnp.stack([west, east], axis=2).reshape(members * 6, band_rows)
 
     global_rows = band_index * band_rows + jnp.arange(band_rows, dtype=jnp.int32)
     row_start = rows_off[:, None]
@@ -106,7 +104,25 @@
     )
     row_weights = jnp.stack([south_weight, north_weight], axis=1)
     ends_part = jnp.einsum("msl,mflq->mfsq", row_weights, colslice, precision=highest)
-    ends_full = lax.psum(ends_part, "band")
+
+    blocks = strip
+    sums = ends_part.reshape(members * 6, span + 2)
+    reach = 1
+    while reach < bands:
+        count = min(4, bands // reach)
+        payload = jnp.concatenate([blocks, sums], axis=1)
+        width = blocks.shape[1]
+        recvs = [
+            lax.ppermute(payload, "band", [(i, (i + k * reach) % bands) for i in range(bands)])
+            for k in range(count - 1, 0, -1)
+        ]
+        blocks = jnp.concatenate([got[:, :width] for got in recvs] + [blocks], axis=1)
+        for got in recvs:
+            sums = sums + got[:, width:]
+        reach *= count
+    strip_all = blocks.reshape(members, 3, 2, parent_total)
+    held_rows = ((band_index + 1) * band_rows + jnp.arange(parent_total, dtype=jnp.int32)) % parent_total
+    ends_full = sums.reshape(members, 3, 2, span + 2)
     inner_weights = interp_matrix(nest_width + 2, span + 2)[1:-1]
     ends = jnp.einsum("jq,mfsq->mfsj", inner_weights, ends_full, precision=highest)
 
@@ -116,7 +132,7 @@
     lower = (3 - frac).astype(jnp.float32) / 3.0
     upper = frac.astype(jnp.float32) / 3.0
     first_row = rows_off[:, None] - 1 + base[None, :]
-    all_rows = jnp.arange(parent_total, dtype=jnp.int32)[None, None, :]
+    all_rows = held_rows[None, None, :]
     side_weights = jnp.where(all_rows == first_row[:, :, None], lower[None, :, None], 0.0) + jnp.where(
         all_rows == first_row[:, :, None] + 1, upper[None, :, None], 0.0
     )
@@ -166,12 +182,16 @@
 
     shift = (rows_off + tile_coarse - 1) // tile_coarse - 1
     moved = coarse
-    step = 1
-    while step < bands:
-        recv = lax.ppermute(moved, "band", [(i, (i + step) % bands) for i in range(bands)])
-        take = ((shift // step) % 2 == 1)[:, None, None, None]
-        moved = jnp.where(take, recv, moved)
-        step *= 2
+    reach = 1
+    while reach < bands:
+        count = min(4, bands // reach)
+        digit = (shift // reach) % count
+        chosen = moved
+        for k in range(1, count):
+            recv = lax.ppermute(moved, "band", [(i, (i + k * reach) % bands) for i in range(bands)])
+            chosen = jnp.where((digit == k)[:, None, None, None], recv, chosen)
+        moved = chosen
+        reach *= count
     half = bands // 2
     low_half = band_index < half
     pieces = []

time: 519 us -> 732 us (1.41)
  blocking collectives: 249 us -> 0 us
  local copies, waits for them, and re-layouts: 98.6 us -> 324 us
  other arithmetic: 26.3 us -> 214 us
  waiting for transfers between devices: 42.7 us -> 62.3 us
  starting transfers between devices: 70.8 us -> 85.6 us
  between operations: 16.4 us -> 25.7 us
    psum x1 -> x0, blocking collectives: 161 us -> none  [per_device(): ends_full = lax.psum(ends_part, 'band')]
    all_gather x1 -> x0, blocking collectives: 87.8 us -> none  [per_device(): gathered = lax.all_gather(strip.reshape(1, -1), 'band', axis=0, tiled=True)]
    dynamic_update_slice x8, local copies, waits for them, and re-layouts: 15.4 us -> 95.3 us  [per_device(): parent_out = lax.dynamic_update_slice(parent_out, merged, start)]
    another operation x2, other arithmetic: 3.98 us -> 63.1 us  [parent_step(): return jnp.stack([height_new, zonal_new, merid_new], axis=1)]
    unnamed x18 -> x75, local copies, waits for them, and re-layouts: 8.2 us -> 62.3 us
    another operation x2, local copies, waits for them, and re-layouts: 48.6 us -> 0.03 us  [per_device(): strip = jnp.stack([west, east], axis=2).reshape(members * 6, band_rows)]
    sub x1, other arithmetic: 2.52 us -> 34.3 us  [parent_step(): height - courant * (shift_cols(zonal) + 0.5 * (merid_ext[:, 2:] - merid_e...]
    add x1, other arithmetic: 0.84 us -> 28.7 us  [parent_step(): (1.0 - friction) * zonal - courant * shift_cols(height_new)]
  transfers between devices with their start and end apart: 17 -> 26, of which waited for: 9 -> 13; matrix products, arithmetic and copies ran while one was open for 18% -> 51% of each run, Pallas kernels for 0% -> 0%
where the time goes in v2:
time: 732 us; the launch traced here: 718 us
  local copies, waits for them, and re-layouts  324 us (44%)
  other arithmetic  214 us (29%)
  starting transfers between devices  85.6 us (12%)
  waiting for transfers between devices  62.3 us (9%)
  between operations  25.7 us (4%)
    dynamic_update_slice x8, local copies, waits for them, and re-layouts, per_device(): parent_out = lax.dynamic_update_slice(parent_out, merged, start)  95.3 us
    another operation x2, other arithmetic, parent_step(): return jnp.stack([height_new, zonal_new, merid_new], axis=1)  63.1 us
    unnamed x75, local copies, waits for them, and re-layouts  62.3 us
    sub x1, other arithmetic, parent_step(): height - courant * (shift_cols(zonal) + 0.5 * (merid_ext[:, 2:] - merid_e...  34.3 us
    ppermute x7, waiting for transfers between devices, per_device(): lax.ppermute(moved, 'band', [(i, (i + k * reach) % bands) for i in range(...  34.1 us
    add x1, other arithmetic, parent_step(): (1.0 - friction) * zonal - courant * shift_cols(height_new)  28.7 us
    slice x4, local copies, waits for them, and re-layouts, with_halo(): tail = cells[:, :, cells.shape[2] - width:]  24.9 us
    concatenate x2, local copies, waits for them, and re-layouts, shift_cols(): return 0.5 * (jnp.roll(field, -1, axis=-1) - jnp.roll(field, 1, axis=-1))  24.5 us
  transfers between devices with their start and end apart: 26, of which 13 were waited for; matrix products, arithmetic and copies ran while one was open for 51% of the time, Pallas kernels for 0%

profile of v2, /device:TPU:112, one launch (start us, length us, event | category | flops | bytes accessed | tf_op | source)
XLA Modules:
  0.0 718.2 jit_solution(8013135795723370674)
XLA Ops:
  2.5 4.8 collective-permute-start.1
  7.3 2.6 collective-permute-start
  12.2 5.7 collective-permute-start.5
  18.7 4.2 collective-permute-start.4
  22.9 5.5 fusion.110
  28.4 9.5 %copy.421 = f32[8,1,16,4096]{2,0,3,1:T(8,128)} copy(f32[8,1,16,4096]{3,2,1,0:T(8,128)} %get-tuple-element.49) | data formatting | bytes 4194304
  38.6 21.9 %fusion.109 = (f32[8,16,4095]{1,0,2:T(8,128)}, f32[8,16,4095]{1,0,2:T(8,128)}) fusion(f32[8,16,4096]{1,0,2:T(8,128)} %bitcast.149), kind=kLoop, calls=%fused_computation.260 | loop fusion | bytes 8386560 | tf_op jit(solution)/shard_map/jit(_roll_static)/slice | solution.py:46
  75.6 9.6 %copy.423 = f32[8,1,16,4096]{2,0,3,1:T(8,128)} copy(f32[8,1,16,4096]{3,2,1,0:T(8,128)} %get-tuple-element.50) | data formatting | bytes 4194304
  85.2 8.8 %copy.420 = f32[8,1,16,4096]{2,0,3,1:T(8,128)} copy(f32[8,1,16,4096]{3,2,1,0:T(8,128)S(1)} %get-tuple-element.48) | data formatting | bytes 4194304
  94.6 8.8 %copy.369 = f32[8,1,1,4096]{2,0,3,1:T(8,128)} copy(f32[8,1,1,4096]{3,0,2,1:T(8,128)S(1)} %collective-permute-done.1) | data formatting | bytes 262144 | tf_op jit(solution)/shard_map/ppermute | solution.py:29
  103.4 8.8 %copy.368 = f32[8,1,1,4096]{2,0,3,1:T(8,128)} copy(f32[8,1,1,4096]{3,0,2,1:T(8,128)S(1)} %collective-permute-done) | data formatting | bytes 262144 | tf_op jit(solution)/shard_map/ppermute | solution.py:27
  112.3 23.6 %maximum_bitcast_fusion = f32[8,18,4096]{1,0,2:T(8,128)} fusion(f32[8,1,1,4096]{2,0,3,1:T(8,128)} %copy.369, f32[8,1,16,4096]{2,0,3,1:T(8,128)} %copy.423, f32[8,1,1,4096]{2,0,3,1:T(8,128)} %copy.368), kind=kLoop, calls=%fused_computation.12 | loop fusion | flops 1179648 | bytes 4718592 | tf_op jit(solution)/shard_map/squeeze | solution.py:51
  135.8 34.3 %fusion.6 = f32[8,16,4096]{1,0,2:T(8,128)} fusion(f32[8,18,4096]{1,0,2:T(8,128)} %maximum_bitcast_fusion, f32[8,16,1]{1,0,2:T(8,128)S(1)} %get-tuple-element.45, f32[8,16,4095]{1,0,2:T(8,128)} %get-tuple-element.47, f32[8,16,4095]{1,0,2:T(8,128)} %get-tuple-element.46, f32[8,16,1]{1,0,2:T(8,128)S(1)} %get-tuple-element.44, f32[8,1,16,4096]{2,0,3,1:T(8,128)} %copy.420), kind=kLoop, calls=%fused_computation.10 | loop fusion | flops 3670016 | bytes 12582912 | tf_op jit(solution)/shard_map/sub | solution.py:52
  171.0 23.7 %slice_bitcast_fusion = (f32[8,1,16,4095]{2,0,3,1:T(8,128)}, f32[8,1,16,4095]{2,0,3,1:T(8,128)}) fusion(f32[8,16,4096]{1,0,2:T(8,128)} %fusion.6), kind=kLoop, calls=%fused_computation.18 | loop fusion | bytes 8386560 | tf_op jit(solution)/shard_map/jit(_roll_static)/concatenate | solution.py:46
  197.4 12.1 %fusion.107 = (f32[8,1,1,4096]{2,0,3,1:T(8,128)}, f32[8,1,1,4096]{2,0,3,1:T(8,128)}) fusion(f32[8,1,16,4096]{2,0,3,1:T(8,128)S(1)} %bitcast.147), kind=kLoop, calls=%fused_computation.258 | loop fusion | bytes 524288 | tf_op jit(solution)/shard_map/slice | solution.py:24
  209.5 9.7 %copy.371 = f32[8,1,1,4096]{3,0,2,1:T(8,128)S(1)} copy(f32[8,1,1,4096]{2,0,3,1:T(8,128)} %get-tuple-element.43) | data formatting | bytes 262144 | tf_op jit(solution)/shard_map/slice | solution.py:23
  219.2 4.3 collective-permute-start.3
  223.5 9.7 %copy.370 = f32[8,1,1,4096]{3,0,2,1:T(8,128)S(1)} copy(f32[8,1,1,4096]{2,0,3,1:T(8,128)} %get-tuple-element.42) | data formatting | bytes 262144 | tf_op jit(solution)/shard_map/slice | solution.py:24
  233.2 6.3 collective-permute-start.2
  239.6 28.7 %fusion.9 = f32[8,1,16,4096]{2,0,3,1:T(8,128)} fusion(f32[8,1,16,1]{2,0,3,1:T(8,128)S(1)} %get-tuple-element.39, f32[8,1,16,4095]{2,0,3,1:T(8,128)} %get-tuple-element.41, f32[8,1,16,4095]{2,0,3,1:T(8,128)} %get-tuple-element.40, f32[8,1,16,1]{2,0,3,1:T(8,128)S(1)} %get-tuple-element.38, f32[8,1,16,4096]{2,0,3,1:T(8,128)} %copy.423, f32[8,1,16,4096]{2,0,3,1:T(8,128)} %copy.421), kind=kLoop, calls=%fused_computation.16 | loop fusion | flops 4194304 | bytes 10485760 | tf_op jit(solution)/shard_map/add | solution.py:56
  268.2 8.9 %copy.373 = f32[8,1,1,4096]{2,0,3,1:T(8,128)} copy(f32[8,1,1,4096]{3,0,2,1:T(8,128)S(1)} %collective-permute-done.3) | data formatting | bytes 262144 | tf_op jit(solution)/shard_map/ppermute | solution.py:29
  277.1 8.7 %copy.372 = f32[8,1,1,4096]{2,0,3,1:T(8,128)} copy(f32[8,1,1,4096]{3,0,2,1:T(8,128)S(1)} %collective-permute-done.2) | data formatting | bytes 262144 | tf_op jit(solution)/shard_map/ppermute | solution.py:27
  285.8 23.6 %maximum_bitcast_fusion.1 = f32[8,18,4096]{1,0,2:T(8,128)} fusion(f32[8,1,1,4096]{2,0,3,1:T(8,128)} %copy.373, f32[8,1,16,4096]{2,0,3,1:T(8,128)} %bitcast.143, f32[8,1,1,4096]{2,0,3,1:T(8,128)} %copy.372), kind=kLoop, calls=%fused_computation.17 | loop fusion | flops 1179648 | bytes 4718592 | tf_op jit(solution)/shard_map/squeeze | solution.py:55
  309.4 29.5 %fusion.3 = f32[8,1,16,4096]{2,0,3,1:T(8,128)} fusion(f32[8,18,4096]{1,0,2:T(8,128)} %maximum_bitcast_fusion.1, f32[8,1,16,4096]{2,0,3,1:T(8,128)} %copy.423, f32[8,1,16,4096]{2,0,3,1:T(8,128)} %copy.421), kind=kLoop, calls=%fused_computation.6 | loop fusion | flops 3145728 | bytes 10485760 | tf_op jit(solution)/shard_map/stack | solution.py:62
  339.0 33.6 %pad_maximum_fusion = f32[8,3,16,4096]{2,0,3,1:T(8,128)} fusion(f32[8,1,16,4096]{2,0,3,1:T(8,128)} %fusion.3, f32[8,1,16,4096]{2,0,3,1:T(8,128)} %fusion.9, f32[8,1,16,4096]{2,0,3,1:T(8,128)} %bitcast.144), kind=kLoop, calls=%fused_computation.1 | loop fusion | flops 3145728 | bytes 12582912 | tf_op jit(solution)/shard_map/stack | solution.py:62
  372.6 12.8 %constant_dynamic-slice_fusion = (f32[1,3,16,258]{2,0,3,1:T(1,128)}, f32[1,3,16,258]{2,0,3,1:T(1,128)}, f32[1,3,16,258]{2,0,3,1:T(1,128)}, f32[1,3,16,258]{2,0,3...) fusion(f32[8,3,16,4096]{2,0,3,1:T(8,128)} %pad_maximum_fusion, ...), kind=kLoop, calls=%fused_computation.176 | loop fusion | bytes 792608 | tf_op jit(solution)/shard_map/dynamic_slice | solution.py:87
  385.4 10.0 %concatenate.170 = f32[8,3,16,258]{2,0,3,1:T(8,128)S(1)} concatenate(f32[1,3,16,258]{2,0,3,1:T(1,128)} %get-tuple-element.37, f32[1,3,16,258]{2,0,3,1:T(1,128)} %get-tuple-element.36, f32[1,3,16,258]{2,0,3,1:T(1,128)} %get-tuple-element.35, f32[1,3,16,258]{2,0,3,1:T(1,128)} %get-tuple-element.34, f32[1,3,16,258]{2,0,3,1:T(1,128)} %get-tuple-element.33, ...), dimensions={0} | concatenate | bytes 792576 | tf_op jit(solution)/shard_map/concatenate | solution.py:85
  395.4 3.8 fusion.12
  399.5 3.6 collective-permute-start.7
  403.2 3.0 collective-permute-start.8
  421.1 3.2 collective-permute-start.9
  424.3 2.2 collective-permute-start.10
  428.7 3.7 collective-permute-done.11
  433.3 11.4 %collective-permute-start.12 = (f32[48,514]{1,0:T(8,128)}, f32[48,514]{1,0:T(8,128)S(1)}, u32[]{:S(2)}, u32[]{:S(2)}) collective-permute-start(f32[48,514]{1,0:T(8,128)} %concatenate.173), channel_id=1, source_target_pairs={{0,16},{1,17},{2,18},{3,19},{4,20},{5,21},{6,22},{7,23},{8,24},{9,... | collective-permute-start | bytes 296072 | tf_op jit(solution)/shard_map/ppermute | solution.py:116
  457.5 3.6 select_select_fusion.6
  465.0 3.1 select_select_fusion.5
  474.6 4.8 collective-permute-start.13
  480.0 7.4 %collective-permute-done.13 = f32[8,3,8,256]{3,1,0,2:T(4,128)S(1)} collective-permute-done((f32[8,3,8,256]{3,1,0,2:T(4,128)S(1)}, f32[8,3,8,256]{3,1,0,2:T(4,128)S(1)}, u32[]{:S(2)}, u32[]{:S(2)}) %collective-permute-start.13) | collective-permute-done | bytes 196640 | tf_op jit(solution)/shard_map/ppermute | solution.py:191
  487.4 6.9 collective-permute-done.14
  497.2 3.3 collective-permute-start.18
  500.6 5.8 collective-permute-done.16
  506.3 4.3 collective-permute-done.17
  510.6 3.0 collective-permute-done.18
  516.1 6.7 collective-permute-done.19
  525.6 14.6 %collective-permute-start.22 = (f32[8,3,8,256]{3,1,0,2:T(4,128)S(1)}, f32[8,3,8,256]{3,1,0,2:T(4,128)S(1)}, u32[]{:S(2)}, u32[]{:S(2)}) collective-permute-start(f32[8,3,8,256]{3,1,0,2:T(4,128)S(1)} %broadcast_select_fusion.8), channel_id=1, source_target_pairs={{0,0},{2,1},{4,2},{6,3},{8,4},{10,5},{12,6},{14,7},{16,8},{18,9},{... | collective-permute-start | bytes 589832 | tf_op jit(solution)/shard_map/ppermute | solution.py:202
  546.3 11.3 %collective-permute-done.23 = f32[8,3,8,256]{3,1,0,2:T(4,128)S(1)} collective-permute-done((f32[8,3,8,256]{3,1,0,2:T(4,128)S(1)}, f32[8,3,8,256]{3,1,0,2:T(4,128)S(1)}, u32[]{:S(2)}, u32[]{:S(2)}) %collective-permute-start.23) | collective-permute-done | bytes 196640 | tf_op jit(solution)/shard_map/ppermute | solution.py:202
  557.8 7.8 %collective-permute-done.21 = f32[8,3,8,256]{3,1,0,2:T(4,128)S(1)} collective-permute-done((f32[8,3,8,256]{3,1,0,2:T(4,128)S(1)}, f32[8,3,8,256]{3,1,0,2:T(4,128)S(1)}, u32[]{:S(2)}, u32[]{:S(2)}) %collective-permute-start.21) | collective-permute-done | bytes 196640 | tf_op jit(solution)/shard_map/ppermute | solution.py:202
  567.9 2.3 broadcast_select_fusion.7
  570.2 11.9 %dynamic_update_slice.24 = f32[8,3,16,4096]{2,0,3,1:T(8,128)} dynamic-update-slice(f32[8,3,16,4096]{2,0,3,1:T(8,128)} %pad_maximum_fusion, f32[1,3,16,256]{2,0,3,1:T(1,128)S(1)} %broadcast_select_fusion.7, s32[]{:T(128)} %constant.200.clone.1, s32[]{:T(128)} %constant.200.clone.1, s32[]{:T(128)} %constant.200.clone.1, s32[]{:T(128)S(6)} %select_n.454) | dynamic-update-slice | bytes 98308 | tf_op jit(solution)/shard_map/dynamic_update_slice | solution.py:215
  582.4 2.4 broadcast_select_fusion.6
  584.8 11.9 %dynamic_update_slice.25 = f32[8,3,16,4096]{2,0,3,1:T(8,128)} dynamic-update-slice(f32[8,3,16,4096]{2,0,3,1:T(8,128)} %dynamic_update_slice.24, f32[1,3,16,256]{2,0,3,1:T(1,128)S(1)} %broadcast_select_fusion.6, s32[]{:T(128)} %constant.203.clone.1, s32[]{:T(128)} %constant.200.clone.1, s32[]{:T(128)} %constant.200.clone.1, s32[]{:T(128)S(6)} %select_n.456) | dynamic-update-slice | bytes 98308 | tf_op jit(solution)/shard_map/dynamic_update_slice | solution.py:215
  600.6 3.3 broadcast_select_fusion.5
  603.9 11.9 %dynamic_update_slice.26 = f32[8,3,16,4096]{2,0,3,1:T(8,128)} dynamic-update-slice(f32[8,3,16,4096]{2,0,3,1:T(8,128)} %dynamic_update_slice.25, f32[1,3,16,256]{2,0,3,1:T(1,128)} %broadcast_select_fusion.5, s32[]{:T(128)} %constant.208.clone.1, s32[]{:T(128)} %constant.200.clone.1, s32[]{:T(128)} %constant.200.clone.1, s32[]{:T(128)S(6)} %select_n.458) | dynamic-update-slice | bytes 98308 | tf_op jit(solution)/shard_map/dynamic_update_slice | solution.py:215
  615.8 3.2 broadcast_select_fusion.4
  619.1 11.9 %dynamic_update_slice.27 = f32[8,3,16,4096]{2,0,3,1:T(8,128)} dynamic-update-slice(f32[8,3,16,4096]{2,0,3,1:T(8,128)} %dynamic_update_slice.26, f32[1,3,16,256]{2,0,3,1:T(1,128)} %broadcast_select_fusion.4, s32[]{:T(128)} %constant.204.clone.1, s32[]{:T(128)} %constant.200.clone.1, s32[]{:T(128)} %constant.200.clone.1, s32[]{:T(128)S(6)} %select_n.460) | dynamic-update-slice | bytes 98308 | tf_op jit(solution)/shard_map/dynamic_update_slice | solution.py:215
  631.0 3.1 broadcast_select_fusion.3
  634.1 11.9 %dynamic_update_slice.28 = f32[8,3,16,4096]{2,0,3,1:T(8,128)} dynamic-update-slice(f32[8,3,16,4096]{2,0,3,1:T(8,128)} %dynamic_update_slice.27, f32[1,3,16,256]{2,0,3,1:T(1,128)} %broadcast_select_fusion.3, s32[]{:T(128)} %constant.207.clone.1, s32[]{:T(128)} %constant.200.clone.1, s32[]{:T(128)} %constant.200.clone.1, s32[]{:T(128)S(6)} %select_n.462) | dynamic-update-slice | bytes 98308 | tf_op jit(solution)/shard_map/dynamic_update_slice | solution.py:215
  646.0 2.4 broadcast_select_fusion.2
  648.4 11.9 %dynamic_update_slice.29 = f32[8,3,16,4096]{2,0,3,1:T(8,128)} dynamic-update-slice(f32[8,3,16,4096]{2,0,3,1:T(8,128)} %dynamic_update_slice.28, f32[1,3,16,256]{2,0,3,1:T(1,128)S(1)} %broadcast_select_fusion.2, s32[]{:T(128)} %constant.212.clone.1, s32[]{:T(128)} %constant.200.clone.1, s32[]{:T(128)} %constant.200.clone.1, s32[]{:T(128)S(6)} %select_n.464) | dynamic-update-slice | bytes 98308 | tf_op jit(solution)/shard_map/dynamic_update_slice | solution.py:215
  660.3 2.4 broadcast_select_fusion.1
  662.6 11.9 %dynamic_update_slice.30 = f32[8,3,16,4096]{2,0,3,1:T(8,128)} dynamic-update-slice(f32[8,3,16,4096]{2,0,3,1:T(8,128)} %dynamic_update_slice.29, f32[1,3,16,256]{2,0,3,1:T(1,128)S(1)} %broadcast_select_fusion.1, s32[]{:T(128)} %constant.213.clone.1, s32[]{:T(128)} %constant.200.clone.1, s32[]{:T(128)} %constant.200.clone.1, s32[]{:T(128)S(6)} %select_n.466) | dynamic-update-slice | bytes 98308 | tf_op jit(solution)/shard_map/dynamic_update_slice | solution.py:215
  674.5 2.4 broadcast_select_fusion
  676.9 11.9 %dynamic_update_slice.31 = f32[8,3,16,4096]{2,0,3,1:T(8,128)} dynamic-update-slice(f32[8,3,16,4096]{2,0,3,1:T(8,128)} %dynamic_update_slice.30, f32[1,3,16,256]{2,0,3,1:T(1,128)S(1)} %broadcast_select_fusion, s32[]{:T(128)} %constant.202.clone.1, s32[]{:T(128)} %constant.200.clone.1, s32[]{:T(128)} %constant.200.clone.1, s32[]{:T(128)S(6)} %select_n.468) | dynamic-update-slice | bytes 98308 | tf_op jit(solution)/shard_map/dynamic_update_slice | solution.py:215
  688.8 29.0 %copy.415 = f32[8,3,16,4096]{3,2,1,0:T(8,128)} copy(f32[8,3,16,4096]{2,0,3,1:T(8,128)} %dynamic_update_slice.31) | data formatting | bytes 12582912
  (204 shorter events, 63.5 us)
Async XLA Ops:
  2.5 92.1 %collective-permute-start.1 = (f32[8,1,1,4096]{3,0,2,1:T(8,128)S(1)}, f32[8,1,1,4096]{3,0,2,1:T(8,128)S(1)}, u32[]{:S(2)}, u32[]{:S(2)}) collective-permute-start(f32[8,1,1,4096]{3,0,2,1:T(8,128)S(1)} %copy.424), channel_id=1, source_target_pairs={{1,0},{2,1},{3,2},{4,3},{5,4},{6,5},{7,6},{8,7},{9,8},{10,9},{11,1... | collective-permute-start | bytes 393224 | tf_op jit(solution)/shard_map/ppermute | solution.py:29
  7.3 96.1 %collective-permute-start = (f32[8,1,1,4096]{3,0,2,1:T(8,128)S(1)}, f32[8,1,1,4096]{3,0,2,1:T(8,128)S(1)}, u32[]{:S(2)}, u32[]{:S(2)}) collective-permute-start(f32[8,1,1,4096]{3,0,2,1:T(8,128)S(1)} %copy.422), channel_id=1, source_target_pairs={{0,1},{1,2},{2,3},{3,4},{4,5},{5,6},{6,7},{7,8},{8,9},{9,10},{10,1... | collective-permute-start | bytes 393224 | tf_op jit(solution)/shard_map/ppermute | solution.py:27
  12.2 432.5 %collective-permute-start.5 = (f32[8,3,6,768]{3,0,2,1:T(8,128)}, f32[8,3,6,768]{3,0,2,1:T(8,128)}, u32[]{:S(2)}, u32[]{:S(2)}) collective-permute-start(f32[8,3,6,768]{3,0,2,1:T(8,128)} %copy.426), channel_id=1, source_target_pairs={{1,0},{2,1},{3,2},{4,3},{5,4},{6,5},{7,6},{8,7},{9,8},{10,9},{11,1... | collective-permute-start | bytes 1327112 | tf_op jit(solution)/shard_map/ppermute | solution.py:29
  18.7 427.1 %collective-permute-start.4 = (f32[8,3,6,768]{3,0,2,1:T(8,128)}, f32[8,3,6,768]{3,0,2,1:T(8,128)}, u32[]{:S(2)}, u32[]{:S(2)}) collective-permute-start(f32[8,3,6,768]{3,0,2,1:T(8,128)} %copy.425), channel_id=1, source_target_pairs={{0,1},{1,2},{2,3},{3,4},{4,5},{5,6},{6,7},{7,8},{8,9},{9,10},{10,1... | collective-permute-start | bytes 1327112 | tf_op jit(solution)/shard_map/ppermute | solution.py:27
  38.6 21.9 %copy-start.9 = (s32[8,2]{0,1:T(2,128)S(1)}, s32[8,2]{0,1:T(2,128)}, u32[]{:S(2)}) copy-start(s32[8,2]{0,1:T(2,128)} %param.5) | copy-start | bytes 196
  61.8 32.2 %copy-start.17 = (s32[8]{0:T(128)}, s32[8]{0:T(128)S(1)}, u32[]{:S(2)}) copy-start(s32[8]{0:T(128)S(1)} %get-tuple-element.119) | copy-start | bytes 100
  63.5 30.5 %copy-start.24 = (s32[16]{0:T(128)}, s32[16]{0:T(128)S(1)}, u32[]{:S(2)}) copy-start(s32[16]{0:T(128)S(1)} %iota_add_fusion.2) | copy-start | bytes 196
  170.2 24.5 %slice-start = ((s8[16777216]{0:T(1024)(128)(4,1)}), s8[4194304]{0:T(1024)(128)(4,1)S(1)}, s32[]{:S(2)}) async-start(s8[16777216]{0:T(1024)(128)(4,1)} %bitcast.145), calls=%async_computation | async-start | bytes 8388608
  171.0 23.7 %slice-start.1 = ((s8[16777216]{0:T(1024)(128)(4,1)}), s8[4194304]{0:T(1024)(128)(4,1)S(1)}, s32[]{:S(2)}) async-start(s8[16777216]{0:T(1024)(128)(4,1)} %bitcast.145), calls=%async_computation.1 | async-start | bytes 8388608
  171.0 25.4 %slice-start.2 = ((s8[16777216]{0:T(1024)(128)(4,1)}), s8[4194304]{0:T(1024)(128)(4,1)S(1)}, s32[]{:S(2)}) async-start(s8[16777216]{0:T(1024)(128)(4,1)} %bitcast.145), calls=%async_computation.2 | async-start | bytes 8388608
  171.0 26.4 %slice-start.3 = ((s8[16777216]{0:T(1024)(128)(4,1)}), s8[4194304]{0:T(1024)(128)(4,1)S(1)}, s32[]{:S(2)}) async-start(s8[16777216]{0:T(1024)(128)(4,1)} %bitcast.145), calls=%async_computation.3 | async-start | bytes 8388608
  219.2 49.0 %collective-permute-start.3 = (f32[8,1,1,4096]{3,0,2,1:T(8,128)S(1)}, f32[8,1,1,4096]{3,0,2,1:T(8,128)S(1)}, u32[]{:S(2)}, u32[]{:S(2)}) collective-permute-start(f32[8,1,1,4096]{3,0,2,1:T(8,128)S(1)} %copy.371), channel_id=1, source_target_pairs={{1,0},{2,1},{3,2},{4,3},{5,4},{6,5},{7,6},{8,7},{9,8},{10,9},{11,1... | collective-permute-start | bytes 393224 | tf_op jit(solution)/shard_map/ppermute | solution.py:29
  233.2 43.9 %collective-permute-start.2 = (f32[8,1,1,4096]{3,0,2,1:T(8,128)S(1)}, f32[8,1,1,4096]{3,0,2,1:T(8,128)S(1)}, u32[]{:S(2)}, u32[]{:S(2)}) collective-permute-start(f32[8,1,1,4096]{3,0,2,1:T(8,128)S(1)} %copy.370), channel_id=1, source_target_pairs={{0,1},{1,2},{2,3},{3,4},{4,5},{5,6},{6,7},{7,8},{8,9},{9,10},{10,1... | collective-permute-start | bytes 393224 | tf_op jit(solution)/shard_map/ppermute | solution.py:27
  338.9 56.5 %copy-start.11 = (f32[8,1,16]{2,1,0:T(1,128)S(1)}, f32[8,1,16]{2,1,0:T(1,128)}, u32[]{:S(2)}) copy-start(f32[8,1,16]{2,1,0:T(1,128)} %get-tuple-element.136) | copy-start | bytes 1540
  338.9 56.5 %copy-start.12 = (f32[8,1,16]{2,1,0:T(1,128)S(1)}, f32[8,1,16]{2,1,0:T(1,128)}, u32[]{:S(2)}) copy-start(f32[8,1,16]{2,1,0:T(1,128)} %get-tuple-element.137) | copy-start | bytes 1540
  338.9 76.8 %copy-start.14 = (f32[770]{0:T(1024)S(1)}, f32[770]{0:T(1024)}, u32[]{:S(2)}) copy-start(f32[770]{0:T(1024)} %get-tuple-element.140) | copy-start | bytes 9244
  338.9 76.9 %copy-start.13 = (f32[770]{0:T(1024)S(1)}, f32[770]{0:T(1024)}, u32[]{:S(2)}) copy-start(f32[770]{0:T(1024)} %get-tuple-element.141) | copy-start | bytes 9244
  339.0 76.9 %copy-start.16 = (s32[770]{0:T(1024)S(1)}, s32[770]{0:T(1024)}, u32[]{:S(2)}) copy-start(s32[770]{0:T(1024)} %get-tuple-element.139) | copy-start | bytes 9244
  339.0 77.0 %copy-start.15 = (s32[770]{0:T(1024)S(1)}, s32[770]{0:T(1024)}, u32[]{:S(2)}) copy-start(s32[770]{0:T(1024)} %get-tuple-element.138) | copy-start | bytes 9244
  372.6 78.6 %copy-start.19 = (s32[8,36]{1,0:T(8,128)S(1)}, s32[8,36]{1,0:T(8,128)}, u32[]{:S(2)}) copy-start(s32[8,36]{1,0:T(8,128)} %get-tuple-element.120) | copy-start | bytes 3460
  372.6 78.6 %copy-start.20 = (s32[8,36]{1,0:T(8,128)S(1)}, s32[8,36]{1,0:T(8,128)}, u32[]{:S(2)}) copy-start(s32[8,36]{1,0:T(8,128)} %get-tuple-element.121) | copy-start | bytes 3460
  372.6 78.6 %copy-start.23 = (s32[512]{0:T(512)S(1)}, s32[512]{0:T(512)}, u32[]{:S(2)}) copy-start(s32[512]{0:T(512)} %add_select_fusion.3) | copy-start | bytes 6148
  399.5 21.3 %collective-permute-start.6 = (f32[48,274]{1,0:T(8,128)S(1)}, f32[48,274]{1,0:T(8,128)S(1)}, u32[]{:S(2)}, u32[]{:S(2)}) collective-permute-start(f32[48,274]{1,0:T(8,128)S(1)} %pad_maximum_fusion.17), channel_id=1, source_target_pairs={{0,3},{1,4},{2,5},{3,6},{4,7},{5,8},{6,9},{7,10},{8,11},{9,12},{10... | collective-permute-start | bytes 157832 | tf_op jit(solution)/shard_map/ppermute | solution.py:116
  399.5 21.3 %collective-permute-start.7 = (f32[48,274]{1,0:T(8,128)S(1)}, f32[48,274]{1,0:T(8,128)S(1)}, u32[]{:S(2)}, u32[]{:S(2)}) collective-permute-start(f32[48,274]{1,0:T(8,128)S(1)} %pad_maximum_fusion.17), channel_id=1, source_target_pairs={{0,2},{1,3},{2,4},{3,5},{4,6},{5,7},{6,8},{7,9},{8,10},{9,11},{10,... | collective-permute-start | bytes 157832 | tf_op jit(solution)/shard_map/ppermute | solution.py:116
  403.2 17.6 %collective-permute-start.8 = (f32[48,274]{1,0:T(8,128)S(1)}, f32[48,274]{1,0:T(8,128)S(1)}, u32[]{:S(2)}, u32[]{:S(2)}) collective-permute-start(f32[48,274]{1,0:T(8,128)S(1)} %pad_maximum_fusion.17), channel_id=1, source_target_pairs={{0,1},{1,2},{2,3},{3,4},{4,5},{5,6},{6,7},{7,8},{8,9},{9,10},{10,1... | collective-permute-start | bytes 157832 | tf_op jit(solution)/shard_map/ppermute | solution.py:116
  421.1 6.9 collective-permute-start.9
  424.3 4.4 collective-permute-start.10
  426.5 5.9 collective-permute-start.11
  433.3 17.0 %collective-permute-start.12 = (f32[48,514]{1,0:T(8,128)}, f32[48,514]{1,0:T(8,128)S(1)}, u32[]{:S(2)}, u32[]{:S(2)}) collective-permute-start(f32[48,514]{1,0:T(8,128)} %concatenate.173), channel_id=1, source_target_pairs={{0,16},{1,17},{2,18},{3,19},{4,20},{5,21},{6,22},{7,23},{8,24},{9,... | collective-permute-start | bytes 296072 | tf_op jit(solution)/shard_map/ppermute | solution.py:116
  450.2 0.6 copy-start.7
  453.9 10.1 %copy-start.3 = (f32[8,768]{1,0:T(8,128)}, f32[8,768]{1,0:T(8,128)S(1)}, u32[]{:S(2)}) copy-start(f32[8,768]{1,0:T(8,128)S(1)} %get-tuple-element.97) | copy-start | bytes 73732
  453.9 10.1 %copy-start.5 = (f32[8,768]{1,0:T(8,128)}, f32[8,768]{1,0:T(8,128)S(1)}, u32[]{:S(2)}) copy-start(f32[8,768]{1,0:T(8,128)S(1)} %get-tuple-element.98) | copy-start | bytes 73732
  465.0 3.6 copy-start.1
  465.0 3.6 copy-start.4
  465.0 3.6 copy-start.6
  465.0 4.7 copy-start.2
  470.8 2.3 copy-start.10
  471.1 8.9 %copy-start.27 = (s32[8]{0:T(128)S(1)}, s32[8]{0:T(128)}, u32[]{:S(2)}) copy-start(s32[8]{0:T(128)} %get-tuple-element.133) | copy-start | bytes 100
  471.1 23.2 %copy-start.22 = (pred[8]{0:T(512)(128)(4,1)S(1)}, pred[8]{0:T(512)(128)(4,1)}, u32[]{:S(2)}) copy-start(pred[8]{0:T(512)(128)(4,1)} %get-tuple-element.132) | copy-start | bytes 28
  471.1 29.4 %copy-start.26 = (s32[8]{0:T(128)S(1)}, s32[8]{0:T(128)}, u32[]{:S(2)}) copy-start(s32[8]{0:T(128)} %get-tuple-element.13) | copy-start | bytes 100
  471.1 42.5 %copy-start.21 = (pred[8]{0:T(512)(128)(4,1)S(1)}, pred[8]{0:T(512)(128)(4,1)}, u32[]{:S(2)}) copy-start(pred[8]{0:T(512)(128)(4,1)} %get-tuple-element.12) | copy-start | bytes 28
  471.2 44.9 %copy-start.18 = (s32[8]{0:T(128)S(1)}, s32[8]{0:T(128)}, u32[]{:S(2)}) copy-start(s32[8]{0:T(128)} %copy-done.17) | copy-start | bytes 100
  471.2 44.9 %copy-start.25 = (s32[16]{0:T(128)S(1)}, s32[16]{0:T(128)}, u32[]{:S(2)}) copy-start(s32[16]{0:T(128)} %copy-done.24) | copy-start | bytes 196
  471.2 51.7 %copy-start.28 = (pred[8]{0:T(512)(128)(4,1)S(1)}, pred[8]{0:T(512)(128)(4,1)}, u32[]{:S(2)}) copy-start(pred[8]{0:T(512)(128)(4,1)} %get-tuple-element.10) | copy-start | bytes 28
  471.8 94.2 %copy-start.8 = (s32[8]{0:T(128)S(1)}, s32[8]{0:T(128)}, u32[]{:S(2)}) copy-start(s32[8]{0:T(128)} %get-tuple-element.115) | copy-start | bytes 100
  473.1 244.7 %copy-start = (f32[8,3,24,768]{3,2,1,0:T(8,128)}, f32[8,3,24,768]{3,2,1,0:T(8,128)S(1)}, u32[]{:S(2)}) copy-start(f32[8,3,24,768]{3,2,1,0:T(8,128)S(1)} %pad_maximum_fusion.2) | copy-start | bytes 5308420
  474.6 12.8 %collective-permute-start.13 = (f32[8,3,8,256]{3,1,0,2:T(4,128)S(1)}, f32[8,3,8,256]{3,1,0,2:T(4,128)S(1)}, u32[]{:S(2)}, u32[]{:S(2)}) collective-permute-start(f32[8,3,8,256]{3,1,0,2:T(4,128)S(1)} %copy_multiply_fusion), channel_id=1, source_target_pairs={{0,3},{1,4},{2,5},{3,6},{4,7},{5,8},{6,9},{7,10},{8,11},{9,12},{10... | collective-permute-start | bytes 589832 | tf_op jit(solution)/shard_map/ppermute | solution.py:191
  479.4 15.0 %collective-permute-start.14 = (f32[8,3,8,256]{3,1,0,2:T(4,128)S(1)}, f32[8,3,8,256]{3,1,0,2:T(4,128)S(1)}, u32[]{:S(2)}, u32[]{:S(2)}) collective-permute-start(f32[8,3,8,256]{3,1,0,2:T(4,128)S(1)} %copy_multiply_fusion), channel_id=1, source_target_pairs={{0,2},{1,3},{2,4},{3,5},{4,6},{5,7},{6,8},{7,9},{8,10},{9,11},{10,... | collective-permute-start | bytes 589832 | tf_op jit(solution)/shard_map/ppermute | solution.py:191
  479.4 15.0 %collective-permute-start.15 = (f32[8,3,8,256]{3,1,0,2:T(4,128)S(1)}, f32[8,3,8,256]{3,1,0,2:T(4,128)S(1)}, u32[]{:S(2)}, u32[]{:S(2)}) collective-permute-start(f32[8,3,8,256]{3,1,0,2:T(4,128)S(1)} %copy_multiply_fusion), channel_id=1, source_target_pairs={{0,1},{1,2},{2,3},{3,4},{4,5},{5,6},{6,7},{7,8},{8,9},{9,10},{10,1... | collective-permute-start | bytes 589832 | tf_op jit(solution)/shard_map/ppermute | solution.py:191
  494.7 11.7 %collective-permute-start.16 = (f32[8,3,8,256]{3,1,0,2:T(4,128)S(1)}, f32[8,3,8,256]{3,1,0,2:T(4,128)S(1)}, u32[]{:S(2)}, u32[]{:S(2)}) collective-permute-start(f32[8,3,8,256]{3,1,0,2:T(4,128)S(1)} %select_select_fusion.10), channel_id=1, source_target_pairs={{0,12},{1,13},{2,14},{3,15},{4,16},{5,17},{6,18},{7,19},{8,20},{9,... | collective-permute-start | bytes 589832 | tf_op jit(solution)/shard_map/ppermute | solution.py:191
  496.6 14.0 %collective-permute-start.17 = (f32[8,3,8,256]{3,1,0,2:T(4,128)S(1)}, f32[8,3,8,256]{3,1,0,2:T(4,128)S(1)}, u32[]{:S(2)}, u32[]{:S(2)}) collective-permute-start(f32[8,3,8,256]{3,1,0,2:T(4,128)S(1)} %select_select_fusion.10), channel_id=1, source_target_pairs={{0,8},{1,9},{2,10},{3,11},{4,12},{5,13},{6,14},{7,15},{8,16},{9,17... | collective-permute-start | bytes 589832 | tf_op jit(solution)/shard_map/ppermute | solution.py:191
  497.2 16.4 %collective-permute-start.18 = (f32[8,3,8,256]{3,1,0,2:T(4,128)S(1)}, f32[8,3,8,256]{3,1,0,2:T(4,128)S(1)}, u32[]{:S(2)}, u32[]{:S(2)}) collective-permute-start(f32[8,3,8,256]{3,1,0,2:T(4,128)S(1)} %select_select_fusion.10), channel_id=1, source_target_pairs={{0,4},{1,5},{2,6},{3,7},{4,8},{5,9},{6,10},{7,11},{8,12},{9,13},{1... | collective-permute-start | bytes 589832 | tf_op jit(solution)/shard_map/ppermute | solution.py:191
  513.9 9.0 %collective-permute-start.19 = (f32[8,3,8,256]{3,1,0,2:T(4,128)S(1)}, f32[8,3,8,256]{3,1,0,2:T(4,128)S(1)}, u32[]{:S(2)}, u32[]{:S(2)}) collective-permute-start(f32[8,3,8,256]{3,1,0,2:T(4,128)S(1)} %select_select_fusion.9), channel_id=1, source_target_pairs={{0,16},{1,17},{2,18},{3,19},{4,20},{5,21},{6,22},{7,23},{8,24},{9,... | collective-permute-start | bytes 589832 | tf_op jit(solution)/shard_map/ppermute | solution.py:191
  523.0 19.8 %collective-permute-start.24 = (f32[8,3,8,256]{3,1,0,2:T(4,128)S(1)}, f32[8,3,8,256]{3,1,0,2:T(4,128)S(1)}, u32[]{:S(2)}, u32[]{:S(2)}) collective-permute-start(f32[8,3,8,256]{3,1,0,2:T(4,128)S(1)} %broadcast_select_fusion.8), channel_id=1, source_target_pairs={{1,0},{3,1},{5,2},{7,3},{9,4},{11,5},{13,6},{15,7},{17,8},{19,9},{... | collective-permute-start | bytes 589832 | tf_op jit(solution)/shard_map/ppermute | solution.py:202
  523.7 20.6 %collective-permute-start.25 = (f32[8,3,8,256]{3,1,0,2:T(4,128)S(1)}, f32[8,3,8,256]{3,1,0,2:T(4,128)S(1)}, u32[]{:S(2)}, u32[]{:S(2)}) collective-permute-start(f32[8,3,8,256]{3,1,0,2:T(4,128)S(1)} %broadcast_select_fusion.8), channel_id=1, source_target_pairs={{1,16},{3,17},{5,18},{7,19},{9,20},{11,21},{13,22},{15,23},{17,24}... | collective-permute-start | bytes 589832 | tf_op jit(solution)/shard_map/ppermute | solution.py:202
  525.6 20.8 %collective-permute-start.22 = (f32[8,3,8,256]{3,1,0,2:T(4,128)S(1)}, f32[8,3,8,256]{3,1,0,2:T(4,128)S(1)}, u32[]{:S(2)}, u32[]{:S(2)}) collective-permute-start(f32[8,3,8,256]{3,1,0,2:T(4,128)S(1)} %broadcast_select_fusion.8), channel_id=1, source_target_pairs={{0,0},{2,1},{4,2},{6,3},{8,4},{10,5},{12,6},{14,7},{16,8},{18,9},{... | collective-permute-start | bytes 589832 | tf_op jit(solution)/shard_map/ppermute | solution.py:202
  540.2 17.5 %collective-permute-start.23 = (f32[8,3,8,256]{3,1,0,2:T(4,128)S(1)}, f32[8,3,8,256]{3,1,0,2:T(4,128)S(1)}, u32[]{:S(2)}, u32[]{:S(2)}) collective-permute-start(f32[8,3,8,256]{3,1,0,2:T(4,128)S(1)} %broadcast_select_fusion.8), channel_id=1, source_target_pairs={{0,16},{2,17},{4,18},{6,19},{8,20},{10,21},{12,22},{14,23},{16,24}... | collective-permute-start | bytes 589832 | tf_op jit(solution)/shard_map/ppermute | solution.py:202
  542.1 15.7 %collective-permute-start.20 = (f32[8,3,8,256]{3,1,0,2:T(4,128)S(1)}, f32[8,3,8,256]{3,1,0,2:T(4,128)S(1)}, u32[]{:S(2)}, u32[]{:S(2)}) collective-permute-start(f32[8,3,8,256]{3,1,0,2:T(4,128)S(1)} %broadcast_select_fusion.8), channel_id=1, source_target_pairs={{31,0},{1,1},{3,2},{5,3},{7,4},{9,5},{11,6},{13,7},{15,8},{17,9},{... | collective-permute-start | bytes 589832 | tf_op jit(solution)/shard_map/ppermute | solution.py:202
  542.8 22.8 %collective-permute-start.21 = (f32[8,3,8,256]{3,1,0,2:T(4,128)S(1)}, f32[8,3,8,256]{3,1,0,2:T(4,128)S(1)}, u32[]{:S(2)}, u32[]{:S(2)}) collective-permute-start(f32[8,3,8,256]{3,1,0,2:T(4,128)S(1)} %broadcast_select_fusion.8), channel_id=1, source_target_pairs={{31,16},{1,17},{3,18},{5,19},{7,20},{9,21},{11,22},{13,23},{15,24}... | collective-permute-start | bytes 589832 | tf_op jit(solution)/shard_map/ppermute | solution.py:202

commit v3 on v2

--- a/solution.py
+++ b/solution.py
@@ -90,9 +90,16 @@
         axis=0,
     )
 
-    west = two * colslice[..., 0] + one * colslice[..., 1]
-    east = one * colslice[..., span] + two * colslice[..., span + 1]
-    strip = jnp.stack([west, east], axis=2).reshape(members * 6, band_rows)
+    window_cols = jnp.arange(span + 2, dtype=jnp.int32)[:, None]
+    west_side = jnp.arange(2, dtype=jnp.int32)[None, :] == 0
+    column_weights = (
+        jnp.where(west_side & (window_cols == 0), two, 0.0)
+        + jnp.where(west_side & (window_cols == 1), one, 0.0)
+        + jnp.where(~west_side & (window_cols == span), one, 0.0)
+        + jnp.where(~west_side & (window_cols == span + 1), two, 0.0)
+    )
+    strip = jnp.einsum("mflq,qs->mfsl", colslice, column_weights, precision=highest)
+    strip = strip.reshape(members * 6, band_rows)
 
     global_rows = band_index * band_rows + jnp.arange(band_rows, dtype=jnp.int32)
     row_start = rows_off[:, None]

time: 732 us -> 267 us (0.36); the launches traced: 718 us -> 265 us
  local copies, waits for them, and re-layouts: 324 us -> 53.4 us
  other arithmetic: 214 us -> 32.1 us
    dynamic_update_slice x8, local copies, waits for them, and re-layouts: 95.3 us -> 15.3 us  [per_device(): parent_out = lax.dynamic_update_slice(parent_out, merged, start)]
    another operation x2, other arithmetic: 63.1 us -> 1.39 us  [parent_step(): return jnp.stack([height_new, zonal_new, merid_new], axis=1)]
    unnamed x75 -> x78, local copies, waits for them, and re-layouts: 62.3 us -> 8.35 us
    sub x1, other arithmetic: 34.3 us -> 2.52 us  [parent_step(): height - courant * (shift_cols(zonal) + 0.5 * (merid_ext[:, 2:] - merid_e...]
    add x1, other arithmetic: 28.7 us -> 0.84 us  [parent_step(): (1.0 - friction) * zonal - courant * shift_cols(height_new)]
    concatenate x2, local copies, waits for them, and re-layouts: 24.5 us -> 0.82 us  [shift_cols(): return 0.5 * (jnp.roll(field, -1, axis=-1) - jnp.roll(field, 1, axis=-1))]
    slice x4 -> x2, local copies, waits for them, and re-layouts: 24.9 us -> 1.53 us  [with_halo(): tail = cells[:, :, cells.shape[2] - width:]]
    squeeze x1, other arithmetic: 23.6 us -> 0.54 us  [parent_step(): height_ext = with_halo(height_new[:, None], 1)[:, 0]]
  transfers between devices with their start and end apart: 26 -> 26, of which waited for: 13 -> 14; matrix products, arithmetic and copies ran while one was open for 51% -> 13% of each run, Pallas kernels for 0% -> 0%
where the time goes in v3:
time: 267 us; the launch traced here: 265 us
  starting transfers between devices  85.5 us (32%)
  waiting for transfers between devices  60.6 us (23%)
  local copies, waits for them, and re-layouts  53.4 us (20%)
  other arithmetic  32.1 us (12%)
  between operations  27.4 us (10%)
  matrix products  6.12 us (2%)
    ppermute x6, waiting for transfers between devices, per_device(): got.append(lax.ppermute(moved, 'band', pairs))  28.6 us
    ppermute x7, waiting for transfers between devices, per_device(): lax.ppermute(moved, 'band', [(i, (i + k * reach) % bands) for i in range(...  24.9 us
    ppermute x6, starting transfers between devices, per_device(): got.append(lax.ppermute(moved, 'band', pairs))  21.5 us
    ppermute x7, starting transfers between devices, per_device(): lax.ppermute(payload, 'band', [(i, (i + k * reach) % bands) for i in rang...  19.1 us
    ppermute x7, starting transfers between devices, per_device(): lax.ppermute(moved, 'band', [(i, (i + k * reach) % bands) for i in range(...  17.3 us
    dynamic_update_slice x8, local copies, waits for them, and re-layouts, per_device(): parent_out = lax.dynamic_update_slice(parent_out, merged, start)  15.3 us
    ppermute x3, starting transfers between devices, with_halo(): lax.ppermute(head, 'band', shift_pairs(count, -1))  14.5 us
    ppermute x3, starting transfers between devices, with_halo(): lax.ppermute(tail, 'band', shift_pairs(count, 1))  13.1 us
  transfers between devices with their start and end apart: 26, of which 14 were waited for; matrix products, arithmetic and copies ran while one was open for 13% of the time, Pallas kernels for 0%

profile of v3, /device:TPU:112, one launch (start us, length us, event | category | flops | bytes accessed | tf_op | source)
XLA Modules:
  0.0 265.1 jit_solution(15510134226777016767)
XLA Ops:
  0.6 2.4 slice_bitcast_fusion.8
  3.1 4.8 %collective-permute-start.1 = (f32[8,1,1,4096]{3,2,0,1:T(1,128)}, f32[8,1,1,4096]{3,2,0,1:T(1,128)S(1)}, u32[]{:S(2)}, u32[]{:S(2)}) collective-permute-start(f32[8,1,1,4096]{3,2,0,1:T(1,128)} %get-tuple-element.25), channel_id=1, source_target_pairs={{1,0},{2,1},{3,2},{4,3},{5,4},{6,5},{7,6},{8,7},{9,8},{10,9},{11,1... | collective-permute-start | bytes 393224 | tf_op jit(solution)/shard_map/ppermute | solution.py:29
  7.8 2.6 collective-permute-start
  10.4 1.3 fusion.121
  11.9 5.7 %collective-permute-start.5 = (f32[8,3,6,768]{3,0,2,1:T(8,128)S(1)}, f32[8,3,6,768]{3,0,2,1:T(8,128)S(1)}, u32[]{:S(2)}, u32[]{:S(2)}) collective-permute-start(f32[8,3,6,768]{3,0,2,1:T(8,128)S(1)} %copy.142), channel_id=1, source_target_pairs={{1,0},{2,1},{3,2},{4,3},{5,4},{6,5},{7,6},{8,7},{9,8},{10,9},{11,1... | collective-permute-start | bytes 1327112 | tf_op jit(solution)/shard_map/ppermute | solution.py:29
  18.5 4.2 %collective-permute-start.4 = (f32[8,3,6,768]{3,0,2,1:T(8,128)}, f32[8,3,6,768]{3,0,2,1:T(8,128)}, u32[]{:S(2)}, u32[]{:S(2)}) collective-permute-start(f32[8,3,6,768]{3,0,2,1:T(8,128)} %copy.141), channel_id=1, source_target_pairs={{0,1},{1,2},{2,3},{3,4},{4,5},{5,6},{6,7},{7,8},{8,9},{9,10},{10,1... | collective-permute-start | bytes 1327112 | tf_op jit(solution)/shard_map/ppermute | solution.py:27
  22.7 3.9 %slice_bitcast_fusion.3 = (f32[8,16,4096]{2,1,0:T(8,128)S(1)}, f32[8,1,16,4096]{3,2,0,1:T(8,128)}) fusion(f32[8,3,16,4096]{3,2,1,0:T(8,128)} %param.3), kind=kLoop, calls=%fused_computation.24 | loop fusion | bytes 8388608 | tf_op jit(solution)/shard_map/squeeze | solution.py:50
  26.7 2.0 fusion.120
  41.8 2.2 maximum_bitcast_fusion
  44.0 2.5 fusion.6
  47.6 4.1 %collective-permute-start.3 = (f32[8,1,1,4096]{3,2,0,1:T(1,128)S(1)}, f32[8,1,1,4096]{3,2,0,1:T(1,128)S(1)}, u32[]{:S(2)}, u32[]{:S(2)}) collective-permute-start(f32[8,1,1,4096]{3,2,0,1:T(1,128)S(1)} %get-tuple-element.35), channel_id=1, source_target_pairs={{1,0},{2,1},{3,2},{4,3},{5,4},{6,5},{7,6},{8,7},{9,8},{10,9},{11,1... | collective-permute-start | bytes 393224 | tf_op jit(solution)/shard_map/ppermute | solution.py:29
  51.7 6.3 %collective-permute-start.2 = (f32[8,1,1,4096]{3,2,0,1:T(1,128)S(1)}, f32[8,1,1,4096]{3,2,0,1:T(1,128)S(1)}, u32[]{:S(2)}, u32[]{:S(2)}) collective-permute-start(f32[8,1,1,4096]{3,2,0,1:T(1,128)S(1)} %get-tuple-element.34), channel_id=1, source_target_pairs={{0,1},{1,2},{2,3},{3,4},{4,5},{5,6},{6,7},{7,8},{8,9},{9,10},{10,1... | collective-permute-start | bytes 393224 | tf_op jit(solution)/shard_map/ppermute | solution.py:27
  59.0 2.0 collective-permute-done.2
  63.6 2.0 copy-done
  66.2 2.9 %fusion.81 = f32[2,8,3,16]{3,0,2,1:T(2,128)S(1)} fusion(f32[8,3,16,258]{3,2,1,0:T(8,128)S(1)} %dynamic-slice_dynamic-update-slice_fusion, pred[258]{0:T(512)(128)(4,1)S(1)} %get-tuple-element.127, pred[258]{0:T(512)(128)(4,1)S(1)} %get-tuple-element.128, pred[258]{0:T(512)(128)(4,1)S(1)} %get-tuple-element.129, pred[258]{0:T(512)(128)(4,1)S(1)} %get-tuple-element.130, ...), kind=kOutput, calls=%fused_computation.190 | convolution fusion | flops 2383404 | bytes 400396 | tf_op jit(solution)/shard_map/mflq,qs->mfsl/dot_general | solution.py:101
  69.2 7.1 %collective-permute-start.6 = (f32[48,274]{1,0:T(8,128)S(1)}, f32[48,274]{1,0:T(8,128)S(1)}, u32[]{:S(2)}, u32[]{:S(2)}) collective-permute-start(f32[48,274]{1,0:T(8,128)S(1)} %pad_maximum_fusion.17), channel_id=1, source_target_pairs={{0,3},{1,4},{2,5},{3,6},{4,7},{5,8},{6,9},{7,10},{8,11},{9,12},{10... | collective-permute-start | bytes 157832 | tf_op jit(solution)/shard_map/ppermute | solution.py:123
  76.3 3.1 %collective-permute-start.7 = (f32[48,274]{1,0:T(8,128)S(1)}, f32[48,274]{1,0:T(8,128)S(1)}, u32[]{:S(2)}, u32[]{:S(2)}) collective-permute-start(f32[48,274]{1,0:T(8,128)S(1)} %pad_maximum_fusion.17), channel_id=1, source_target_pairs={{0,2},{1,3},{2,4},{3,5},{4,6},{5,7},{6,8},{7,9},{8,10},{9,11},{10,... | collective-permute-start | bytes 157832 | tf_op jit(solution)/shard_map/ppermute | solution.py:123
  98.3 5.6 %collective-permute-start.9 = (f32[48,322]{1,0:T(8,128)S(1)}, f32[48,322]{1,0:T(8,128)S(1)}, u32[]{:S(2)}, u32[]{:S(2)}) collective-permute-start(f32[48,322]{1,0:T(8,128)S(1)} %concatenate.172), channel_id=1, source_target_pairs={{0,12},{1,13},{2,14},{3,15},{4,16},{5,17},{6,18},{7,19},{8,20},{9,... | collective-permute-start | bytes 185480 | tf_op jit(solution)/shard_map/ppermute | solution.py:123
  104.0 2.2 collective-permute-start.10
  108.3 3.7 %collective-permute-done.11 = f32[48,322]{1,0:T(8,128)S(1)} collective-permute-done((f32[48,322]{1,0:T(8,128)S(1)}, f32[48,322]{1,0:T(8,128)S(1)}, u32[]{:S(2)}, u32[]{:S(2)}) %collective-permute-start.11) | collective-permute-done | bytes 61856 | tf_op jit(solution)/shard_map/ppermute | solution.py:123
  112.9 1.0 collective-permute-start.12
  115.9 1.2 copy.95
  117.1 1.9 pad_maximum_fusion.1
  124.1 1.4 fusion.133
  125.5 1.6 fusion.132
  127.5 3.6 %select_select_fusion.6 = (f32[8,36,768]{2,1,0:T(8,128)S(1)}, f32[8,36,768]{2,1,0:T(8,128)}) fusion(f32[8,768]{1,0:T(8,128)S(1)} %get-tuple-element.79, f32[8,768]{1,0:T(8,128)S(1)} %get-tuple-element.78, pred[36]{0:T(512)(128)(4,1)S(1)} %get-tuple-element.131, pred[36]{0:T(512)(128)(4,1)S(1)} %get-tuple-element.132, f32[8,35,768]{2,1,0:T(8,128)} %get-tuple-element.69, ...), kind=kLoop, calls=%fused_computation.79 | loop fusion | flops 1990656 | bytes 6193224 | tf_op jit(solution)/shard_map/jit(_where)/select_n | solution.py:153
  131.0 1.6 fusion.129
  132.6 1.5 fusion.131
  134.9 1.5 copy.109
  136.4 3.0 %select_select_fusion.5 = (f32[8,36,768]{2,1,0:T(8,128)S(1)}, f32[8,36,768]{2,1,0:T(8,128)S(1)}, f32[8,36,768]{2,1,0:T(8,128)S(1)}, f32[8,36,768]{2,1,0:T(8,128)S(1)}) fusion(f32[8,768]{1,0:T(8,128)S(1)} %get-tuple-element.82, f32[8,768]{1,0:T(8,128)S(1)} %get-tuple-element.83, pred[36]{0:T(512)(128)(4,1)S(1)} %get-tuple-element.131, ...), kind=kLoop, calls=%fused_computation.78 | loop fusion | flops 3981312 | bytes 8896584 | tf_op jit(solution)/shard_map/jit(_where)/select_n | solution.py:153
  145.7 1.1 fusion.42
  147.3 3.1 %collective-permute-start.13 = (f32[8,3,8,256]{3,1,0,2:T(4,128)S(1)}, f32[8,3,8,256]{3,1,0,2:T(4,128)S(1)}, u32[]{:S(2)}, u32[]{:S(2)}) collective-permute-start(f32[8,3,8,256]{3,1,0,2:T(4,128)S(1)} %copy_multiply_fusion), channel_id=1, source_target_pairs={{0,3},{1,4},{2,5},{3,6},{4,7},{5,8},{6,9},{7,10},{8,11},{9,12},{10... | collective-permute-start | bytes 589832 | tf_op jit(solution)/shard_map/ppermute | solution.py:198
  150.4 2.8 %collective-permute-start.15 = (f32[8,3,8,256]{3,1,0,2:T(4,128)S(1)}, f32[8,3,8,256]{3,1,0,2:T(4,128)S(1)}, u32[]{:S(2)}, u32[]{:S(2)}) collective-permute-start(f32[8,3,8,256]{3,1,0,2:T(4,128)S(1)} %copy_multiply_fusion), channel_id=1, source_target_pairs={{0,1},{1,2},{2,3},{3,4},{4,5},{5,6},{6,7},{7,8},{8,9},{9,10},{10,1... | collective-permute-start | bytes 589832 | tf_op jit(solution)/shard_map/ppermute | solution.py:198
  153.2 4.7 %collective-permute-done.13 = f32[8,3,8,256]{3,1,0,2:T(4,128)S(1)} collective-permute-done((f32[8,3,8,256]{3,1,0,2:T(4,128)S(1)}, f32[8,3,8,256]{3,1,0,2:T(4,128)S(1)}, u32[]{:S(2)}, u32[]{:S(2)}) %collective-permute-start.13) | collective-permute-done | bytes 196640 | tf_op jit(solution)/shard_map/ppermute | solution.py:198
  157.8 6.5 %collective-permute-done.14 = f32[8,3,8,256]{3,1,0,2:T(4,128)S(1)} collective-permute-done((f32[8,3,8,256]{3,1,0,2:T(4,128)S(1)}, f32[8,3,8,256]{3,1,0,2:T(4,128)S(1)}, u32[]{:S(2)}, u32[]{:S(2)}) %collective-permute-start.14) | collective-permute-done | bytes 196640 | tf_op jit(solution)/shard_map/ppermute | solution.py:198
  164.6 1.1 collective-permute-start.16
  166.6 4.9 %collective-permute-start.18 = (f32[8,3,8,256]{3,1,0,2:T(4,128)S(1)}, f32[8,3,8,256]{3,1,0,2:T(4,128)S(1)}, u32[]{:S(2)}, u32[]{:S(2)}) collective-permute-start(f32[8,3,8,256]{3,1,0,2:T(4,128)S(1)} %select_select_fusion.10), channel_id=1, source_target_pairs={{0,4},{1,5},{2,6},{3,7},{4,8},{5,9},{6,10},{7,11},{8,12},{9,13},{1... | collective-permute-start | bytes 589832 | tf_op jit(solution)/shard_map/ppermute | solution.py:198
  171.5 3.8 %collective-permute-done.16 = f32[8,3,8,256]{3,1,0,2:T(4,128)S(1)} collective-permute-done((f32[8,3,8,256]{3,1,0,2:T(4,128)S(1)}, f32[8,3,8,256]{3,1,0,2:T(4,128)S(1)}, u32[]{:S(2)}, u32[]{:S(2)}) %collective-permute-start.16) | collective-permute-done | bytes 196640 | tf_op jit(solution)/shard_map/ppermute | solution.py:198
  175.3 3.8 %collective-permute-done.17 = f32[8,3,8,256]{3,1,0,2:T(4,128)S(1)} collective-permute-done((f32[8,3,8,256]{3,1,0,2:T(4,128)S(1)}, f32[8,3,8,256]{3,1,0,2:T(4,128)S(1)}, u32[]{:S(2)}, u32[]{:S(2)}) %collective-permute-start.17) | collective-permute-done | bytes 196640 | tf_op jit(solution)/shard_map/ppermute | solution.py:198
  179.1 1.6 collective-permute-done.18
  180.9 4.5 %collective-permute-start.19 = (f32[8,3,8,256]{3,1,0,2:T(4,128)S(1)}, f32[8,3,8,256]{3,1,0,2:T(4,128)S(1)}, u32[]{:S(2)}, u32[]{:S(2)}) collective-permute-start(f32[8,3,8,256]{3,1,0,2:T(4,128)S(1)} %select_select_fusion.9), channel_id=1, source_target_pairs={{0,16},{1,17},{2,18},{3,19},{4,20},{5,21},{6,22},{7,23},{8,24},{9,... | collective-permute-start | bytes 589832 | tf_op jit(solution)/shard_map/ppermute | solution.py:198
  185.5 4.7 %collective-permute-done.19 = f32[8,3,8,256]{3,1,0,2:T(4,128)S(1)} collective-permute-done((f32[8,3,8,256]{3,1,0,2:T(4,128)S(1)}, f32[8,3,8,256]{3,1,0,2:T(4,128)S(1)}, u32[]{:S(2)}, u32[]{:S(2)}) %collective-permute-start.19) | collective-permute-done | bytes 196640 | tf_op jit(solution)/shard_map/ppermute | solution.py:198
  191.0 1.3 collective-permute-start.25
  192.3 15.7 %collective-permute-start.22 = (f32[8,3,8,256]{3,1,0,2:T(4,128)S(1)}, f32[8,3,8,256]{3,1,0,2:T(4,128)S(1)}, u32[]{:S(2)}, u32[]{:S(2)}) collective-permute-start(f32[8,3,8,256]{3,1,0,2:T(4,128)S(1)} %broadcast_select_fusion), channel_id=1, source_target_pairs={{0,0},{2,1},{4,2},{6,3},{8,4},{10,5},{12,6},{14,7},{16,8},{18,9},{... | collective-permute-start | bytes 589832 | tf_op jit(solution)/shard_map/ppermute | solution.py:209
  208.0 1.9 collective-permute-start.23
  210.6 1.3 collective-permute-start.21
  212.0 1.7 collective-permute-done.22
  213.7 9.0 %collective-permute-done.23 = f32[8,3,8,256]{3,1,0,2:T(4,128)S(1)} collective-permute-done((f32[8,3,8,256]{3,1,0,2:T(4,128)S(1)}, f32[8,3,8,256]{3,1,0,2:T(4,128)S(1)}, u32[]{:S(2)}, u32[]{:S(2)}) %collective-permute-start.23) | collective-permute-done | bytes 196640 | tf_op jit(solution)/shard_map/ppermute | solution.py:209
  222.8 17.8 %collective-permute-done.21 = f32[8,3,8,256]{3,1,0,2:T(4,128)S(1)} collective-permute-done((f32[8,3,8,256]{3,1,0,2:T(4,128)S(1)}, f32[8,3,8,256]{3,1,0,2:T(4,128)S(1)}, u32[]{:S(2)}, u32[]{:S(2)}) %collective-permute-start.21) | collective-permute-done | bytes 196640 | tf_op jit(solution)/shard_map/ppermute | solution.py:209
  242.0 1.0 copy_select_fusion.7
  243.0 1.9 dynamic_update_slice.24
  244.9 1.0 copy_select_fusion.6
  245.9 1.9 dynamic_update_slice.25
  247.8 1.0 copy_select_fusion.5
  248.8 1.9 dynamic_update_slice.26
  250.7 1.0 copy_select_fusion.4
  251.7 1.9 dynamic_update_slice.27
  253.6 1.0 copy_select_fusion.3
  254.6 1.9 dynamic_update_slice.28
  256.5 1.0 copy_select_fusion.2
  257.5 1.9 dynamic_update_slice.29
  259.4 1.0 copy_select_fusion.1
  260.3 1.9 dynamic_update_slice.30
  263.2 1.9 dynamic_update_slice.31
  (193 shorter events, 35.7 us)
Async XLA Ops:
  3.1 38.7 %collective-permute-start.1 = (f32[8,1,1,4096]{3,2,0,1:T(1,128)}, f32[8,1,1,4096]{3,2,0,1:T(1,128)S(1)}, u32[]{:S(2)}, u32[]{:S(2)}) collective-permute-start(f32[8,1,1,4096]{3,2,0,1:T(1,128)} %get-tuple-element.25), channel_id=1, source_target_pairs={{1,0},{2,1},{3,2},{4,3},{5,4},{6,5},{7,6},{8,7},{9,8},{10,9},{11,1... | collective-permute-start | bytes 393224 | tf_op jit(solution)/shard_map/ppermute | solution.py:29
  7.8 33.9 %collective-permute-start = (f32[8,1,1,4096]{3,2,0,1:T(1,128)}, f32[8,1,1,4096]{3,2,0,1:T(1,128)S(1)}, u32[]{:S(2)}, u32[]{:S(2)}) collective-permute-start(f32[8,1,1,4096]{3,2,0,1:T(1,128)} %get-tuple-element.24), channel_id=1, source_target_pairs={{0,1},{1,2},{2,3},{3,4},{4,5},{5,6},{6,7},{7,8},{8,9},{9,10},{10,1... | collective-permute-start | bytes 393224 | tf_op jit(solution)/shard_map/ppermute | solution.py:27
  11.9 103.8 %collective-permute-start.5 = (f32[8,3,6,768]{3,0,2,1:T(8,128)S(1)}, f32[8,3,6,768]{3,0,2,1:T(8,128)S(1)}, u32[]{:S(2)}, u32[]{:S(2)}) collective-permute-start(f32[8,3,6,768]{3,0,2,1:T(8,128)S(1)} %copy.142), channel_id=1, source_target_pairs={{1,0},{2,1},{3,2},{4,3},{5,4},{6,5},{7,6},{8,7},{9,8},{10,9},{11,1... | collective-permute-start | bytes 1327112 | tf_op jit(solution)/shard_map/ppermute | solution.py:29
  18.5 97.4 %collective-permute-start.4 = (f32[8,3,6,768]{3,0,2,1:T(8,128)}, f32[8,3,6,768]{3,0,2,1:T(8,128)}, u32[]{:S(2)}, u32[]{:S(2)}) collective-permute-start(f32[8,3,6,768]{3,0,2,1:T(8,128)} %copy.141), channel_id=1, source_target_pairs={{0,1},{1,2},{2,3},{3,4},{4,5},{5,6},{6,7},{7,8},{8,9},{9,10},{10,1... | collective-permute-start | bytes 1327112 | tf_op jit(solution)/shard_map/ppermute | solution.py:27
  26.7 2.0 copy-start.15
  29.4 14.6 %copy-start.16 = (s32[8]{0:T(128)}, s32[8]{0:T(128)S(1)}, u32[]{:S(2)}) copy-start(s32[8]{0:T(128)S(1)} %get-tuple-element.100) | copy-start | bytes 100
  30.0 11.7 %copy-start.25 = (s32[16]{0:T(128)}, s32[16]{0:T(128)S(1)}, u32[]{:S(2)}) copy-start(s32[16]{0:T(128)S(1)} %iota_add_fusion.2) | copy-start | bytes 196
  41.7 2.3 copy-start.1
  44.0 14.0 %slice-start = ((s8[6291456]{0:T(1024)(128)(4,1)}), s8[4194304]{0:T(1024)(128)(4,1)S(1)}, s32[]{:S(2)}) async-start(s8[6291456]{0:T(1024)(128)(4,1)} %bitcast.174), calls=%async_computation | async-start | bytes 8388608
  44.0 14.0 %slice-start.1 = ((s8[6291456]{0:T(1024)(128)(4,1)}), s8[2097152]{0:T(1024)(128)(4,1)S(1)}, s32[]{:S(2)}) async-start(s8[6291456]{0:T(1024)(128)(4,1)} %bitcast.174), calls=%async_computation.1 | async-start | bytes 4194304
  47.6 11.4 %collective-permute-start.3 = (f32[8,1,1,4096]{3,2,0,1:T(1,128)S(1)}, f32[8,1,1,4096]{3,2,0,1:T(1,128)S(1)}, u32[]{:S(2)}, u32[]{:S(2)}) collective-permute-start(f32[8,1,1,4096]{3,2,0,1:T(1,128)S(1)} %get-tuple-element.35), channel_id=1, source_target_pairs={{1,0},{2,1},{3,2},{4,3},{5,4},{6,5},{7,6},{8,7},{9,8},{10,9},{11,1... | collective-permute-start | bytes 393224 | tf_op jit(solution)/shard_map/ppermute | solution.py:29
  51.7 9.3 %collective-permute-start.2 = (f32[8,1,1,4096]{3,2,0,1:T(1,128)S(1)}, f32[8,1,1,4096]{3,2,0,1:T(1,128)S(1)}, u32[]{:S(2)}, u32[]{:S(2)}) collective-permute-start(f32[8,1,1,4096]{3,2,0,1:T(1,128)S(1)} %get-tuple-element.34), channel_id=1, source_target_pairs={{0,1},{1,2},{2,3},{3,4},{4,5},{5,6},{6,7},{7,8},{8,9},{9,10},{10,1... | collective-permute-start | bytes 393224 | tf_op jit(solution)/shard_map/ppermute | solution.py:27
  62.9 2.7 %copy-start = (f32[8,3,16,4096]{3,2,1,0:T(8,128)}, f32[8,3,16,4096]{3,2,1,0:T(8,128)S(1)}, u32[]{:S(2)}) copy-start(f32[8,3,16,4096]{3,2,1,0:T(8,128)S(1)} %pad_maximum_fusion) | copy-start | bytes 18874372
  69.2 28.8 %collective-permute-start.6 = (f32[48,274]{1,0:T(8,128)S(1)}, f32[48,274]{1,0:T(8,128)S(1)}, u32[]{:S(2)}, u32[]{:S(2)}) collective-permute-start(f32[48,274]{1,0:T(8,128)S(1)} %pad_maximum_fusion.17), channel_id=1, source_target_pairs={{0,3},{1,4},{2,5},{3,6},{4,7},{5,8},{6,9},{7,10},{8,11},{9,12},{10... | collective-permute-start | bytes 157832 | tf_op jit(solution)/shard_map/ppermute | solution.py:123
  76.3 21.7 %collective-permute-start.7 = (f32[48,274]{1,0:T(8,128)S(1)}, f32[48,274]{1,0:T(8,128)S(1)}, u32[]{:S(2)}, u32[]{:S(2)}) collective-permute-start(f32[48,274]{1,0:T(8,128)S(1)} %pad_maximum_fusion.17), channel_id=1, source_target_pairs={{0,2},{1,3},{2,4},{3,5},{4,6},{5,7},{6,8},{7,9},{8,10},{9,11},{10,... | collective-permute-start | bytes 157832 | tf_op jit(solution)/shard_map/ppermute | solution.py:123
  79.4 18.6 %collective-permute-start.8 = (f32[48,274]{1,0:T(8,128)S(1)}, f32[48,274]{1,0:T(8,128)S(1)}, u32[]{:S(2)}, u32[]{:S(2)}) collective-permute-start(f32[48,274]{1,0:T(8,128)S(1)} %pad_maximum_fusion.17), channel_id=1, source_target_pairs={{0,1},{1,2},{2,3},{3,4},{4,5},{5,6},{6,7},{7,8},{8,9},{9,10},{10,1... | collective-permute-start | bytes 157832 | tf_op jit(solution)/shard_map/ppermute | solution.py:123
  98.3 9.1 %collective-permute-start.9 = (f32[48,322]{1,0:T(8,128)S(1)}, f32[48,322]{1,0:T(8,128)S(1)}, u32[]{:S(2)}, u32[]{:S(2)}) collective-permute-start(f32[48,322]{1,0:T(8,128)S(1)} %concatenate.172), channel_id=1, source_target_pairs={{0,12},{1,13},{2,14},{3,15},{4,16},{5,17},{6,18},{7,19},{8,20},{9,... | collective-permute-start | bytes 185480 | tf_op jit(solution)/shard_map/ppermute | solution.py:123
  104.0 4.4 %collective-permute-start.10 = (f32[48,322]{1,0:T(8,128)S(1)}, f32[48,322]{1,0:T(8,128)S(1)}, u32[]{:S(2)}, u32[]{:S(2)}) collective-permute-start(f32[48,322]{1,0:T(8,128)S(1)} %concatenate.172), channel_id=1, source_target_pairs={{0,8},{1,9},{2,10},{3,11},{4,12},{5,13},{6,14},{7,15},{8,16},{9,17... | collective-permute-start | bytes 185480 | tf_op jit(solution)/shard_map/ppermute | solution.py:123
  106.1 5.9 %collective-permute-start.11 = (f32[48,322]{1,0:T(8,128)S(1)}, f32[48,322]{1,0:T(8,128)S(1)}, u32[]{:S(2)}, u32[]{:S(2)}) collective-permute-start(f32[48,322]{1,0:T(8,128)S(1)} %concatenate.172), channel_id=1, source_target_pairs={{0,4},{1,5},{2,6},{3,7},{4,8},{5,9},{6,10},{7,11},{8,12},{9,13},{1... | collective-permute-start | bytes 185480 | tf_op jit(solution)/shard_map/ppermute | solution.py:123
  112.9 6.6 %collective-permute-start.12 = (f32[48,514]{1,0:T(8,128)}, f32[48,514]{1,0:T(8,128)S(1)}, u32[]{:S(2)}, u32[]{:S(2)}) collective-permute-start(f32[48,514]{1,0:T(8,128)} %concatenate.173), channel_id=1, source_target_pairs={{0,16},{1,17},{2,18},{3,19},{4,20},{5,21},{6,22},{7,23},{8,24},{9,... | collective-permute-start | bytes 296072 | tf_op jit(solution)/shard_map/ppermute | solution.py:123
  117.1 3.1 %copy-start.9 = (f32[8,3,2,16]{3,1,2,0:T(4,128)S(1)}, f32[8,3,2,16]{3,1,2,0:T(4,128)}, u32[]{:S(2)}) copy-start(f32[8,3,2,16]{3,1,2,0:T(4,128)} %copy.104) | copy-start | bytes 9220
  117.1 3.1 %copy-start.10 = (f32[8,3,2,16]{3,1,2,0:T(4,128)S(1)}, f32[8,3,2,16]{3,1,2,0:T(4,128)}, u32[]{:S(2)}) copy-start(f32[8,3,2,16]{3,1,2,0:T(4,128)} %copy.105) | copy-start | bytes 9220
  117.1 3.1 %copy-start.11 = (f32[8,3,2,64]{3,1,2,0:T(4,128)S(1)}, f32[8,3,2,64]{3,1,2,0:T(4,128)}, u32[]{:S(2)}) copy-start(f32[8,3,2,64]{3,1,2,0:T(4,128)} %copy.100) | copy-start | bytes 36868
  117.1 3.1 %copy-start.12 = (f32[8,3,2,64]{3,1,2,0:T(4,128)S(1)}, f32[8,3,2,64]{3,1,2,0:T(4,128)}, u32[]{:S(2)}) copy-start(f32[8,3,2,64]{3,1,2,0:T(4,128)} %copy.101) | copy-start | bytes 36868
  117.1 3.1 %copy-start.13 = (f32[8,3,2,64]{3,1,2,0:T(4,128)S(1)}, f32[8,3,2,64]{3,1,2,0:T(4,128)}, u32[]{:S(2)}) copy-start(f32[8,3,2,64]{3,1,2,0:T(4,128)} %copy.102) | copy-start | bytes 36868
  117.1 3.4 %copy-start.24 = (s32[512]{0:T(512)S(1)}, s32[512]{0:T(512)}, u32[]{:S(2)}) copy-start(s32[512]{0:T(512)} %add_select_fusion.3) | copy-start | bytes 6148
  117.1 3.4 %copy-start.30 = (f32[36]{0:T(128)S(1)}, f32[36]{0:T(128)}, u32[]{:S(2)}) copy-start(f32[36]{0:T(128)} %get-tuple-element.123) | copy-start | bytes 436
  117.1 3.4 %copy-start.31 = (f32[36]{0:T(128)S(1)}, f32[36]{0:T(128)}, u32[]{:S(2)}) copy-start(f32[36]{0:T(128)} %get-tuple-element.124) | copy-start | bytes 436
  119.0 3.9 %copy-start.18 = (f32[768]{0:T(1024)S(1)}, f32[768]{0:T(1024)}, u32[]{:S(2)}) copy-start(f32[768]{0:T(1024)} %slice.482) | copy-start | bytes 9220
  119.0 3.9 %copy-start.19 = (f32[768]{0:T(1024)S(1)}, f32[768]{0:T(1024)}, u32[]{:S(2)}) copy-start(f32[768]{0:T(1024)} %slice.481) | copy-start | bytes 9220
  119.0 3.9 %copy-start.20 = (s32[768]{0:T(1024)S(1)}, s32[768]{0:T(1024)}, u32[]{:S(2)}) copy-start(s32[768]{0:T(1024)} %slice.480) | copy-start | bytes 9220
  119.0 3.9 %copy-start.21 = (s32[768]{0:T(1024)S(1)}, s32[768]{0:T(1024)}, u32[]{:S(2)}) copy-start(s32[768]{0:T(1024)} %slice.479) | copy-start | bytes 9220
  119.5 0.6 copy-start.14
  123.8 3.6 %copy-start.5 = (f32[8,768]{1,0:T(8,128)}, f32[8,768]{1,0:T(8,128)S(1)}, u32[]{:S(2)}) copy-start(f32[8,768]{1,0:T(8,128)S(1)} %get-tuple-element.78) | copy-start | bytes 73732
  123.8 3.6 %copy-start.7 = (f32[8,768]{1,0:T(8,128)}, f32[8,768]{1,0:T(8,128)S(1)}, u32[]{:S(2)}) copy-start(f32[8,768]{1,0:T(8,128)S(1)} %get-tuple-element.79) | copy-start | bytes 73732
  139.6 1.2 copy-start.3
  139.6 1.2 copy-start.6
  139.6 1.2 copy-start.8
  141.5 0.9 copy-start.4
  145.7 1.4 copy-start.2
  145.7 7.5 %copy-start.28 = (s32[8]{0:T(128)S(1)}, s32[8]{0:T(128)}, u32[]{:S(2)}) copy-start(s32[8]{0:T(128)} %get-tuple-element.114) | copy-start | bytes 100
  145.7 18.6 %copy-start.23 = (pred[8]{0:T(512)(128)(4,1)S(1)}, pred[8]{0:T(512)(128)(4,1)}, u32[]{:S(2)}) copy-start(pred[8]{0:T(512)(128)(4,1)} %get-tuple-element.113) | copy-start | bytes 28
  146.8 24.8 %copy-start.27 = (s32[8]{0:T(128)S(1)}, s32[8]{0:T(128)}, u32[]{:S(2)}) copy-start(s32[8]{0:T(128)} %get-tuple-element.5) | copy-start | bytes 100
  146.8 33.9 %copy-start.22 = (pred[8]{0:T(512)(128)(4,1)S(1)}, pred[8]{0:T(512)(128)(4,1)}, u32[]{:S(2)}) copy-start(pred[8]{0:T(512)(128)(4,1)} %get-tuple-element.4) | copy-start | bytes 28
  147.0 38.4 %copy-start.17 = (s32[8]{0:T(128)S(1)}, s32[8]{0:T(128)}, u32[]{:S(2)}) copy-start(s32[8]{0:T(128)} %copy-done.16) | copy-start | bytes 100
  147.0 38.4 %copy-start.26 = (s32[16]{0:T(128)S(1)}, s32[16]{0:T(128)}, u32[]{:S(2)}) copy-start(s32[16]{0:T(128)} %copy-done.25) | copy-start | bytes 196
  147.0 43.2 %copy-start.29 = (pred[8]{0:T(512)(128)(4,1)S(1)}, pred[8]{0:T(512)(128)(4,1)}, u32[]{:S(2)}) copy-start(pred[8]{0:T(512)(128)(4,1)} %get-tuple-element.2) | copy-start | bytes 28
  147.3 10.6 %collective-permute-start.13 = (f32[8,3,8,256]{3,1,0,2:T(4,128)S(1)}, f32[8,3,8,256]{3,1,0,2:T(4,128)S(1)}, u32[]{:S(2)}, u32[]{:S(2)}) collective-permute-start(f32[8,3,8,256]{3,1,0,2:T(4,128)S(1)} %copy_multiply_fusion), channel_id=1, source_target_pairs={{0,3},{1,4},{2,5},{3,6},{4,7},{5,8},{6,9},{7,10},{8,11},{9,12},{10... | collective-permute-start | bytes 589832 | tf_op jit(solution)/shard_map/ppermute | solution.py:198
  150.4 13.9 %collective-permute-start.14 = (f32[8,3,8,256]{3,1,0,2:T(4,128)S(1)}, f32[8,3,8,256]{3,1,0,2:T(4,128)S(1)}, u32[]{:S(2)}, u32[]{:S(2)}) collective-permute-start(f32[8,3,8,256]{3,1,0,2:T(4,128)S(1)} %copy_multiply_fusion), channel_id=1, source_target_pairs={{0,2},{1,3},{2,4},{3,5},{4,6},{5,7},{6,8},{7,9},{8,10},{9,11},{10,... | collective-permute-start | bytes 589832 | tf_op jit(solution)/shard_map/ppermute | solution.py:198
  150.4 13.9 %collective-permute-start.15 = (f32[8,3,8,256]{3,1,0,2:T(4,128)S(1)}, f32[8,3,8,256]{3,1,0,2:T(4,128)S(1)}, u32[]{:S(2)}, u32[]{:S(2)}) collective-permute-start(f32[8,3,8,256]{3,1,0,2:T(4,128)S(1)} %copy_multiply_fusion), channel_id=1, source_target_pairs={{0,1},{1,2},{2,3},{3,4},{4,5},{5,6},{6,7},{7,8},{8,9},{9,10},{10,1... | collective-permute-start | bytes 589832 | tf_op jit(solution)/shard_map/ppermute | solution.py:198
  164.6 10.7 %collective-permute-start.16 = (f32[8,3,8,256]{3,1,0,2:T(4,128)S(1)}, f32[8,3,8,256]{3,1,0,2:T(4,128)S(1)}, u32[]{:S(2)}, u32[]{:S(2)}) collective-permute-start(f32[8,3,8,256]{3,1,0,2:T(4,128)S(1)} %select_select_fusion.10), channel_id=1, source_target_pairs={{0,12},{1,13},{2,14},{3,15},{4,16},{5,17},{6,18},{7,19},{8,20},{9,... | collective-permute-start | bytes 589832 | tf_op jit(solution)/shard_map/ppermute | solution.py:198
  165.7 13.4 %collective-permute-start.17 = (f32[8,3,8,256]{3,1,0,2:T(4,128)S(1)}, f32[8,3,8,256]{3,1,0,2:T(4,128)S(1)}, u32[]{:S(2)}, u32[]{:S(2)}) collective-permute-start(f32[8,3,8,256]{3,1,0,2:T(4,128)S(1)} %select_select_fusion.10), channel_id=1, source_target_pairs={{0,8},{1,9},{2,10},{3,11},{4,12},{5,13},{6,14},{7,15},{8,16},{9,17... | collective-permute-start | bytes 589832 | tf_op jit(solution)/shard_map/ppermute | solution.py:198
  166.6 14.1 %collective-permute-start.18 = (f32[8,3,8,256]{3,1,0,2:T(4,128)S(1)}, f32[8,3,8,256]{3,1,0,2:T(4,128)S(1)}, u32[]{:S(2)}, u32[]{:S(2)}) collective-permute-start(f32[8,3,8,256]{3,1,0,2:T(4,128)S(1)} %select_select_fusion.10), channel_id=1, source_target_pairs={{0,4},{1,5},{2,6},{3,7},{4,8},{5,9},{6,10},{7,11},{8,12},{9,13},{1... | collective-permute-start | bytes 589832 | tf_op jit(solution)/shard_map/ppermute | solution.py:198
  180.9 9.3 %collective-permute-start.19 = (f32[8,3,8,256]{3,1,0,2:T(4,128)S(1)}, f32[8,3,8,256]{3,1,0,2:T(4,128)S(1)}, u32[]{:S(2)}, u32[]{:S(2)}) collective-permute-start(f32[8,3,8,256]{3,1,0,2:T(4,128)S(1)} %select_select_fusion.9), channel_id=1, source_target_pairs={{0,16},{1,17},{2,18},{3,19},{4,20},{5,21},{6,22},{7,23},{8,24},{9,... | collective-permute-start | bytes 589832 | tf_op jit(solution)/shard_map/ppermute | solution.py:198
  190.3 20.3 %collective-permute-start.24 = (f32[8,3,8,256]{3,1,0,2:T(4,128)S(1)}, f32[8,3,8,256]{3,1,0,2:T(4,128)S(1)}, u32[]{:S(2)}, u32[]{:S(2)}) collective-permute-start(f32[8,3,8,256]{3,1,0,2:T(4,128)S(1)} %broadcast_select_fusion), channel_id=1, source_target_pairs={{1,0},{3,1},{5,2},{7,3},{9,4},{11,5},{13,6},{15,7},{17,8},{19,9},{... | collective-permute-start | bytes 589832 | tf_op jit(solution)/shard_map/ppermute | solution.py:209
  191.0 20.9 %collective-permute-start.25 = (f32[8,3,8,256]{3,1,0,2:T(4,128)S(1)}, f32[8,3,8,256]{3,1,0,2:T(4,128)S(1)}, u32[]{:S(2)}, u32[]{:S(2)}) collective-permute-start(f32[8,3,8,256]{3,1,0,2:T(4,128)S(1)} %broadcast_select_fusion), channel_id=1, source_target_pairs={{1,16},{3,17},{5,18},{7,19},{9,20},{11,21},{13,22},{15,23},{17,24}... | collective-permute-start | bytes 589832 | tf_op jit(solution)/shard_map/ppermute | solution.py:209
  192.3 21.4 %collective-permute-start.22 = (f32[8,3,8,256]{3,1,0,2:T(4,128)S(1)}, f32[8,3,8,256]{3,1,0,2:T(4,128)S(1)}, u32[]{:S(2)}, u32[]{:S(2)}) collective-permute-start(f32[8,3,8,256]{3,1,0,2:T(4,128)S(1)} %broadcast_select_fusion), channel_id=1, source_target_pairs={{0,0},{2,1},{4,2},{6,3},{8,4},{10,5},{12,6},{14,7},{16,8},{18,9},{... | collective-permute-start | bytes 589832 | tf_op jit(solution)/shard_map/ppermute | solution.py:209
  208.0 14.7 %collective-permute-start.23 = (f32[8,3,8,256]{3,1,0,2:T(4,128)S(1)}, f32[8,3,8,256]{3,1,0,2:T(4,128)S(1)}, u32[]{:S(2)}, u32[]{:S(2)}) collective-permute-start(f32[8,3,8,256]{3,1,0,2:T(4,128)S(1)} %broadcast_select_fusion), channel_id=1, source_target_pairs={{0,16},{2,17},{4,18},{6,19},{8,20},{10,21},{12,22},{14,23},{16,24}... | collective-permute-start | bytes 589832 | tf_op jit(solution)/shard_map/ppermute | solution.py:209
  209.9 12.9 %collective-permute-start.20 = (f32[8,3,8,256]{3,1,0,2:T(4,128)S(1)}, f32[8,3,8,256]{3,1,0,2:T(4,128)S(1)}, u32[]{:S(2)}, u32[]{:S(2)}) collective-permute-start(f32[8,3,8,256]{3,1,0,2:T(4,128)S(1)} %broadcast_select_fusion), channel_id=1, source_target_pairs={{31,0},{1,1},{3,2},{5,3},{7,4},{9,5},{11,6},{13,7},{15,8},{17,9},{... | collective-permute-start | bytes 589832 | tf_op jit(solution)/shard_map/ppermute | solution.py:209
  210.6 30.0 %collective-permute-start.21 = (f32[8,3,8,256]{3,1,0,2:T(4,128)S(1)}, f32[8,3,8,256]{3,1,0,2:T(4,128)S(1)}, u32[]{:S(2)}, u32[]{:S(2)}) collective-permute-start(f32[8,3,8,256]{3,1,0,2:T(4,128)S(1)} %broadcast_select_fusion), channel_id=1, source_target_pairs={{31,16},{1,17},{3,18},{5,19},{7,20},{9,21},{11,22},{13,23},{15,24}... | collective-permute-start | bytes 589832 | tf_op jit(solution)/shard_map/ppermute | solution.py:209

commit v4 on v3

--- a/solution.py
+++ b/solution.py
@@ -48,11 +48,28 @@
 
 def parent_step(parent_state):
     height, zonal, meridional = (parent_state[:, 0], parent_state[:, 1], parent_state[:, 2])
-    merid_ext = with_halo(meridional[:, None], 1)[:, 0]
+    count = lax.axis_size("band")
+    band_index = lax.axis_index("band")
+    rows = height.shape[1]
+    tail = jnp.stack(
+        [meridional[:, rows - 2], meridional[:, rows - 1], zonal[:, rows - 1], height[:, rows - 1]], axis=1
+    )
+    head = jnp.stack([meridional[:, 0], meridional[:, 1], zonal[:, 0], height[:, 0]], axis=1)
+    prev = lax.ppermute(tail, "band", shift_pairs(count, 1))
+    next_ = lax.ppermute(head, "band", shift_pairs(count, -1))
+    merid_ext = jnp.concatenate([prev[:, 1:2], meridional, next_[:, 0:1]], axis=1)
     height_new = height - courant * (
         shift_cols(zonal) + 0.5 * (merid_ext[:, 2:] - merid_ext[:, :-2])
     )
-    height_ext = with_halo(height_new[:, None], 1)[:, 0]
+    height_prev = prev[:, 3] - courant * (
+        shift_cols(prev[:, 2]) + 0.5 * (meridional[:, 0] - prev[:, 0])
+    )
+    height_next = next_[:, 3] - courant * (
+        shift_cols(next_[:, 2]) + 0.5 * (next_[:, 1] - meridional[:, rows - 1])
+    )
+    height_prev = jnp.where(band_index == 0, 0.0, height_prev)
+    height_next = jnp.where(band_index == count - 1, 0.0, height_next)
+    height_ext = jnp.concatenate([height_prev[:, None], height_new, height_next[:, None]], axis=1)
     zonal_new = (1.0 - friction) * zonal - courant * shift_cols(height_new) + rotation * meridional
     merid_new = (
         (1.0 - friction) * meridional
@@ -116,7 +133,7 @@
     sums = ends_part.reshape(members * 6, span + 2)
     reach = 1
     while reach < bands:
-        count = min(4, bands // reach)
+        count = min(8, bands // reach)
         payload = jnp.concatenate([blocks, sums], axis=1)
         width = blocks.shape[1]
         recvs = [
@@ -187,30 +204,23 @@
     col_sums = jnp.einsum("mfrj,jp->mfrp", nest, block_cols, precision=highest)
     coarse = col_sums.reshape(members, 3, tile_coarse, 3, span).sum(axis=3) / 9.0
 
-    shift = (rows_off + tile_coarse - 1) // tile_coarse - 1
-    moved = coarse
-    reach = 1
-    while reach < bands:
-        count = min(4, bands // reach)
-        digit = (shift // reach) % count
-        chosen = moved
-        for k in range(1, count):
-            recv = lax.ppermute(moved, "band", [(i, (i + k * reach) % bands) for i in range(bands)])
-            chosen = jnp.where((digit == k)[:, None, None, None], recv, chosen)
-        moved = chosen
-        reach *= count
-    half = bands // 2
-    low_half = band_index < half
-    pieces = []
-    for i in range(3):
-        got = []
-        for h in range(2):
-            pairs = [((2 * p - 1 + i) % bands, p) for p in range(h * half, (h + 1) * half)]
-            got.append(lax.ppermute(moved, "band", pairs))
-        pieces.append(jnp.where(low_half, got[0], got[1]))
-    near = jnp.concatenate(pieces, axis=2)
-    lead = tile_coarse * (shift + 1) - rows_off
-    patch = jax.vmap(lambda blk, e: lax.dynamic_slice_in_dim(blk, e, band_rows, axis=1))(near, lead)
+    radix = 4
+    band_shift = rows_off // band_rows
+    sub_shift = rows_off % band_rows
+    low_digit = band_shift % radix
+    high_digit = band_shift // radix
+    lowest = -2 * (radix - 1) - 2
+    fetched = []
+    for k in range(lowest, 2):
+        pairs = [(2 * p + k, p) for p in range(bands) if 0 <= 2 * p + k < bands]
+        fetched.append(lax.ppermute(coarse, "band", pairs))
+    stacked = jnp.concatenate(fetched, axis=2)
+    lead = (-lowest) * tile_coarse - band_rows * low_digit - sub_shift
+    near = jax.vmap(lambda blk, e: lax.dynamic_slice_in_dim(blk, e, band_rows, axis=1))(stacked, lead)
+    patch = near
+    for j in range(1, radix):
+        recv = lax.ppermute(near, "band", shift_pairs(bands, j * radix))
+        patch = jnp.where((high_digit == j)[:, None, None, None], recv, patch)
 
     relative_rows = global_rows[None, :] - rows_off[:, None]
     covered = (relative_rows >= 0) & (relative_rows < span)

time: 267 us -> 255 us (0.955)
  the two profiles are of different devices: /device:TPU:112 before, /device:TPU:54 now
where the time goes in v4:
time: 255 us; the launch traced here: 253 us
  starting transfers between devices  87.8 us (34%)
  local copies, waits for them, and re-layouts  54.4 us (21%)
  waiting for transfers between devices  43.6 us (17%)
  other arithmetic  33.4 us (13%)
  between operations  26.5 us (10%)
  matrix products  6.81 us (3%)
    ppermute x10, starting transfers between devices, per_device(): fetched.append(lax.ppermute(coarse, 'band', pairs))  30.2 us
    ppermute x10, starting transfers between devices, per_device(): lax.ppermute(payload, 'band', [(i, (i + k * reach) % bands) for i in rang...  25.5 us
    ppermute x10, waiting for transfers between devices, per_device(): fetched.append(lax.ppermute(coarse, 'band', pairs))  23.4 us
    ppermute x3, waiting for transfers between devices, per_device(): recv = lax.ppermute(near, 'band', shift_pairs(bands, j * radix))  17.9 us
    ppermute x3, starting transfers between devices, per_device(): recv = lax.ppermute(near, 'band', shift_pairs(bands, j * radix))  15.7 us
    dynamic_update_slice x8, local copies, waits for them, and re-layouts, per_device(): parent_out = lax.dynamic_update_slice(parent_out, merged, start)  15.3 us
    unnamed x114, local copies, waits for them, and re-layouts  8.96 us
    select_n x6, other arithmetic, fix(): jnp.where(is_south, ends[:, f, 0][:, None, :], jnp.where(is_north, ends[:...  8.92 us
  transfers between devices with their start and end apart: 27, of which 7 were waited for; matrix products, arithmetic and copies ran while one was open for 12% of the time, Pallas kernels for 0%

profile of v4, /device:TPU:54, one launch (start us, length us, event | category | flops | bytes accessed | tf_op | source)
XLA Modules:
  0.0 252.6 jit_solution(10511810360590468853)
XLA Ops:
  0.6 3.3 %slice_bitcast_fusion.4 = (f32[8,16,4096]{2,1,0:T(8,128)S(1)}, f32[8,16,4096]{2,1,0:T(8,128)S(1)}, f32[8,16,4096]{2,1,0:T(8,128)S(1)}) fusion(f32[8,3,16,4096]{3,2,1,0:T(8,128)} %param.3), kind=kLoop, calls=%fused_computation.28 | loop fusion | bytes 12582912 | tf_op jit(solution)/shard_map/squeeze | solution.py:50
  4.6 1.1 pad_maximum_fusion.20
  5.8 3.3 %collective-permute-start = (f32[8,4,4096]{2,1,0:T(4,128)}, f32[8,4,4096]{2,1,0:T(4,128)S(1)}, u32[]{:S(2)}, u32[]{:S(2)}) collective-permute-start(f32[8,4,4096]{2,1,0:T(4,128)} %pad_maximum_fusion.20), channel_id=1, source_target_pairs={{1,0},{2,1},{3,2},{4,3},{5,4},{6,5},{7,6},{8,7},{9,8},{10,9},{11,1... | collective-permute-start | bytes 1572872 | tf_op jit(solution)/shard_map/ppermute | solution.py:59
  9.1 1.2 pad_maximum_fusion.21
  10.2 4.9 %collective-permute-start.1 = (f32[8,4,4096]{2,1,0:T(4,128)}, f32[8,4,4096]{2,1,0:T(4,128)S(1)}, u32[]{:S(2)}, u32[]{:S(2)}) collective-permute-start(f32[8,4,4096]{2,1,0:T(4,128)} %pad_maximum_fusion.21), channel_id=1, source_target_pairs={{0,1},{1,2},{2,3},{3,4},{4,5},{5,6},{6,7},{7,8},{8,9},{9,10},{10,1... | collective-permute-start | bytes 1572872 | tf_op jit(solution)/shard_map/ppermute | solution.py:58
  16.2 2.4 collective-permute-start.3
  18.6 1.0 copy.147
  19.6 5.8 %collective-permute-start.2 = (f32[8,3,6,768]{3,0,2,1:T(8,128)}, f32[8,3,6,768]{3,0,2,1:T(8,128)}, u32[]{:S(2)}, u32[]{:S(2)}) collective-permute-start(f32[8,3,6,768]{3,0,2,1:T(8,128)} %copy.147), channel_id=1, source_target_pairs={{0,1},{1,2},{2,3},{3,4},{4,5},{5,6},{6,7},{7,8},{8,9},{9,10},{10,1... | collective-permute-start | bytes 1327112 | tf_op jit(solution)/shard_map/ppermute | solution.py:27
  25.4 2.7 %fusion.122 = (f32[8,16,4095]{2,1,0:T(8,128)}, f32[8,16,4095]{2,1,0:T(8,128)}) fusion(f32[8,16,4096]{2,1,0:T(8,128)S(1)} %get-tuple-element.18), kind=kLoop, calls=%fused_computation.301 | loop fusion | bytes 8386560 | tf_op jit(solution)/shard_map/jit(_roll_static)/slice | solution.py:46
  42.7 3.7 %fusion.8 = f32[8,16,4096]{2,1,0:T(8,128)S(1)} fusion(f32[8,16,4096]{2,1,0:T(8,128)S(1)} %copy-done.1, f32[8,1,4096]{2,1,0:T(1,128)S(1)} %get-tuple-element.71, f32[8,1,4096]{2,1,0:T(1,128)S(1)} %get-tuple-element.72, f32[8,16,1]{2,1,0:T(8,128)S(1)} %get-tuple-element.32, f32[8,16,4095]{2,1,0:T(8,128)} %get-tuple-element.34, ...), kind=kLoop, calls=%fused_computation.16 | loop fusion | flops 4718592 | bytes 10747904 | tf_op jit(solution)/shard_map/sub | solution.py:61
  50.4 2.0 copy-done.2
  53.0 2.9 %fusion.85 = f32[2,8,3,16]{3,0,2,1:T(2,128)S(1)} fusion(f32[8,3,16,258]{3,2,1,0:T(8,128)S(1)} %dynamic-slice_dynamic-update-slice_fusion, pred[258]{0:T(512)(128)(4,1)S(1)} %get-tuple-element.128, pred[258]{0:T(512)(128)(4,1)S(1)} %get-tuple-element.129, pred[258]{0:T(512)(128)(4,1)S(1)} %get-tuple-element.130, pred[258]{0:T(512)(128)(4,1)S(1)} %get-tuple-element.131, ...), kind=kOutput, calls=%fused_computation.221 | convolution fusion | flops 2383404 | bytes 400396 | tf_op jit(solution)/shard_map/mflq,qs->mfsl/dot_general | solution.py:118
  57.8 6.4 %collective-permute-start.6 = (f32[48,274]{1,0:T(8,128)S(1)}, f32[48,274]{1,0:T(8,128)S(1)}, u32[]{:S(2)}, u32[]{:S(2)}) collective-permute-start(f32[48,274]{1,0:T(8,128)S(1)} %pad_maximum_fusion.22), channel_id=1, source_target_pairs={{0,5},{1,6},{2,7},{3,8},{4,9},{5,10},{6,11},{7,12},{8,13},{9,14},{... | collective-permute-start | bytes 157832 | tf_op jit(solution)/shard_map/ppermute | solution.py:140
  64.3 7.3 %collective-permute-start.8 = (f32[48,274]{1,0:T(8,128)S(1)}, f32[48,274]{1,0:T(8,128)S(1)}, u32[]{:S(2)}, u32[]{:S(2)}) collective-permute-start(f32[48,274]{1,0:T(8,128)S(1)} %pad_maximum_fusion.22), channel_id=1, source_target_pairs={{0,3},{1,4},{2,5},{3,6},{4,7},{5,8},{6,9},{7,10},{8,11},{9,12},{10... | collective-permute-start | bytes 157832 | tf_op jit(solution)/shard_map/ppermute | solution.py:140
  71.6 1.5 collective-permute-start.9
  73.1 5.1 %collective-permute-start.10 = (f32[48,274]{1,0:T(8,128)S(1)}, f32[48,274]{1,0:T(8,128)S(1)}, u32[]{:S(2)}, u32[]{:S(2)}) collective-permute-start(f32[48,274]{1,0:T(8,128)S(1)} %pad_maximum_fusion.22), channel_id=1, source_target_pairs={{0,1},{1,2},{2,3},{3,4},{4,5},{5,6},{6,7},{7,8},{8,9},{9,10},{10,1... | collective-permute-start | bytes 157832 | tf_op jit(solution)/shard_map/ppermute | solution.py:140
  80.8 1.2 copy.104
  82.0 2.0 copy.102
  85.6 3.2 %collective-permute-start.12 = (f32[48,386]{1,0:T(8,128)}, f32[48,386]{1,0:T(8,128)S(1)}, u32[]{:S(2)}, u32[]{:S(2)}) collective-permute-start(f32[48,386]{1,0:T(8,128)} %concatenate.252), channel_id=1, source_target_pairs={{0,16},{1,17},{2,18},{3,19},{4,20},{5,21},{6,22},{7,23},{8,24},{9,... | collective-permute-start | bytes 222344 | tf_op jit(solution)/shard_map/ppermute | solution.py:140
  89.2 2.1 pad_maximum_fusion.1
  91.9 2.0 collective-permute-done.13
  94.9 1.5 fusion.46
  97.0 1.0 slice_add_fusion
  99.3 1.4 fusion.138
  100.6 1.6 fusion.137
  102.6 3.6 %select_select_fusion.6 = (f32[8,36,768]{2,1,0:T(8,128)S(1)}, f32[8,36,768]{2,1,0:T(8,128)}) fusion(f32[8,768]{1,0:T(8,128)S(1)} %get-tuple-element.74, f32[8,768]{1,0:T(8,128)S(1)} %get-tuple-element.73, pred[36]{0:T(512)(128)(4,1)S(1)} %get-tuple-element.132, pred[36]{0:T(512)(128)(4,1)S(1)} %get-tuple-element.133, f32[8,35,768]{2,1,0:T(8,128)} %get-tuple-element.70, ...), kind=kLoop, calls=%fused_computation.83 | loop fusion | flops 1990656 | bytes 6193224 | tf_op jit(solution)/shard_map/jit(_where)/select_n | solution.py:170
  106.1 1.6 fusion.134
  107.7 1.4 fusion.136
  109.9 1.5 copy.119
  111.4 3.0 %select_select_fusion.5 = (f32[8,36,768]{2,1,0:T(8,128)S(1)}, f32[8,36,768]{2,1,0:T(8,128)S(1)}, f32[8,36,768]{2,1,0:T(8,128)S(1)}, f32[8,36,768]{2,1,0:T(8,128)S(1)}) fusion(f32[8,768]{1,0:T(8,128)S(1)} %get-tuple-element.77, f32[8,768]{1,0:T(8,128)S(1)} %get-tuple-element.78, pred[36]{0:T(512)(128)(4,1)S(1)} %get-tuple-element.132, ...), kind=kLoop, calls=%fused_computation.82 | loop fusion | flops 3981312 | bytes 8896584 | tf_op jit(solution)/shard_map/jit(_where)/select_n | solution.py:170
  120.7 1.1 fusion.44
  122.3 1.3 collective-permute-start.14
  123.6 1.9 collective-permute-start.15
  140.9 7.0 %collective-permute-start.17 = (f32[8,3,8,256]{3,1,0,2:T(4,128)S(1)}, f32[8,3,8,256]{3,1,0,2:T(4,128)S(1)}, u32[]{:S(2)}, u32[]{:S(2)}) collective-permute-start(f32[8,3,8,256]{3,1,0,2:T(4,128)S(1)} %copy_multiply_fusion), channel_id=1, source_target_pairs={{1,3},{3,4},{5,5},{7,6},{9,7},{11,8},{13,9},{15,10},{17,11},{19,12... | collective-permute-start | bytes 589832 | tf_op jit(solution)/shard_map/ppermute | solution.py:216
  148.5 2.7 %collective-permute-start.19 = (f32[8,3,8,256]{3,1,0,2:T(4,128)S(1)}, f32[8,3,8,256]{3,1,0,2:T(4,128)S(1)}, u32[]{:S(2)}, u32[]{:S(2)}) collective-permute-start(f32[8,3,8,256]{3,1,0,2:T(4,128)S(1)} %copy_multiply_fusion), channel_id=1, source_target_pairs={{1,2},{3,3},{5,4},{7,5},{9,6},{11,7},{13,8},{15,9},{17,10},{19,11}... | collective-permute-start | bytes 589832 | tf_op jit(solution)/shard_map/ppermute | solution.py:216
  151.3 0.9 collective-permute-start.20
  152.3 7.0 %collective-permute-start.21 = (f32[8,3,8,256]{3,1,0,2:T(4,128)S(1)}, f32[8,3,8,256]{3,1,0,2:T(4,128)S(1)}, u32[]{:S(2)}, u32[]{:S(2)}) collective-permute-start(f32[8,3,8,256]{3,1,0,2:T(4,128)S(1)} %copy_multiply_fusion), channel_id=1, source_target_pairs={{1,1},{3,2},{5,3},{7,4},{9,5},{11,6},{13,7},{15,8},{17,9},{19,10},... | collective-permute-start | bytes 589832 | tf_op jit(solution)/shard_map/ppermute | solution.py:216
  160.2 7.4 %collective-permute-start.23 = (f32[8,3,8,256]{3,1,0,2:T(4,128)S(1)}, f32[8,3,8,256]{3,1,0,2:T(4,128)S(1)}, u32[]{:S(2)}, u32[]{:S(2)}) collective-permute-start(f32[8,3,8,256]{3,1,0,2:T(4,128)S(1)} %copy_multiply_fusion), channel_id=1, source_target_pairs={{1,0},{3,1},{5,2},{7,3},{9,4},{11,5},{13,6},{15,7},{17,8},{19,9},{... | collective-permute-start | bytes 589832 | tf_op jit(solution)/shard_map/ppermute | solution.py:216
  167.7 13.7 %collective-permute-done.19 = f32[8,3,8,256]{3,1,0,2:T(4,128)S(1)} collective-permute-done((f32[8,3,8,256]{3,1,0,2:T(4,128)S(1)}, f32[8,3,8,256]{3,1,0,2:T(4,128)S(1)}, u32[]{:S(2)}, u32[]{:S(2)}) %collective-permute-start.19) | collective-permute-done | bytes 196640 | tf_op jit(solution)/shard_map/ppermute | solution.py:216
  181.7 9.7 %collective-permute-done.23 = f32[8,3,8,256]{3,1,0,2:T(4,128)S(1)} collective-permute-done((f32[8,3,8,256]{3,1,0,2:T(4,128)S(1)}, f32[8,3,8,256]{3,1,0,2:T(4,128)S(1)}, u32[]{:S(2)}, u32[]{:S(2)}) %collective-permute-start.23) | collective-permute-done | bytes 196640 | tf_op jit(solution)/shard_map/ppermute | solution.py:216
  191.4 1.5 copy-done.30
  192.9 2.6 %gather_fusion = f32[8,3,16,256]{3,1,2,0:T(4,128)S(1)} fusion(f32[8,3,80,256]{3,1,0,2:T(4,128)} %copy-done.30, s32[8]{0:T(128)S(1)} %get-tuple-element.99), kind=kCustom, calls=%fused_computation | custom fusion | bytes 786560 | tf_op jit(solution)/shard_map/vmap()/gather | solution.py:219
  195.6 1.9 collective-permute-start.24
  197.5 1.9 collective-permute-start.25
  199.4 11.8 %collective-permute-start.26 = (f32[8,3,16,256]{3,2,1,0:T(8,128)S(1)}, f32[8,3,16,256]{3,2,1,0:T(8,128)S(1)}, u32[]{:S(2)}, u32[]{:S(2)}) collective-permute-start(f32[8,3,16,256]{3,2,1,0:T(8,128)S(1)} %copy.133), channel_id=1, source_target_pairs={{0,4},{1,5},{2,6},{3,7},{4,8},{5,9},{6,10},{7,11},{8,12},{9,13},{1... | collective-permute-start | bytes 1179656 | tf_op jit(solution)/shard_map/ppermute | solution.py:222
  211.3 2.1 collective-permute-done.24
  213.4 13.7 %collective-permute-done.25 = f32[8,3,16,256]{3,2,1,0:T(8,128)S(1)} collective-permute-done((f32[8,3,16,256]{3,2,1,0:T(8,128)S(1)}, f32[8,3,16,256]{3,2,1,0:T(8,128)S(1)}, u32[]{:S(2)}, u32[]{:S(2)}) %collective-permute-start.25) | collective-permute-done | bytes 393248 | tf_op jit(solution)/shard_map/ppermute | solution.py:222
  227.1 2.2 collective-permute-done.26
  229.5 1.0 slice_select_fusion.7
  230.4 1.9 dynamic_update_slice.24
  232.4 1.0 slice_select_fusion.6
  233.3 1.9 dynamic_update_slice.25
  235.2 1.0 slice_select_fusion.5
  236.2 1.9 dynamic_update_slice.26
  238.1 1.0 slice_select_fusion.4
  239.1 1.9 dynamic_update_slice.27
  241.0 1.0 slice_select_fusion.3
  242.0 1.9 dynamic_update_slice.28
  243.9 1.0 slice_select_fusion.2
  244.9 1.9 dynamic_update_slice.29
  246.8 1.0 slice_select_fusion.1
  247.8 1.9 dynamic_update_slice.30
  249.7 1.0 slice_select_fusion
  250.6 1.9 dynamic_update_slice.31
  (237 shorter events, 31.1 us)
Async XLA Ops:
  3.9 6.3 %copy-start = (f32[8,16,4096]{2,1,0:T(8,128)}, f32[8,16,4096]{2,1,0:T(8,128)S(1)}, u32[]{:S(2)}) copy-start(f32[8,16,4096]{2,1,0:T(8,128)S(1)} %get-tuple-element.19) | copy-start | bytes 6291460
  3.9 11.3 %copy-start.5 = (f32[8,3,24,768]{3,2,1,0:T(8,128)S(1)}, f32[8,3,24,768]{3,2,1,0:T(8,128)}, u32[]{:S(2)}) copy-start(f32[8,3,24,768]{3,2,1,0:T(8,128)} %param.4) | copy-start | bytes 5308420
  5.8 35.0 %collective-permute-start = (f32[8,4,4096]{2,1,0:T(4,128)}, f32[8,4,4096]{2,1,0:T(4,128)S(1)}, u32[]{:S(2)}, u32[]{:S(2)}) collective-permute-start(f32[8,4,4096]{2,1,0:T(4,128)} %pad_maximum_fusion.20), channel_id=1, source_target_pairs={{1,0},{2,1},{3,2},{4,3},{5,4},{6,5},{7,6},{8,7},{9,8},{10,9},{11,1... | collective-permute-start | bytes 1572872 | tf_op jit(solution)/shard_map/ppermute | solution.py:59
  10.2 30.9 %collective-permute-start.1 = (f32[8,4,4096]{2,1,0:T(4,128)}, f32[8,4,4096]{2,1,0:T(4,128)S(1)}, u32[]{:S(2)}, u32[]{:S(2)}) collective-permute-start(f32[8,4,4096]{2,1,0:T(4,128)} %pad_maximum_fusion.21), channel_id=1, source_target_pairs={{0,1},{1,2},{2,3},{3,4},{4,5},{5,6},{6,7},{7,8},{8,9},{9,10},{10,1... | collective-permute-start | bytes 1572872 | tf_op jit(solution)/shard_map/ppermute | solution.py:58
  16.2 48.0 %collective-permute-start.3 = (f32[8,3,6,768]{3,0,2,1:T(8,128)}, f32[8,3,6,768]{3,0,2,1:T(8,128)}, u32[]{:S(2)}, u32[]{:S(2)}) collective-permute-start(f32[8,3,6,768]{3,0,2,1:T(8,128)} %copy.148), channel_id=1, source_target_pairs={{1,0},{2,1},{3,2},{4,3},{5,4},{6,5},{7,6},{8,7},{9,8},{10,9},{11,1... | collective-permute-start | bytes 1327112 | tf_op jit(solution)/shard_map/ppermute | solution.py:29
  19.6 44.7 %collective-permute-start.2 = (f32[8,3,6,768]{3,0,2,1:T(8,128)}, f32[8,3,6,768]{3,0,2,1:T(8,128)}, u32[]{:S(2)}, u32[]{:S(2)}) collective-permute-start(f32[8,3,6,768]{3,0,2,1:T(8,128)} %copy.147), channel_id=1, source_target_pairs={{0,1},{1,2},{2,3},{3,4},{4,5},{5,6},{6,7},{7,8},{8,9},{9,10},{10,1... | collective-permute-start | bytes 1327112 | tf_op jit(solution)/shard_map/ppermute | solution.py:27
  25.4 2.8 %copy-start.34 = (s32[8,2]{0,1:T(2,128)S(1)}, s32[8,2]{0,1:T(2,128)}, u32[]{:S(2)}) copy-start(s32[8,2]{0,1:T(2,128)} %param.5) | copy-start | bytes 196
  38.6 4.1 %copy-start.35 = (s32[8]{0:T(128)}, s32[8]{0:T(128)S(1)}, u32[]{:S(2)}) copy-start(s32[8]{0:T(128)S(1)} %get-tuple-element.103) | copy-start | bytes 100
  41.8 5.4 %slice-start = ((s8[6291456]{0:T(1024)(128)(4,1)}), s8[4194304]{0:T(1024)(128)(4,1)S(1)}, s32[]{:S(2)}) async-start(s8[6291456]{0:T(1024)(128)(4,1)} %bitcast.193), calls=%async_computation | async-start | bytes 8388608
  42.7 4.5 %slice-start.1 = ((s8[6291456]{0:T(1024)(128)(4,1)}), s8[2097152]{0:T(1024)(128)(4,1)S(1)}, s32[]{:S(2)}) async-start(s8[6291456]{0:T(1024)(128)(4,1)} %bitcast.193), calls=%async_computation.1 | async-start | bytes 4194304
  49.7 2.7 %copy-start.2 = (f32[8,3,16,4096]{3,2,1,0:T(8,128)}, f32[8,3,16,4096]{3,2,1,0:T(8,128)S(1)}, u32[]{:S(2)}) copy-start(f32[8,3,16,4096]{3,2,1,0:T(8,128)S(1)} %pad_maximum_fusion) | copy-start | bytes 18874372
  55.9 32.8 %copy-start.10 = (f32[2,8,3,16]{3,0,2,1:T(2,128)}, f32[2,8,3,16]{3,0,2,1:T(2,128)S(1)}, u32[]{:S(2)}) copy-start(f32[2,8,3,16]{3,0,2,1:T(2,128)S(1)} %fusion.85) | copy-start | bytes 9220
  56.0 15.6 %collective-permute-start.4 = (f32[48,274]{1,0:T(8,128)S(1)}, f32[48,274]{1,0:T(8,128)S(1)}, u32[]{:S(2)}, u32[]{:S(2)}) collective-permute-start(f32[48,274]{1,0:T(8,128)S(1)} %pad_maximum_fusion.22), channel_id=1, source_target_pairs={{0,7},{1,8},{2,9},{3,10},{4,11},{5,12},{6,13},{7,14},{8,15},{9,16}... | collective-permute-start | bytes 157832 | tf_op jit(solution)/shard_map/ppermute | solution.py:140
  56.6 16.5 %collective-permute-start.5 = (f32[48,274]{1,0:T(8,128)S(1)}, f32[48,274]{1,0:T(8,128)S(1)}, u32[]{:S(2)}, u32[]{:S(2)}) collective-permute-start(f32[48,274]{1,0:T(8,128)S(1)} %pad_maximum_fusion.22), channel_id=1, source_target_pairs={{0,6},{1,7},{2,8},{3,9},{4,10},{5,11},{6,12},{7,13},{8,14},{9,15},... | collective-permute-start | bytes 157832 | tf_op jit(solution)/shard_map/ppermute | solution.py:140
  57.8 26.2 %collective-permute-start.6 = (f32[48,274]{1,0:T(8,128)S(1)}, f32[48,274]{1,0:T(8,128)S(1)}, u32[]{:S(2)}, u32[]{:S(2)}) collective-permute-start(f32[48,274]{1,0:T(8,128)S(1)} %pad_maximum_fusion.22), channel_id=1, source_target_pairs={{0,5},{1,6},{2,7},{3,8},{4,9},{5,10},{6,11},{7,12},{8,13},{9,14},{... | collective-permute-start | bytes 157832 | tf_op jit(solution)/shard_map/ppermute | solution.py:140
  64.2 19.8 %collective-permute-start.7 = (f32[48,274]{1,0:T(8,128)S(1)}, f32[48,274]{1,0:T(8,128)S(1)}, u32[]{:S(2)}, u32[]{:S(2)}) collective-permute-start(f32[48,274]{1,0:T(8,128)S(1)} %pad_maximum_fusion.22), channel_id=1, source_target_pairs={{0,4},{1,5},{2,6},{3,7},{4,8},{5,9},{6,10},{7,11},{8,12},{9,13},{1... | collective-permute-start | bytes 157832 | tf_op jit(solution)/shard_map/ppermute | solution.py:140
  64.3 19.8 %collective-permute-start.8 = (f32[48,274]{1,0:T(8,128)S(1)}, f32[48,274]{1,0:T(8,128)S(1)}, u32[]{:S(2)}, u32[]{:S(2)}) collective-permute-start(f32[48,274]{1,0:T(8,128)S(1)} %pad_maximum_fusion.22), channel_id=1, source_target_pairs={{0,3},{1,4},{2,5},{3,6},{4,7},{5,8},{6,9},{7,10},{8,11},{9,12},{10... | collective-permute-start | bytes 157832 | tf_op jit(solution)/shard_map/ppermute | solution.py:140
  71.6 12.5 %collective-permute-start.9 = (f32[48,274]{1,0:T(8,128)S(1)}, f32[48,274]{1,0:T(8,128)S(1)}, u32[]{:S(2)}, u32[]{:S(2)}) collective-permute-start(f32[48,274]{1,0:T(8,128)S(1)} %pad_maximum_fusion.22), channel_id=1, source_target_pairs={{0,2},{1,3},{2,4},{3,5},{4,6},{5,7},{6,8},{7,9},{8,10},{9,11},{10,... | collective-permute-start | bytes 157832 | tf_op jit(solution)/shard_map/ppermute | solution.py:140
  73.1 11.0 %collective-permute-start.10 = (f32[48,274]{1,0:T(8,128)S(1)}, f32[48,274]{1,0:T(8,128)S(1)}, u32[]{:S(2)}, u32[]{:S(2)}) collective-permute-start(f32[48,274]{1,0:T(8,128)S(1)} %pad_maximum_fusion.22), channel_id=1, source_target_pairs={{0,1},{1,2},{2,3},{3,4},{4,5},{5,6},{6,7},{7,8},{8,9},{9,10},{10,1... | collective-permute-start | bytes 157832 | tf_op jit(solution)/shard_map/ppermute | solution.py:140
  84.0 4.8 %copy-start.18 = (f32[48,16]{1,0:T(8,128)}, f32[48,16]{1,0:T(8,128)S(1)}, u32[]{:S(2)}) copy-start(f32[48,16]{1,0:T(8,128)S(1)} %slice.605) | copy-start | bytes 9220
  84.0 4.8 %copy-start.16 = (f32[48,16]{1,0:T(8,128)}, f32[48,16]{1,0:T(8,128)S(1)}, u32[]{:S(2)}) copy-start(f32[48,16]{1,0:T(8,128)S(1)} %slice.606) | copy-start | bytes 9220
  84.0 4.8 %copy-start.20 = (f32[48,16]{1,0:T(8,128)}, f32[48,16]{1,0:T(8,128)S(1)}, u32[]{:S(2)}) copy-start(f32[48,16]{1,0:T(8,128)S(1)} %slice.607) | copy-start | bytes 9220
  84.0 4.7 %copy-start.22 = (f32[48,16]{1,0:T(8,128)}, f32[48,16]{1,0:T(8,128)S(1)}, u32[]{:S(2)}) copy-start(f32[48,16]{1,0:T(8,128)S(1)} %slice.608) | copy-start | bytes 9220
  84.1 4.7 %copy-start.24 = (f32[48,16]{1,0:T(8,128)}, f32[48,16]{1,0:T(8,128)S(1)}, u32[]{:S(2)}) copy-start(f32[48,16]{1,0:T(8,128)S(1)} %slice.609) | copy-start | bytes 9220
  84.1 4.7 %copy-start.26 = (f32[48,16]{1,0:T(8,128)}, f32[48,16]{1,0:T(8,128)S(1)}, u32[]{:S(2)}) copy-start(f32[48,16]{1,0:T(8,128)S(1)} %slice.610) | copy-start | bytes 9220
  84.1 4.7 %copy-start.28 = (f32[48,16]{1,0:T(8,128)}, f32[48,16]{1,0:T(8,128)S(1)}, u32[]{:S(2)}) copy-start(f32[48,16]{1,0:T(8,128)S(1)} %slice.611) | copy-start | bytes 9220
  84.4 4.5 %copy-start.8 = (f32[48,258]{1,0:T(8,128)}, f32[48,258]{1,0:T(8,128)S(1)}, u32[]{:S(2)}) copy-start(f32[48,258]{1,0:T(8,128)S(1)} %slice_add_fusion.3) | copy-start | bytes 148612
  85.1 6.4 %collective-permute-start.11 = (f32[48,386]{1,0:T(8,128)}, f32[48,386]{1,0:T(8,128)S(1)}, u32[]{:S(2)}, u32[]{:S(2)}) collective-permute-start(f32[48,386]{1,0:T(8,128)} %concatenate.252), channel_id=1, source_target_pairs={{0,24},{1,25},{2,26},{3,27},{4,28},{5,29},{6,30},{7,31},{8,0},{9,1... | collective-permute-start | bytes 222344 | tf_op jit(solution)/shard_map/ppermute | solution.py:140
  85.6 6.3 %collective-permute-start.12 = (f32[48,386]{1,0:T(8,128)}, f32[48,386]{1,0:T(8,128)S(1)}, u32[]{:S(2)}, u32[]{:S(2)}) collective-permute-start(f32[48,386]{1,0:T(8,128)} %concatenate.252), channel_id=1, source_target_pairs={{0,16},{1,17},{2,18},{3,19},{4,20},{5,21},{6,22},{7,23},{8,24},{9,... | collective-permute-start | bytes 222344 | tf_op jit(solution)/shard_map/ppermute | solution.py:140
  88.8 5.1 %collective-permute-start.13 = (f32[48,386]{1,0:T(8,128)}, f32[48,386]{1,0:T(8,128)S(1)}, u32[]{:S(2)}, u32[]{:S(2)}) collective-permute-start(f32[48,386]{1,0:T(8,128)} %concatenate.252), channel_id=1, source_target_pairs={{0,8},{1,9},{2,10},{3,11},{4,12},{5,13},{6,14},{7,15},{8,16},{9,17... | collective-permute-start | bytes 222344 | tf_op jit(solution)/shard_map/ppermute | solution.py:140
  89.1 2.2 copy-start.11
  89.1 2.2 copy-start.19
  89.1 2.2 copy-start.17
  89.2 2.3 copy-start.21
  89.2 2.3 copy-start.23
  89.2 2.3 copy-start.25
  89.2 2.3 copy-start.27
  89.2 2.3 copy-start.29
  91.3 5.7 %copy-start.9 = (f32[48,258]{1,0:T(8,128)S(1)}, f32[48,258]{1,0:T(8,128)}, u32[]{:S(2)}) copy-start(f32[48,258]{1,0:T(8,128)} %copy-done.8) | copy-start | bytes 148612
  91.3 6.8 %copy-start.37 = (f32[768]{0:T(1024)S(1)}, f32[768]{0:T(1024)}, u32[]{:S(2)}) copy-start(f32[768]{0:T(1024)} %slice.618) | copy-start | bytes 9220
  91.3 6.8 %copy-start.38 = (f32[768]{0:T(1024)S(1)}, f32[768]{0:T(1024)}, u32[]{:S(2)}) copy-start(f32[768]{0:T(1024)} %slice.617) | copy-start | bytes 9220
  91.3 6.8 %copy-start.39 = (s32[768]{0:T(1024)S(1)}, s32[768]{0:T(1024)}, u32[]{:S(2)}) copy-start(s32[768]{0:T(1024)} %slice.616) | copy-start | bytes 9220
  91.3 6.8 %copy-start.40 = (s32[768]{0:T(1024)S(1)}, s32[768]{0:T(1024)}, u32[]{:S(2)}) copy-start(s32[768]{0:T(1024)} %slice.615) | copy-start | bytes 9220
  91.6 2.4 copy-start.31
  91.9 2.1 copy-start.32
  99.0 3.6 %copy-start.12 = (f32[8,768]{1,0:T(8,128)}, f32[8,768]{1,0:T(8,128)S(1)}, u32[]{:S(2)}) copy-start(f32[8,768]{1,0:T(8,128)S(1)} %get-tuple-element.73) | copy-start | bytes 73732
  99.0 3.6 %copy-start.14 = (f32[8,768]{1,0:T(8,128)}, f32[8,768]{1,0:T(8,128)S(1)}, u32[]{:S(2)}) copy-start(f32[8,768]{1,0:T(8,128)S(1)} %get-tuple-element.74) | copy-start | bytes 73732
  120.7 4.8 %copy-start.36 = (s32[8]{0:T(128)S(1)}, s32[8]{0:T(128)}, u32[]{:S(2)}) copy-start(s32[8]{0:T(128)} %copy-done.35) | copy-start | bytes 100
  120.7 4.8 %copy-start.42 = (s32[16]{0:T(128)S(1)}, s32[16]{0:T(128)}, u32[]{:S(2)}) copy-start(s32[16]{0:T(128)} %copy-done.41) | copy-start | bytes 196
  122.3 26.3 %collective-permute-start.14 = (f32[8,3,8,256]{3,1,0,2:T(4,128)S(1)}, f32[8,3,8,256]{3,1,0,2:T(4,128)S(1)}, u32[]{:S(2)}, u32[]{:S(2)}) collective-permute-start(f32[8,3,8,256]{3,1,0,2:T(4,128)S(1)} %copy_multiply_fusion), channel_id=1, source_target_pairs={{0,4},{2,5},{4,6},{6,7},{8,8},{10,9},{12,10},{14,11},{16,12},{18,1... | collective-permute-start | bytes 589832 | tf_op jit(solution)/shard_map/ppermute | solution.py:216
  123.6 27.7 %collective-permute-start.15 = (f32[8,3,8,256]{3,1,0,2:T(4,128)S(1)}, f32[8,3,8,256]{3,1,0,2:T(4,128)S(1)}, u32[]{:S(2)}, u32[]{:S(2)}) collective-permute-start(f32[8,3,8,256]{3,1,0,2:T(4,128)S(1)} %copy_multiply_fusion), channel_id=1, source_target_pairs={{1,4},{3,5},{5,6},{7,7},{9,8},{11,9},{13,10},{15,11},{17,12},{19,1... | collective-permute-start | bytes 589832 | tf_op jit(solution)/shard_map/ppermute | solution.py:216
  140.2 12.2 %collective-permute-start.16 = (f32[8,3,8,256]{3,1,0,2:T(4,128)S(1)}, f32[8,3,8,256]{3,1,0,2:T(4,128)S(1)}, u32[]{:S(2)}, u32[]{:S(2)}) collective-permute-start(f32[8,3,8,256]{3,1,0,2:T(4,128)S(1)} %copy_multiply_fusion), channel_id=1, source_target_pairs={{0,3},{2,4},{4,5},{6,6},{8,7},{10,8},{12,9},{14,10},{16,11},{18,12... | collective-permute-start | bytes 589832 | tf_op jit(solution)/shard_map/ppermute | solution.py:216
  140.9 18.5 %collective-permute-start.17 = (f32[8,3,8,256]{3,1,0,2:T(4,128)S(1)}, f32[8,3,8,256]{3,1,0,2:T(4,128)S(1)}, u32[]{:S(2)}, u32[]{:S(2)}) collective-permute-start(f32[8,3,8,256]{3,1,0,2:T(4,128)S(1)} %copy_multiply_fusion), channel_id=1, source_target_pairs={{1,3},{3,4},{5,5},{7,6},{9,7},{11,8},{13,9},{15,10},{17,11},{19,12... | collective-permute-start | bytes 589832 | tf_op jit(solution)/shard_map/ppermute | solution.py:216
  147.9 12.3 %collective-permute-start.18 = (f32[8,3,8,256]{3,1,0,2:T(4,128)S(1)}, f32[8,3,8,256]{3,1,0,2:T(4,128)S(1)}, u32[]{:S(2)}, u32[]{:S(2)}) collective-permute-start(f32[8,3,8,256]{3,1,0,2:T(4,128)S(1)} %copy_multiply_fusion), channel_id=1, source_target_pairs={{0,2},{2,3},{4,4},{6,5},{8,6},{10,7},{12,8},{14,9},{16,10},{18,11}... | collective-permute-start | bytes 589832 | tf_op jit(solution)/shard_map/ppermute | solution.py:216
  148.5 32.8 %collective-permute-start.19 = (f32[8,3,8,256]{3,1,0,2:T(4,128)S(1)}, f32[8,3,8,256]{3,1,0,2:T(4,128)S(1)}, u32[]{:S(2)}, u32[]{:S(2)}) collective-permute-start(f32[8,3,8,256]{3,1,0,2:T(4,128)S(1)} %copy_multiply_fusion), channel_id=1, source_target_pairs={{1,2},{3,3},{5,4},{7,5},{9,6},{11,7},{13,8},{15,9},{17,10},{19,11}... | collective-permute-start | bytes 589832 | tf_op jit(solution)/shard_map/ppermute | solution.py:216
  151.3 30.1 %collective-permute-start.20 = (f32[8,3,8,256]{3,1,0,2:T(4,128)S(1)}, f32[8,3,8,256]{3,1,0,2:T(4,128)S(1)}, u32[]{:S(2)}, u32[]{:S(2)}) collective-permute-start(f32[8,3,8,256]{3,1,0,2:T(4,128)S(1)} %copy_multiply_fusion), channel_id=1, source_target_pairs={{0,1},{2,2},{4,3},{6,4},{8,5},{10,6},{12,7},{14,8},{16,9},{18,10},... | collective-permute-start | bytes 589832 | tf_op jit(solution)/shard_map/ppermute | solution.py:216
  152.3 29.1 %collective-permute-start.21 = (f32[8,3,8,256]{3,1,0,2:T(4,128)S(1)}, f32[8,3,8,256]{3,1,0,2:T(4,128)S(1)}, u32[]{:S(2)}, u32[]{:S(2)}) collective-permute-start(f32[8,3,8,256]{3,1,0,2:T(4,128)S(1)} %copy_multiply_fusion), channel_id=1, source_target_pairs={{1,1},{3,2},{5,3},{7,4},{9,5},{11,6},{13,7},{15,8},{17,9},{19,10},... | collective-permute-start | bytes 589832 | tf_op jit(solution)/shard_map/ppermute | solution.py:216
  159.4 22.2 %collective-permute-start.22 = (f32[8,3,8,256]{3,1,0,2:T(4,128)S(1)}, f32[8,3,8,256]{3,1,0,2:T(4,128)S(1)}, u32[]{:S(2)}, u32[]{:S(2)}) collective-permute-start(f32[8,3,8,256]{3,1,0,2:T(4,128)S(1)} %copy_multiply_fusion), channel_id=1, source_target_pairs={{0,0},{2,1},{4,2},{6,3},{8,4},{10,5},{12,6},{14,7},{16,8},{18,9},{... | collective-permute-start | bytes 589832 | tf_op jit(solution)/shard_map/ppermute | solution.py:216
  160.2 31.1 %collective-permute-start.23 = (f32[8,3,8,256]{3,1,0,2:T(4,128)S(1)}, f32[8,3,8,256]{3,1,0,2:T(4,128)S(1)}, u32[]{:S(2)}, u32[]{:S(2)}) collective-permute-start(f32[8,3,8,256]{3,1,0,2:T(4,128)S(1)} %copy_multiply_fusion), channel_id=1, source_target_pairs={{1,0},{3,1},{5,2},{7,3},{9,4},{11,5},{13,6},{15,7},{17,8},{19,9},{... | collective-permute-start | bytes 589832 | tf_op jit(solution)/shard_map/ppermute | solution.py:216
  167.6 43.6 %copy-start.44 = (s32[8]{0:T(128)S(1)}, s32[8]{0:T(128)}, u32[]{:S(2)}) copy-start(s32[8]{0:T(128)} %get-tuple-element.3) | copy-start | bytes 100
  167.6 61.6 %copy-start.43 = (pred[8]{0:T(512)(128)(4,1)S(1)}, pred[8]{0:T(512)(128)(4,1)}, u32[]{:S(2)}) copy-start(pred[8]{0:T(512)(128)(4,1)} %get-tuple-element.2) | copy-start | bytes 28
  195.6 17.9 %collective-permute-start.24 = (f32[8,3,16,256]{3,2,1,0:T(8,128)S(1)}, f32[8,3,16,256]{3,2,1,0:T(8,128)S(1)}, u32[]{:S(2)}, u32[]{:S(2)}) collective-permute-start(f32[8,3,16,256]{3,2,1,0:T(8,128)S(1)} %copy.133), channel_id=1, source_target_pairs={{0,12},{1,13},{2,14},{3,15},{4,16},{5,17},{6,18},{7,19},{8,20},{9,... | collective-permute-start | bytes 1179656 | tf_op jit(solution)/shard_map/ppermute | solution.py:222
  197.5 29.6 %collective-permute-start.25 = (f32[8,3,16,256]{3,2,1,0:T(8,128)S(1)}, f32[8,3,16,256]{3,2,1,0:T(8,128)S(1)}, u32[]{:S(2)}, u32[]{:S(2)}) collective-permute-start(f32[8,3,16,256]{3,2,1,0:T(8,128)S(1)} %copy.133), channel_id=1, source_target_pairs={{0,8},{1,9},{2,10},{3,11},{4,12},{5,13},{6,14},{7,15},{8,16},{9,17... | collective-permute-start | bytes 1179656 | tf_op jit(solution)/shard_map/ppermute | solution.py:222
  199.4 29.8 %collective-permute-start.26 = (f32[8,3,16,256]{3,2,1,0:T(8,128)S(1)}, f32[8,3,16,256]{3,2,1,0:T(8,128)S(1)}, u32[]{:S(2)}, u32[]{:S(2)}) collective-permute-start(f32[8,3,16,256]{3,2,1,0:T(8,128)S(1)} %copy.133), channel_id=1, source_target_pairs={{0,4},{1,5},{2,6},{3,7},{4,8},{5,9},{6,10},{7,11},{8,12},{9,13},{1... | collective-permute-start | bytes 1179656 | tf_op jit(solution)/shard_map/ppermute | solution.py:222
  (10 other events, 12.5 us)

commit v5 on v4

--- a/solution.py
+++ b/solution.py
@@ -135,6 +135,8 @@
     while reach < bands:
         count = min(8, bands // reach)
         payload = jnp.concatenate([blocks, sums], axis=1)
+        if reach == 1:
+            nest_state, payload = lax.optimization_barrier((nest_state, payload))
         width = blocks.shape[1]
         recvs = [
             lax.ppermute(payload, "band", [(i, (i + k * reach) % bands) for i in range(bands)])
@@ -224,12 +226,10 @@
 
     relative_rows = global_rows[None, :] - rows_off[:, None]
     covered = (relative_rows >= 0) & (relative_rows < span)
+    merged = jnp.where(covered[:, None, :, None], patch, colslice[..., 1 : span + 1])
     parent_out = stepped
     for m in range(members):
-        start = (m, 0, 0, cols_off[m])
-        current = lax.dynamic_slice(parent_out, start, (1, 3, band_rows, span))
-        merged = jnp.where(covered[m][None, None, :, None], patch[m : m + 1], current)
-        parent_out = lax.dynamic_update_slice(parent_out, merged, start)
+        parent_out = lax.dynamic_update_slice(parent_out, merged[m : m + 1], (m, 0, 0, cols_off[m]))
     return (parent_out, nest)
 
 

time: 255 us -> 238 us (0.933)
  the two profiles are of different devices: /device:TPU:54 before, /device:TPU:14 now
where the time goes in v5:
time: 238 us; the launch traced here: 236 us
  waiting for transfers between devices  68.6 us (29%)
  starting transfers between devices  66.3 us (28%)
  local copies, waits for them, and re-layouts  48.1 us (20%)
  between operations  26.9 us (11%)
  other arithmetic  19.5 us (8%)
  matrix products  6.83 us (3%)
    ppermute x10, waiting for transfers between devices, per_device(): fetched.append(lax.ppermute(coarse, 'band', pairs))  31.4 us
    ppermute x10, starting transfers between devices, per_device(): fetched.append(lax.ppermute(coarse, 'band', pairs))  25.7 us
    ppermute x3, waiting for transfers between devices, per_device(): recv = lax.ppermute(near, 'band', shift_pairs(bands, j * radix))  24.1 us
    ppermute x10, starting transfers between devices, per_device(): lax.ppermute(payload, 'band', [(i, (i + k * reach) % bands) for i in rang...  18.5 us
    dynamic_update_slice x8, local copies, waits for them, and re-layouts, per_device(): lax.dynamic_update_slice(parent_out, merged[m:m + 1], (m, 0, 0, cols_off[...  15.2 us
    unnamed x66, local copies, waits for them, and re-layouts  6.38 us
    ppermute x1, waiting for transfers between devices, parent_step(): prev = lax.ppermute(tail, 'band', shift_pairs(count, 1))  5.76 us
    ppermute x3, starting transfers between devices, per_device(): recv = lax.ppermute(near, 'band', shift_pairs(bands, j * radix))  5.48 us
  transfers between devices with their start and end apart: 27, of which 12 were waited for; matrix products, arithmetic and copies ran while one was open for 9% of the time, Pallas kernels for 0%

profile of v5, /device:TPU:14, one launch (start us, length us, event | category | flops | bytes accessed | tf_op | source)
XLA Modules:
  0.0 236.4 jit_solution(16750481829679966223)
XLA Ops:
  0.6 3.3 %slice_bitcast_fusion.4 = (f32[8,16,4096]{2,1,0:T(8,128)S(1)}, f32[8,16,4096]{2,1,0:T(8,128)S(1)}, f32[8,16,4096]{2,1,0:T(8,128)S(1)}) fusion(f32[8,3,16,4096]{3,2,1,0:T(8,128)} %param.3), kind=kLoop, calls=%fused_computation.28 | loop fusion | bytes 12582912 | tf_op jit(solution)/shard_map/squeeze | solution.py:50
  4.6 1.1 pad_maximum_fusion.20
  5.8 3.3 %collective-permute-start = (f32[8,4,4096]{2,1,0:T(4,128)}, f32[8,4,4096]{2,1,0:T(4,128)S(1)}, u32[]{:S(2)}, u32[]{:S(2)}) collective-permute-start(f32[8,4,4096]{2,1,0:T(4,128)} %pad_maximum_fusion.20), channel_id=1, source_target_pairs={{1,0},{2,1},{3,2},{4,3},{5,4},{6,5},{7,6},{8,7},{9,8},{10,9},{11,1... | collective-permute-start | bytes 1572872 | tf_op jit(solution)/shard_map/ppermute | solution.py:59
  9.1 1.2 pad_maximum_fusion.21
  10.2 4.9 %collective-permute-start.1 = (f32[8,4,4096]{2,1,0:T(4,128)}, f32[8,4,4096]{2,1,0:T(4,128)S(1)}, u32[]{:S(2)}, u32[]{:S(2)}) collective-permute-start(f32[8,4,4096]{2,1,0:T(4,128)} %pad_maximum_fusion.21), channel_id=1, source_target_pairs={{0,1},{1,2},{2,3},{3,4},{4,5},{5,6},{6,7},{7,8},{8,9},{9,10},{10,1... | collective-permute-start | bytes 1572872 | tf_op jit(solution)/shard_map/ppermute | solution.py:58
  15.2 2.8 %fusion.122 = (f32[8,16,4095]{2,1,0:T(8,128)}, f32[8,16,4095]{2,1,0:T(8,128)}) fusion(f32[8,16,4096]{2,1,0:T(8,128)S(1)} %get-tuple-element.22), kind=kLoop, calls=%fused_computation.285 | loop fusion | bytes 8386560 | tf_op jit(solution)/shard_map/jit(_roll_static)/slice | solution.py:46
  31.9 5.8 %collective-permute-done.1 = f32[8,4,4096]{2,1,0:T(4,128)S(1)} collective-permute-done((f32[8,4,4096]{2,1,0:T(4,128)}, f32[8,4,4096]{2,1,0:T(4,128)S(1)}, u32[]{:S(2)}, u32[]{:S(2)}) %collective-permute-start.1) | collective-permute-done | bytes 524320 | tf_op jit(solution)/shard_map/ppermute | solution.py:58
  38.3 0.9 broadcast_select_fusion.1
  39.2 3.7 %fusion.8 = f32[8,16,4096]{2,1,0:T(8,128)S(1)} fusion(f32[8,16,4096]{2,1,0:T(8,128)S(1)} %copy-done.1, f32[8,1,4096]{2,1,0:T(1,128)S(1)} %get-tuple-element.75, f32[8,1,4096]{2,1,0:T(1,128)S(1)} %get-tuple-element.76, f32[8,16,1]{2,1,0:T(8,128)S(1)} %get-tuple-element.36, f32[8,16,4095]{2,1,0:T(8,128)} %get-tuple-element.38, ...), kind=kLoop, calls=%fused_computation.16 | loop fusion | flops 4718592 | bytes 10747904 | tf_op jit(solution)/shard_map/sub | solution.py:61
  43.7 0.9 fusion.4
  44.6 0.9 fusion.12
  46.7 2.0 copy-done.3
  49.4 2.9 %fusion.85 = f32[2,8,3,16]{3,0,2,1:T(2,128)S(1)} fusion(f32[8,3,16,258]{3,2,1,0:T(8,128)S(1)} %dynamic-slice_dynamic-update-slice_fusion, pred[258]{0:T(512)(128)(4,1)S(1)} %get-tuple-element.128, pred[258]{0:T(512)(128)(4,1)S(1)} %get-tuple-element.129, pred[258]{0:T(512)(128)(4,1)S(1)} %get-tuple-element.130, pred[258]{0:T(512)(128)(4,1)S(1)} %get-tuple-element.131, ...), kind=kOutput, calls=%fused_computation.213 | convolution fusion | flops 2383404 | bytes 400396 | tf_op jit(solution)/shard_map/mflq,qs->mfsl/dot_general | solution.py:118
  52.4 2.5 %collective-permute-start.4 = (f32[48,274]{1,0:T(8,128)S(1)}, f32[48,274]{1,0:T(8,128)S(1)}, u32[]{:S(2)}, u32[]{:S(2)}) collective-permute-start(f32[48,274]{1,0:T(8,128)S(1)} %pad_maximum_fusion.22), channel_id=1, source_target_pairs={{0,7},{1,8},{2,9},{3,10},{4,11},{5,12},{6,13},{7,14},{8,15},{9,16}... | collective-permute-start | bytes 157832 | tf_op jit(solution)/shard_map/ppermute | solution.py:142
  55.4 2.2 collective-permute-start.6
  57.6 3.9 %collective-permute-start.7 = (f32[48,274]{1,0:T(8,128)S(1)}, f32[48,274]{1,0:T(8,128)S(1)}, u32[]{:S(2)}, u32[]{:S(2)}) collective-permute-start(f32[48,274]{1,0:T(8,128)S(1)} %pad_maximum_fusion.22), channel_id=1, source_target_pairs={{0,4},{1,5},{2,6},{3,7},{4,8},{5,9},{6,10},{7,11},{8,12},{9,13},{1... | collective-permute-start | bytes 157832 | tf_op jit(solution)/shard_map/ppermute | solution.py:142
  61.4 0.8 collective-permute-start.8
  62.3 0.9 collective-permute-start.9
  63.1 2.7 %collective-permute-start.10 = (f32[48,274]{1,0:T(8,128)S(1)}, f32[48,274]{1,0:T(8,128)S(1)}, u32[]{:S(2)}, u32[]{:S(2)}) collective-permute-start(f32[48,274]{1,0:T(8,128)S(1)} %pad_maximum_fusion.22), channel_id=1, source_target_pairs={{0,1},{1,2},{2,3},{3,4},{4,5},{5,6},{6,7},{7,8},{8,9},{9,10},{10,1... | collective-permute-start | bytes 157832 | tf_op jit(solution)/shard_map/ppermute | solution.py:142
  69.1 1.7 copy.100
  72.0 2.2 collective-permute-start.11
  74.8 2.2 collective-permute-start.13
  76.9 2.0 fusion.126
  78.9 5.1 %collective-permute-start.3 = (f32[8,3,6,768]{3,0,2,1:T(8,128)}, f32[8,3,6,768]{3,0,2,1:T(8,128)}, u32[]{:S(2)}, u32[]{:S(2)}) collective-permute-start(f32[8,3,6,768]{3,0,2,1:T(8,128)} %get-tuple-element.50), channel_id=1, source_target_pairs={{1,0},{2,1},{3,2},{4,3},{5,4},{6,5},{7,6},{8,7},{9,8},{10,9},{11,1... | collective-permute-start | bytes 1327112 | tf_op jit(solution)/shard_map/ppermute | solution.py:29
  84.0 3.4 %collective-permute-start.2 = (f32[8,3,6,768]{3,0,2,1:T(8,128)S(1)}, f32[8,3,6,768]{3,0,2,1:T(8,128)}, u32[]{:S(2)}, u32[]{:S(2)}) collective-permute-start(f32[8,3,6,768]{3,0,2,1:T(8,128)S(1)} %get-tuple-element.49), channel_id=1, source_target_pairs={{0,1},{1,2},{2,3},{3,4},{4,5},{5,6},{6,7},{7,8},{8,9},{9,10},{10,1... | collective-permute-start | bytes 1327112 | tf_op jit(solution)/shard_map/ppermute | solution.py:27
  88.6 0.8 fusion.46
  90.3 0.9 slice_add_fusion
  92.3 1.6 fusion.38
  93.9 2.6 %collective-permute-done.3 = f32[8,3,6,768]{3,0,2,1:T(8,128)} collective-permute-done((f32[8,3,6,768]{3,0,2,1:T(8,128)}, f32[8,3,6,768]{3,0,2,1:T(8,128)}, u32[]{:S(2)}, u32[]{:S(2)}) %collective-permute-start.3) | collective-permute-done | bytes 442400 | tf_op jit(solution)/shard_map/ppermute | solution.py:29
  96.5 1.2 copy.104
  97.7 4.8 %collective-permute-done.2 = f32[8,3,6,768]{3,0,2,1:T(8,128)} collective-permute-done((f32[8,3,6,768]{3,0,2,1:T(8,128)S(1)}, f32[8,3,6,768]{3,0,2,1:T(8,128)}, u32[]{:S(2)}, u32[]{:S(2)}) %collective-permute-start.2) | collective-permute-done | bytes 442400 | tf_op jit(solution)/shard_map/ppermute | solution.py:27
  102.5 1.2 copy.102
  106.1 0.9 select_select_fusion.5
  108.6 0.9 select_select_fusion.1
  112.4 1.1 fusion.44
  113.9 1.3 collective-permute-start.14
  115.2 3.3 %collective-permute-start.15 = (f32[8,3,8,256]{3,1,0,2:T(4,128)S(1)}, f32[8,3,8,256]{3,1,0,2:T(4,128)S(1)}, u32[]{:S(2)}, u32[]{:S(2)}) collective-permute-start(f32[8,3,8,256]{3,1,0,2:T(4,128)S(1)} %copy_multiply_fusion), channel_id=1, source_target_pairs={{1,4},{3,5},{5,6},{7,7},{9,8},{11,9},{13,10},{15,11},{17,12},{19,1... | collective-permute-start | bytes 589832 | tf_op jit(solution)/shard_map/ppermute | solution.py:218
  133.7 1.3 collective-permute-start.16
  135.0 1.9 collective-permute-start.17
  136.9 1.3 collective-permute-start.18
  138.2 9.6 %collective-permute-start.19 = (f32[8,3,8,256]{3,1,0,2:T(4,128)S(1)}, f32[8,3,8,256]{3,1,0,2:T(4,128)S(1)}, u32[]{:S(2)}, u32[]{:S(2)}) collective-permute-start(f32[8,3,8,256]{3,1,0,2:T(4,128)S(1)} %copy_multiply_fusion), channel_id=1, source_target_pairs={{1,2},{3,3},{5,4},{7,5},{9,6},{11,7},{13,8},{15,9},{17,10},{19,11}... | collective-permute-start | bytes 589832 | tf_op jit(solution)/shard_map/ppermute | solution.py:218
  147.8 1.6 collective-permute-start.20
  149.7 2.3 collective-permute-start.21
  152.0 5.2 %collective-permute-done.17 = f32[8,3,8,256]{3,1,0,2:T(4,128)S(1)} collective-permute-done((f32[8,3,8,256]{3,1,0,2:T(4,128)S(1)}, f32[8,3,8,256]{3,1,0,2:T(4,128)S(1)}, u32[]{:S(2)}, u32[]{:S(2)}) %collective-permute-start.17) | collective-permute-done | bytes 196640 | tf_op jit(solution)/shard_map/ppermute | solution.py:218
  157.2 1.3 collective-permute-start.22
  158.6 1.9 collective-permute-start.23
  161.2 20.0 %collective-permute-done.21 = f32[8,3,8,256]{3,1,0,2:T(4,128)S(1)} collective-permute-done((f32[8,3,8,256]{3,1,0,2:T(4,128)S(1)}, f32[8,3,8,256]{3,1,0,2:T(4,128)S(1)}, u32[]{:S(2)}, u32[]{:S(2)}) %collective-permute-start.21) | collective-permute-done | bytes 196640 | tf_op jit(solution)/shard_map/ppermute | solution.py:218
  181.3 5.6 %collective-permute-done.23 = f32[8,3,8,256]{3,1,0,2:T(4,128)S(1)} collective-permute-done((f32[8,3,8,256]{3,1,0,2:T(4,128)S(1)}, f32[8,3,8,256]{3,1,0,2:T(4,128)S(1)}, u32[]{:S(2)}, u32[]{:S(2)}) %collective-permute-start.23) | collective-permute-done | bytes 196640 | tf_op jit(solution)/shard_map/ppermute | solution.py:218
  187.0 1.5 copy-done.6
  188.4 2.6 %gather_fusion = f32[8,3,16,256]{3,1,2,0:T(4,128)S(1)} fusion(f32[8,3,80,256]{3,1,0,2:T(4,128)} %copy-done.6, s32[8]{0:T(128)S(1)} %copy-done.9), kind=kCustom, calls=%fused_computation | custom fusion | bytes 786560 | tf_op jit(solution)/shard_map/vmap()/gather | solution.py:221
  191.2 1.6 collective-permute-start.24
  192.8 1.9 collective-permute-start.25
  194.7 1.9 collective-permute-start.26
  196.8 5.6 %collective-permute-done.24 = f32[8,3,16,256]{3,2,1,0:T(8,128)S(1)} collective-permute-done((f32[8,3,16,256]{3,2,1,0:T(8,128)S(1)}, f32[8,3,16,256]{3,2,1,0:T(8,128)S(1)}, u32[]{:S(2)}, u32[]{:S(2)}) %collective-permute-start.24) | collective-permute-done | bytes 393248 | tf_op jit(solution)/shard_map/ppermute | solution.py:224
  202.3 6.7 %collective-permute-done.25 = f32[8,3,16,256]{3,2,1,0:T(8,128)S(1)} collective-permute-done((f32[8,3,16,256]{3,2,1,0:T(8,128)S(1)}, f32[8,3,16,256]{3,2,1,0:T(8,128)S(1)}, u32[]{:S(2)}, u32[]{:S(2)}) %collective-permute-start.25) | collective-permute-done | bytes 393248 | tf_op jit(solution)/shard_map/ppermute | solution.py:224
  209.0 11.9 %collective-permute-done.26 = f32[8,3,16,256]{3,2,1,0:T(8,128)S(1)} collective-permute-done((f32[8,3,16,256]{3,2,1,0:T(8,128)S(1)}, f32[8,3,16,256]{3,2,1,0:T(8,128)S(1)}, u32[]{:S(2)}, u32[]{:S(2)}) %collective-permute-start.26) | collective-permute-done | bytes 393248 | tf_op jit(solution)/shard_map/ppermute | solution.py:224
  221.2 1.9 dynamic_update_slice.24
  223.1 1.9 dynamic_update_slice.25
  225.0 1.9 dynamic_update_slice.26
  226.9 1.9 dynamic_update_slice.27
  228.8 1.9 dynamic_update_slice.28
  230.7 1.9 dynamic_update_slice.29
  232.6 1.9 dynamic_update_slice.30
  234.5 1.9 dynamic_update_slice.31
  (184 shorter events, 25.2 us)
Async XLA Ops:
  3.9 6.3 %copy-start = (f32[8,16,4096]{2,1,0:T(8,128)}, f32[8,16,4096]{2,1,0:T(8,128)S(1)}, u32[]{:S(2)}) copy-start(f32[8,16,4096]{2,1,0:T(8,128)S(1)} %get-tuple-element.23) | copy-start | bytes 6291460
  5.8 25.7 %collective-permute-start = (f32[8,4,4096]{2,1,0:T(4,128)}, f32[8,4,4096]{2,1,0:T(4,128)S(1)}, u32[]{:S(2)}, u32[]{:S(2)}) collective-permute-start(f32[8,4,4096]{2,1,0:T(4,128)} %pad_maximum_fusion.20), channel_id=1, source_target_pairs={{1,0},{2,1},{3,2},{4,3},{5,4},{6,5},{7,6},{8,7},{9,8},{10,9},{11,1... | collective-permute-start | bytes 1572872 | tf_op jit(solution)/shard_map/ppermute | solution.py:59
  10.2 27.4 %collective-permute-start.1 = (f32[8,4,4096]{2,1,0:T(4,128)}, f32[8,4,4096]{2,1,0:T(4,128)S(1)}, u32[]{:S(2)}, u32[]{:S(2)}) collective-permute-start(f32[8,4,4096]{2,1,0:T(4,128)} %pad_maximum_fusion.21), channel_id=1, source_target_pairs={{0,1},{1,2},{2,3},{3,4},{4,5},{5,6},{6,7},{7,8},{8,9},{9,10},{10,1... | collective-permute-start | bytes 1572872 | tf_op jit(solution)/shard_map/ppermute | solution.py:58
  15.2 2.8 %copy-start.10 = (s32[8,2]{0,1:T(2,128)S(1)}, s32[8,2]{0,1:T(2,128)}, u32[]{:S(2)}) copy-start(s32[8,2]{0,1:T(2,128)} %param.5) | copy-start | bytes 196
  29.3 9.9 %copy-start.15 = (s32[8]{0:T(128)}, s32[8]{0:T(128)S(1)}, u32[]{:S(2)}) copy-start(s32[8]{0:T(128)S(1)} %get-tuple-element.107) | copy-start | bytes 100
  30.6 7.7 %copy-start.1 = (f32[8,16,4096]{2,1,0:T(8,128)S(1)}, f32[8,16,4096]{2,1,0:T(8,128)}, u32[]{:S(2)}) copy-start(f32[8,16,4096]{2,1,0:T(8,128)} %copy-done) | copy-start | bytes 6291460
  31.2 7.9 %copy-start.20 = (s32[16]{0:T(128)}, s32[16]{0:T(128)S(1)}, u32[]{:S(2)}) copy-start(s32[16]{0:T(128)S(1)} %iota_add_fusion.2) | copy-start | bytes 196
  31.7 7.5 %copy-start.2 = (f32[8,16,4095]{2,1,0:T(8,128)S(1)}, f32[8,16,4095]{2,1,0:T(8,128)}, u32[]{:S(2)}) copy-start(f32[8,16,4095]{2,1,0:T(8,128)} %get-tuple-element.37) | copy-start | bytes 6289924
  38.3 5.5 %slice-start = ((s8[6291456]{0:T(1024)(128)(4,1)}), s8[4194304]{0:T(1024)(128)(4,1)S(1)}, s32[]{:S(2)}) async-start(s8[6291456]{0:T(1024)(128)(4,1)} %bitcast.177), calls=%async_computation | async-start | bytes 8388608
  39.2 4.6 %slice-start.1 = ((s8[6291456]{0:T(1024)(128)(4,1)}), s8[2097152]{0:T(1024)(128)(4,1)S(1)}, s32[]{:S(2)}) async-start(s8[6291456]{0:T(1024)(128)(4,1)} %bitcast.177), calls=%async_computation.1 | async-start | bytes 4194304
  46.0 2.7 %copy-start.3 = (f32[8,3,16,4096]{3,2,1,0:T(8,128)}, f32[8,3,16,4096]{3,2,1,0:T(8,128)S(1)}, u32[]{:S(2)}) copy-start(f32[8,3,16,4096]{3,2,1,0:T(8,128)S(1)} %pad_maximum_fusion) | copy-start | bytes 18874372
  46.0 23.1 %copy-start.4 = (f32[8,3,24,768]{3,2,1,0:T(8,128)S(1)}, f32[8,3,24,768]{3,2,1,0:T(8,128)}, u32[]{:S(2)}) copy-start(f32[8,3,24,768]{3,2,1,0:T(8,128)} %param.4) | copy-start | bytes 5308420
  52.4 9.9 %collective-permute-start.4 = (f32[48,274]{1,0:T(8,128)S(1)}, f32[48,274]{1,0:T(8,128)S(1)}, u32[]{:S(2)}, u32[]{:S(2)}) collective-permute-start(f32[48,274]{1,0:T(8,128)S(1)} %pad_maximum_fusion.22), channel_id=1, source_target_pairs={{0,7},{1,8},{2,9},{3,10},{4,11},{5,12},{6,13},{7,14},{8,15},{9,16}... | collective-permute-start | bytes 157832 | tf_op jit(solution)/shard_map/ppermute | solution.py:142
  54.8 8.3 %collective-permute-start.5 = (f32[48,274]{1,0:T(8,128)S(1)}, f32[48,274]{1,0:T(8,128)S(1)}, u32[]{:S(2)}, u32[]{:S(2)}) collective-permute-start(f32[48,274]{1,0:T(8,128)S(1)} %pad_maximum_fusion.22), channel_id=1, source_target_pairs={{0,6},{1,7},{2,8},{3,9},{4,10},{5,11},{6,12},{7,13},{8,14},{9,15},... | collective-permute-start | bytes 157832 | tf_op jit(solution)/shard_map/ppermute | solution.py:142
  55.4 15.5 %collective-permute-start.6 = (f32[48,274]{1,0:T(8,128)S(1)}, f32[48,274]{1,0:T(8,128)S(1)}, u32[]{:S(2)}, u32[]{:S(2)}) collective-permute-start(f32[48,274]{1,0:T(8,128)S(1)} %pad_maximum_fusion.22), channel_id=1, source_target_pairs={{0,5},{1,6},{2,7},{3,8},{4,9},{5,10},{6,11},{7,12},{8,13},{9,14},{... | collective-permute-start | bytes 157832 | tf_op jit(solution)/shard_map/ppermute | solution.py:142
  57.6 13.3 %collective-permute-start.7 = (f32[48,274]{1,0:T(8,128)S(1)}, f32[48,274]{1,0:T(8,128)S(1)}, u32[]{:S(2)}, u32[]{:S(2)}) collective-permute-start(f32[48,274]{1,0:T(8,128)S(1)} %pad_maximum_fusion.22), channel_id=1, source_target_pairs={{0,4},{1,5},{2,6},{3,7},{4,8},{5,9},{6,10},{7,11},{8,12},{9,13},{1... | collective-permute-start | bytes 157832 | tf_op jit(solution)/shard_map/ppermute | solution.py:142
  61.4 9.5 %collective-permute-start.8 = (f32[48,274]{1,0:T(8,128)S(1)}, f32[48,274]{1,0:T(8,128)S(1)}, u32[]{:S(2)}, u32[]{:S(2)}) collective-permute-start(f32[48,274]{1,0:T(8,128)S(1)} %pad_maximum_fusion.22), channel_id=1, source_target_pairs={{0,3},{1,4},{2,5},{3,6},{4,7},{5,8},{6,9},{7,10},{8,11},{9,12},{10... | collective-permute-start | bytes 157832 | tf_op jit(solution)/shard_map/ppermute | solution.py:142
  62.3 8.7 %collective-permute-start.9 = (f32[48,274]{1,0:T(8,128)S(1)}, f32[48,274]{1,0:T(8,128)S(1)}, u32[]{:S(2)}, u32[]{:S(2)}) collective-permute-start(f32[48,274]{1,0:T(8,128)S(1)} %pad_maximum_fusion.22), channel_id=1, source_target_pairs={{0,2},{1,3},{2,4},{3,5},{4,6},{5,7},{6,8},{7,9},{8,10},{9,11},{10,... | collective-permute-start | bytes 157832 | tf_op jit(solution)/shard_map/ppermute | solution.py:142
  63.1 7.8 %collective-permute-start.10 = (f32[48,274]{1,0:T(8,128)S(1)}, f32[48,274]{1,0:T(8,128)S(1)}, u32[]{:S(2)}, u32[]{:S(2)}) collective-permute-start(f32[48,274]{1,0:T(8,128)S(1)} %pad_maximum_fusion.22), channel_id=1, source_target_pairs={{0,1},{1,2},{2,3},{3,4},{4,5},{5,6},{6,7},{7,8},{8,9},{9,10},{10,1... | collective-permute-start | bytes 157832 | tf_op jit(solution)/shard_map/ppermute | solution.py:142
  70.9 17.6 %copy-start.17 = (s32[8,36]{1,0:T(8,128)S(1)}, s32[8,36]{1,0:T(8,128)}, u32[]{:S(2)}) copy-start(s32[8,36]{1,0:T(8,128)} %get-tuple-element.108) | copy-start | bytes 3460
  70.9 17.6 %copy-start.18 = (s32[8,36]{1,0:T(8,128)S(1)}, s32[8,36]{1,0:T(8,128)}, u32[]{:S(2)}) copy-start(s32[8,36]{1,0:T(8,128)} %get-tuple-element.109) | copy-start | bytes 3460
  70.9 17.6 %copy-start.19 = (s32[512]{0:T(512)S(1)}, s32[512]{0:T(512)}, u32[]{:S(2)}) copy-start(s32[512]{0:T(512)} %add_select_fusion.3) | copy-start | bytes 6148
  72.0 15.6 %collective-permute-start.11 = (f32[48,386]{1,0:T(8,128)}, f32[48,386]{1,0:T(8,128)S(1)}, u32[]{:S(2)}, u32[]{:S(2)}) collective-permute-start(f32[48,386]{1,0:T(8,128)} %concatenate.252), channel_id=1, source_target_pairs={{0,24},{1,25},{2,26},{3,27},{4,28},{5,29},{6,30},{7,31},{8,0},{9,1... | collective-permute-start | bytes 222344 | tf_op jit(solution)/shard_map/ppermute | solution.py:142
  74.1 13.4 %collective-permute-start.12 = (f32[48,386]{1,0:T(8,128)}, f32[48,386]{1,0:T(8,128)S(1)}, u32[]{:S(2)}, u32[]{:S(2)}) collective-permute-start(f32[48,386]{1,0:T(8,128)} %concatenate.252), channel_id=1, source_target_pairs={{0,16},{1,17},{2,18},{3,19},{4,20},{5,21},{6,22},{7,23},{8,24},{9,... | collective-permute-start | bytes 222344 | tf_op jit(solution)/shard_map/ppermute | solution.py:142
  74.8 12.9 %collective-permute-start.13 = (f32[48,386]{1,0:T(8,128)}, f32[48,386]{1,0:T(8,128)S(1)}, u32[]{:S(2)}, u32[]{:S(2)}) collective-permute-start(f32[48,386]{1,0:T(8,128)} %concatenate.252), channel_id=1, source_target_pairs={{0,8},{1,9},{2,10},{3,11},{4,12},{5,13},{6,14},{7,15},{8,16},{9,17... | collective-permute-start | bytes 222344 | tf_op jit(solution)/shard_map/ppermute | solution.py:142
  78.9 17.6 %collective-permute-start.3 = (f32[8,3,6,768]{3,0,2,1:T(8,128)}, f32[8,3,6,768]{3,0,2,1:T(8,128)}, u32[]{:S(2)}, u32[]{:S(2)}) collective-permute-start(f32[8,3,6,768]{3,0,2,1:T(8,128)} %get-tuple-element.50), channel_id=1, source_target_pairs={{1,0},{2,1},{3,2},{4,3},{5,4},{6,5},{7,6},{8,7},{9,8},{10,9},{11,1... | collective-permute-start | bytes 1327112 | tf_op jit(solution)/shard_map/ppermute | solution.py:29
  84.0 18.5 %collective-permute-start.2 = (f32[8,3,6,768]{3,0,2,1:T(8,128)S(1)}, f32[8,3,6,768]{3,0,2,1:T(8,128)}, u32[]{:S(2)}, u32[]{:S(2)}) collective-permute-start(f32[8,3,6,768]{3,0,2,1:T(8,128)S(1)} %get-tuple-element.49), channel_id=1, source_target_pairs={{0,1},{1,2},{2,3},{3,4},{4,5},{5,6},{6,7},{7,8},{8,9},{9,10},{10,1... | collective-permute-start | bytes 1327112 | tf_op jit(solution)/shard_map/ppermute | solution.py:27
  87.6 0.6 copy-start.7
  87.6 0.6 copy-start.8
  103.6 0.7 copy-start.12
  103.6 0.7 copy-start.13
  111.7 0.7 copy-start.14
  112.4 1.3 copy-start.5
  112.4 6.1 %copy-start.11 = (s32[8,2]{0,1:T(2,128)S(1)}, s32[8,2]{0,1:T(2,128)}, u32[]{:S(2)}) copy-start(s32[8,2]{0,1:T(2,128)} %param.5) | copy-start | bytes 196
  113.9 24.3 %collective-permute-start.14 = (f32[8,3,8,256]{3,1,0,2:T(4,128)S(1)}, f32[8,3,8,256]{3,1,0,2:T(4,128)S(1)}, u32[]{:S(2)}, u32[]{:S(2)}) collective-permute-start(f32[8,3,8,256]{3,1,0,2:T(4,128)S(1)} %copy_multiply_fusion), channel_id=1, source_target_pairs={{0,4},{2,5},{4,6},{6,7},{8,8},{10,9},{12,10},{14,11},{16,12},{18,1... | collective-permute-start | bytes 589832 | tf_op jit(solution)/shard_map/ppermute | solution.py:218
  115.2 32.6 %collective-permute-start.15 = (f32[8,3,8,256]{3,1,0,2:T(4,128)S(1)}, f32[8,3,8,256]{3,1,0,2:T(4,128)S(1)}, u32[]{:S(2)}, u32[]{:S(2)}) collective-permute-start(f32[8,3,8,256]{3,1,0,2:T(4,128)S(1)} %copy_multiply_fusion), channel_id=1, source_target_pairs={{1,4},{3,5},{5,6},{7,7},{9,8},{11,9},{13,10},{15,11},{17,12},{19,1... | collective-permute-start | bytes 589832 | tf_op jit(solution)/shard_map/ppermute | solution.py:218
  133.7 16.0 %collective-permute-start.16 = (f32[8,3,8,256]{3,1,0,2:T(4,128)S(1)}, f32[8,3,8,256]{3,1,0,2:T(4,128)S(1)}, u32[]{:S(2)}, u32[]{:S(2)}) collective-permute-start(f32[8,3,8,256]{3,1,0,2:T(4,128)S(1)} %copy_multiply_fusion), channel_id=1, source_target_pairs={{0,3},{2,4},{4,5},{6,6},{8,7},{10,8},{12,9},{14,10},{16,11},{18,12... | collective-permute-start | bytes 589832 | tf_op jit(solution)/shard_map/ppermute | solution.py:218
  135.0 22.3 %collective-permute-start.17 = (f32[8,3,8,256]{3,1,0,2:T(4,128)S(1)}, f32[8,3,8,256]{3,1,0,2:T(4,128)S(1)}, u32[]{:S(2)}, u32[]{:S(2)}) collective-permute-start(f32[8,3,8,256]{3,1,0,2:T(4,128)S(1)} %copy_multiply_fusion), channel_id=1, source_target_pairs={{1,3},{3,4},{5,5},{7,6},{9,7},{11,8},{13,9},{15,10},{17,11},{19,12... | collective-permute-start | bytes 589832 | tf_op jit(solution)/shard_map/ppermute | solution.py:218
  136.9 21.7 %collective-permute-start.18 = (f32[8,3,8,256]{3,1,0,2:T(4,128)S(1)}, f32[8,3,8,256]{3,1,0,2:T(4,128)S(1)}, u32[]{:S(2)}, u32[]{:S(2)}) collective-permute-start(f32[8,3,8,256]{3,1,0,2:T(4,128)S(1)} %copy_multiply_fusion), channel_id=1, source_target_pairs={{0,2},{2,3},{4,4},{6,5},{8,6},{10,7},{12,8},{14,9},{16,10},{18,11}... | collective-permute-start | bytes 589832 | tf_op jit(solution)/shard_map/ppermute | solution.py:218
  138.2 22.7 %collective-permute-start.19 = (f32[8,3,8,256]{3,1,0,2:T(4,128)S(1)}, f32[8,3,8,256]{3,1,0,2:T(4,128)S(1)}, u32[]{:S(2)}, u32[]{:S(2)}) collective-permute-start(f32[8,3,8,256]{3,1,0,2:T(4,128)S(1)} %copy_multiply_fusion), channel_id=1, source_target_pairs={{1,2},{3,3},{5,4},{7,5},{9,6},{11,7},{13,8},{15,9},{17,10},{19,11}... | collective-permute-start | bytes 589832 | tf_op jit(solution)/shard_map/ppermute | solution.py:218
  147.8 13.3 %collective-permute-start.20 = (f32[8,3,8,256]{3,1,0,2:T(4,128)S(1)}, f32[8,3,8,256]{3,1,0,2:T(4,128)S(1)}, u32[]{:S(2)}, u32[]{:S(2)}) collective-permute-start(f32[8,3,8,256]{3,1,0,2:T(4,128)S(1)} %copy_multiply_fusion), channel_id=1, source_target_pairs={{0,1},{2,2},{4,3},{6,4},{8,5},{10,6},{12,7},{14,8},{16,9},{18,10},... | collective-permute-start | bytes 589832 | tf_op jit(solution)/shard_map/ppermute | solution.py:218
  149.5 39.0 %copy-start.9 = (s32[8]{0:T(128)S(1)}, s32[8]{0:T(128)}, u32[]{:S(2)}) copy-start(s32[8]{0:T(128)} %get-tuple-element.103) | copy-start | bytes 100
  149.7 31.5 %collective-permute-start.21 = (f32[8,3,8,256]{3,1,0,2:T(4,128)S(1)}, f32[8,3,8,256]{3,1,0,2:T(4,128)S(1)}, u32[]{:S(2)}, u32[]{:S(2)}) collective-permute-start(f32[8,3,8,256]{3,1,0,2:T(4,128)S(1)} %copy_multiply_fusion), channel_id=1, source_target_pairs={{1,1},{3,2},{5,3},{7,4},{9,5},{11,6},{13,7},{15,8},{17,9},{19,10},... | collective-permute-start | bytes 589832 | tf_op jit(solution)/shard_map/ppermute | solution.py:218
  157.2 24.1 %collective-permute-start.22 = (f32[8,3,8,256]{3,1,0,2:T(4,128)S(1)}, f32[8,3,8,256]{3,1,0,2:T(4,128)S(1)}, u32[]{:S(2)}, u32[]{:S(2)}) collective-permute-start(f32[8,3,8,256]{3,1,0,2:T(4,128)S(1)} %copy_multiply_fusion), channel_id=1, source_target_pairs={{0,0},{2,1},{4,2},{6,3},{8,4},{10,5},{12,6},{14,7},{16,8},{18,9},{... | collective-permute-start | bytes 589832 | tf_op jit(solution)/shard_map/ppermute | solution.py:218
  158.6 28.3 %collective-permute-start.23 = (f32[8,3,8,256]{3,1,0,2:T(4,128)S(1)}, f32[8,3,8,256]{3,1,0,2:T(4,128)S(1)}, u32[]{:S(2)}, u32[]{:S(2)}) collective-permute-start(f32[8,3,8,256]{3,1,0,2:T(4,128)S(1)} %copy_multiply_fusion), channel_id=1, source_target_pairs={{1,0},{3,1},{5,2},{7,3},{9,4},{11,5},{13,6},{15,7},{17,8},{19,9},{... | collective-permute-start | bytes 589832 | tf_op jit(solution)/shard_map/ppermute | solution.py:218
  160.6 36.1 %copy-start.16 = (s32[8]{0:T(128)S(1)}, s32[8]{0:T(128)}, u32[]{:S(2)}) copy-start(s32[8]{0:T(128)} %copy-done.15) | copy-start | bytes 100
  160.6 36.1 %copy-start.21 = (s32[16]{0:T(128)S(1)}, s32[16]{0:T(128)}, u32[]{:S(2)}) copy-start(s32[16]{0:T(128)} %copy-done.20) | copy-start | bytes 196
  187.0 1.5 copy-start.6
  191.2 11.2 %collective-permute-start.24 = (f32[8,3,16,256]{3,2,1,0:T(8,128)S(1)}, f32[8,3,16,256]{3,2,1,0:T(8,128)S(1)}, u32[]{:S(2)}, u32[]{:S(2)}) collective-permute-start(f32[8,3,16,256]{3,2,1,0:T(8,128)S(1)} %copy.133), channel_id=1, source_target_pairs={{0,12},{1,13},{2,14},{3,15},{4,16},{5,17},{6,18},{7,19},{8,20},{9,... | collective-permute-start | bytes 1179656 | tf_op jit(solution)/shard_map/ppermute | solution.py:224
  192.8 16.2 %collective-permute-start.25 = (f32[8,3,16,256]{3,2,1,0:T(8,128)S(1)}, f32[8,3,16,256]{3,2,1,0:T(8,128)S(1)}, u32[]{:S(2)}, u32[]{:S(2)}) collective-permute-start(f32[8,3,16,256]{3,2,1,0:T(8,128)S(1)} %copy.133), channel_id=1, source_target_pairs={{0,8},{1,9},{2,10},{3,11},{4,12},{5,13},{6,14},{7,15},{8,16},{9,17... | collective-permute-start | bytes 1179656 | tf_op jit(solution)/shard_map/ppermute | solution.py:224
  194.7 26.1 %collective-permute-start.26 = (f32[8,3,16,256]{3,2,1,0:T(8,128)S(1)}, f32[8,3,16,256]{3,2,1,0:T(8,128)S(1)}, u32[]{:S(2)}, u32[]{:S(2)}) collective-permute-start(f32[8,3,16,256]{3,2,1,0:T(8,128)S(1)} %copy.133), channel_id=1, source_target_pairs={{0,4},{1,5},{2,6},{3,7},{4,8},{5,9},{6,10},{7,11},{8,12},{9,13},{1... | collective-permute-start | bytes 1179656 | tf_op jit(solution)/shard_map/ppermute | solution.py:224

commit v6 on v5

--- a/solution.py
+++ b/solution.py
@@ -206,23 +206,26 @@
     col_sums = jnp.einsum("mfrj,jp->mfrp", nest, block_cols, precision=highest)
     coarse = col_sums.reshape(members, 3, tile_coarse, 3, span).sum(axis=3) / 9.0
 
-    radix = 4
-    band_shift = rows_off // band_rows
-    sub_shift = rows_off % band_rows
-    low_digit = band_shift % radix
-    high_digit = band_shift // radix
-    lowest = -2 * (radix - 1) - 2
-    fetched = []
-    for k in range(lowest, 2):
-        pairs = [(2 * p + k, p) for p in range(bands) if 0 <= 2 * p + k < bands]
-        fetched.append(lax.ppermute(coarse, "band", pairs))
-    stacked = jnp.concatenate(fetched, axis=2)
-    lead = (-lowest) * tile_coarse - band_rows * low_digit - sub_shift
-    near = jax.vmap(lambda blk, e: lax.dynamic_slice_in_dim(blk, e, band_rows, axis=1))(stacked, lead)
-    patch = near
-    for j in range(1, radix):
-        recv = lax.ppermute(near, "band", shift_pairs(bands, j * radix))
-        patch = jnp.where((high_digit == j)[:, None, None, None], recv, patch)
+    shift = (rows_off + tile_coarse - 1) // tile_coarse - 1
+    moved = coarse
+    step = 1
+    while step < bands:
+        recv = lax.ppermute(moved, "band", [(i, (i + step) % bands) for i in range(bands)])
+        take = ((shift // step) % 2 == 1)[:, None, None, None]
+        moved = jnp.where(take, recv, moved)
+        step *= 2
+    half = bands // 2
+    low_half = band_index < half
+    pieces = []
+    for i in range(3):
+        got = []
+        for h in range(2):
+            pairs = [((2 * p - 1 + i) % bands, p) for p in range(h * half, (h + 1) * half)]
+            got.append(lax.ppermute(moved, "band", pairs))
+        pieces.append(jnp.where(low_half, got[0], got[1]))
+    near = jnp.concatenate(pieces, axis=2)
+    lead = tile_coarse * (shift + 1) - rows_off
+    patch = jax.vmap(lambda blk, e: lax.dynamic_slice_in_dim(blk, e, band_rows, axis=1))(near, lead)
 
     relative_rows = global_rows[None, :] - rows_off[:, None]
     covered = (relative_rows >= 0) & (relative_rows < span)

time: 238 us -> 220 us (0.924)
  the two profiles are of different devices: /device:TPU:14 before, /device:TPU:112 now
where the time goes in v6:
time: 220 us; the launch traced here: 219 us
  starting transfers between devices  61.1 us (28%)
  waiting for transfers between devices  59.3 us (27%)
  local copies, waits for them, and re-layouts  44.1 us (20%)
  between operations  26.4 us (12%)
  other arithmetic  21.1 us (10%)
  matrix products  6.81 us (3%)
    ppermute x5, waiting for transfers between devices, per_device(): lax.ppermute(moved, 'band', [(i, (i + step) % bands) for i in range(bands)])  30 us
    ppermute x10, starting transfers between devices, per_device(): lax.ppermute(payload, 'band', [(i, (i + k * reach) % bands) for i in rang...  20.1 us
    ppermute x6, waiting for transfers between devices, per_device(): got.append(lax.ppermute(moved, 'band', pairs))  18.6 us
    ppermute x6, starting transfers between devices, per_device(): got.append(lax.ppermute(moved, 'band', pairs))  16.3 us
    dynamic_update_slice x8, local copies, waits for them, and re-layouts, per_device(): lax.dynamic_update_slice(parent_out, merged[m:m + 1], (m, 0, 0, cols_off[...  15.2 us
    ppermute x5, starting transfers between devices, per_device(): lax.ppermute(moved, 'band', [(i, (i + step) % bands) for i in range(bands)])  9.89 us
    ppermute x1, waiting for transfers between devices, with_halo(): lax.ppermute(tail, 'band', shift_pairs(count, 1))  5.3 us
    ppermute x1, starting transfers between devices, parent_step(): next_ = lax.ppermute(head, 'band', shift_pairs(count, -1))  4.76 us
  transfers between devices with their start and end apart: 25, of which 10 were waited for; matrix products, arithmetic and copies ran while one was open for 10% of the time, Pallas kernels for 0%

profile of v6, /device:TPU:112, one launch (start us, length us, event | category | flops | bytes accessed | tf_op | source)
XLA Modules:
  0.0 218.9 jit_solution(13803837341232962443)
XLA Ops:
  0.6 3.3 %slice_bitcast_fusion.4 = (f32[8,16,4096]{2,1,0:T(8,128)S(1)}, f32[8,16,4096]{2,1,0:T(8,128)S(1)}, f32[8,16,4096]{2,1,0:T(8,128)S(1)}) fusion(f32[8,3,16,4096]{3,2,1,0:T(8,128)} %param.3), kind=kLoop, calls=%fused_computation.28 | loop fusion | bytes 12582912 | tf_op jit(solution)/shard_map/squeeze | solution.py:50
  4.6 1.1 pad_maximum_fusion.21
  5.8 4.8 %collective-permute-start = (f32[8,4,4096]{2,1,0:T(4,128)}, f32[8,4,4096]{2,1,0:T(4,128)S(1)}, u32[]{:S(2)}, u32[]{:S(2)}) collective-permute-start(f32[8,4,4096]{2,1,0:T(4,128)} %pad_maximum_fusion.21), channel_id=1, source_target_pairs={{1,0},{2,1},{3,2},{4,3},{5,4},{6,5},{7,6},{8,7},{9,8},{10,9},{11,1... | collective-permute-start | bytes 1572872 | tf_op jit(solution)/shard_map/ppermute | solution.py:59
  10.5 1.1 pad_maximum_fusion.22
  11.7 2.6 %collective-permute-start.1 = (f32[8,4,4096]{2,1,0:T(4,128)}, f32[8,4,4096]{2,1,0:T(4,128)S(1)}, u32[]{:S(2)}, u32[]{:S(2)}) collective-permute-start(f32[8,4,4096]{2,1,0:T(4,128)} %pad_maximum_fusion.22), channel_id=1, source_target_pairs={{0,1},{1,2},{2,3},{3,4},{4,5},{5,6},{6,7},{7,8},{8,9},{9,10},{10,1... | collective-permute-start | bytes 1572872 | tf_op jit(solution)/shard_map/ppermute | solution.py:58
  14.3 2.7 %fusion.129 = (f32[8,16,4095]{2,1,0:T(8,128)}, f32[8,16,4095]{2,1,0:T(8,128)}) fusion(f32[8,16,4096]{2,1,0:T(8,128)S(1)} %get-tuple-element.22), kind=kLoop, calls=%fused_computation.307 | loop fusion | bytes 8386560 | tf_op jit(solution)/shard_map/jit(_roll_static)/slice | solution.py:46
  17.0 0.7 fusion.148
  30.0 0.7 broadcast_add_fusion.1
  31.3 2.8 %collective-permute-done.1 = f32[8,4,4096]{2,1,0:T(4,128)S(1)} collective-permute-done((f32[8,4,4096]{2,1,0:T(4,128)}, f32[8,4,4096]{2,1,0:T(4,128)S(1)}, u32[]{:S(2)}, u32[]{:S(2)}) %collective-permute-start.1) | collective-permute-done | bytes 524320 | tf_op jit(solution)/shard_map/ppermute | solution.py:58
  34.7 0.9 broadcast_select_fusion.1
  35.6 3.7 %fusion.8 = f32[8,16,4096]{2,1,0:T(8,128)S(1)} fusion(f32[8,16,4096]{2,1,0:T(8,128)S(1)} %copy-done.1, f32[8,1,4096]{2,1,0:T(1,128)S(1)} %get-tuple-element.75, f32[8,1,4096]{2,1,0:T(1,128)S(1)} %get-tuple-element.76, f32[8,16,1]{2,1,0:T(8,128)S(1)} %get-tuple-element.36, f32[8,16,4095]{2,1,0:T(8,128)} %get-tuple-element.38, ...), kind=kLoop, calls=%fused_computation.16 | loop fusion | flops 4718592 | bytes 10747904 | tf_op jit(solution)/shard_map/sub | solution.py:61
  39.4 0.7 slice_bitcast_fusion
  40.2 0.9 fusion.4
  41.1 0.9 fusion.12
  43.2 2.0 copy-done.3
  45.9 2.9 %fusion.85 = f32[2,8,3,16]{3,0,2,1:T(2,128)S(1)} fusion(f32[8,3,16,258]{3,2,1,0:T(8,128)S(1)} %dynamic-slice_dynamic-update-slice_fusion, pred[258]{0:T(512)(128)(4,1)S(1)} %get-tuple-element.130, pred[258]{0:T(512)(128)(4,1)S(1)} %get-tuple-element.131, pred[258]{0:T(512)(128)(4,1)S(1)} %get-tuple-element.132, pred[258]{0:T(512)(128)(4,1)S(1)} %get-tuple-element.133, ...), kind=kOutput, calls=%fused_computation.212 | convolution fusion | flops 2383404 | bytes 400396 | tf_op jit(solution)/shard_map/mflq,qs->mfsl/dot_general | solution.py:118
  48.8 3.4 %collective-permute-start.4 = (f32[48,274]{1,0:T(8,128)S(1)}, f32[48,274]{1,0:T(8,128)S(1)}, u32[]{:S(2)}, u32[]{:S(2)}) collective-permute-start(f32[48,274]{1,0:T(8,128)S(1)} %pad_maximum_fusion.23), channel_id=1, source_target_pairs={{0,7},{1,8},{2,9},{3,10},{4,11},{5,12},{6,13},{7,14},{8,15},{9,16}... | collective-permute-start | bytes 157832 | tf_op jit(solution)/shard_map/ppermute | solution.py:142
  52.2 5.5 %collective-permute-start.6 = (f32[48,274]{1,0:T(8,128)S(1)}, f32[48,274]{1,0:T(8,128)S(1)}, u32[]{:S(2)}, u32[]{:S(2)}) collective-permute-start(f32[48,274]{1,0:T(8,128)S(1)} %pad_maximum_fusion.23), channel_id=1, source_target_pairs={{0,5},{1,6},{2,7},{3,8},{4,9},{5,10},{6,11},{7,12},{8,13},{9,14},{... | collective-permute-start | bytes 157832 | tf_op jit(solution)/shard_map/ppermute | solution.py:142
  57.7 5.2 %collective-permute-start.8 = (f32[48,274]{1,0:T(8,128)S(1)}, f32[48,274]{1,0:T(8,128)S(1)}, u32[]{:S(2)}, u32[]{:S(2)}) collective-permute-start(f32[48,274]{1,0:T(8,128)S(1)} %pad_maximum_fusion.23), channel_id=1, source_target_pairs={{0,3},{1,4},{2,5},{3,6},{4,7},{5,8},{6,9},{7,10},{8,11},{9,12},{10... | collective-permute-start | bytes 157832 | tf_op jit(solution)/shard_map/ppermute | solution.py:142
  62.9 1.8 collective-permute-start.9
  65.8 0.7 slice.592
  66.5 0.7 slice.591
  68.5 1.7 copy.94
  70.3 1.1 collective-permute-done.10
  71.6 0.8 concatenate.252
  72.8 3.2 %collective-permute-start.12 = (f32[48,386]{1,0:T(8,128)}, f32[48,386]{1,0:T(8,128)S(1)}, u32[]{:S(2)}, u32[]{:S(2)}) collective-permute-start(f32[48,386]{1,0:T(8,128)} %concatenate.252), channel_id=1, source_target_pairs={{0,16},{1,17},{2,18},{3,19},{4,20},{5,21},{6,22},{7,23},{8,24},{9,... | collective-permute-start | bytes 222344 | tf_op jit(solution)/shard_map/ppermute | solution.py:142
  76.0 2.0 fusion.133
  78.0 4.6 %collective-permute-start.3 = (f32[8,3,6,768]{3,0,2,1:T(8,128)}, f32[8,3,6,768]{3,0,2,1:T(8,128)}, u32[]{:S(2)}, u32[]{:S(2)}) collective-permute-start(f32[8,3,6,768]{3,0,2,1:T(8,128)} %get-tuple-element.50), channel_id=1, source_target_pairs={{1,0},{2,1},{3,2},{4,3},{5,4},{6,5},{7,6},{8,7},{9,8},{10,9},{11,1... | collective-permute-start | bytes 1327112 | tf_op jit(solution)/shard_map/ppermute | solution.py:29
  82.7 2.9 %collective-permute-start.2 = (f32[8,3,6,768]{3,0,2,1:T(8,128)S(1)}, f32[8,3,6,768]{3,0,2,1:T(8,128)}, u32[]{:S(2)}, u32[]{:S(2)}) collective-permute-start(f32[8,3,6,768]{3,0,2,1:T(8,128)S(1)} %get-tuple-element.49), channel_id=1, source_target_pairs={{0,1},{1,2},{2,3},{3,4},{4,5},{5,6},{6,7},{7,8},{8,9},{9,10},{10,1... | collective-permute-start | bytes 1327112 | tf_op jit(solution)/shard_map/ppermute | solution.py:27
  86.8 0.8 fusion.46
  88.5 0.9 slice_add_fusion
  89.7 0.8 copy.111
  90.5 1.6 fusion.38
  92.1 1.5 collective-permute-done.3
  93.6 1.2 copy.98
  94.8 5.3 %collective-permute-done.2 = f32[8,3,6,768]{3,0,2,1:T(8,128)} collective-permute-done((f32[8,3,6,768]{3,0,2,1:T(8,128)S(1)}, f32[8,3,6,768]{3,0,2,1:T(8,128)}, u32[]{:S(2)}, u32[]{:S(2)}) %collective-permute-start.2) | collective-permute-done | bytes 442400 | tf_op jit(solution)/shard_map/ppermute | solution.py:27
  100.0 1.2 copy.96
  103.7 0.9 select_select_fusion.5
  106.2 0.9 select_select_fusion.1
  109.9 1.1 fusion.44
  111.5 2.5 %collective-permute-start.14 = (f32[8,3,8,256]{3,1,0,2:T(4,128)S(1)}, f32[8,3,8,256]{3,1,0,2:T(4,128)S(1)}, u32[]{:S(2)}, u32[]{:S(2)}) collective-permute-start(f32[8,3,8,256]{3,1,0,2:T(4,128)S(1)} %copy_multiply_fusion), channel_id=1, source_target_pairs={{0,1},{1,2},{2,3},{3,4},{4,5},{5,6},{6,7},{7,8},{8,9},{9,10},{10,1... | collective-permute-start | bytes 589832 | tf_op jit(solution)/shard_map/ppermute | solution.py:213
  114.0 6.4 %collective-permute-done.14 = f32[8,3,8,256]{3,1,0,2:T(4,128)S(1)} collective-permute-done((f32[8,3,8,256]{3,1,0,2:T(4,128)S(1)}, f32[8,3,8,256]{3,1,0,2:T(4,128)S(1)}, u32[]{:S(2)}, u32[]{:S(2)}) %collective-permute-start.14) | collective-permute-done | bytes 196640 | tf_op jit(solution)/shard_map/ppermute | solution.py:213
  120.7 5.4 %collective-permute-start.15 = (f32[8,3,8,256]{3,1,0,2:T(4,128)S(1)}, f32[8,3,8,256]{3,1,0,2:T(4,128)S(1)}, u32[]{:S(2)}, u32[]{:S(2)}) collective-permute-start(f32[8,3,8,256]{3,1,0,2:T(4,128)S(1)} %broadcast_select_fusion.2), channel_id=1, source_target_pairs={{0,2},{1,3},{2,4},{3,5},{4,6},{5,7},{6,8},{7,9},{8,10},{9,11},{10,... | collective-permute-start | bytes 589832 | tf_op jit(solution)/shard_map/ppermute | solution.py:213
  126.0 6.7 %collective-permute-done.15 = f32[8,3,8,256]{3,1,0,2:T(4,128)S(1)} collective-permute-done((f32[8,3,8,256]{3,1,0,2:T(4,128)S(1)}, f32[8,3,8,256]{3,1,0,2:T(4,128)S(1)}, u32[]{:S(2)}, u32[]{:S(2)}) %collective-permute-start.15) | collective-permute-done | bytes 196640 | tf_op jit(solution)/shard_map/ppermute | solution.py:213
  132.9 7.9 %collective-permute-done.16 = f32[8,3,8,256]{3,1,0,2:T(4,128)S(1)} collective-permute-done((f32[8,3,8,256]{3,1,0,2:T(4,128)S(1)}, f32[8,3,8,256]{3,1,0,2:T(4,128)S(1)}, u32[]{:S(2)}, u32[]{:S(2)}) %collective-permute-start.16) | collective-permute-done | bytes 196640 | tf_op jit(solution)/shard_map/ppermute | solution.py:213
  141.0 9.0 %collective-permute-done.17 = f32[8,3,8,256]{3,1,0,2:T(4,128)S(1)} collective-permute-done((f32[8,3,8,256]{3,1,0,2:T(4,128)S(1)}, f32[8,3,8,256]{3,1,0,2:T(4,128)S(1)}, u32[]{:S(2)}, u32[]{:S(2)}) %collective-permute-start.17) | collective-permute-done | bytes 196640 | tf_op jit(solution)/shard_map/ppermute | solution.py:213
  150.1 1.9 collective-permute-start.18
  167.0 0.7 collective-permute-start.23
  167.7 1.3 collective-permute-start.24
  169.1 10.4 %collective-permute-start.21 = (f32[8,3,8,256]{3,1,0,2:T(4,128)S(1)}, f32[8,3,8,256]{3,1,0,2:T(4,128)S(1)}, u32[]{:S(2)}, u32[]{:S(2)}) collective-permute-start(f32[8,3,8,256]{3,1,0,2:T(4,128)S(1)} %broadcast_select_fusion.6), channel_id=1, source_target_pairs={{0,0},{2,1},{4,2},{6,3},{8,4},{10,5},{12,6},{14,7},{16,8},{18,9},{... | collective-permute-start | bytes 589832 | tf_op jit(solution)/shard_map/ppermute | solution.py:224
  179.5 1.9 collective-permute-start.22
  181.4 0.7 collective-permute-start.19
  182.1 1.3 collective-permute-start.20
  183.5 7.9 %collective-permute-done.22 = f32[8,3,8,256]{3,1,0,2:T(4,128)S(1)} collective-permute-done((f32[8,3,8,256]{3,1,0,2:T(4,128)S(1)}, f32[8,3,8,256]{3,1,0,2:T(4,128)S(1)}, u32[]{:S(2)}, u32[]{:S(2)}) %collective-permute-start.22) | collective-permute-done | bytes 196640 | tf_op jit(solution)/shard_map/ppermute | solution.py:224
  191.5 10.6 %collective-permute-done.20 = f32[8,3,8,256]{3,1,0,2:T(4,128)S(1)} collective-permute-done((f32[8,3,8,256]{3,1,0,2:T(4,128)S(1)}, f32[8,3,8,256]{3,1,0,2:T(4,128)S(1)}, u32[]{:S(2)}, u32[]{:S(2)}) %collective-permute-start.20) | collective-permute-done | bytes 196640 | tf_op jit(solution)/shard_map/ppermute | solution.py:224
  202.6 0.9 gather_fusion
  203.7 1.9 dynamic_update_slice.24
  205.6 1.9 dynamic_update_slice.25
  207.5 1.9 dynamic_update_slice.26
  209.4 1.9 dynamic_update_slice.27
  211.3 1.9 dynamic_update_slice.28
  213.2 1.9 dynamic_update_slice.29
  215.1 1.9 dynamic_update_slice.30
  217.0 1.9 dynamic_update_slice.31
  (178 shorter events, 20.4 us)
Async XLA Ops:
  3.9 7.8 %copy-start = (f32[8,16,4096]{2,1,0:T(8,128)}, f32[8,16,4096]{2,1,0:T(8,128)S(1)}, u32[]{:S(2)}) copy-start(f32[8,16,4096]{2,1,0:T(8,128)S(1)} %get-tuple-element.23) | copy-start | bytes 6291460
  5.8 25.1 %collective-permute-start = (f32[8,4,4096]{2,1,0:T(4,128)}, f32[8,4,4096]{2,1,0:T(4,128)S(1)}, u32[]{:S(2)}, u32[]{:S(2)}) collective-permute-start(f32[8,4,4096]{2,1,0:T(4,128)} %pad_maximum_fusion.21), channel_id=1, source_target_pairs={{1,0},{2,1},{3,2},{4,3},{5,4},{6,5},{7,6},{8,7},{9,8},{10,9},{11,1... | collective-permute-start | bytes 1572872 | tf_op jit(solution)/shard_map/ppermute | solution.py:59
  11.7 22.4 %collective-permute-start.1 = (f32[8,4,4096]{2,1,0:T(4,128)}, f32[8,4,4096]{2,1,0:T(4,128)S(1)}, u32[]{:S(2)}, u32[]{:S(2)}) collective-permute-start(f32[8,4,4096]{2,1,0:T(4,128)} %pad_maximum_fusion.22), channel_id=1, source_target_pairs={{0,1},{1,2},{2,3},{3,4},{4,5},{5,6},{6,7},{7,8},{8,9},{9,10},{10,1... | collective-permute-start | bytes 1572872 | tf_op jit(solution)/shard_map/ppermute | solution.py:58
  14.3 2.8 %copy-start.9 = (s32[8,2]{0,1:T(2,128)S(1)}, s32[8,2]{0,1:T(2,128)}, u32[]{:S(2)}) copy-start(s32[8,2]{0,1:T(2,128)} %param.5) | copy-start | bytes 196
  28.1 7.5 %copy-start.13 = (s32[8]{0:T(128)}, s32[8]{0:T(128)S(1)}, u32[]{:S(2)}) copy-start(s32[8]{0:T(128)S(1)} %get-tuple-element.107) | copy-start | bytes 100
  30.0 4.7 %copy-start.1 = (f32[8,16,4096]{2,1,0:T(8,128)S(1)}, f32[8,16,4096]{2,1,0:T(8,128)}, u32[]{:S(2)}) copy-start(f32[8,16,4096]{2,1,0:T(8,128)} %copy-done) | copy-start | bytes 6291460
  30.7 5.0 %copy-start.18 = (s32[16]{0:T(128)}, s32[16]{0:T(128)S(1)}, u32[]{:S(2)}) copy-start(s32[16]{0:T(128)S(1)} %iota_add_fusion.2) | copy-start | bytes 196
  31.1 4.5 %copy-start.2 = (f32[8,16,4095]{2,1,0:T(8,128)S(1)}, f32[8,16,4095]{2,1,0:T(8,128)}, u32[]{:S(2)}) copy-start(f32[8,16,4095]{2,1,0:T(8,128)} %get-tuple-element.37) | copy-start | bytes 6289924
  34.7 5.5 %slice-start = ((s8[6291456]{0:T(1024)(128)(4,1)}), s8[4194304]{0:T(1024)(128)(4,1)S(1)}, s32[]{:S(2)}) async-start(s8[6291456]{0:T(1024)(128)(4,1)} %bitcast.177), calls=%async_computation | async-start | bytes 8388608
  35.6 4.6 %slice-start.1 = ((s8[6291456]{0:T(1024)(128)(4,1)}), s8[2097152]{0:T(1024)(128)(4,1)S(1)}, s32[]{:S(2)}) async-start(s8[6291456]{0:T(1024)(128)(4,1)} %bitcast.177), calls=%async_computation.1 | async-start | bytes 4194304
  42.5 2.7 %copy-start.3 = (f32[8,3,16,4096]{3,2,1,0:T(8,128)}, f32[8,3,16,4096]{3,2,1,0:T(8,128)S(1)}, u32[]{:S(2)}) copy-start(f32[8,3,16,4096]{3,2,1,0:T(8,128)S(1)} %pad_maximum_fusion) | copy-start | bytes 18874372
  42.5 26.0 %copy-start.4 = (f32[8,3,24,768]{3,2,1,0:T(8,128)S(1)}, f32[8,3,24,768]{3,2,1,0:T(8,128)}, u32[]{:S(2)}) copy-start(f32[8,3,24,768]{3,2,1,0:T(8,128)} %param.4) | copy-start | bytes 5308420
  48.8 14.1 %collective-permute-start.4 = (f32[48,274]{1,0:T(8,128)S(1)}, f32[48,274]{1,0:T(8,128)S(1)}, u32[]{:S(2)}, u32[]{:S(2)}) collective-permute-start(f32[48,274]{1,0:T(8,128)S(1)} %pad_maximum_fusion.23), channel_id=1, source_target_pairs={{0,7},{1,8},{2,9},{3,10},{4,11},{5,12},{6,13},{7,14},{8,15},{9,16}... | collective-permute-start | bytes 157832 | tf_op jit(solution)/shard_map/ppermute | solution.py:142
  52.2 12.5 %collective-permute-start.5 = (f32[48,274]{1,0:T(8,128)S(1)}, f32[48,274]{1,0:T(8,128)S(1)}, u32[]{:S(2)}, u32[]{:S(2)}) collective-permute-start(f32[48,274]{1,0:T(8,128)S(1)} %pad_maximum_fusion.23), channel_id=1, source_target_pairs={{0,6},{1,7},{2,8},{3,9},{4,10},{5,11},{6,12},{7,13},{8,14},{9,15},... | collective-permute-start | bytes 157832 | tf_op jit(solution)/shard_map/ppermute | solution.py:142
  52.2 18.0 %collective-permute-start.6 = (f32[48,274]{1,0:T(8,128)S(1)}, f32[48,274]{1,0:T(8,128)S(1)}, u32[]{:S(2)}, u32[]{:S(2)}) collective-permute-start(f32[48,274]{1,0:T(8,128)S(1)} %pad_maximum_fusion.23), channel_id=1, source_target_pairs={{0,5},{1,6},{2,7},{3,8},{4,9},{5,10},{6,11},{7,12},{8,13},{9,14},{... | collective-permute-start | bytes 157832 | tf_op jit(solution)/shard_map/ppermute | solution.py:142
  57.7 12.5 %collective-permute-start.7 = (f32[48,274]{1,0:T(8,128)S(1)}, f32[48,274]{1,0:T(8,128)S(1)}, u32[]{:S(2)}, u32[]{:S(2)}) collective-permute-start(f32[48,274]{1,0:T(8,128)S(1)} %pad_maximum_fusion.23), channel_id=1, source_target_pairs={{0,4},{1,5},{2,6},{3,7},{4,8},{5,9},{6,10},{7,11},{8,12},{9,13},{1... | collective-permute-start | bytes 157832 | tf_op jit(solution)/shard_map/ppermute | solution.py:142
  57.7 12.6 %collective-permute-start.8 = (f32[48,274]{1,0:T(8,128)S(1)}, f32[48,274]{1,0:T(8,128)S(1)}, u32[]{:S(2)}, u32[]{:S(2)}) collective-permute-start(f32[48,274]{1,0:T(8,128)S(1)} %pad_maximum_fusion.23), channel_id=1, source_target_pairs={{0,3},{1,4},{2,5},{3,6},{4,7},{5,8},{6,9},{7,10},{8,11},{9,12},{10... | collective-permute-start | bytes 157832 | tf_op jit(solution)/shard_map/ppermute | solution.py:142
  62.9 7.4 %collective-permute-start.9 = (f32[48,274]{1,0:T(8,128)S(1)}, f32[48,274]{1,0:T(8,128)S(1)}, u32[]{:S(2)}, u32[]{:S(2)}) collective-permute-start(f32[48,274]{1,0:T(8,128)S(1)} %pad_maximum_fusion.23), channel_id=1, source_target_pairs={{0,2},{1,3},{2,4},{3,5},{4,6},{5,7},{6,8},{7,9},{8,10},{9,11},{10,... | collective-permute-start | bytes 157832 | tf_op jit(solution)/shard_map/ppermute | solution.py:142
  64.7 6.8 %collective-permute-start.10 = (f32[48,274]{1,0:T(8,128)S(1)}, f32[48,274]{1,0:T(8,128)S(1)}, u32[]{:S(2)}, u32[]{:S(2)}) collective-permute-start(f32[48,274]{1,0:T(8,128)S(1)} %pad_maximum_fusion.23), channel_id=1, source_target_pairs={{0,1},{1,2},{2,3},{3,4},{4,5},{5,6},{6,7},{7,8},{8,9},{9,10},{10,1... | collective-permute-start | bytes 157832 | tf_op jit(solution)/shard_map/ppermute | solution.py:142
  70.3 16.5 %copy-start.15 = (s32[8,36]{1,0:T(8,128)S(1)}, s32[8,36]{1,0:T(8,128)}, u32[]{:S(2)}) copy-start(s32[8,36]{1,0:T(8,128)} %get-tuple-element.108) | copy-start | bytes 3460
  70.3 16.5 %copy-start.16 = (s32[8,36]{1,0:T(8,128)S(1)}, s32[8,36]{1,0:T(8,128)}, u32[]{:S(2)}) copy-start(s32[8,36]{1,0:T(8,128)} %get-tuple-element.109) | copy-start | bytes 3460
  70.3 16.5 %copy-start.17 = (s32[512]{0:T(512)S(1)}, s32[512]{0:T(512)}, u32[]{:S(2)}) copy-start(s32[512]{0:T(512)} %add_select_fusion.3) | copy-start | bytes 6148
  72.4 13.3 %collective-permute-start.11 = (f32[48,386]{1,0:T(8,128)}, f32[48,386]{1,0:T(8,128)S(1)}, u32[]{:S(2)}, u32[]{:S(2)}) collective-permute-start(f32[48,386]{1,0:T(8,128)} %concatenate.252), channel_id=1, source_target_pairs={{0,24},{1,25},{2,26},{3,27},{4,28},{5,29},{6,30},{7,31},{8,0},{9,1... | collective-permute-start | bytes 222344 | tf_op jit(solution)/shard_map/ppermute | solution.py:142
  72.8 12.9 %collective-permute-start.12 = (f32[48,386]{1,0:T(8,128)}, f32[48,386]{1,0:T(8,128)S(1)}, u32[]{:S(2)}, u32[]{:S(2)}) collective-permute-start(f32[48,386]{1,0:T(8,128)} %concatenate.252), channel_id=1, source_target_pairs={{0,16},{1,17},{2,18},{3,19},{4,20},{5,21},{6,22},{7,23},{8,24},{9,... | collective-permute-start | bytes 222344 | tf_op jit(solution)/shard_map/ppermute | solution.py:142
  76.0 9.8 %collective-permute-start.13 = (f32[48,386]{1,0:T(8,128)}, f32[48,386]{1,0:T(8,128)S(1)}, u32[]{:S(2)}, u32[]{:S(2)}) collective-permute-start(f32[48,386]{1,0:T(8,128)} %concatenate.252), channel_id=1, source_target_pairs={{0,8},{1,9},{2,10},{3,11},{4,12},{5,13},{6,14},{7,15},{8,16},{9,17... | collective-permute-start | bytes 222344 | tf_op jit(solution)/shard_map/ppermute | solution.py:142
  78.0 15.6 %collective-permute-start.3 = (f32[8,3,6,768]{3,0,2,1:T(8,128)}, f32[8,3,6,768]{3,0,2,1:T(8,128)}, u32[]{:S(2)}, u32[]{:S(2)}) collective-permute-start(f32[8,3,6,768]{3,0,2,1:T(8,128)} %get-tuple-element.50), channel_id=1, source_target_pairs={{1,0},{2,1},{3,2},{4,3},{5,4},{6,5},{7,6},{8,7},{9,8},{10,9},{11,1... | collective-permute-start | bytes 1327112 | tf_op jit(solution)/shard_map/ppermute | solution.py:29
  82.7 17.4 %collective-permute-start.2 = (f32[8,3,6,768]{3,0,2,1:T(8,128)S(1)}, f32[8,3,6,768]{3,0,2,1:T(8,128)}, u32[]{:S(2)}, u32[]{:S(2)}) collective-permute-start(f32[8,3,6,768]{3,0,2,1:T(8,128)S(1)} %get-tuple-element.49), channel_id=1, source_target_pairs={{0,1},{1,2},{2,3},{3,4},{4,5},{5,6},{6,7},{7,8},{8,9},{9,10},{10,1... | collective-permute-start | bytes 1327112 | tf_op jit(solution)/shard_map/ppermute | solution.py:27
  85.8 0.6 copy-start.6
  85.8 0.6 copy-start.7
  101.2 0.6 copy-start.10
  101.2 0.6 copy-start.11
  109.3 0.7 copy-start.12
  109.9 1.4 copy-start.5
  109.9 4.1 %copy-start.20 = (s32[8]{0:T(128)S(1)}, s32[8]{0:T(128)}, u32[]{:S(2)}) copy-start(s32[8]{0:T(128)} %get-tuple-element.7) | copy-start | bytes 100
  111.2 55.6 %copy-start.21 = (pred[8]{0:T(512)(128)(4,1)S(1)}, pred[8]{0:T(512)(128)(4,1)}, u32[]{:S(2)}) copy-start(pred[8]{0:T(512)(128)(4,1)} %get-tuple-element.6) | copy-start | bytes 28
  111.3 57.7 %copy-start.14 = (s32[8]{0:T(128)S(1)}, s32[8]{0:T(128)}, u32[]{:S(2)}) copy-start(s32[8]{0:T(128)} %copy-done.13) | copy-start | bytes 100
  111.3 57.7 %copy-start.19 = (s32[16]{0:T(128)S(1)}, s32[16]{0:T(128)}, u32[]{:S(2)}) copy-start(s32[16]{0:T(128)} %copy-done.18) | copy-start | bytes 196
  111.5 8.9 %collective-permute-start.14 = (f32[8,3,8,256]{3,1,0,2:T(4,128)S(1)}, f32[8,3,8,256]{3,1,0,2:T(4,128)S(1)}, u32[]{:S(2)}, u32[]{:S(2)}) collective-permute-start(f32[8,3,8,256]{3,1,0,2:T(4,128)S(1)} %copy_multiply_fusion), channel_id=1, source_target_pairs={{0,1},{1,2},{2,3},{3,4},{4,5},{5,6},{6,7},{7,8},{8,9},{9,10},{10,1... | collective-permute-start | bytes 589832 | tf_op jit(solution)/shard_map/ppermute | solution.py:213
  120.7 12.1 %collective-permute-start.15 = (f32[8,3,8,256]{3,1,0,2:T(4,128)S(1)}, f32[8,3,8,256]{3,1,0,2:T(4,128)S(1)}, u32[]{:S(2)}, u32[]{:S(2)}) collective-permute-start(f32[8,3,8,256]{3,1,0,2:T(4,128)S(1)} %broadcast_select_fusion.2), channel_id=1, source_target_pairs={{0,2},{1,3},{2,4},{3,5},{4,6},{5,7},{6,8},{7,9},{8,10},{9,11},{10,... | collective-permute-start | bytes 589832 | tf_op jit(solution)/shard_map/ppermute | solution.py:213
  132.9 7.9 %collective-permute-start.16 = (f32[8,3,8,256]{3,1,0,2:T(4,128)S(1)}, f32[8,3,8,256]{3,1,0,2:T(4,128)S(1)}, u32[]{:S(2)}, u32[]{:S(2)}) collective-permute-start(f32[8,3,8,256]{3,1,0,2:T(4,128)S(1)} %broadcast_select_fusion.3), channel_id=1, source_target_pairs={{0,4},{1,5},{2,6},{3,7},{4,8},{5,9},{6,10},{7,11},{8,12},{9,13},{1... | collective-permute-start | bytes 589832 | tf_op jit(solution)/shard_map/ppermute | solution.py:213
  140.9 9.1 %collective-permute-start.17 = (f32[8,3,8,256]{3,1,0,2:T(4,128)S(1)}, f32[8,3,8,256]{3,1,0,2:T(4,128)S(1)}, u32[]{:S(2)}, u32[]{:S(2)}) collective-permute-start(f32[8,3,8,256]{3,1,0,2:T(4,128)S(1)} %broadcast_select_fusion.4), channel_id=1, source_target_pairs={{0,8},{1,9},{2,10},{3,11},{4,12},{5,13},{6,14},{7,15},{8,16},{9,17... | collective-permute-start | bytes 589832 | tf_op jit(solution)/shard_map/ppermute | solution.py:213
  150.1 16.7 %collective-permute-start.18 = (f32[8,3,8,256]{3,1,0,2:T(4,128)S(1)}, f32[8,3,8,256]{3,1,0,2:T(4,128)S(1)}, u32[]{:S(2)}, u32[]{:S(2)}) collective-permute-start(f32[8,3,8,256]{3,1,0,2:T(4,128)S(1)} %broadcast_select_fusion.5), channel_id=1, source_target_pairs={{0,16},{1,17},{2,18},{3,19},{4,20},{5,21},{6,22},{7,23},{8,24},{9,... | collective-permute-start | bytes 589832 | tf_op jit(solution)/shard_map/ppermute | solution.py:213
  167.0 35.6 %copy-start.8 = (s32[8]{0:T(128)S(1)}, s32[8]{0:T(128)}, u32[]{:S(2)}) copy-start(s32[8]{0:T(128)} %get-tuple-element.103) | copy-start | bytes 100
  167.0 15.1 %collective-permute-start.23 = (f32[8,3,8,256]{3,1,0,2:T(4,128)S(1)}, f32[8,3,8,256]{3,1,0,2:T(4,128)S(1)}, u32[]{:S(2)}, u32[]{:S(2)}) collective-permute-start(f32[8,3,8,256]{3,1,0,2:T(4,128)S(1)} %broadcast_select_fusion.6), channel_id=1, source_target_pairs={{1,0},{3,1},{5,2},{7,3},{9,4},{11,5},{13,6},{15,7},{17,8},{19,9},{... | collective-permute-start | bytes 589832 | tf_op jit(solution)/shard_map/ppermute | solution.py:224
  167.7 15.7 %collective-permute-start.24 = (f32[8,3,8,256]{3,1,0,2:T(4,128)S(1)}, f32[8,3,8,256]{3,1,0,2:T(4,128)S(1)}, u32[]{:S(2)}, u32[]{:S(2)}) collective-permute-start(f32[8,3,8,256]{3,1,0,2:T(4,128)S(1)} %broadcast_select_fusion.6), channel_id=1, source_target_pairs={{1,16},{3,17},{5,18},{7,19},{9,20},{11,21},{13,22},{15,23},{17,24}... | collective-permute-start | bytes 589832 | tf_op jit(solution)/shard_map/ppermute | solution.py:224
  169.1 14.4 %collective-permute-start.21 = (f32[8,3,8,256]{3,1,0,2:T(4,128)S(1)}, f32[8,3,8,256]{3,1,0,2:T(4,128)S(1)}, u32[]{:S(2)}, u32[]{:S(2)}) collective-permute-start(f32[8,3,8,256]{3,1,0,2:T(4,128)S(1)} %broadcast_select_fusion.6), channel_id=1, source_target_pairs={{0,0},{2,1},{4,2},{6,3},{8,4},{10,5},{12,6},{14,7},{16,8},{18,9},{... | collective-permute-start | bytes 589832 | tf_op jit(solution)/shard_map/ppermute | solution.py:224
  179.5 12.0 %collective-permute-start.22 = (f32[8,3,8,256]{3,1,0,2:T(4,128)S(1)}, f32[8,3,8,256]{3,1,0,2:T(4,128)S(1)}, u32[]{:S(2)}, u32[]{:S(2)}) collective-permute-start(f32[8,3,8,256]{3,1,0,2:T(4,128)S(1)} %broadcast_select_fusion.6), channel_id=1, source_target_pairs={{0,16},{2,17},{4,18},{6,19},{8,20},{10,21},{12,22},{14,23},{16,24}... | collective-permute-start | bytes 589832 | tf_op jit(solution)/shard_map/ppermute | solution.py:224
  181.4 10.1 %collective-permute-start.19 = (f32[8,3,8,256]{3,1,0,2:T(4,128)S(1)}, f32[8,3,8,256]{3,1,0,2:T(4,128)S(1)}, u32[]{:S(2)}, u32[]{:S(2)}) collective-permute-start(f32[8,3,8,256]{3,1,0,2:T(4,128)S(1)} %broadcast_select_fusion.6), channel_id=1, source_target_pairs={{31,0},{1,1},{3,2},{5,3},{7,4},{9,5},{11,6},{13,7},{15,8},{17,9},{... | collective-permute-start | bytes 589832 | tf_op jit(solution)/shard_map/ppermute | solution.py:224
  182.1 20.1 %collective-permute-start.20 = (f32[8,3,8,256]{3,1,0,2:T(4,128)S(1)}, f32[8,3,8,256]{3,1,0,2:T(4,128)S(1)}, u32[]{:S(2)}, u32[]{:S(2)}) collective-permute-start(f32[8,3,8,256]{3,1,0,2:T(4,128)S(1)} %broadcast_select_fusion.6), channel_id=1, source_target_pairs={{31,16},{1,17},{3,18},{5,19},{7,20},{9,21},{11,22},{13,23},{15,24}... | collective-permute-start | bytes 589832 | tf_op jit(solution)/shard_map/ppermute | solution.py:224

commit v7 on v6

--- a/solution.py
+++ b/solution.py
@@ -76,7 +76,7 @@
         - courant * (0.5 * (height_ext[:, 2:] - height_ext[:, :-2]))
         - rotation * zonal
     )
-    return jnp.stack([height_new, zonal_new, merid_new], axis=1)
+    return jnp.stack([height_new, zonal_new, merid_new], axis=1), prev
 
 
 def per_device(parent_state, nest_state, offsets):
@@ -97,7 +97,9 @@
     two = jnp.float32(2.0) / jnp.float32(3.0)
     one = jnp.float32(1.0) / jnp.float32(3.0)
 
-    stepped = parent_step(parent_state)
+    stepped, arrived = parent_step(parent_state)
+    nest_state, arrived = lax.optimization_barrier((nest_state, arrived))
+    nest_ext = with_halo(nest_state, 2 * NSTEPS)
 
     colslice = jnp.concatenate(
         [
@@ -136,7 +138,7 @@
         count = min(8, bands // reach)
         payload = jnp.concatenate([blocks, sums], axis=1)
         if reach == 1:
-            nest_state, payload = lax.optimization_barrier((nest_state, payload))
+            payload, nest_ext = lax.optimization_barrier((payload, nest_ext))
         width = blocks.shape[1]
         recvs = [
             lax.ppermute(payload, "band", [(i, (i + k * reach) % bands) for i in range(bands)])
@@ -164,7 +166,6 @@
     )
     side_ext = jnp.einsum("mkr,mfsr->mfsk", side_weights, strip_all, precision=highest)
 
-    nest_ext = with_halo(nest_state, halo)
     is_south = (nest_global == -1)[None, :, None]
     is_north = (nest_global == nest_total)[None, :, None]
 

time: 220 us -> 261 us (1.19)
  local copies, waits for them, and re-layouts: 44.1 us -> 72.2 us
  other arithmetic: 21.1 us -> 32 us
  starting transfers between devices: 61.1 us -> 68.2 us
  waiting for transfers between devices: 59.3 us -> 52.3 us
    concatenate x11, local copies, waits for them, and re-layouts: 0.36 us -> 13.1 us  [per_device(): jnp.concatenate([got[:, :width] for got in recvs] + [blocks], axis=1)]
    select_n x6, other arithmetic: 3.93 us -> 9.12 us  [fix(): jnp.where(is_south, ends[:, f, 0][:, None, :], jnp.where(is_north, ends[:...]
    slice x10, local copies, waits for them, and re-layouts: 0.04 us -> 4.32 us  [per_device(): got[:, :width]]
    ppermute x6, starting transfers between devices: 16.3 us -> 19.4 us  [per_device(): got.append(lax.ppermute(moved, 'band', pairs))]
    another operation x2, local copies, waits for them, and re-layouts: 0.3 us -> 2.97 us  [dx(): west_col = side_ext[:, f, 0][:, :, None]]
    unnamed x57 -> x101, local copies, waits for them, and re-layouts: 4.3 us -> 6.11 us
  transfers between devices with their start and end apart: 25 -> 25, of which waited for: 10 -> 8; matrix products, arithmetic and copies ran while one was open for 10% -> 14% of each run, Pallas kernels for 0% -> 0%
where the time goes in v7:
time: 261 us; the launch traced here: 259 us
  local copies, waits for them, and re-layouts  72.2 us (28%)
  starting transfers between devices  68.2 us (26%)
  waiting for transfers between devices  52.3 us (20%)
  other arithmetic  32 us (12%)
  between operations  26.7 us (10%)
  matrix products  7.93 us (3%)
    ppermute x5, waiting for transfers between devices, per_device(): lax.ppermute(moved, 'band', [(i, (i + step) % bands) for i in range(bands)])  28.1 us
    ppermute x10, starting transfers between devices, per_device(): lax.ppermute(payload, 'band', [(i, (i + k * reach) % bands) for i in rang...  21.9 us
    ppermute x6, starting transfers between devices, per_device(): got.append(lax.ppermute(moved, 'band', pairs))  19.4 us
    ppermute x6, waiting for transfers between devices, per_device(): got.append(lax.ppermute(moved, 'band', pairs))  18.4 us
    dynamic_update_slice x8, local copies, waits for them, and re-layouts, per_device(): lax.dynamic_update_slice(parent_out, merged[m:m + 1], (m, 0, 0, cols_off[...  15.2 us
    concatenate x11, local copies, waits for them, and re-layouts, per_device(): jnp.concatenate([got[:, :width] for got in recvs] + [blocks], axis=1)  13.1 us
    ppermute x5, starting transfers between devices, per_device(): lax.ppermute(moved, 'band', [(i, (i + step) % bands) for i in range(bands)])  9.6 us
    select_n x6, other arithmetic, fix(): jnp.where(is_south, ends[:, f, 0][:, None, :], jnp.where(is_north, ends[:...  9.12 us
  transfers between devices with their start and end apart: 25, of which 8 were waited for; matrix products, arithmetic and copies ran while one was open for 14% of the time, Pallas kernels for 0%

profile of v7, /device:TPU:112, one launch (start us, length us, event | category | flops | bytes accessed | tf_op | source)
XLA Modules:
  0.0 259.3 jit_solution(12142503918263914902)
XLA Ops:
  0.6 3.3 %slice_bitcast_fusion.4 = (f32[8,16,4096]{2,1,0:T(8,128)S(1)}, f32[8,16,4096]{2,1,0:T(8,128)S(1)}, f32[8,16,4096]{2,1,0:T(8,128)S(1)}) fusion(f32[8,3,16,4096]{3,2,1,0:T(8,128)} %param.3), kind=kLoop, calls=%fused_computation.28 | loop fusion | bytes 12582912 | tf_op jit(solution)/shard_map/squeeze | solution.py:50
  4.6 1.1 pad_maximum_fusion.21
  5.8 4.8 %collective-permute-start = (f32[8,4,4096]{2,1,0:T(4,128)}, f32[8,4,4096]{2,1,0:T(4,128)S(1)}, u32[]{:S(2)}, u32[]{:S(2)}) collective-permute-start(f32[8,4,4096]{2,1,0:T(4,128)} %pad_maximum_fusion.21), channel_id=1, source_target_pairs={{1,0},{2,1},{3,2},{4,3},{5,4},{6,5},{7,6},{8,7},{9,8},{10,9},{11,1... | collective-permute-start | bytes 1572872 | tf_op jit(solution)/shard_map/ppermute | solution.py:59
  10.5 1.1 pad_maximum_fusion.22
  11.7 2.6 collective-permute-start.1
  14.3 2.8 %fusion.134 = (f32[8,16,4095]{2,1,0:T(8,128)}, f32[8,16,4095]{2,1,0:T(8,128)}) fusion(f32[8,16,4096]{2,1,0:T(8,128)S(1)} %get-tuple-element.24), kind=kLoop, calls=%fused_computation.311 | loop fusion | bytes 8386560 | tf_op jit(solution)/shard_map/jit(_roll_static)/slice | solution.py:46
  35.6 3.4 %fusion.8 = f32[8,16,4096]{2,1,0:T(8,128)S(1)} fusion(f32[8,16,4096]{2,1,0:T(8,128)S(1)} %copy-done.1, f32[8,1,4096]{2,1,0:T(1,128)S(1)} %get-tuple-element.77, f32[8,1,4096]{2,1,0:T(1,128)S(1)} %get-tuple-element.78, f32[8,16,1]{2,1,0:T(8,128)S(1)} %get-tuple-element.38, f32[8,16,4095]{2,1,0:T(8,128)} %get-tuple-element.40, ...), kind=kLoop, calls=%fused_computation.16 | loop fusion | flops 4718592 | bytes 10747904 | tf_op jit(solution)/shard_map/sub | solution.py:61
  41.3 5.6 %collective-permute-start.3 = (f32[8,3,6,768]{3,0,2,1:T(8,128)S(1)}, f32[8,3,6,768]{3,0,2,1:T(8,128)S(1)}, u32[]{:S(2)}, u32[]{:S(2)}) collective-permute-start(f32[8,3,6,768]{3,0,2,1:T(8,128)S(1)} %get-tuple-element.52), channel_id=1, source_target_pairs={{1,0},{2,1},{3,2},{4,3},{5,4},{6,5},{7,6},{8,7},{9,8},{10,9},{11,1... | collective-permute-start | bytes 1327112 | tf_op jit(solution)/shard_map/ppermute | solution.py:29
  46.9 4.4 %collective-permute-start.2 = (f32[8,3,6,768]{3,0,2,1:T(8,128)S(1)}, f32[8,3,6,768]{3,0,2,1:T(8,128)S(1)}, u32[]{:S(2)}, u32[]{:S(2)}) collective-permute-start(f32[8,3,6,768]{3,0,2,1:T(8,128)S(1)} %get-tuple-element.51), channel_id=1, source_target_pairs={{0,1},{1,2},{2,3},{3,4},{4,5},{5,6},{6,7},{7,8},{8,9},{9,10},{10,1... | collective-permute-start | bytes 1327112 | tf_op jit(solution)/shard_map/ppermute | solution.py:27
  54.7 2.0 copy-done.3
  57.4 2.9 %fusion.89 = f32[2,8,3,16]{3,0,2,1:T(2,128)S(1)} fusion(f32[8,3,16,258]{3,2,1,0:T(8,128)S(1)} %dynamic-slice_dynamic-update-slice_fusion, pred[258]{0:T(512)(128)(4,1)S(1)} %copy-done.36, pred[258]{0:T(512)(128)(4,1)S(1)} %copy-done.37, pred[258]{0:T(512)(128)(4,1)S(1)} %copy-done.38, pred[258]{0:T(512)(128)(4,1)S(1)} %copy-done.39, ...), kind=kOutput, calls=%fused_computation.216 | convolution fusion | flops 2383404 | bytes 400396 | tf_op jit(solution)/shard_map/mflq,qs->mfsl/dot_general | solution.py:120
  60.5 5.5 %collective-permute-done.2 = f32[8,3,6,768]{3,0,2,1:T(8,128)S(1)} collective-permute-done((f32[8,3,6,768]{3,0,2,1:T(8,128)S(1)}, f32[8,3,6,768]{3,0,2,1:T(8,128)S(1)}, u32[]{:S(2)}, u32[]{:S(2)}) %collective-permute-start.2) | collective-permute-done | bytes 442400 | tf_op jit(solution)/shard_map/ppermute | solution.py:27
  66.2 1.9 pad_maximum_fusion.1
  68.1 3.6 %collective-permute-start.4 = (f32[48,274]{1,0:T(8,128)S(1)}, f32[48,274]{1,0:T(8,128)S(1)}, u32[]{:S(2)}, u32[]{:S(2)}) collective-permute-start(f32[48,274]{1,0:T(8,128)S(1)} %pad_maximum_fusion.23), channel_id=1, source_target_pairs={{0,7},{1,8},{2,9},{3,10},{4,11},{5,12},{6,13},{7,14},{8,15},{9,16}... | collective-permute-start | bytes 157832 | tf_op jit(solution)/shard_map/ppermute | solution.py:144
  72.3 7.1 %collective-permute-start.6 = (f32[48,274]{1,0:T(8,128)S(1)}, f32[48,274]{1,0:T(8,128)S(1)}, u32[]{:S(2)}, u32[]{:S(2)}) collective-permute-start(f32[48,274]{1,0:T(8,128)S(1)} %pad_maximum_fusion.23), channel_id=1, source_target_pairs={{0,5},{1,6},{2,7},{3,8},{4,9},{5,10},{6,11},{7,12},{8,13},{9,14},{... | collective-permute-start | bytes 157832 | tf_op jit(solution)/shard_map/ppermute | solution.py:144
  79.4 4.7 %collective-permute-start.8 = (f32[48,274]{1,0:T(8,128)S(1)}, f32[48,274]{1,0:T(8,128)S(1)}, u32[]{:S(2)}, u32[]{:S(2)}) collective-permute-start(f32[48,274]{1,0:T(8,128)S(1)} %pad_maximum_fusion.23), channel_id=1, source_target_pairs={{0,3},{1,4},{2,5},{3,6},{4,7},{5,8},{6,9},{7,10},{8,11},{9,12},{10... | collective-permute-start | bytes 157832 | tf_op jit(solution)/shard_map/ppermute | solution.py:144
  84.1 2.4 collective-permute-start.9
  95.4 1.8 concatenate.252
  97.6 3.2 %collective-permute-start.12 = (f32[48,386]{1,0:T(8,128)}, f32[48,386]{1,0:T(8,128)S(1)}, u32[]{:S(2)}, u32[]{:S(2)}) collective-permute-start(f32[48,386]{1,0:T(8,128)} %concatenate.252), channel_id=1, source_target_pairs={{0,16},{1,17},{2,18},{3,19},{4,20},{5,21},{6,22},{7,23},{8,24},{9,... | collective-permute-start | bytes 222344 | tf_op jit(solution)/shard_map/ppermute | solution.py:144
  100.9 1.4 copy.110
  102.2 1.4 copy.103
  103.6 1.3 copy.104
  104.9 1.4 copy.105
  106.3 1.3 copy.106
  107.6 1.3 copy.107
  108.9 1.3 copy.108
  110.3 1.4 copy.109
  114.2 1.8 concatenate.263
  116.0 1.8 fusion.50
  118.4 1.6 slice_add_fusion
  120.1 1.6 reshape.799
  121.6 1.8 fusion.42
  124.3 1.4 fusion.150
  125.7 1.6 fusion.149
  127.3 1.5 copy.112
  128.8 1.5 copy.111
  130.3 3.7 %select_select_fusion.6 = (f32[8,36,768]{2,1,0:T(8,128)S(1)}, f32[8,36,768]{2,1,0:T(8,128)}) fusion(f32[8,768]{1,0:T(8,128)} %get-tuple-element.88, f32[8,768]{1,0:T(8,128)} %get-tuple-element.87, pred[36]{0:T(512)(128)(4,1)S(1)} %get-tuple-element.136, pred[36]{0:T(512)(128)(4,1)S(1)} %get-tuple-element.137, f32[8,35,768]{2,1,0:T(8,128)} %get-tuple-element.76, ...), kind=kLoop, calls=%fused_computation.89 | loop fusion | flops 1990656 | bytes 6193224 | tf_op jit(solution)/shard_map/jit(_where)/select_n | solution.py:173
  134.0 1.6 fusion.146
  135.5 1.4 fusion.148
  137.0 1.5 copy.114
  138.4 1.5 copy.113
  139.9 3.1 %select_select_fusion.5 = (f32[8,36,768]{2,1,0:T(8,128)S(1)}, f32[8,36,768]{2,1,0:T(8,128)S(1)}, f32[8,36,768]{2,1,0:T(8,128)S(1)}, f32[8,36,768]{2,1,0:T(8,128)S(1)}) fusion(f32[8,768]{1,0:T(8,128)} %copy-done.18, f32[8,768]{1,0:T(8,128)} %copy-done.20, pred[36]{0:T(512)(128)(4,1)S(1)} %get-tuple-element.136, pred[36]{0:T(512)(128)(4,1)S(1)} %get-tuple-element.137, ...), kind=kLoop, calls=%fused_computation.88 | loop fusion | flops 3981312 | bytes 8896584 | tf_op jit(solution)/shard_map/jit(_where)/select_n | solution.py:173
  149.5 1.1 fusion.48
  151.0 2.7 %collective-permute-start.14 = (f32[8,3,8,256]{3,1,0,2:T(4,128)S(1)}, f32[8,3,8,256]{3,1,0,2:T(4,128)S(1)}, u32[]{:S(2)}, u32[]{:S(2)}) collective-permute-start(f32[8,3,8,256]{3,1,0,2:T(4,128)S(1)} %copy_multiply_fusion), channel_id=1, source_target_pairs={{0,1},{1,2},{2,3},{3,4},{4,5},{5,6},{6,7},{7,8},{8,9},{9,10},{10,1... | collective-permute-start | bytes 589832 | tf_op jit(solution)/shard_map/ppermute | solution.py:214
  153.7 6.2 %collective-permute-done.14 = f32[8,3,8,256]{3,1,0,2:T(4,128)S(1)} collective-permute-done((f32[8,3,8,256]{3,1,0,2:T(4,128)S(1)}, f32[8,3,8,256]{3,1,0,2:T(4,128)S(1)}, u32[]{:S(2)}, u32[]{:S(2)}) %collective-permute-start.14) | collective-permute-done | bytes 196640 | tf_op jit(solution)/shard_map/ppermute | solution.py:214
  160.2 4.3 %collective-permute-start.15 = (f32[8,3,8,256]{3,1,0,2:T(4,128)S(1)}, f32[8,3,8,256]{3,1,0,2:T(4,128)S(1)}, u32[]{:S(2)}, u32[]{:S(2)}) collective-permute-start(f32[8,3,8,256]{3,1,0,2:T(4,128)S(1)} %broadcast_select_fusion.2), channel_id=1, source_target_pairs={{0,2},{1,3},{2,4},{3,5},{4,6},{5,7},{6,8},{7,9},{8,10},{9,11},{10,... | collective-permute-start | bytes 589832 | tf_op jit(solution)/shard_map/ppermute | solution.py:214
  164.5 6.4 %collective-permute-done.15 = f32[8,3,8,256]{3,1,0,2:T(4,128)S(1)} collective-permute-done((f32[8,3,8,256]{3,1,0,2:T(4,128)S(1)}, f32[8,3,8,256]{3,1,0,2:T(4,128)S(1)}, u32[]{:S(2)}, u32[]{:S(2)}) %collective-permute-start.15) | collective-permute-done | bytes 196640 | tf_op jit(solution)/shard_map/ppermute | solution.py:214
  171.4 7.9 %collective-permute-done.16 = f32[8,3,8,256]{3,1,0,2:T(4,128)S(1)} collective-permute-done((f32[8,3,8,256]{3,1,0,2:T(4,128)S(1)}, f32[8,3,8,256]{3,1,0,2:T(4,128)S(1)}, u32[]{:S(2)}, u32[]{:S(2)}) %collective-permute-start.16) | collective-permute-done | bytes 196640 | tf_op jit(solution)/shard_map/ppermute | solution.py:214
  179.4 1.6 collective-permute-start.17
  181.0 7.6 %collective-permute-done.17 = f32[8,3,8,256]{3,1,0,2:T(4,128)S(1)} collective-permute-done((f32[8,3,8,256]{3,1,0,2:T(4,128)S(1)}, f32[8,3,8,256]{3,1,0,2:T(4,128)S(1)}, u32[]{:S(2)}, u32[]{:S(2)}) %collective-permute-start.17) | collective-permute-done | bytes 196640 | tf_op jit(solution)/shard_map/ppermute | solution.py:214
  205.2 1.3 collective-permute-start.24
  206.6 13.5 %collective-permute-start.21 = (f32[8,3,8,256]{3,1,0,2:T(4,128)S(1)}, f32[8,3,8,256]{3,1,0,2:T(4,128)S(1)}, u32[]{:S(2)}, u32[]{:S(2)}) collective-permute-start(f32[8,3,8,256]{3,1,0,2:T(4,128)S(1)} %broadcast_select_fusion.6), channel_id=1, source_target_pairs={{0,0},{2,1},{4,2},{6,3},{8,4},{10,5},{12,6},{14,7},{16,8},{18,9},{... | collective-permute-start | bytes 589832 | tf_op jit(solution)/shard_map/ppermute | solution.py:225
  220.1 1.9 collective-permute-start.22
  222.8 1.3 collective-permute-start.20
  224.2 7.9 %collective-permute-done.22 = f32[8,3,8,256]{3,1,0,2:T(4,128)S(1)} collective-permute-done((f32[8,3,8,256]{3,1,0,2:T(4,128)S(1)}, f32[8,3,8,256]{3,1,0,2:T(4,128)S(1)}, u32[]{:S(2)}, u32[]{:S(2)}) %collective-permute-start.22) | collective-permute-done | bytes 196640 | tf_op jit(solution)/shard_map/ppermute | solution.py:225
  232.2 10.5 %collective-permute-done.20 = f32[8,3,8,256]{3,1,0,2:T(4,128)S(1)} collective-permute-done((f32[8,3,8,256]{3,1,0,2:T(4,128)S(1)}, f32[8,3,8,256]{3,1,0,2:T(4,128)S(1)}, u32[]{:S(2)}, u32[]{:S(2)}) %collective-permute-start.20) | collective-permute-done | bytes 196640 | tf_op jit(solution)/shard_map/ppermute | solution.py:225
  244.2 1.9 dynamic_update_slice.24
  246.1 1.9 dynamic_update_slice.25
  248.0 1.9 dynamic_update_slice.26
  249.9 1.9 dynamic_update_slice.27
  251.8 1.9 dynamic_update_slice.28
  253.7 1.9 dynamic_update_slice.29
  255.6 1.9 dynamic_update_slice.30
  257.5 1.9 dynamic_update_slice.31
  (222 shorter events, 41.2 us)
Async XLA Ops:
  3.9 7.8 %copy-start = (f32[8,16,4096]{2,1,0:T(8,128)}, f32[8,16,4096]{2,1,0:T(8,128)S(1)}, u32[]{:S(2)}) copy-start(f32[8,16,4096]{2,1,0:T(8,128)S(1)} %get-tuple-element.25) | copy-start | bytes 6291460
  5.8 27.6 %collective-permute-start = (f32[8,4,4096]{2,1,0:T(4,128)}, f32[8,4,4096]{2,1,0:T(4,128)S(1)}, u32[]{:S(2)}, u32[]{:S(2)}) collective-permute-start(f32[8,4,4096]{2,1,0:T(4,128)} %pad_maximum_fusion.21), channel_id=1, source_target_pairs={{1,0},{2,1},{3,2},{4,3},{5,4},{6,5},{7,6},{8,7},{9,8},{10,9},{11,1... | collective-permute-start | bytes 1572872 | tf_op jit(solution)/shard_map/ppermute | solution.py:59
  11.7 22.4 %collective-permute-start.1 = (f32[8,4,4096]{2,1,0:T(4,128)}, f32[8,4,4096]{2,1,0:T(4,128)S(1)}, u32[]{:S(2)}, u32[]{:S(2)}) collective-permute-start(f32[8,4,4096]{2,1,0:T(4,128)} %pad_maximum_fusion.22), channel_id=1, source_target_pairs={{0,1},{1,2},{2,3},{3,4},{4,5},{5,6},{6,7},{7,8},{8,9},{9,10},{10,1... | collective-permute-start | bytes 1572872 | tf_op jit(solution)/shard_map/ppermute | solution.py:58
  14.3 2.8 %copy-start.27 = (s32[8,2]{0,1:T(2,128)S(1)}, s32[8,2]{0,1:T(2,128)}, u32[]{:S(2)}) copy-start(s32[8,2]{0,1:T(2,128)} %param.5) | copy-start | bytes 196
  27.8 6.6 %copy-start.32 = (s32[8]{0:T(128)}, s32[8]{0:T(128)S(1)}, u32[]{:S(2)}) copy-start(s32[8]{0:T(128)S(1)} %get-tuple-element.109) | copy-start | bytes 100
  32.5 2.2 copy-start.1
  33.7 1.9 copy-start.2
  39.0 12.3 %slice-start = ((s8[6291456]{0:T(1024)(128)(4,1)}), s8[4194304]{0:T(1024)(128)(4,1)S(1)}, s32[]{:S(2)}) async-start(s8[6291456]{0:T(1024)(128)(4,1)} %bitcast.181), calls=%async_computation | async-start | bytes 8388608
  39.1 1.6 copy-start.4
  39.1 12.2 %slice-start.1 = ((s8[6291456]{0:T(1024)(128)(4,1)}), s8[2097152]{0:T(1024)(128)(4,1)S(1)}, s32[]{:S(2)}) async-start(s8[6291456]{0:T(1024)(128)(4,1)} %bitcast.181), calls=%async_computation.1 | async-start | bytes 4194304
  41.3 19.0 %collective-permute-start.3 = (f32[8,3,6,768]{3,0,2,1:T(8,128)S(1)}, f32[8,3,6,768]{3,0,2,1:T(8,128)S(1)}, u32[]{:S(2)}, u32[]{:S(2)}) collective-permute-start(f32[8,3,6,768]{3,0,2,1:T(8,128)S(1)} %get-tuple-element.52), channel_id=1, source_target_pairs={{1,0},{2,1},{3,2},{4,3},{5,4},{6,5},{7,6},{8,7},{9,8},{10,9},{11,1... | collective-permute-start | bytes 1327112 | tf_op jit(solution)/shard_map/ppermute | solution.py:29
  46.9 19.1 %collective-permute-start.2 = (f32[8,3,6,768]{3,0,2,1:T(8,128)S(1)}, f32[8,3,6,768]{3,0,2,1:T(8,128)S(1)}, u32[]{:S(2)}, u32[]{:S(2)}) collective-permute-start(f32[8,3,6,768]{3,0,2,1:T(8,128)S(1)} %get-tuple-element.51), channel_id=1, source_target_pairs={{0,1},{1,2},{2,3},{3,4},{4,5},{5,6},{6,7},{7,8},{8,9},{9,10},{10,1... | collective-permute-start | bytes 1327112 | tf_op jit(solution)/shard_map/ppermute | solution.py:27
  53.2 4.1 %copy-start.36 = (pred[258]{0:T(512)(128)(4,1)S(1)}, pred[258]{0:T(512)(128)(4,1)}, u32[]{:S(2)}) copy-start(pred[258]{0:T(512)(128)(4,1)} %get-tuple-element.132) | copy-start | bytes 778
  53.2 4.1 %copy-start.37 = (pred[258]{0:T(512)(128)(4,1)S(1)}, pred[258]{0:T(512)(128)(4,1)}, u32[]{:S(2)}) copy-start(pred[258]{0:T(512)(128)(4,1)} %get-tuple-element.133) | copy-start | bytes 778
  53.2 4.1 %copy-start.38 = (pred[258]{0:T(512)(128)(4,1)S(1)}, pred[258]{0:T(512)(128)(4,1)}, u32[]{:S(2)}) copy-start(pred[258]{0:T(512)(128)(4,1)} %get-tuple-element.134) | copy-start | bytes 778
  53.2 4.1 %copy-start.39 = (pred[258]{0:T(512)(128)(4,1)S(1)}, pred[258]{0:T(512)(128)(4,1)}, u32[]{:S(2)}) copy-start(pred[258]{0:T(512)(128)(4,1)} %get-tuple-element.135) | copy-start | bytes 778
  53.2 4.1 %copy-start.40 = (pred[2]{0:T(512)(128)(4,1)S(1)}, pred[2]{0:T(512)(128)(4,1)}, u32[]{:S(2)}) copy-start(pred[2]{0:T(512)(128)(4,1)} %get-tuple-element.130) | copy-start | bytes 10
  53.2 4.1 %copy-start.41 = (pred[2]{0:T(512)(128)(4,1)S(1)}, pred[2]{0:T(512)(128)(4,1)}, u32[]{:S(2)}) copy-start(pred[2]{0:T(512)(128)(4,1)} %get-tuple-element.131) | copy-start | bytes 10
  54.0 2.7 %copy-start.3 = (f32[8,3,16,4096]{3,2,1,0:T(8,128)}, f32[8,3,16,4096]{3,2,1,0:T(8,128)S(1)}, u32[]{:S(2)}) copy-start(f32[8,3,16,4096]{3,2,1,0:T(8,128)S(1)} %pad_maximum_fusion) | copy-start | bytes 18874372
  57.3 8.7 %copy-start.11 = (f32[48,258]{1,0:T(8,128)}, f32[48,258]{1,0:T(8,128)S(1)}, u32[]{:S(2)}) copy-start(f32[48,258]{1,0:T(8,128)S(1)} %reshape.798) | copy-start | bytes 148612
  60.2 5.8 %copy-start.13 = (f32[2,8,3,16]{3,0,2,1:T(2,128)}, f32[2,8,3,16]{3,0,2,1:T(2,128)S(1)}, u32[]{:S(2)}) copy-start(f32[2,8,3,16]{3,0,2,1:T(2,128)S(1)} %fusion.89) | copy-start | bytes 9220
  66.1 21.5 %copy-start.31 = (f32[770]{0:T(1024)S(1)}, f32[770]{0:T(1024)}, u32[]{:S(2)}) copy-start(f32[770]{0:T(1024)} %convert_multiply_fusion) | copy-start | bytes 9244
  66.1 22.1 %copy-start.30 = (f32[770]{0:T(1024)S(1)}, f32[770]{0:T(1024)}, u32[]{:S(2)}) copy-start(f32[770]{0:T(1024)} %convert_multiply_fusion.1) | copy-start | bytes 9244
  66.2 22.8 %copy-start.29 = (s32[770]{0:T(1024)S(1)}, s32[770]{0:T(1024)}, u32[]{:S(2)}) copy-start(s32[770]{0:T(1024)} %broadcast_add_fusion.2) | copy-start | bytes 9244
  66.2 23.4 %copy-start.28 = (s32[770]{0:T(1024)S(1)}, s32[770]{0:T(1024)}, u32[]{:S(2)}) copy-start(s32[770]{0:T(1024)} %add_select_fusion.2) | copy-start | bytes 9244
  66.2 28.4 %copy-start.12 = (f32[48,258]{1,0:T(8,128)S(1)}, f32[48,258]{1,0:T(8,128)}, u32[]{:S(2)}) copy-start(f32[48,258]{1,0:T(8,128)} %copy-done.11) | copy-start | bytes 148612
  68.1 16.1 %collective-permute-start.4 = (f32[48,274]{1,0:T(8,128)S(1)}, f32[48,274]{1,0:T(8,128)S(1)}, u32[]{:S(2)}, u32[]{:S(2)}) collective-permute-start(f32[48,274]{1,0:T(8,128)S(1)} %pad_maximum_fusion.23), channel_id=1, source_target_pairs={{0,7},{1,8},{2,9},{3,10},{4,11},{5,12},{6,13},{7,14},{8,15},{9,16}... | collective-permute-start | bytes 157832 | tf_op jit(solution)/shard_map/ppermute | solution.py:144
  71.6 14.9 %collective-permute-start.5 = (f32[48,274]{1,0:T(8,128)S(1)}, f32[48,274]{1,0:T(8,128)S(1)}, u32[]{:S(2)}, u32[]{:S(2)}) collective-permute-start(f32[48,274]{1,0:T(8,128)S(1)} %pad_maximum_fusion.23), channel_id=1, source_target_pairs={{0,6},{1,7},{2,8},{3,9},{4,10},{5,11},{6,12},{7,13},{8,14},{9,15},... | collective-permute-start | bytes 157832 | tf_op jit(solution)/shard_map/ppermute | solution.py:144
  72.3 19.2 %collective-permute-start.6 = (f32[48,274]{1,0:T(8,128)S(1)}, f32[48,274]{1,0:T(8,128)S(1)}, u32[]{:S(2)}, u32[]{:S(2)}) collective-permute-start(f32[48,274]{1,0:T(8,128)S(1)} %pad_maximum_fusion.23), channel_id=1, source_target_pairs={{0,5},{1,6},{2,7},{3,8},{4,9},{5,10},{6,11},{7,12},{8,13},{9,14},{... | collective-permute-start | bytes 157832 | tf_op jit(solution)/shard_map/ppermute | solution.py:144
  79.4 12.7 %collective-permute-start.7 = (f32[48,274]{1,0:T(8,128)S(1)}, f32[48,274]{1,0:T(8,128)S(1)}, u32[]{:S(2)}, u32[]{:S(2)}) collective-permute-start(f32[48,274]{1,0:T(8,128)S(1)} %pad_maximum_fusion.23), channel_id=1, source_target_pairs={{0,4},{1,5},{2,6},{3,7},{4,8},{5,9},{6,10},{7,11},{8,12},{9,13},{1... | collective-permute-start | bytes 157832 | tf_op jit(solution)/shard_map/ppermute | solution.py:144
  79.4 13.3 %collective-permute-start.8 = (f32[48,274]{1,0:T(8,128)S(1)}, f32[48,274]{1,0:T(8,128)S(1)}, u32[]{:S(2)}, u32[]{:S(2)}) collective-permute-start(f32[48,274]{1,0:T(8,128)S(1)} %pad_maximum_fusion.23), channel_id=1, source_target_pairs={{0,3},{1,4},{2,5},{3,6},{4,7},{5,8},{6,9},{7,10},{8,11},{9,12},{10... | collective-permute-start | bytes 157832 | tf_op jit(solution)/shard_map/ppermute | solution.py:144
  84.1 9.2 %collective-permute-start.9 = (f32[48,274]{1,0:T(8,128)S(1)}, f32[48,274]{1,0:T(8,128)S(1)}, u32[]{:S(2)}, u32[]{:S(2)}) collective-permute-start(f32[48,274]{1,0:T(8,128)S(1)} %pad_maximum_fusion.23), channel_id=1, source_target_pairs={{0,2},{1,3},{2,4},{3,5},{4,6},{5,7},{6,8},{7,9},{8,10},{9,11},{10,... | collective-permute-start | bytes 157832 | tf_op jit(solution)/shard_map/ppermute | solution.py:144
  86.6 7.4 %collective-permute-start.10 = (f32[48,274]{1,0:T(8,128)S(1)}, f32[48,274]{1,0:T(8,128)S(1)}, u32[]{:S(2)}, u32[]{:S(2)}) collective-permute-start(f32[48,274]{1,0:T(8,128)S(1)} %pad_maximum_fusion.23), channel_id=1, source_target_pairs={{0,1},{1,2},{2,3},{3,4},{4,5},{5,6},{6,7},{7,8},{8,9},{9,10},{10,1... | collective-permute-start | bytes 157832 | tf_op jit(solution)/shard_map/ppermute | solution.py:144
  97.2 14.5 %collective-permute-start.11 = (f32[48,386]{1,0:T(8,128)}, f32[48,386]{1,0:T(8,128)S(1)}, u32[]{:S(2)}, u32[]{:S(2)}) collective-permute-start(f32[48,386]{1,0:T(8,128)} %concatenate.252), channel_id=1, source_target_pairs={{0,24},{1,25},{2,26},{3,27},{4,28},{5,29},{6,30},{7,31},{8,0},{9,1... | collective-permute-start | bytes 222344 | tf_op jit(solution)/shard_map/ppermute | solution.py:144
  97.6 14.7 %collective-permute-start.12 = (f32[48,386]{1,0:T(8,128)}, f32[48,386]{1,0:T(8,128)S(1)}, u32[]{:S(2)}, u32[]{:S(2)}) collective-permute-start(f32[48,386]{1,0:T(8,128)} %concatenate.252), channel_id=1, source_target_pairs={{0,16},{1,17},{2,18},{3,19},{4,20},{5,21},{6,22},{7,23},{8,24},{9,... | collective-permute-start | bytes 222344 | tf_op jit(solution)/shard_map/ppermute | solution.py:144
  100.8 12.1 %collective-permute-start.13 = (f32[48,386]{1,0:T(8,128)}, f32[48,386]{1,0:T(8,128)S(1)}, u32[]{:S(2)}, u32[]{:S(2)}) collective-permute-start(f32[48,386]{1,0:T(8,128)} %concatenate.252), channel_id=1, source_target_pairs={{0,8},{1,9},{2,10},{3,11},{4,12},{5,13},{6,14},{7,15},{8,16},{9,17... | collective-permute-start | bytes 222344 | tf_op jit(solution)/shard_map/ppermute | solution.py:144
  111.6 1.3 copy-start.24
  124.0 1.7 copy-start.14
  124.0 1.7 copy-start.16
  124.0 1.7 copy-start.18
  124.0 1.7 copy-start.20
  143.1 1.2 copy-start.6
  143.1 1.2 copy-start.7
  143.1 1.2 copy-start.8
  143.1 1.2 copy-start.22
  143.2 1.2 copy-start.23
  145.2 1.0 copy-start.10
  145.2 1.0 copy-start.15
  149.4 1.4 copy-start.5
  149.5 4.3 %copy-start.42 = (s32[8]{0:T(128)S(1)}, s32[8]{0:T(128)}, u32[]{:S(2)}) copy-start(s32[8]{0:T(128)} %get-tuple-element.9) | copy-start | bytes 100
  150.8 53.6 %copy-start.43 = (pred[8]{0:T(512)(128)(4,1)S(1)}, pred[8]{0:T(512)(128)(4,1)}, u32[]{:S(2)}) copy-start(pred[8]{0:T(512)(128)(4,1)} %get-tuple-element.8) | copy-start | bytes 28
  150.8 55.7 %copy-start.33 = (s32[8]{0:T(128)S(1)}, s32[8]{0:T(128)}, u32[]{:S(2)}) copy-start(s32[8]{0:T(128)} %copy-done.32) | copy-start | bytes 100
  150.8 55.7 %copy-start.35 = (s32[16]{0:T(128)S(1)}, s32[16]{0:T(128)}, u32[]{:S(2)}) copy-start(s32[16]{0:T(128)} %copy-done.34) | copy-start | bytes 196
  151.0 8.9 %collective-permute-start.14 = (f32[8,3,8,256]{3,1,0,2:T(4,128)S(1)}, f32[8,3,8,256]{3,1,0,2:T(4,128)S(1)}, u32[]{:S(2)}, u32[]{:S(2)}) collective-permute-start(f32[8,3,8,256]{3,1,0,2:T(4,128)S(1)} %copy_multiply_fusion), channel_id=1, source_target_pairs={{0,1},{1,2},{2,3},{3,4},{4,5},{5,6},{6,7},{7,8},{8,9},{9,10},{10,1... | collective-permute-start | bytes 589832 | tf_op jit(solution)/shard_map/ppermute | solution.py:214
  160.2 10.7 %collective-permute-start.15 = (f32[8,3,8,256]{3,1,0,2:T(4,128)S(1)}, f32[8,3,8,256]{3,1,0,2:T(4,128)S(1)}, u32[]{:S(2)}, u32[]{:S(2)}) collective-permute-start(f32[8,3,8,256]{3,1,0,2:T(4,128)S(1)} %broadcast_select_fusion.2), channel_id=1, source_target_pairs={{0,2},{1,3},{2,4},{3,5},{4,6},{5,7},{6,8},{7,9},{8,10},{9,11},{10,... | collective-permute-start | bytes 589832 | tf_op jit(solution)/shard_map/ppermute | solution.py:214
  171.0 8.2 %collective-permute-start.16 = (f32[8,3,8,256]{3,1,0,2:T(4,128)S(1)}, f32[8,3,8,256]{3,1,0,2:T(4,128)S(1)}, u32[]{:S(2)}, u32[]{:S(2)}) collective-permute-start(f32[8,3,8,256]{3,1,0,2:T(4,128)S(1)} %broadcast_select_fusion.3), channel_id=1, source_target_pairs={{0,4},{1,5},{2,6},{3,7},{4,8},{5,9},{6,10},{7,11},{8,12},{9,13},{1... | collective-permute-start | bytes 589832 | tf_op jit(solution)/shard_map/ppermute | solution.py:214
  179.4 9.2 %collective-permute-start.17 = (f32[8,3,8,256]{3,1,0,2:T(4,128)S(1)}, f32[8,3,8,256]{3,1,0,2:T(4,128)S(1)}, u32[]{:S(2)}, u32[]{:S(2)}) collective-permute-start(f32[8,3,8,256]{3,1,0,2:T(4,128)S(1)} %broadcast_select_fusion.4), channel_id=1, source_target_pairs={{0,8},{1,9},{2,10},{3,11},{4,12},{5,13},{6,14},{7,15},{8,16},{9,17... | collective-permute-start | bytes 589832 | tf_op jit(solution)/shard_map/ppermute | solution.py:214
  188.7 15.6 %collective-permute-start.18 = (f32[8,3,8,256]{3,1,0,2:T(4,128)S(1)}, f32[8,3,8,256]{3,1,0,2:T(4,128)S(1)}, u32[]{:S(2)}, u32[]{:S(2)}) collective-permute-start(f32[8,3,8,256]{3,1,0,2:T(4,128)S(1)} %broadcast_select_fusion.5), channel_id=1, source_target_pairs={{0,16},{1,17},{2,18},{3,19},{4,20},{5,21},{6,22},{7,23},{8,24},{9,... | collective-permute-start | bytes 589832 | tf_op jit(solution)/shard_map/ppermute | solution.py:214
  204.5 18.2 %collective-permute-start.23 = (f32[8,3,8,256]{3,1,0,2:T(4,128)S(1)}, f32[8,3,8,256]{3,1,0,2:T(4,128)S(1)}, u32[]{:S(2)}, u32[]{:S(2)}) collective-permute-start(f32[8,3,8,256]{3,1,0,2:T(4,128)S(1)} %broadcast_select_fusion.6), channel_id=1, source_target_pairs={{1,0},{3,1},{5,2},{7,3},{9,4},{11,5},{13,6},{15,7},{17,8},{19,9},{... | collective-permute-start | bytes 589832 | tf_op jit(solution)/shard_map/ppermute | solution.py:225
  205.2 18.8 %collective-permute-start.24 = (f32[8,3,8,256]{3,1,0,2:T(4,128)S(1)}, f32[8,3,8,256]{3,1,0,2:T(4,128)S(1)}, u32[]{:S(2)}, u32[]{:S(2)}) collective-permute-start(f32[8,3,8,256]{3,1,0,2:T(4,128)S(1)} %broadcast_select_fusion.6), channel_id=1, source_target_pairs={{1,16},{3,17},{5,18},{7,19},{9,20},{11,21},{13,22},{15,23},{17,24}... | collective-permute-start | bytes 589832 | tf_op jit(solution)/shard_map/ppermute | solution.py:225
  206.6 17.5 %collective-permute-start.21 = (f32[8,3,8,256]{3,1,0,2:T(4,128)S(1)}, f32[8,3,8,256]{3,1,0,2:T(4,128)S(1)}, u32[]{:S(2)}, u32[]{:S(2)}) collective-permute-start(f32[8,3,8,256]{3,1,0,2:T(4,128)S(1)} %broadcast_select_fusion.6), channel_id=1, source_target_pairs={{0,0},{2,1},{4,2},{6,3},{8,4},{10,5},{12,6},{14,7},{16,8},{18,9},{... | collective-permute-start | bytes 589832 | tf_op jit(solution)/shard_map/ppermute | solution.py:225
  220.1 12.0 %collective-permute-start.22 = (f32[8,3,8,256]{3,1,0,2:T(4,128)S(1)}, f32[8,3,8,256]{3,1,0,2:T(4,128)S(1)}, u32[]{:S(2)}, u32[]{:S(2)}) collective-permute-start(f32[8,3,8,256]{3,1,0,2:T(4,128)S(1)} %broadcast_select_fusion.6), channel_id=1, source_target_pairs={{0,16},{2,17},{4,18},{6,19},{8,20},{10,21},{12,22},{14,23},{16,24}... | collective-permute-start | bytes 589832 | tf_op jit(solution)/shard_map/ppermute | solution.py:225
  222.1 10.1 %collective-permute-start.19 = (f32[8,3,8,256]{3,1,0,2:T(4,128)S(1)}, f32[8,3,8,256]{3,1,0,2:T(4,128)S(1)}, u32[]{:S(2)}, u32[]{:S(2)}) collective-permute-start(f32[8,3,8,256]{3,1,0,2:T(4,128)S(1)} %broadcast_select_fusion.6), channel_id=1, source_target_pairs={{31,0},{1,1},{3,2},{5,3},{7,4},{9,5},{11,6},{13,7},{15,8},{17,9},{... | collective-permute-start | bytes 589832 | tf_op jit(solution)/shard_map/ppermute | solution.py:225
  222.8 19.9 %collective-permute-start.20 = (f32[8,3,8,256]{3,1,0,2:T(4,128)S(1)}, f32[8,3,8,256]{3,1,0,2:T(4,128)S(1)}, u32[]{:S(2)}, u32[]{:S(2)}) collective-permute-start(f32[8,3,8,256]{3,1,0,2:T(4,128)S(1)} %broadcast_select_fusion.6), channel_id=1, source_target_pairs={{31,16},{1,17},{3,18},{5,19},{7,20},{9,21},{11,22},{13,23},{15,24}... | collective-permute-start | bytes 589832 | tf_op jit(solution)/shard_map/ppermute | solution.py:225
  (7 other events, 5.6 us)

commit v8 on v6

--- a/solution.py
+++ b/solution.py
@@ -135,8 +135,6 @@
     while reach < bands:
         count = min(8, bands // reach)
         payload = jnp.concatenate([blocks, sums], axis=1)
-        if reach == 1:
-            nest_state, payload = lax.optimization_barrier((nest_state, payload))
         width = blocks.shape[1]
         recvs = [
             lax.ppermute(payload, "band", [(i, (i + k * reach) % bands) for i in range(bands)])

time: 220 us -> 248 us (1.13)
  local copies, waits for them, and re-layouts: 44.1 us -> 65 us
  waiting for transfers between devices: 59.3 us -> 46.5 us
  other arithmetic: 21.1 us -> 31.9 us
  starting transfers between devices: 61.1 us -> 67.8 us
    concatenate x11, local copies, waits for them, and re-layouts: 0.36 us -> 8.07 us  [per_device(): jnp.concatenate([got[:, :width] for got in recvs] + [blocks], axis=1)]
    ppermute x1, waiting for transfers between devices: 5.3 us -> 0.01 us  [with_halo(): lax.ppermute(tail, 'band', shift_pairs(count, 1))]
    select_n x6, other arithmetic: 3.93 us -> 9.1 us  [fix(): jnp.where(is_south, ends[:, f, 0][:, None, :], jnp.where(is_north, ends[:...]
    ppermute x1, waiting for transfers between devices: 2.82 us -> 0.01 us  [parent_step(): prev = lax.ppermute(tail, 'band', shift_pairs(count, 1))]
    another operation x2, local copies, waits for them, and re-layouts: 0.3 us -> 2.98 us  [dx(): west_col = side_ext[:, f, 0][:, :, None]]
    unnamed x57 -> x131, local copies, waits for them, and re-layouts: 4.3 us -> 6.98 us
    slice x5, local copies, waits for them, and re-layouts: 1.61 us -> 4.11 us  [dx(): right = jnp.concatenate([field[:, :, 1:], east_col], axis=2)]
    slice x6, local copies, waits for them, and re-layouts: 0.84 us -> 3.34 us  [dy(): up = jnp.concatenate([field[:, 1:], zero], axis=1)]
  transfers between devices with their start and end apart: 25 -> 25, of which waited for: 10 -> 7; matrix products, arithmetic and copies ran while one was open for 10% -> 17% of each run, Pallas kernels for 0% -> 0%
where the time goes in v8:
time: 248 us; the launch traced here: 246 us
  starting transfers between devices  67.8 us (27%)
  local copies, waits for them, and re-layouts  65 us (26%)
  waiting for transfers between devices  46.5 us (19%)
  other arithmetic  31.9 us (13%)
  between operations  27.1 us (11%)
  matrix products  7.93 us (3%)
    ppermute x5, waiting for transfers between devices, per_device(): lax.ppermute(moved, 'band', [(i, (i + step) % bands) for i in range(bands)])  28.2 us
    ppermute x10, starting transfers between devices, per_device(): lax.ppermute(payload, 'band', [(i, (i + k * reach) % bands) for i in rang...  21.9 us
    ppermute x6, waiting for transfers between devices, per_device(): got.append(lax.ppermute(moved, 'band', pairs))  18.3 us
    ppermute x6, starting transfers between devices, per_device(): got.append(lax.ppermute(moved, 'band', pairs))  17.8 us
    dynamic_update_slice x8, local copies, waits for them, and re-layouts, per_device(): lax.dynamic_update_slice(parent_out, merged[m:m + 1], (m, 0, 0, cols_off[...  15.2 us
    ppermute x5, starting transfers between devices, per_device(): lax.ppermute(moved, 'band', [(i, (i + step) % bands) for i in range(bands)])  10.9 us
    select_n x6, other arithmetic, fix(): jnp.where(is_south, ends[:, f, 0][:, None, :], jnp.where(is_north, ends[:...  9.1 us
    concatenate x11, local copies, waits for them, and re-layouts, per_device(): jnp.concatenate([got[:, :width] for got in recvs] + [blocks], axis=1)  8.07 us
  transfers between devices with their start and end apart: 25, of which 7 were waited for; matrix products, arithmetic and copies ran while one was open for 17% of the time, Pallas kernels for 0%

profile of v8, /device:TPU:112, one launch (start us, length us, event | category | flops | bytes accessed | tf_op | source)
XLA Modules:
  0.0 246.3 jit_solution(2808332859471575244)
XLA Ops:
  0.6 3.3 %slice_bitcast_fusion.4 = (f32[8,16,4096]{2,1,0:T(8,128)S(1)}, f32[8,16,4096]{2,1,0:T(8,128)S(1)}, f32[8,16,4096]{2,1,0:T(8,128)S(1)}) fusion(f32[8,3,16,4096]{3,2,1,0:T(8,128)} %param.3), kind=kLoop, calls=%fused_computation.28 | loop fusion | bytes 12582912 | tf_op jit(solution)/shard_map/squeeze | solution.py:50
  4.6 1.1 pad_maximum_fusion.21
  5.8 4.8 %collective-permute-start = (f32[8,4,4096]{2,1,0:T(4,128)}, f32[8,4,4096]{2,1,0:T(4,128)S(1)}, u32[]{:S(2)}, u32[]{:S(2)}) collective-permute-start(f32[8,4,4096]{2,1,0:T(4,128)} %pad_maximum_fusion.21), channel_id=1, source_target_pairs={{1,0},{2,1},{3,2},{4,3},{5,4},{6,5},{7,6},{8,7},{9,8},{10,9},{11,1... | collective-permute-start | bytes 1572872 | tf_op jit(solution)/shard_map/ppermute | solution.py:59
  10.5 1.1 pad_maximum_fusion.22
  11.7 2.6 %collective-permute-start.1 = (f32[8,4,4096]{2,1,0:T(4,128)}, f32[8,4,4096]{2,1,0:T(4,128)S(1)}, u32[]{:S(2)}, u32[]{:S(2)}) collective-permute-start(f32[8,4,4096]{2,1,0:T(4,128)} %pad_maximum_fusion.22), channel_id=1, source_target_pairs={{0,1},{1,2},{2,3},{3,4},{4,5},{5,6},{6,7},{7,8},{8,9},{9,10},{10,1... | collective-permute-start | bytes 1572872 | tf_op jit(solution)/shard_map/ppermute | solution.py:58
  14.4 0.9 copy.139
  15.3 5.7 %collective-permute-start.3 = (f32[8,3,6,768]{3,0,2,1:T(8,128)}, f32[8,3,6,768]{3,0,2,1:T(8,128)}, u32[]{:S(2)}, u32[]{:S(2)}) collective-permute-start(f32[8,3,6,768]{3,0,2,1:T(8,128)} %copy.139), channel_id=1, source_target_pairs={{1,0},{2,1},{3,2},{4,3},{5,4},{6,5},{7,6},{8,7},{9,8},{10,9},{11,1... | collective-permute-start | bytes 1327112 | tf_op jit(solution)/shard_map/ppermute | solution.py:29
  20.9 0.9 copy.138
  21.9 4.2 %collective-permute-start.2 = (f32[8,3,6,768]{3,0,2,1:T(8,128)}, f32[8,3,6,768]{3,0,2,1:T(8,128)}, u32[]{:S(2)}, u32[]{:S(2)}) collective-permute-start(f32[8,3,6,768]{3,0,2,1:T(8,128)} %copy.138), channel_id=1, source_target_pairs={{0,1},{1,2},{2,3},{3,4},{4,5},{5,6},{6,7},{7,8},{8,9},{9,10},{10,1... | collective-permute-start | bytes 1327112 | tf_op jit(solution)/shard_map/ppermute | solution.py:27
  26.1 2.8 %fusion.129 = (f32[8,16,4095]{2,1,0:T(8,128)}, f32[8,16,4095]{2,1,0:T(8,128)}) fusion(f32[8,16,4096]{2,1,0:T(8,128)S(1)} %get-tuple-element.18), kind=kLoop, calls=%fused_computation.307 | loop fusion | bytes 8386560 | tf_op jit(solution)/shard_map/jit(_roll_static)/slice | solution.py:46
  46.8 0.9 broadcast_select_fusion.1
  47.7 3.7 %fusion.8 = f32[8,16,4096]{2,1,0:T(8,128)S(1)} fusion(f32[8,16,4096]{2,1,0:T(8,128)S(1)} %copy-done.1, f32[8,1,4096]{2,1,0:T(1,128)S(1)} %get-tuple-element.71, f32[8,1,4096]{2,1,0:T(1,128)S(1)} %get-tuple-element.72, f32[8,16,1]{2,1,0:T(8,128)S(1)} %get-tuple-element.32, f32[8,16,4095]{2,1,0:T(8,128)} %get-tuple-element.34, ...), kind=kLoop, calls=%fused_computation.16 | loop fusion | flops 4718592 | bytes 10747904 | tf_op jit(solution)/shard_map/sub | solution.py:61
  52.2 0.9 fusion.4
  53.1 0.9 fusion.12
  55.5 2.0 copy-done.3
  58.1 2.9 %fusion.85 = f32[2,8,3,16]{3,0,2,1:T(2,128)S(1)} fusion(f32[8,3,16,258]{3,2,1,0:T(8,128)S(1)} %dynamic-slice_dynamic-update-slice_fusion, pred[258]{0:T(512)(128)(4,1)S(1)} %copy-done.50, pred[258]{0:T(512)(128)(4,1)S(1)} %copy-done.51, pred[258]{0:T(512)(128)(4,1)S(1)} %copy-done.52, pred[258]{0:T(512)(128)(4,1)S(1)} %copy-done.53, ...), kind=kOutput, calls=%fused_computation.212 | convolution fusion | flops 2383404 | bytes 400396 | tf_op jit(solution)/shard_map/mflq,qs->mfsl/dot_general | solution.py:118
  61.1 3.1 %collective-permute-start.4 = (f32[48,274]{1,0:T(8,128)S(1)}, f32[48,274]{1,0:T(8,128)S(1)}, u32[]{:S(2)}, u32[]{:S(2)}) collective-permute-start(f32[48,274]{1,0:T(8,128)S(1)} %pad_maximum_fusion.23), channel_id=1, source_target_pairs={{0,7},{1,8},{2,9},{3,10},{4,11},{5,12},{6,13},{7,14},{8,15},{9,16}... | collective-permute-start | bytes 157832 | tf_op jit(solution)/shard_map/ppermute | solution.py:140
  64.8 5.5 %collective-permute-start.6 = (f32[48,274]{1,0:T(8,128)S(1)}, f32[48,274]{1,0:T(8,128)S(1)}, u32[]{:S(2)}, u32[]{:S(2)}) collective-permute-start(f32[48,274]{1,0:T(8,128)S(1)} %pad_maximum_fusion.23), channel_id=1, source_target_pairs={{0,5},{1,6},{2,7},{3,8},{4,9},{5,10},{6,11},{7,12},{8,13},{9,14},{... | collective-permute-start | bytes 157832 | tf_op jit(solution)/shard_map/ppermute | solution.py:140
  70.3 2.7 %collective-permute-start.7 = (f32[48,274]{1,0:T(8,128)S(1)}, f32[48,274]{1,0:T(8,128)S(1)}, u32[]{:S(2)}, u32[]{:S(2)}) collective-permute-start(f32[48,274]{1,0:T(8,128)S(1)} %pad_maximum_fusion.23), channel_id=1, source_target_pairs={{0,4},{1,5},{2,6},{3,7},{4,8},{5,9},{6,10},{7,11},{8,12},{9,13},{1... | collective-permute-start | bytes 157832 | tf_op jit(solution)/shard_map/ppermute | solution.py:140
  73.1 6.0 %collective-permute-start.8 = (f32[48,274]{1,0:T(8,128)S(1)}, f32[48,274]{1,0:T(8,128)S(1)}, u32[]{:S(2)}, u32[]{:S(2)}) collective-permute-start(f32[48,274]{1,0:T(8,128)S(1)} %pad_maximum_fusion.23), channel_id=1, source_target_pairs={{0,3},{1,4},{2,5},{3,6},{4,7},{5,8},{6,9},{7,10},{8,11},{9,12},{10... | collective-permute-start | bytes 157832 | tf_op jit(solution)/shard_map/ppermute | solution.py:140
  82.4 2.0 copy.98
  84.3 2.0 copy.96
  87.9 3.2 %collective-permute-start.12 = (f32[48,386]{1,0:T(8,128)}, f32[48,386]{1,0:T(8,128)S(1)}, u32[]{:S(2)}, u32[]{:S(2)}) collective-permute-start(f32[48,386]{1,0:T(8,128)} %concatenate.252), channel_id=1, source_target_pairs={{0,16},{1,17},{2,18},{3,19},{4,20},{5,21},{6,22},{7,23},{8,24},{9,... | collective-permute-start | bytes 222344 | tf_op jit(solution)/shard_map/ppermute | solution.py:140
  91.6 2.2 pad_maximum_fusion.1
  101.4 1.8 concatenate.263
  103.2 1.8 fusion.46
  105.6 1.6 slice_add_fusion
  107.2 1.6 reshape.799
  108.8 1.8 fusion.38
  111.5 1.4 fusion.145
  112.9 1.6 fusion.144
  114.5 1.5 copy.112
  115.9 1.5 copy.111
  117.4 3.7 %select_select_fusion.6 = (f32[8,36,768]{2,1,0:T(8,128)S(1)}, f32[8,36,768]{2,1,0:T(8,128)}) fusion(f32[8,768]{1,0:T(8,128)} %get-tuple-element.82, f32[8,768]{1,0:T(8,128)} %get-tuple-element.81, pred[36]{0:T(512)(128)(4,1)S(1)} %get-tuple-element.130, pred[36]{0:T(512)(128)(4,1)S(1)} %get-tuple-element.131, f32[8,35,768]{2,1,0:T(8,128)} %get-tuple-element.70, ...), kind=kLoop, calls=%fused_computation.83 | loop fusion | flops 1990656 | bytes 6193224 | tf_op jit(solution)/shard_map/jit(_where)/select_n | solution.py:170
  121.1 1.6 fusion.141
  122.7 1.4 fusion.143
  124.1 1.5 copy.114
  125.6 1.5 copy.113
  127.0 3.1 %select_select_fusion.5 = (f32[8,36,768]{2,1,0:T(8,128)S(1)}, f32[8,36,768]{2,1,0:T(8,128)S(1)}, f32[8,36,768]{2,1,0:T(8,128)S(1)}, f32[8,36,768]{2,1,0:T(8,128)S(1)}) fusion(f32[8,768]{1,0:T(8,128)} %copy-done.18, f32[8,768]{1,0:T(8,128)} %copy-done.20, pred[36]{0:T(512)(128)(4,1)S(1)} %get-tuple-element.130, pred[36]{0:T(512)(128)(4,1)S(1)} %get-tuple-element.131, ...), kind=kLoop, calls=%fused_computation.82 | loop fusion | flops 3981312 | bytes 8896584 | tf_op jit(solution)/shard_map/jit(_where)/select_n | solution.py:170
  133.3 0.9 select_select_fusion.1
  136.6 1.1 fusion.44
  138.2 2.4 collective-permute-start.14
  140.6 6.5 %collective-permute-done.14 = f32[8,3,8,256]{3,1,0,2:T(4,128)S(1)} collective-permute-done((f32[8,3,8,256]{3,1,0,2:T(4,128)S(1)}, f32[8,3,8,256]{3,1,0,2:T(4,128)S(1)}, u32[]{:S(2)}, u32[]{:S(2)}) %collective-permute-start.14) | collective-permute-done | bytes 196640 | tf_op jit(solution)/shard_map/ppermute | solution.py:211
  147.3 4.4 %collective-permute-start.15 = (f32[8,3,8,256]{3,1,0,2:T(4,128)S(1)}, f32[8,3,8,256]{3,1,0,2:T(4,128)S(1)}, u32[]{:S(2)}, u32[]{:S(2)}) collective-permute-start(f32[8,3,8,256]{3,1,0,2:T(4,128)S(1)} %broadcast_select_fusion.2), channel_id=1, source_target_pairs={{0,2},{1,3},{2,4},{3,5},{4,6},{5,7},{6,8},{7,9},{8,10},{9,11},{10,... | collective-permute-start | bytes 589832 | tf_op jit(solution)/shard_map/ppermute | solution.py:211
  151.7 6.3 %collective-permute-done.15 = f32[8,3,8,256]{3,1,0,2:T(4,128)S(1)} collective-permute-done((f32[8,3,8,256]{3,1,0,2:T(4,128)S(1)}, f32[8,3,8,256]{3,1,0,2:T(4,128)S(1)}, u32[]{:S(2)}, u32[]{:S(2)}) %collective-permute-start.15) | collective-permute-done | bytes 196640 | tf_op jit(solution)/shard_map/ppermute | solution.py:211
  158.3 7.8 %collective-permute-done.16 = f32[8,3,8,256]{3,1,0,2:T(4,128)S(1)} collective-permute-done((f32[8,3,8,256]{3,1,0,2:T(4,128)S(1)}, f32[8,3,8,256]{3,1,0,2:T(4,128)S(1)}, u32[]{:S(2)}, u32[]{:S(2)}) %collective-permute-start.16) | collective-permute-done | bytes 196640 | tf_op jit(solution)/shard_map/ppermute | solution.py:211
  166.2 1.7 collective-permute-start.17
  167.9 7.7 %collective-permute-done.17 = f32[8,3,8,256]{3,1,0,2:T(4,128)S(1)} collective-permute-done((f32[8,3,8,256]{3,1,0,2:T(4,128)S(1)}, f32[8,3,8,256]{3,1,0,2:T(4,128)S(1)}, u32[]{:S(2)}, u32[]{:S(2)}) %collective-permute-start.17) | collective-permute-done | bytes 196640 | tf_op jit(solution)/shard_map/ppermute | solution.py:211
  175.7 2.2 collective-permute-start.18
  193.8 1.3 collective-permute-start.24
  195.2 12.0 %collective-permute-start.21 = (f32[8,3,8,256]{3,1,0,2:T(4,128)S(1)}, f32[8,3,8,256]{3,1,0,2:T(4,128)S(1)}, u32[]{:S(2)}, u32[]{:S(2)}) collective-permute-start(f32[8,3,8,256]{3,1,0,2:T(4,128)S(1)} %broadcast_select_fusion.6), channel_id=1, source_target_pairs={{0,0},{2,1},{4,2},{6,3},{8,4},{10,5},{12,6},{14,7},{16,8},{18,9},{... | collective-permute-start | bytes 589832 | tf_op jit(solution)/shard_map/ppermute | solution.py:222
  207.2 1.9 collective-permute-start.22
  209.8 1.3 collective-permute-start.20
  211.3 7.9 %collective-permute-done.22 = f32[8,3,8,256]{3,1,0,2:T(4,128)S(1)} collective-permute-done((f32[8,3,8,256]{3,1,0,2:T(4,128)S(1)}, f32[8,3,8,256]{3,1,0,2:T(4,128)S(1)}, u32[]{:S(2)}, u32[]{:S(2)}) %collective-permute-start.22) | collective-permute-done | bytes 196640 | tf_op jit(solution)/shard_map/ppermute | solution.py:222
  219.3 10.3 %collective-permute-done.20 = f32[8,3,8,256]{3,1,0,2:T(4,128)S(1)} collective-permute-done((f32[8,3,8,256]{3,1,0,2:T(4,128)S(1)}, f32[8,3,8,256]{3,1,0,2:T(4,128)S(1)}, u32[]{:S(2)}, u32[]{:S(2)}) %collective-permute-start.20) | collective-permute-done | bytes 196640 | tf_op jit(solution)/shard_map/ppermute | solution.py:222
  230.0 0.9 gather_fusion
  231.1 1.9 dynamic_update_slice.24
  233.0 1.9 dynamic_update_slice.25
  234.9 1.9 dynamic_update_slice.26
  236.8 1.9 dynamic_update_slice.27
  238.7 1.9 dynamic_update_slice.28
  240.6 1.9 dynamic_update_slice.29
  242.5 1.9 dynamic_update_slice.30
  244.4 1.9 dynamic_update_slice.31
  (251 shorter events, 35.2 us)
Async XLA Ops:
  3.9 7.8 %copy-start = (f32[8,16,4096]{2,1,0:T(8,128)}, f32[8,16,4096]{2,1,0:T(8,128)S(1)}, u32[]{:S(2)}) copy-start(f32[8,16,4096]{2,1,0:T(8,128)S(1)} %get-tuple-element.19) | copy-start | bytes 6291460
  3.9 10.3 %copy-start.5 = (f32[8,3,24,768]{3,2,1,0:T(8,128)S(1)}, f32[8,3,24,768]{3,2,1,0:T(8,128)}, u32[]{:S(2)}) copy-start(f32[8,3,24,768]{3,2,1,0:T(8,128)} %param.4) | copy-start | bytes 5308420
  5.8 39.9 %collective-permute-start = (f32[8,4,4096]{2,1,0:T(4,128)}, f32[8,4,4096]{2,1,0:T(4,128)S(1)}, u32[]{:S(2)}, u32[]{:S(2)}) collective-permute-start(f32[8,4,4096]{2,1,0:T(4,128)} %pad_maximum_fusion.21), channel_id=1, source_target_pairs={{1,0},{2,1},{3,2},{4,3},{5,4},{6,5},{7,6},{8,7},{9,8},{10,9},{11,1... | collective-permute-start | bytes 1572872 | tf_op jit(solution)/shard_map/ppermute | solution.py:59
  11.7 34.4 %collective-permute-start.1 = (f32[8,4,4096]{2,1,0:T(4,128)}, f32[8,4,4096]{2,1,0:T(4,128)S(1)}, u32[]{:S(2)}, u32[]{:S(2)}) collective-permute-start(f32[8,4,4096]{2,1,0:T(4,128)} %pad_maximum_fusion.22), channel_id=1, source_target_pairs={{0,1},{1,2},{2,3},{3,4},{4,5},{5,6},{6,7},{7,8},{8,9},{9,10},{10,1... | collective-permute-start | bytes 1572872 | tf_op jit(solution)/shard_map/ppermute | solution.py:58
  15.3 55.1 %collective-permute-start.3 = (f32[8,3,6,768]{3,0,2,1:T(8,128)}, f32[8,3,6,768]{3,0,2,1:T(8,128)}, u32[]{:S(2)}, u32[]{:S(2)}) collective-permute-start(f32[8,3,6,768]{3,0,2,1:T(8,128)} %copy.139), channel_id=1, source_target_pairs={{1,0},{2,1},{3,2},{4,3},{5,4},{6,5},{7,6},{8,7},{9,8},{10,9},{11,1... | collective-permute-start | bytes 1327112 | tf_op jit(solution)/shard_map/ppermute | solution.py:29
  21.9 51.2 %collective-permute-start.2 = (f32[8,3,6,768]{3,0,2,1:T(8,128)}, f32[8,3,6,768]{3,0,2,1:T(8,128)}, u32[]{:S(2)}, u32[]{:S(2)}) collective-permute-start(f32[8,3,6,768]{3,0,2,1:T(8,128)} %copy.138), channel_id=1, source_target_pairs={{0,1},{1,2},{2,3},{3,4},{4,5},{5,6},{6,7},{7,8},{8,9},{9,10},{10,1... | collective-permute-start | bytes 1327112 | tf_op jit(solution)/shard_map/ppermute | solution.py:27
  26.1 2.8 %copy-start.41 = (s32[8,2]{0,1:T(2,128)S(1)}, s32[8,2]{0,1:T(2,128)}, u32[]{:S(2)}) copy-start(s32[8,2]{0,1:T(2,128)} %param.5) | copy-start | bytes 196
  39.6 8.0 %copy-start.46 = (s32[8]{0:T(128)}, s32[8]{0:T(128)S(1)}, u32[]{:S(2)}) copy-start(s32[8]{0:T(128)S(1)} %get-tuple-element.103) | copy-start | bytes 100
  44.8 1.9 copy-start.1
  46.8 5.4 %slice-start = ((s8[6291456]{0:T(1024)(128)(4,1)}), s8[4194304]{0:T(1024)(128)(4,1)S(1)}, s32[]{:S(2)}) async-start(s8[6291456]{0:T(1024)(128)(4,1)} %bitcast.177), calls=%async_computation | async-start | bytes 8388608
  47.6 4.5 %slice-start.1 = ((s8[6291456]{0:T(1024)(128)(4,1)}), s8[2097152]{0:T(1024)(128)(4,1)S(1)}, s32[]{:S(2)}) async-start(s8[6291456]{0:T(1024)(128)(4,1)} %bitcast.177), calls=%async_computation.1 | async-start | bytes 4194304
  54.0 4.1 %copy-start.50 = (pred[258]{0:T(512)(128)(4,1)S(1)}, pred[258]{0:T(512)(128)(4,1)}, u32[]{:S(2)}) copy-start(pred[258]{0:T(512)(128)(4,1)} %get-tuple-element.126) | copy-start | bytes 778
  54.0 4.1 %copy-start.51 = (pred[258]{0:T(512)(128)(4,1)S(1)}, pred[258]{0:T(512)(128)(4,1)}, u32[]{:S(2)}) copy-start(pred[258]{0:T(512)(128)(4,1)} %get-tuple-element.127) | copy-start | bytes 778
  54.0 4.1 %copy-start.52 = (pred[258]{0:T(512)(128)(4,1)S(1)}, pred[258]{0:T(512)(128)(4,1)}, u32[]{:S(2)}) copy-start(pred[258]{0:T(512)(128)(4,1)} %get-tuple-element.128) | copy-start | bytes 778
  54.0 4.1 %copy-start.53 = (pred[258]{0:T(512)(128)(4,1)S(1)}, pred[258]{0:T(512)(128)(4,1)}, u32[]{:S(2)}) copy-start(pred[258]{0:T(512)(128)(4,1)} %get-tuple-element.129) | copy-start | bytes 778
  54.0 4.1 %copy-start.54 = (pred[2]{0:T(512)(128)(4,1)S(1)}, pred[2]{0:T(512)(128)(4,1)}, u32[]{:S(2)}) copy-start(pred[2]{0:T(512)(128)(4,1)} %get-tuple-element.124) | copy-start | bytes 10
  54.0 4.1 %copy-start.55 = (pred[2]{0:T(512)(128)(4,1)S(1)}, pred[2]{0:T(512)(128)(4,1)}, u32[]{:S(2)}) copy-start(pred[2]{0:T(512)(128)(4,1)} %get-tuple-element.125) | copy-start | bytes 10
  54.7 2.7 %copy-start.3 = (f32[8,3,16,4096]{3,2,1,0:T(8,128)}, f32[8,3,16,4096]{3,2,1,0:T(8,128)S(1)}, u32[]{:S(2)}) copy-start(f32[8,3,16,4096]{3,2,1,0:T(8,128)S(1)} %pad_maximum_fusion) | copy-start | bytes 18874372
  54.7 25.0 %copy-start.45 = (f32[770]{0:T(1024)S(1)}, f32[770]{0:T(1024)}, u32[]{:S(2)}) copy-start(f32[770]{0:T(1024)} %convert_multiply_fusion) | copy-start | bytes 9244
  54.8 25.6 %copy-start.44 = (f32[770]{0:T(1024)S(1)}, f32[770]{0:T(1024)}, u32[]{:S(2)}) copy-start(f32[770]{0:T(1024)} %convert_multiply_fusion.1) | copy-start | bytes 9244
  54.8 26.3 %copy-start.43 = (s32[770]{0:T(1024)S(1)}, s32[770]{0:T(1024)}, u32[]{:S(2)}) copy-start(s32[770]{0:T(1024)} %broadcast_add_fusion.2) | copy-start | bytes 9244
  54.8 26.9 %copy-start.42 = (s32[770]{0:T(1024)S(1)}, s32[770]{0:T(1024)}, u32[]{:S(2)}) copy-start(s32[770]{0:T(1024)} %add_select_fusion.2) | copy-start | bytes 9244
  61.0 30.1 %copy-start.12 = (f32[2,8,3,16]{3,0,2,1:T(2,128)}, f32[2,8,3,16]{3,0,2,1:T(2,128)S(1)}, u32[]{:S(2)}) copy-start(f32[2,8,3,16]{3,0,2,1:T(2,128)S(1)} %fusion.85) | copy-start | bytes 9220
  61.1 18.0 %collective-permute-start.4 = (f32[48,274]{1,0:T(8,128)S(1)}, f32[48,274]{1,0:T(8,128)S(1)}, u32[]{:S(2)}, u32[]{:S(2)}) collective-permute-start(f32[48,274]{1,0:T(8,128)S(1)} %pad_maximum_fusion.23), channel_id=1, source_target_pairs={{0,7},{1,8},{2,9},{3,10},{4,11},{5,12},{6,13},{7,14},{8,15},{9,16}... | collective-permute-start | bytes 157832 | tf_op jit(solution)/shard_map/ppermute | solution.py:140
  64.2 14.8 %collective-permute-start.5 = (f32[48,274]{1,0:T(8,128)S(1)}, f32[48,274]{1,0:T(8,128)S(1)}, u32[]{:S(2)}, u32[]{:S(2)}) collective-permute-start(f32[48,274]{1,0:T(8,128)S(1)} %pad_maximum_fusion.23), channel_id=1, source_target_pairs={{0,6},{1,7},{2,8},{3,9},{4,10},{5,11},{6,12},{7,13},{8,14},{9,15},... | collective-permute-start | bytes 157832 | tf_op jit(solution)/shard_map/ppermute | solution.py:140
  64.8 21.5 %collective-permute-start.6 = (f32[48,274]{1,0:T(8,128)S(1)}, f32[48,274]{1,0:T(8,128)S(1)}, u32[]{:S(2)}, u32[]{:S(2)}) collective-permute-start(f32[48,274]{1,0:T(8,128)S(1)} %pad_maximum_fusion.23), channel_id=1, source_target_pairs={{0,5},{1,6},{2,7},{3,8},{4,9},{5,10},{6,11},{7,12},{8,13},{9,14},{... | collective-permute-start | bytes 157832 | tf_op jit(solution)/shard_map/ppermute | solution.py:140
  70.3 16.0 %collective-permute-start.7 = (f32[48,274]{1,0:T(8,128)S(1)}, f32[48,274]{1,0:T(8,128)S(1)}, u32[]{:S(2)}, u32[]{:S(2)}) collective-permute-start(f32[48,274]{1,0:T(8,128)S(1)} %pad_maximum_fusion.23), channel_id=1, source_target_pairs={{0,4},{1,5},{2,6},{3,7},{4,8},{5,9},{6,10},{7,11},{8,12},{9,13},{1... | collective-permute-start | bytes 157832 | tf_op jit(solution)/shard_map/ppermute | solution.py:140
  73.1 13.3 %collective-permute-start.8 = (f32[48,274]{1,0:T(8,128)S(1)}, f32[48,274]{1,0:T(8,128)S(1)}, u32[]{:S(2)}, u32[]{:S(2)}) collective-permute-start(f32[48,274]{1,0:T(8,128)S(1)} %pad_maximum_fusion.23), channel_id=1, source_target_pairs={{0,3},{1,4},{2,5},{3,6},{4,7},{5,8},{6,9},{7,10},{8,11},{9,12},{10... | collective-permute-start | bytes 157832 | tf_op jit(solution)/shard_map/ppermute | solution.py:140
  79.1 7.4 %collective-permute-start.9 = (f32[48,274]{1,0:T(8,128)S(1)}, f32[48,274]{1,0:T(8,128)S(1)}, u32[]{:S(2)}, u32[]{:S(2)}) collective-permute-start(f32[48,274]{1,0:T(8,128)S(1)} %pad_maximum_fusion.23), channel_id=1, source_target_pairs={{0,2},{1,3},{2,4},{3,5},{4,6},{5,7},{6,8},{7,9},{8,10},{9,11},{10,... | collective-permute-start | bytes 157832 | tf_op jit(solution)/shard_map/ppermute | solution.py:140
  79.1 7.4 %collective-permute-start.10 = (f32[48,274]{1,0:T(8,128)S(1)}, f32[48,274]{1,0:T(8,128)S(1)}, u32[]{:S(2)}, u32[]{:S(2)}) collective-permute-start(f32[48,274]{1,0:T(8,128)S(1)} %pad_maximum_fusion.23), channel_id=1, source_target_pairs={{0,1},{1,2},{2,3},{3,4},{4,5},{5,6},{6,7},{7,8},{8,9},{9,10},{10,1... | collective-permute-start | bytes 157832 | tf_op jit(solution)/shard_map/ppermute | solution.py:140
  86.3 4.8 %copy-start.26 = (f32[48,16]{1,0:T(8,128)}, f32[48,16]{1,0:T(8,128)S(1)}, u32[]{:S(2)}) copy-start(f32[48,16]{1,0:T(8,128)S(1)} %slice.577) | copy-start | bytes 9220
  86.3 4.8 %copy-start.24 = (f32[48,16]{1,0:T(8,128)}, f32[48,16]{1,0:T(8,128)S(1)}, u32[]{:S(2)}) copy-start(f32[48,16]{1,0:T(8,128)S(1)} %slice.578) | copy-start | bytes 9220
  86.4 4.8 %copy-start.28 = (f32[48,16]{1,0:T(8,128)}, f32[48,16]{1,0:T(8,128)S(1)}, u32[]{:S(2)}) copy-start(f32[48,16]{1,0:T(8,128)S(1)} %slice.579) | copy-start | bytes 9220
  86.4 4.7 %copy-start.30 = (f32[48,16]{1,0:T(8,128)}, f32[48,16]{1,0:T(8,128)S(1)}, u32[]{:S(2)}) copy-start(f32[48,16]{1,0:T(8,128)S(1)} %slice.580) | copy-start | bytes 9220
  86.4 4.7 %copy-start.32 = (f32[48,16]{1,0:T(8,128)}, f32[48,16]{1,0:T(8,128)S(1)}, u32[]{:S(2)}) copy-start(f32[48,16]{1,0:T(8,128)S(1)} %slice.581) | copy-start | bytes 9220
  86.5 4.7 %copy-start.34 = (f32[48,16]{1,0:T(8,128)}, f32[48,16]{1,0:T(8,128)S(1)}, u32[]{:S(2)}) copy-start(f32[48,16]{1,0:T(8,128)S(1)} %slice.582) | copy-start | bytes 9220
  86.5 4.7 %copy-start.36 = (f32[48,16]{1,0:T(8,128)}, f32[48,16]{1,0:T(8,128)S(1)}, u32[]{:S(2)}) copy-start(f32[48,16]{1,0:T(8,128)S(1)} %slice.583) | copy-start | bytes 9220
  86.7 4.5 %copy-start.11 = (f32[48,258]{1,0:T(8,128)}, f32[48,258]{1,0:T(8,128)S(1)}, u32[]{:S(2)}) copy-start(f32[48,258]{1,0:T(8,128)S(1)} %slice_add_fusion.3) | copy-start | bytes 148612
  87.5 11.3 %collective-permute-start.11 = (f32[48,386]{1,0:T(8,128)}, f32[48,386]{1,0:T(8,128)S(1)}, u32[]{:S(2)}, u32[]{:S(2)}) collective-permute-start(f32[48,386]{1,0:T(8,128)} %concatenate.252), channel_id=1, source_target_pairs={{0,24},{1,25},{2,26},{3,27},{4,28},{5,29},{6,30},{7,31},{8,0},{9,1... | collective-permute-start | bytes 222344 | tf_op jit(solution)/shard_map/ppermute | solution.py:140
  87.9 11.6 %collective-permute-start.12 = (f32[48,386]{1,0:T(8,128)}, f32[48,386]{1,0:T(8,128)S(1)}, u32[]{:S(2)}, u32[]{:S(2)}) collective-permute-start(f32[48,386]{1,0:T(8,128)} %concatenate.252), channel_id=1, source_target_pairs={{0,16},{1,17},{2,18},{3,19},{4,20},{5,21},{6,22},{7,23},{8,24},{9,... | collective-permute-start | bytes 222344 | tf_op jit(solution)/shard_map/ppermute | solution.py:140
  91.2 9.0 %collective-permute-start.13 = (f32[48,386]{1,0:T(8,128)}, f32[48,386]{1,0:T(8,128)S(1)}, u32[]{:S(2)}, u32[]{:S(2)}) collective-permute-start(f32[48,386]{1,0:T(8,128)} %concatenate.252), channel_id=1, source_target_pairs={{0,8},{1,9},{2,10},{3,11},{4,12},{5,13},{6,14},{7,15},{8,16},{9,17... | collective-permute-start | bytes 222344 | tf_op jit(solution)/shard_map/ppermute | solution.py:140
  91.5 2.3 copy-start.13
  91.5 3.0 %copy-start.27 = (f32[48,16]{1,0:T(8,128)S(1)}, f32[48,16]{1,0:T(8,128)}, u32[]{:S(2)}) copy-start(f32[48,16]{1,0:T(8,128)} %copy-done.26) | copy-start | bytes 9220
  91.5 3.6 %copy-start.25 = (f32[48,16]{1,0:T(8,128)S(1)}, f32[48,16]{1,0:T(8,128)}, u32[]{:S(2)}) copy-start(f32[48,16]{1,0:T(8,128)} %copy-done.24) | copy-start | bytes 9220
  91.5 4.2 %copy-start.29 = (f32[48,16]{1,0:T(8,128)S(1)}, f32[48,16]{1,0:T(8,128)}, u32[]{:S(2)}) copy-start(f32[48,16]{1,0:T(8,128)} %copy-done.28) | copy-start | bytes 9220
  91.5 4.8 %copy-start.31 = (f32[48,16]{1,0:T(8,128)S(1)}, f32[48,16]{1,0:T(8,128)}, u32[]{:S(2)}) copy-start(f32[48,16]{1,0:T(8,128)} %copy-done.30) | copy-start | bytes 9220
  91.5 5.4 %copy-start.33 = (f32[48,16]{1,0:T(8,128)S(1)}, f32[48,16]{1,0:T(8,128)}, u32[]{:S(2)}) copy-start(f32[48,16]{1,0:T(8,128)} %copy-done.32) | copy-start | bytes 9220
  91.6 6.0 %copy-start.35 = (f32[48,16]{1,0:T(8,128)S(1)}, f32[48,16]{1,0:T(8,128)}, u32[]{:S(2)}) copy-start(f32[48,16]{1,0:T(8,128)} %copy-done.34) | copy-start | bytes 9220
  91.6 6.6 %copy-start.37 = (f32[48,16]{1,0:T(8,128)S(1)}, f32[48,16]{1,0:T(8,128)}, u32[]{:S(2)}) copy-start(f32[48,16]{1,0:T(8,128)} %copy-done.36) | copy-start | bytes 9220
  136.6 4.0 %copy-start.56 = (s32[8]{0:T(128)S(1)}, s32[8]{0:T(128)}, u32[]{:S(2)}) copy-start(s32[8]{0:T(128)} %get-tuple-element.3) | copy-start | bytes 100
  137.9 55.1 %copy-start.57 = (pred[8]{0:T(512)(128)(4,1)S(1)}, pred[8]{0:T(512)(128)(4,1)}, u32[]{:S(2)}) copy-start(pred[8]{0:T(512)(128)(4,1)} %get-tuple-element.2) | copy-start | bytes 28
  138.0 57.2 %copy-start.47 = (s32[8]{0:T(128)S(1)}, s32[8]{0:T(128)}, u32[]{:S(2)}) copy-start(s32[8]{0:T(128)} %copy-done.46) | copy-start | bytes 100
  138.0 57.2 %copy-start.49 = (s32[16]{0:T(128)S(1)}, s32[16]{0:T(128)}, u32[]{:S(2)}) copy-start(s32[16]{0:T(128)} %copy-done.48) | copy-start | bytes 196
  138.2 8.9 %collective-permute-start.14 = (f32[8,3,8,256]{3,1,0,2:T(4,128)S(1)}, f32[8,3,8,256]{3,1,0,2:T(4,128)S(1)}, u32[]{:S(2)}, u32[]{:S(2)}) collective-permute-start(f32[8,3,8,256]{3,1,0,2:T(4,128)S(1)} %copy_multiply_fusion), channel_id=1, source_target_pairs={{0,1},{1,2},{2,3},{3,4},{4,5},{5,6},{6,7},{7,8},{8,9},{9,10},{10,1... | collective-permute-start | bytes 589832 | tf_op jit(solution)/shard_map/ppermute | solution.py:211
  147.3 10.7 %collective-permute-start.15 = (f32[8,3,8,256]{3,1,0,2:T(4,128)S(1)}, f32[8,3,8,256]{3,1,0,2:T(4,128)S(1)}, u32[]{:S(2)}, u32[]{:S(2)}) collective-permute-start(f32[8,3,8,256]{3,1,0,2:T(4,128)S(1)} %broadcast_select_fusion.2), channel_id=1, source_target_pairs={{0,2},{1,3},{2,4},{3,5},{4,6},{5,7},{6,8},{7,9},{8,10},{9,11},{10,... | collective-permute-start | bytes 589832 | tf_op jit(solution)/shard_map/ppermute | solution.py:211
  158.1 7.9 %collective-permute-start.16 = (f32[8,3,8,256]{3,1,0,2:T(4,128)S(1)}, f32[8,3,8,256]{3,1,0,2:T(4,128)S(1)}, u32[]{:S(2)}, u32[]{:S(2)}) collective-permute-start(f32[8,3,8,256]{3,1,0,2:T(4,128)S(1)} %broadcast_select_fusion.3), channel_id=1, source_target_pairs={{0,4},{1,5},{2,6},{3,7},{4,8},{5,9},{6,10},{7,11},{8,12},{9,13},{1... | collective-permute-start | bytes 589832 | tf_op jit(solution)/shard_map/ppermute | solution.py:211
  166.2 9.3 %collective-permute-start.17 = (f32[8,3,8,256]{3,1,0,2:T(4,128)S(1)}, f32[8,3,8,256]{3,1,0,2:T(4,128)S(1)}, u32[]{:S(2)}, u32[]{:S(2)}) collective-permute-start(f32[8,3,8,256]{3,1,0,2:T(4,128)S(1)} %broadcast_select_fusion.4), channel_id=1, source_target_pairs={{0,8},{1,9},{2,10},{3,11},{4,12},{5,13},{6,14},{7,15},{8,16},{9,17... | collective-permute-start | bytes 589832 | tf_op jit(solution)/shard_map/ppermute | solution.py:211
  175.7 17.3 %collective-permute-start.18 = (f32[8,3,8,256]{3,1,0,2:T(4,128)S(1)}, f32[8,3,8,256]{3,1,0,2:T(4,128)S(1)}, u32[]{:S(2)}, u32[]{:S(2)}) collective-permute-start(f32[8,3,8,256]{3,1,0,2:T(4,128)S(1)} %broadcast_select_fusion.5), channel_id=1, source_target_pairs={{0,16},{1,17},{2,18},{3,19},{4,20},{5,21},{6,22},{7,23},{8,24},{9,... | collective-permute-start | bytes 589832 | tf_op jit(solution)/shard_map/ppermute | solution.py:211
  193.1 16.7 %collective-permute-start.23 = (f32[8,3,8,256]{3,1,0,2:T(4,128)S(1)}, f32[8,3,8,256]{3,1,0,2:T(4,128)S(1)}, u32[]{:S(2)}, u32[]{:S(2)}) collective-permute-start(f32[8,3,8,256]{3,1,0,2:T(4,128)S(1)} %broadcast_select_fusion.6), channel_id=1, source_target_pairs={{1,0},{3,1},{5,2},{7,3},{9,4},{11,5},{13,6},{15,7},{17,8},{19,9},{... | collective-permute-start | bytes 589832 | tf_op jit(solution)/shard_map/ppermute | solution.py:222
  193.8 17.3 %collective-permute-start.24 = (f32[8,3,8,256]{3,1,0,2:T(4,128)S(1)}, f32[8,3,8,256]{3,1,0,2:T(4,128)S(1)}, u32[]{:S(2)}, u32[]{:S(2)}) collective-permute-start(f32[8,3,8,256]{3,1,0,2:T(4,128)S(1)} %broadcast_select_fusion.6), channel_id=1, source_target_pairs={{1,16},{3,17},{5,18},{7,19},{9,20},{11,21},{13,22},{15,23},{17,24}... | collective-permute-start | bytes 589832 | tf_op jit(solution)/shard_map/ppermute | solution.py:222
  195.2 16.1 %collective-permute-start.21 = (f32[8,3,8,256]{3,1,0,2:T(4,128)S(1)}, f32[8,3,8,256]{3,1,0,2:T(4,128)S(1)}, u32[]{:S(2)}, u32[]{:S(2)}) collective-permute-start(f32[8,3,8,256]{3,1,0,2:T(4,128)S(1)} %broadcast_select_fusion.6), channel_id=1, source_target_pairs={{0,0},{2,1},{4,2},{6,3},{8,4},{10,5},{12,6},{14,7},{16,8},{18,9},{... | collective-permute-start | bytes 589832 | tf_op jit(solution)/shard_map/ppermute | solution.py:222
  207.2 12.0 %collective-permute-start.22 = (f32[8,3,8,256]{3,1,0,2:T(4,128)S(1)}, f32[8,3,8,256]{3,1,0,2:T(4,128)S(1)}, u32[]{:S(2)}, u32[]{:S(2)}) collective-permute-start(f32[8,3,8,256]{3,1,0,2:T(4,128)S(1)} %broadcast_select_fusion.6), channel_id=1, source_target_pairs={{0,16},{2,17},{4,18},{6,19},{8,20},{10,21},{12,22},{14,23},{16,24}... | collective-permute-start | bytes 589832 | tf_op jit(solution)/shard_map/ppermute | solution.py:222
  209.1 10.1 %collective-permute-start.19 = (f32[8,3,8,256]{3,1,0,2:T(4,128)S(1)}, f32[8,3,8,256]{3,1,0,2:T(4,128)S(1)}, u32[]{:S(2)}, u32[]{:S(2)}) collective-permute-start(f32[8,3,8,256]{3,1,0,2:T(4,128)S(1)} %broadcast_select_fusion.6), channel_id=1, source_target_pairs={{31,0},{1,1},{3,2},{5,3},{7,4},{9,5},{11,6},{13,7},{15,8},{17,9},{... | collective-permute-start | bytes 589832 | tf_op jit(solution)/shard_map/ppermute | solution.py:222
  209.8 19.8 %collective-permute-start.20 = (f32[8,3,8,256]{3,1,0,2:T(4,128)S(1)}, f32[8,3,8,256]{3,1,0,2:T(4,128)S(1)}, u32[]{:S(2)}, u32[]{:S(2)}) collective-permute-start(f32[8,3,8,256]{3,1,0,2:T(4,128)S(1)} %broadcast_select_fusion.6), channel_id=1, source_target_pairs={{31,16},{1,17},{3,18},{5,19},{7,20},{9,21},{11,22},{13,23},{15,24}... | collective-permute-start | bytes 589832 | tf_op jit(solution)/shard_map/ppermute | solution.py:222
  (21 other events, 25.1 us)

commit v9 on v6

--- a/solution.py
+++ b/solution.py
@@ -133,7 +133,7 @@
     sums = ends_part.reshape(members * 6, span + 2)
     reach = 1
     while reach < bands:
-        count = min(8, bands // reach)
+        count = min(4 if reach == 1 else 8, bands // reach)
         payload = jnp.concatenate([blocks, sums], axis=1)
         if reach == 1:
             nest_state, payload = lax.optimization_barrier((nest_state, payload))

time: 220 us -> 219 us (level)
    concatenate x11, local copies, waits for them, and re-layouts: 0.36 us -> 5.54 us  [per_device(): jnp.concatenate([got[:, :width] for got in recvs] + [blocks], axis=1)]
    ppermute x1, waiting for transfers between devices: 5.3 us -> 2.11 us  [with_halo(): lax.ppermute(tail, 'band', shift_pairs(count, 1))]
    ppermute x10, waiting for transfers between devices: 1.12 us -> 3.46 us  [per_device(): lax.ppermute(payload, 'band', [(i, (i + k * reach) % bands) for i in rang...]
  transfers between devices with their start and end apart: 25 -> 25, of which waited for: 10 -> 10; matrix products, arithmetic and copies ran while one was open for 10% -> 11% of each run, Pallas kernels for 0% -> 0%
where the time goes in v9:
time: 219 us; the launch traced here: 218 us
  starting transfers between devices  59.6 us (27%)
  waiting for transfers between devices  58.4 us (27%)
  local copies, waits for them, and re-layouts  46 us (21%)
  between operations  26.4 us (12%)
  other arithmetic  19.6 us (9%)
  matrix products  7.93 us (4%)
    ppermute x5, waiting for transfers between devices, per_device(): lax.ppermute(moved, 'band', [(i, (i + step) % bands) for i in range(bands)])  30.4 us
    ppermute x6, waiting for transfers between devices, per_device(): got.append(lax.ppermute(moved, 'band', pairs))  19.1 us
    ppermute x10, starting transfers between devices, per_device(): lax.ppermute(payload, 'band', [(i, (i + k * reach) % bands) for i in rang...  19.1 us
    ppermute x6, starting transfers between devices, per_device(): got.append(lax.ppermute(moved, 'band', pairs))  15.6 us
    dynamic_update_slice x8, local copies, waits for them, and re-layouts, per_device(): lax.dynamic_update_slice(parent_out, merged[m:m + 1], (m, 0, 0, cols_off[...  15.2 us
    ppermute x5, starting transfers between devices, per_device(): lax.ppermute(moved, 'band', [(i, (i + step) % bands) for i in range(bands)])  10.3 us
    concatenate x11, local copies, waits for them, and re-layouts, per_device(): jnp.concatenate([got[:, :width] for got in recvs] + [blocks], axis=1)  5.54 us
    ppermute x1, starting transfers between devices, with_halo(): lax.ppermute(tail, 'band', shift_pairs(count, 1))  4.79 us
  transfers between devices with their start and end apart: 25, of which 10 were waited for; matrix products, arithmetic and copies ran while one was open for 11% of the time, Pallas kernels for 0%

profile of v9, /device:TPU:112, one launch (start us, length us, event | category | flops | bytes accessed | tf_op | source)
XLA Modules:
  0.0 218.0 jit_solution(10925073905038972309)
XLA Ops:
  0.6 3.3 %slice_bitcast_fusion.4 = (f32[8,16,4096]{2,1,0:T(8,128)S(1)}, f32[8,16,4096]{2,1,0:T(8,128)S(1)}, f32[8,16,4096]{2,1,0:T(8,128)S(1)}) fusion(f32[8,3,16,4096]{3,2,1,0:T(8,128)} %param.3), kind=kLoop, calls=%fused_computation.28 | loop fusion | bytes 12582912 | tf_op jit(solution)/shard_map/squeeze | solution.py:50
  4.5 1.1 pad_maximum_fusion.21
  5.6 4.8 %collective-permute-start = (f32[8,4,4096]{2,1,0:T(4,128)}, f32[8,4,4096]{2,1,0:T(4,128)S(1)}, u32[]{:S(2)}, u32[]{:S(2)}) collective-permute-start(f32[8,4,4096]{2,1,0:T(4,128)} %pad_maximum_fusion.21), channel_id=1, source_target_pairs={{1,0},{2,1},{3,2},{4,3},{5,4},{6,5},{7,6},{8,7},{9,8},{10,9},{11,1... | collective-permute-start | bytes 1572872 | tf_op jit(solution)/shard_map/ppermute | solution.py:59
  10.4 1.2 pad_maximum_fusion.22
  11.6 2.6 %collective-permute-start.1 = (f32[8,4,4096]{2,1,0:T(4,128)}, f32[8,4,4096]{2,1,0:T(4,128)S(1)}, u32[]{:S(2)}, u32[]{:S(2)}) collective-permute-start(f32[8,4,4096]{2,1,0:T(4,128)} %pad_maximum_fusion.22), channel_id=1, source_target_pairs={{0,1},{1,2},{2,3},{3,4},{4,5},{5,6},{6,7},{7,8},{8,9},{9,10},{10,1... | collective-permute-start | bytes 1572872 | tf_op jit(solution)/shard_map/ppermute | solution.py:58
  14.1 2.8 %fusion.129 = (f32[8,16,4095]{2,1,0:T(8,128)}, f32[8,16,4095]{2,1,0:T(8,128)}) fusion(f32[8,16,4096]{2,1,0:T(8,128)S(1)} %get-tuple-element.22), kind=kLoop, calls=%fused_computation.307 | loop fusion | bytes 8386560 | tf_op jit(solution)/shard_map/jit(_roll_static)/slice | solution.py:46
  16.9 0.7 fusion.148
  28.8 0.7 broadcast_add_fusion.1
  30.6 3.3 %collective-permute-done.1 = f32[8,4,4096]{2,1,0:T(4,128)S(1)} collective-permute-done((f32[8,4,4096]{2,1,0:T(4,128)}, f32[8,4,4096]{2,1,0:T(4,128)S(1)}, u32[]{:S(2)}, u32[]{:S(2)}) %collective-permute-start.1) | collective-permute-done | bytes 524320 | tf_op jit(solution)/shard_map/ppermute | solution.py:58
  34.6 0.9 broadcast_select_fusion.1
  35.5 3.7 %fusion.8 = f32[8,16,4096]{2,1,0:T(8,128)S(1)} fusion(f32[8,16,4096]{2,1,0:T(8,128)S(1)} %copy-done.1, f32[8,1,4096]{2,1,0:T(1,128)S(1)} %get-tuple-element.75, f32[8,1,4096]{2,1,0:T(1,128)S(1)} %get-tuple-element.76, f32[8,16,1]{2,1,0:T(8,128)S(1)} %get-tuple-element.36, f32[8,16,4095]{2,1,0:T(8,128)} %get-tuple-element.38, ...), kind=kLoop, calls=%fused_computation.16 | loop fusion | flops 4718592 | bytes 10747904 | tf_op jit(solution)/shard_map/sub | solution.py:61
  39.3 0.7 slice_bitcast_fusion
  40.1 0.9 fusion.4
  41.0 0.9 fusion.12
  43.1 2.0 copy-done.3
  45.7 2.9 %fusion.85 = f32[2,8,3,16]{3,0,2,1:T(2,128)S(1)} fusion(f32[8,3,16,258]{3,2,1,0:T(8,128)S(1)} %dynamic-slice_dynamic-update-slice_fusion, pred[258]{0:T(512)(128)(4,1)S(1)} %get-tuple-element.130, pred[258]{0:T(512)(128)(4,1)S(1)} %get-tuple-element.131, pred[258]{0:T(512)(128)(4,1)S(1)} %get-tuple-element.132, pred[258]{0:T(512)(128)(4,1)S(1)} %get-tuple-element.133, ...), kind=kOutput, calls=%fused_computation.212 | convolution fusion | flops 2383404 | bytes 400396 | tf_op jit(solution)/shard_map/mflq,qs->mfsl/dot_general | solution.py:118
  48.7 6.3 %collective-permute-start.4 = (f32[48,274]{1,0:T(8,128)S(1)}, f32[48,274]{1,0:T(8,128)S(1)}, u32[]{:S(2)}, u32[]{:S(2)}) collective-permute-start(f32[48,274]{1,0:T(8,128)S(1)} %pad_maximum_fusion.23), channel_id=1, source_target_pairs={{0,3},{1,4},{2,5},{3,6},{4,7},{5,8},{6,9},{7,10},{8,11},{9,12},{10... | collective-permute-start | bytes 157832 | tf_op jit(solution)/shard_map/ppermute | solution.py:142
  55.6 0.7 slice.588
  56.3 0.7 slice.587
  58.3 1.8 collective-permute-done.5
  60.1 1.6 collective-permute-done.6
  61.8 0.7 concatenate.252
  63.9 3.0 %collective-permute-start.9 = (f32[48,322]{1,0:T(8,128)}, f32[48,322]{1,0:T(8,128)S(1)}, u32[]{:S(2)}, u32[]{:S(2)}) collective-permute-start(f32[48,322]{1,0:T(8,128)} %concatenate.252), channel_id=1, source_target_pairs={{0,20},{1,21},{2,22},{3,23},{4,24},{5,25},{6,26},{7,27},{8,28},{9,... | collective-permute-start | bytes 185480 | tf_op jit(solution)/shard_map/ppermute | solution.py:142
  66.9 3.3 %collective-permute-start.10 = (f32[48,322]{1,0:T(8,128)}, f32[48,322]{1,0:T(8,128)S(1)}, u32[]{:S(2)}, u32[]{:S(2)}) collective-permute-start(f32[48,322]{1,0:T(8,128)} %concatenate.252), channel_id=1, source_target_pairs={{0,16},{1,17},{2,18},{3,19},{4,20},{5,21},{6,22},{7,23},{8,24},{9,... | collective-permute-start | bytes 185480 | tf_op jit(solution)/shard_map/ppermute | solution.py:142
  70.2 2.7 %collective-permute-start.11 = (f32[48,322]{1,0:T(8,128)}, f32[48,322]{1,0:T(8,128)S(1)}, u32[]{:S(2)}, u32[]{:S(2)}) collective-permute-start(f32[48,322]{1,0:T(8,128)} %concatenate.252), channel_id=1, source_target_pairs={{0,12},{1,13},{2,14},{3,15},{4,16},{5,17},{6,18},{7,19},{8,20},{9,... | collective-permute-start | bytes 185480 | tf_op jit(solution)/shard_map/ppermute | solution.py:142
  72.9 2.5 %collective-permute-start.13 = (f32[48,322]{1,0:T(8,128)}, f32[48,322]{1,0:T(8,128)S(1)}, u32[]{:S(2)}, u32[]{:S(2)}) collective-permute-start(f32[48,322]{1,0:T(8,128)} %concatenate.252), channel_id=1, source_target_pairs={{0,4},{1,5},{2,6},{3,7},{4,8},{5,9},{6,10},{7,11},{8,12},{9,13},{1... | collective-permute-start | bytes 185480 | tf_op jit(solution)/shard_map/ppermute | solution.py:142
  75.4 0.8 fusion.133
  76.9 2.5 %collective-permute-start.3 = (f32[8,3,6,768]{3,0,2,1:T(8,128)}, f32[8,3,6,768]{3,0,2,1:T(8,128)}, u32[]{:S(2)}, u32[]{:S(2)}) collective-permute-start(f32[8,3,6,768]{3,0,2,1:T(8,128)} %get-tuple-element.50), channel_id=1, source_target_pairs={{1,0},{2,1},{3,2},{4,3},{5,4},{6,5},{7,6},{8,7},{9,8},{10,9},{11,1... | collective-permute-start | bytes 1327112 | tf_op jit(solution)/shard_map/ppermute | solution.py:29
  80.1 4.8 %collective-permute-start.2 = (f32[8,3,6,768]{3,0,2,1:T(8,128)S(1)}, f32[8,3,6,768]{3,0,2,1:T(8,128)}, u32[]{:S(2)}, u32[]{:S(2)}) collective-permute-start(f32[8,3,6,768]{3,0,2,1:T(8,128)S(1)} %get-tuple-element.49), channel_id=1, source_target_pairs={{0,1},{1,2},{2,3},{3,4},{4,5},{5,6},{6,7},{7,8},{8,9},{9,10},{10,1... | collective-permute-start | bytes 1327112 | tf_op jit(solution)/shard_map/ppermute | solution.py:27
  88.1 1.7 concatenate.263
  89.8 1.7 fusion.46
  91.9 1.2 slice_add_fusion
  93.2 0.7 reshape.799
  94.1 1.8 fusion.38
  95.9 1.2 copy.98
  97.1 2.1 collective-permute-done.2
  99.2 1.2 copy.96
  102.6 0.9 select_select_fusion.5
  105.1 0.9 select_select_fusion.1
  108.4 1.1 fusion.44
  109.9 0.9 collective-permute-start.14
  110.8 8.1 %collective-permute-done.14 = f32[8,3,8,256]{3,1,0,2:T(4,128)S(1)} collective-permute-done((f32[8,3,8,256]{3,1,0,2:T(4,128)S(1)}, f32[8,3,8,256]{3,1,0,2:T(4,128)S(1)}, u32[]{:S(2)}, u32[]{:S(2)}) %collective-permute-start.14) | collective-permute-done | bytes 196640 | tf_op jit(solution)/shard_map/ppermute | solution.py:213
  119.1 5.1 %collective-permute-start.15 = (f32[8,3,8,256]{3,1,0,2:T(4,128)S(1)}, f32[8,3,8,256]{3,1,0,2:T(4,128)S(1)}, u32[]{:S(2)}, u32[]{:S(2)}) collective-permute-start(f32[8,3,8,256]{3,1,0,2:T(4,128)S(1)} %broadcast_select_fusion.2), channel_id=1, source_target_pairs={{0,2},{1,3},{2,4},{3,5},{4,6},{5,7},{6,8},{7,9},{8,10},{9,11},{10,... | collective-permute-start | bytes 589832 | tf_op jit(solution)/shard_map/ppermute | solution.py:213
  124.2 6.5 %collective-permute-done.15 = f32[8,3,8,256]{3,1,0,2:T(4,128)S(1)} collective-permute-done((f32[8,3,8,256]{3,1,0,2:T(4,128)S(1)}, f32[8,3,8,256]{3,1,0,2:T(4,128)S(1)}, u32[]{:S(2)}, u32[]{:S(2)}) %collective-permute-start.15) | collective-permute-done | bytes 196640 | tf_op jit(solution)/shard_map/ppermute | solution.py:213
  131.3 7.4 %collective-permute-done.16 = f32[8,3,8,256]{3,1,0,2:T(4,128)S(1)} collective-permute-done((f32[8,3,8,256]{3,1,0,2:T(4,128)S(1)}, f32[8,3,8,256]{3,1,0,2:T(4,128)S(1)}, u32[]{:S(2)}, u32[]{:S(2)}) %collective-permute-start.16) | collective-permute-done | bytes 196640 | tf_op jit(solution)/shard_map/ppermute | solution.py:213
  139.3 8.4 %collective-permute-done.17 = f32[8,3,8,256]{3,1,0,2:T(4,128)S(1)} collective-permute-done((f32[8,3,8,256]{3,1,0,2:T(4,128)S(1)}, f32[8,3,8,256]{3,1,0,2:T(4,128)S(1)}, u32[]{:S(2)}, u32[]{:S(2)}) %collective-permute-start.17) | collective-permute-done | bytes 196640 | tf_op jit(solution)/shard_map/ppermute | solution.py:213
  147.9 3.4 %collective-permute-start.18 = (f32[8,3,8,256]{3,1,0,2:T(4,128)S(1)}, f32[8,3,8,256]{3,1,0,2:T(4,128)S(1)}, u32[]{:S(2)}, u32[]{:S(2)}) collective-permute-start(f32[8,3,8,256]{3,1,0,2:T(4,128)S(1)} %broadcast_select_fusion.5), channel_id=1, source_target_pairs={{0,16},{1,17},{2,18},{3,19},{4,20},{5,21},{6,22},{7,23},{8,24},{9,... | collective-permute-start | bytes 589832 | tf_op jit(solution)/shard_map/ppermute | solution.py:213
  166.3 0.7 collective-permute-start.23
  167.0 1.3 collective-permute-start.24
  168.4 9.7 %collective-permute-start.21 = (f32[8,3,8,256]{3,1,0,2:T(4,128)S(1)}, f32[8,3,8,256]{3,1,0,2:T(4,128)S(1)}, u32[]{:S(2)}, u32[]{:S(2)}) collective-permute-start(f32[8,3,8,256]{3,1,0,2:T(4,128)S(1)} %broadcast_select_fusion.6), channel_id=1, source_target_pairs={{0,0},{2,1},{4,2},{6,3},{8,4},{10,5},{12,6},{14,7},{16,8},{18,9},{... | collective-permute-start | bytes 589832 | tf_op jit(solution)/shard_map/ppermute | solution.py:224
  178.1 1.9 collective-permute-start.22
  180.1 0.7 collective-permute-start.19
  180.8 1.3 collective-permute-start.20
  182.2 7.9 %collective-permute-done.22 = f32[8,3,8,256]{3,1,0,2:T(4,128)S(1)} collective-permute-done((f32[8,3,8,256]{3,1,0,2:T(4,128)S(1)}, f32[8,3,8,256]{3,1,0,2:T(4,128)S(1)}, u32[]{:S(2)}, u32[]{:S(2)}) %collective-permute-start.22) | collective-permute-done | bytes 196640 | tf_op jit(solution)/shard_map/ppermute | solution.py:224
  190.2 11.1 %collective-permute-done.20 = f32[8,3,8,256]{3,1,0,2:T(4,128)S(1)} collective-permute-done((f32[8,3,8,256]{3,1,0,2:T(4,128)S(1)}, f32[8,3,8,256]{3,1,0,2:T(4,128)S(1)}, u32[]{:S(2)}, u32[]{:S(2)}) %collective-permute-start.20) | collective-permute-done | bytes 196640 | tf_op jit(solution)/shard_map/ppermute | solution.py:224
  201.7 0.9 gather_fusion
  202.8 1.9 dynamic_update_slice.24
  204.7 1.9 dynamic_update_slice.25
  206.6 1.9 dynamic_update_slice.26
  208.5 1.9 dynamic_update_slice.27
  210.4 1.9 dynamic_update_slice.28
  212.3 1.9 dynamic_update_slice.29
  214.2 1.9 dynamic_update_slice.30
  216.1 1.9 dynamic_update_slice.31
  (174 shorter events, 23.0 us)
Async XLA Ops:
  3.9 7.6 %copy-start = (f32[8,16,4096]{2,1,0:T(8,128)}, f32[8,16,4096]{2,1,0:T(8,128)S(1)}, u32[]{:S(2)}) copy-start(f32[8,16,4096]{2,1,0:T(8,128)S(1)} %get-tuple-element.23) | copy-start | bytes 6291460
  5.6 24.6 %collective-permute-start = (f32[8,4,4096]{2,1,0:T(4,128)}, f32[8,4,4096]{2,1,0:T(4,128)S(1)}, u32[]{:S(2)}, u32[]{:S(2)}) collective-permute-start(f32[8,4,4096]{2,1,0:T(4,128)} %pad_maximum_fusion.21), channel_id=1, source_target_pairs={{1,0},{2,1},{3,2},{4,3},{5,4},{6,5},{7,6},{8,7},{9,8},{10,9},{11,1... | collective-permute-start | bytes 1572872 | tf_op jit(solution)/shard_map/ppermute | solution.py:59
  11.6 22.4 %collective-permute-start.1 = (f32[8,4,4096]{2,1,0:T(4,128)}, f32[8,4,4096]{2,1,0:T(4,128)S(1)}, u32[]{:S(2)}, u32[]{:S(2)}) collective-permute-start(f32[8,4,4096]{2,1,0:T(4,128)} %pad_maximum_fusion.22), channel_id=1, source_target_pairs={{0,1},{1,2},{2,3},{3,4},{4,5},{5,6},{6,7},{7,8},{8,9},{9,10},{10,1... | collective-permute-start | bytes 1572872 | tf_op jit(solution)/shard_map/ppermute | solution.py:58
  14.1 2.8 %copy-start.10 = (s32[8,2]{0,1:T(2,128)S(1)}, s32[8,2]{0,1:T(2,128)}, u32[]{:S(2)}) copy-start(s32[8,2]{0,1:T(2,128)} %param.5) | copy-start | bytes 196
  27.6 1.9 copy-start.11
  28.8 5.8 %copy-start.1 = (f32[8,16,4096]{2,1,0:T(8,128)S(1)}, f32[8,16,4096]{2,1,0:T(8,128)}, u32[]{:S(2)}) copy-start(f32[8,16,4096]{2,1,0:T(8,128)} %copy-done) | copy-start | bytes 6291460
  29.5 0.5 copy-start.16
  30.5 5.0 %copy-start.2 = (f32[8,16,4095]{2,1,0:T(8,128)S(1)}, f32[8,16,4095]{2,1,0:T(8,128)}, u32[]{:S(2)}) copy-start(f32[8,16,4095]{2,1,0:T(8,128)} %get-tuple-element.37) | copy-start | bytes 6289924
  34.6 5.5 %slice-start = ((s8[6291456]{0:T(1024)(128)(4,1)}), s8[4194304]{0:T(1024)(128)(4,1)S(1)}, s32[]{:S(2)}) async-start(s8[6291456]{0:T(1024)(128)(4,1)} %bitcast.177), calls=%async_computation | async-start | bytes 8388608
  35.5 4.6 %slice-start.1 = ((s8[6291456]{0:T(1024)(128)(4,1)}), s8[2097152]{0:T(1024)(128)(4,1)S(1)}, s32[]{:S(2)}) async-start(s8[6291456]{0:T(1024)(128)(4,1)} %bitcast.177), calls=%async_computation.1 | async-start | bytes 4194304
  42.4 2.7 %copy-start.3 = (f32[8,3,16,4096]{3,2,1,0:T(8,128)}, f32[8,3,16,4096]{3,2,1,0:T(8,128)S(1)}, u32[]{:S(2)}) copy-start(f32[8,3,16,4096]{3,2,1,0:T(8,128)S(1)} %pad_maximum_fusion) | copy-start | bytes 18874372
  42.4 21.0 %copy-start.4 = (f32[8,3,24,768]{3,2,1,0:T(8,128)S(1)}, f32[8,3,24,768]{3,2,1,0:T(8,128)}, u32[]{:S(2)}) copy-start(f32[8,3,24,768]{3,2,1,0:T(8,128)} %param.4) | copy-start | bytes 5308420
  48.7 9.6 %collective-permute-start.4 = (f32[48,274]{1,0:T(8,128)S(1)}, f32[48,274]{1,0:T(8,128)S(1)}, u32[]{:S(2)}, u32[]{:S(2)}) collective-permute-start(f32[48,274]{1,0:T(8,128)S(1)} %pad_maximum_fusion.23), channel_id=1, source_target_pairs={{0,3},{1,4},{2,5},{3,6},{4,7},{5,8},{6,9},{7,10},{8,11},{9,12},{10... | collective-permute-start | bytes 157832 | tf_op jit(solution)/shard_map/ppermute | solution.py:142
  55.0 5.1 %collective-permute-start.5 = (f32[48,274]{1,0:T(8,128)S(1)}, f32[48,274]{1,0:T(8,128)S(1)}, u32[]{:S(2)}, u32[]{:S(2)}) collective-permute-start(f32[48,274]{1,0:T(8,128)S(1)} %pad_maximum_fusion.23), channel_id=1, source_target_pairs={{0,2},{1,3},{2,4},{3,5},{4,6},{5,7},{6,8},{7,9},{8,10},{9,11},{10,... | collective-permute-start | bytes 157832 | tf_op jit(solution)/shard_map/ppermute | solution.py:142
  55.0 6.8 %collective-permute-start.6 = (f32[48,274]{1,0:T(8,128)S(1)}, f32[48,274]{1,0:T(8,128)S(1)}, u32[]{:S(2)}, u32[]{:S(2)}) collective-permute-start(f32[48,274]{1,0:T(8,128)S(1)} %pad_maximum_fusion.23), channel_id=1, source_target_pairs={{0,1},{1,2},{2,3},{3,4},{4,5},{5,6},{6,7},{7,8},{8,9},{9,10},{10,1... | collective-permute-start | bytes 157832 | tf_op jit(solution)/shard_map/ppermute | solution.py:142
  62.6 10.3 %collective-permute-start.7 = (f32[48,322]{1,0:T(8,128)}, f32[48,322]{1,0:T(8,128)S(1)}, u32[]{:S(2)}, u32[]{:S(2)}) collective-permute-start(f32[48,322]{1,0:T(8,128)} %concatenate.252), channel_id=1, source_target_pairs={{0,28},{1,29},{2,30},{3,31},{4,0},{5,1},{6,2},{7,3},{8,4},{9,5},{1... | collective-permute-start | bytes 185480 | tf_op jit(solution)/shard_map/ppermute | solution.py:142
  62.9 10.0 %collective-permute-start.8 = (f32[48,322]{1,0:T(8,128)}, f32[48,322]{1,0:T(8,128)S(1)}, u32[]{:S(2)}, u32[]{:S(2)}) collective-permute-start(f32[48,322]{1,0:T(8,128)} %concatenate.252), channel_id=1, source_target_pairs={{0,24},{1,25},{2,26},{3,27},{4,28},{5,29},{6,30},{7,31},{8,0},{9,1... | collective-permute-start | bytes 185480 | tf_op jit(solution)/shard_map/ppermute | solution.py:142
  63.9 25.9 %copy-start.13 = (s32[8,36]{1,0:T(8,128)S(1)}, s32[8,36]{1,0:T(8,128)}, u32[]{:S(2)}) copy-start(s32[8,36]{1,0:T(8,128)} %get-tuple-element.108) | copy-start | bytes 3460
  63.9 25.9 %copy-start.14 = (s32[8,36]{1,0:T(8,128)S(1)}, s32[8,36]{1,0:T(8,128)}, u32[]{:S(2)}) copy-start(s32[8,36]{1,0:T(8,128)} %get-tuple-element.109) | copy-start | bytes 3460
  63.9 25.9 %copy-start.15 = (s32[512]{0:T(512)S(1)}, s32[512]{0:T(512)}, u32[]{:S(2)}) copy-start(s32[512]{0:T(512)} %add_select_fusion.3) | copy-start | bytes 6148
  63.9 13.0 %collective-permute-start.9 = (f32[48,322]{1,0:T(8,128)}, f32[48,322]{1,0:T(8,128)S(1)}, u32[]{:S(2)}, u32[]{:S(2)}) collective-permute-start(f32[48,322]{1,0:T(8,128)} %concatenate.252), channel_id=1, source_target_pairs={{0,20},{1,21},{2,22},{3,23},{4,24},{5,25},{6,26},{7,27},{8,28},{9,... | collective-permute-start | bytes 185480 | tf_op jit(solution)/shard_map/ppermute | solution.py:142
  66.9 13.2 %collective-permute-start.10 = (f32[48,322]{1,0:T(8,128)}, f32[48,322]{1,0:T(8,128)S(1)}, u32[]{:S(2)}, u32[]{:S(2)}) collective-permute-start(f32[48,322]{1,0:T(8,128)} %concatenate.252), channel_id=1, source_target_pairs={{0,16},{1,17},{2,18},{3,19},{4,20},{5,21},{6,22},{7,23},{8,24},{9,... | collective-permute-start | bytes 185480 | tf_op jit(solution)/shard_map/ppermute | solution.py:142
  70.2 15.3 %collective-permute-start.11 = (f32[48,322]{1,0:T(8,128)}, f32[48,322]{1,0:T(8,128)S(1)}, u32[]{:S(2)}, u32[]{:S(2)}) collective-permute-start(f32[48,322]{1,0:T(8,128)} %concatenate.252), channel_id=1, source_target_pairs={{0,12},{1,13},{2,14},{3,15},{4,16},{5,17},{6,18},{7,19},{8,20},{9,... | collective-permute-start | bytes 185480 | tf_op jit(solution)/shard_map/ppermute | solution.py:142
  72.9 13.3 %collective-permute-start.12 = (f32[48,322]{1,0:T(8,128)}, f32[48,322]{1,0:T(8,128)S(1)}, u32[]{:S(2)}, u32[]{:S(2)}) collective-permute-start(f32[48,322]{1,0:T(8,128)} %concatenate.252), channel_id=1, source_target_pairs={{0,8},{1,9},{2,10},{3,11},{4,12},{5,13},{6,14},{7,15},{8,16},{9,17... | collective-permute-start | bytes 185480 | tf_op jit(solution)/shard_map/ppermute | solution.py:142
  72.9 13.9 %collective-permute-start.13 = (f32[48,322]{1,0:T(8,128)}, f32[48,322]{1,0:T(8,128)S(1)}, u32[]{:S(2)}, u32[]{:S(2)}) collective-permute-start(f32[48,322]{1,0:T(8,128)} %concatenate.252), channel_id=1, source_target_pairs={{0,4},{1,5},{2,6},{3,7},{4,8},{5,9},{6,10},{7,11},{8,12},{9,13},{1... | collective-permute-start | bytes 185480 | tf_op jit(solution)/shard_map/ppermute | solution.py:142
  76.9 19.0 %collective-permute-start.3 = (f32[8,3,6,768]{3,0,2,1:T(8,128)}, f32[8,3,6,768]{3,0,2,1:T(8,128)}, u32[]{:S(2)}, u32[]{:S(2)}) collective-permute-start(f32[8,3,6,768]{3,0,2,1:T(8,128)} %get-tuple-element.50), channel_id=1, source_target_pairs={{1,0},{2,1},{3,2},{4,3},{5,4},{6,5},{7,6},{8,7},{9,8},{10,9},{11,1... | collective-permute-start | bytes 1327112 | tf_op jit(solution)/shard_map/ppermute | solution.py:29
  80.1 11.5 %copy-start.6 = (f32[48,322]{1,0:T(8,128)}, f32[48,322]{1,0:T(8,128)S(1)}, u32[]{:S(2)}) copy-start(f32[48,322]{1,0:T(8,128)S(1)} %collective-permute-done.10) | copy-start | bytes 185476
  80.1 19.1 %collective-permute-start.2 = (f32[8,3,6,768]{3,0,2,1:T(8,128)S(1)}, f32[8,3,6,768]{3,0,2,1:T(8,128)}, u32[]{:S(2)}, u32[]{:S(2)}) collective-permute-start(f32[8,3,6,768]{3,0,2,1:T(8,128)S(1)} %get-tuple-element.49), channel_id=1, source_target_pairs={{0,1},{1,2},{2,3},{3,4},{4,5},{5,6},{6,7},{7,8},{8,9},{9,10},{10,1... | collective-permute-start | bytes 1327112 | tf_op jit(solution)/shard_map/ppermute | solution.py:27
  85.5 6.2 %copy-start.7 = (f32[48,322]{1,0:T(8,128)}, f32[48,322]{1,0:T(8,128)S(1)}, u32[]{:S(2)}) copy-start(f32[48,322]{1,0:T(8,128)S(1)} %collective-permute-done.11) | copy-start | bytes 185476
  86.2 5.6 %copy-start.8 = (f32[48,322]{1,0:T(8,128)}, f32[48,322]{1,0:T(8,128)S(1)}, u32[]{:S(2)}) copy-start(f32[48,322]{1,0:T(8,128)S(1)} %collective-permute-done.12) | copy-start | bytes 185476
  86.8 0.6 copy-start.9
  108.3 1.4 copy-start.5
  108.4 2.4 %copy-start.18 = (s32[8]{0:T(128)S(1)}, s32[8]{0:T(128)}, u32[]{:S(2)}) copy-start(s32[8]{0:T(128)} %get-tuple-element.7) | copy-start | bytes 100
  109.6 56.5 %copy-start.19 = (pred[8]{0:T(512)(128)(4,1)S(1)}, pred[8]{0:T(512)(128)(4,1)}, u32[]{:S(2)}) copy-start(pred[8]{0:T(512)(128)(4,1)} %get-tuple-element.6) | copy-start | bytes 28
  109.7 58.6 %copy-start.12 = (s32[8]{0:T(128)S(1)}, s32[8]{0:T(128)}, u32[]{:S(2)}) copy-start(s32[8]{0:T(128)} %copy-done.11) | copy-start | bytes 100
  109.7 58.6 %copy-start.17 = (s32[16]{0:T(128)S(1)}, s32[16]{0:T(128)}, u32[]{:S(2)}) copy-start(s32[16]{0:T(128)} %copy-done.16) | copy-start | bytes 196
  109.9 8.9 %collective-permute-start.14 = (f32[8,3,8,256]{3,1,0,2:T(4,128)S(1)}, f32[8,3,8,256]{3,1,0,2:T(4,128)S(1)}, u32[]{:S(2)}, u32[]{:S(2)}) collective-permute-start(f32[8,3,8,256]{3,1,0,2:T(4,128)S(1)} %copy_multiply_fusion), channel_id=1, source_target_pairs={{0,1},{1,2},{2,3},{3,4},{4,5},{5,6},{6,7},{7,8},{8,9},{9,10},{10,1... | collective-permute-start | bytes 589832 | tf_op jit(solution)/shard_map/ppermute | solution.py:213
  119.1 11.6 %collective-permute-start.15 = (f32[8,3,8,256]{3,1,0,2:T(4,128)S(1)}, f32[8,3,8,256]{3,1,0,2:T(4,128)S(1)}, u32[]{:S(2)}, u32[]{:S(2)}) collective-permute-start(f32[8,3,8,256]{3,1,0,2:T(4,128)S(1)} %broadcast_select_fusion.2), channel_id=1, source_target_pairs={{0,2},{1,3},{2,4},{3,5},{4,6},{5,7},{6,8},{7,9},{8,10},{9,11},{10,... | collective-permute-start | bytes 589832 | tf_op jit(solution)/shard_map/ppermute | solution.py:213
  130.8 7.9 %collective-permute-start.16 = (f32[8,3,8,256]{3,1,0,2:T(4,128)S(1)}, f32[8,3,8,256]{3,1,0,2:T(4,128)S(1)}, u32[]{:S(2)}, u32[]{:S(2)}) collective-permute-start(f32[8,3,8,256]{3,1,0,2:T(4,128)S(1)} %broadcast_select_fusion.3), channel_id=1, source_target_pairs={{0,4},{1,5},{2,6},{3,7},{4,8},{5,9},{6,10},{7,11},{8,12},{9,13},{1... | collective-permute-start | bytes 589832 | tf_op jit(solution)/shard_map/ppermute | solution.py:213
  138.9 8.9 %collective-permute-start.17 = (f32[8,3,8,256]{3,1,0,2:T(4,128)S(1)}, f32[8,3,8,256]{3,1,0,2:T(4,128)S(1)}, u32[]{:S(2)}, u32[]{:S(2)}) collective-permute-start(f32[8,3,8,256]{3,1,0,2:T(4,128)S(1)} %broadcast_select_fusion.4), channel_id=1, source_target_pairs={{0,8},{1,9},{2,10},{3,11},{4,12},{5,13},{6,14},{7,15},{8,16},{9,17... | collective-permute-start | bytes 589832 | tf_op jit(solution)/shard_map/ppermute | solution.py:213
  147.9 18.3 %collective-permute-start.18 = (f32[8,3,8,256]{3,1,0,2:T(4,128)S(1)}, f32[8,3,8,256]{3,1,0,2:T(4,128)S(1)}, u32[]{:S(2)}, u32[]{:S(2)}) collective-permute-start(f32[8,3,8,256]{3,1,0,2:T(4,128)S(1)} %broadcast_select_fusion.5), channel_id=1, source_target_pairs={{0,16},{1,17},{2,18},{3,19},{4,20},{5,21},{6,22},{7,23},{8,24},{9,... | collective-permute-start | bytes 589832 | tf_op jit(solution)/shard_map/ppermute | solution.py:213
  166.3 14.4 %collective-permute-start.23 = (f32[8,3,8,256]{3,1,0,2:T(4,128)S(1)}, f32[8,3,8,256]{3,1,0,2:T(4,128)S(1)}, u32[]{:S(2)}, u32[]{:S(2)}) collective-permute-start(f32[8,3,8,256]{3,1,0,2:T(4,128)S(1)} %broadcast_select_fusion.6), channel_id=1, source_target_pairs={{1,0},{3,1},{5,2},{7,3},{9,4},{11,5},{13,6},{15,7},{17,8},{19,9},{... | collective-permute-start | bytes 589832 | tf_op jit(solution)/shard_map/ppermute | solution.py:224
  167.0 15.1 %collective-permute-start.24 = (f32[8,3,8,256]{3,1,0,2:T(4,128)S(1)}, f32[8,3,8,256]{3,1,0,2:T(4,128)S(1)}, u32[]{:S(2)}, u32[]{:S(2)}) collective-permute-start(f32[8,3,8,256]{3,1,0,2:T(4,128)S(1)} %broadcast_select_fusion.6), channel_id=1, source_target_pairs={{1,16},{3,17},{5,18},{7,19},{9,20},{11,21},{13,22},{15,23},{17,24}... | collective-permute-start | bytes 589832 | tf_op jit(solution)/shard_map/ppermute | solution.py:224
  168.4 13.8 %collective-permute-start.21 = (f32[8,3,8,256]{3,1,0,2:T(4,128)S(1)}, f32[8,3,8,256]{3,1,0,2:T(4,128)S(1)}, u32[]{:S(2)}, u32[]{:S(2)}) collective-permute-start(f32[8,3,8,256]{3,1,0,2:T(4,128)S(1)} %broadcast_select_fusion.6), channel_id=1, source_target_pairs={{0,0},{2,1},{4,2},{6,3},{8,4},{10,5},{12,6},{14,7},{16,8},{18,9},{... | collective-permute-start | bytes 589832 | tf_op jit(solution)/shard_map/ppermute | solution.py:224
  178.1 12.0 %collective-permute-start.22 = (f32[8,3,8,256]{3,1,0,2:T(4,128)S(1)}, f32[8,3,8,256]{3,1,0,2:T(4,128)S(1)}, u32[]{:S(2)}, u32[]{:S(2)}) collective-permute-start(f32[8,3,8,256]{3,1,0,2:T(4,128)S(1)} %broadcast_select_fusion.6), channel_id=1, source_target_pairs={{0,16},{2,17},{4,18},{6,19},{8,20},{10,21},{12,22},{14,23},{16,24}... | collective-permute-start | bytes 589832 | tf_op jit(solution)/shard_map/ppermute | solution.py:224
  180.1 10.1 %collective-permute-start.19 = (f32[8,3,8,256]{3,1,0,2:T(4,128)S(1)}, f32[8,3,8,256]{3,1,0,2:T(4,128)S(1)}, u32[]{:S(2)}, u32[]{:S(2)}) collective-permute-start(f32[8,3,8,256]{3,1,0,2:T(4,128)S(1)} %broadcast_select_fusion.6), channel_id=1, source_target_pairs={{31,0},{1,1},{3,2},{5,3},{7,4},{9,5},{11,6},{13,7},{15,8},{17,9},{... | collective-permute-start | bytes 589832 | tf_op jit(solution)/shard_map/ppermute | solution.py:224
  180.8 20.6 %collective-permute-start.20 = (f32[8,3,8,256]{3,1,0,2:T(4,128)S(1)}, f32[8,3,8,256]{3,1,0,2:T(4,128)S(1)}, u32[]{:S(2)}, u32[]{:S(2)}) collective-permute-start(f32[8,3,8,256]{3,1,0,2:T(4,128)S(1)} %broadcast_select_fusion.6), channel_id=1, source_target_pairs={{31,16},{1,17},{3,18},{5,19},{7,20},{9,21},{11,22},{13,23},{15,24}... | collective-permute-start | bytes 589832 | tf_op jit(solution)/shard_map/ppermute | solution.py:224
